TPU v7x, 32 devices: a whole 2x2x4 slice. The times are simulated.
32 devices in a mesh: ctx: 8 (over z, y), seq: 4 (over x, core).
Axes of the slice: x: 2, y: 2, z: 4, core: 2. Of those that a mesh axis runs over, the one named last changes fastest.
Arguments:
- tokens: bfloat16 [16384, 1024], P(('ctx', 'seq')), may hold values from -60 to 60
- w_qkv: bfloat16 [1024, 3072], replicated, may hold values from -1 to 1
- w_out: bfloat16 [1024, 1024], replicated, may hold values from -0.1875 to 0.1875
- counts: int32 [256], replicated, may hold values from 1 to 64
- rand_seg: int32 [256, 3], replicated, may hold values from 0 to 7, all different within a row; in each aligned block of 8 rows (0 to 7, 8 to 15, ...) at most 4 rows name the same one
- rand_off: int32 [256, 3], replicated, may hold values from 0 to 7
Outputs:
- mixed: bfloat16 [16384, 1024], P(('ctx', 'seq'))
Inputs may be any that keep to these rules, and one draw needn't show every extreme that they name: `rand_seg`: each row names 3 different segments; among the 8 rows of one device no segment is named more than 4 times, a bound that some block reaches.
All inputs are finite; a program needn't handle non-finite values.
Results may differ from a plain program's by a relative error of at most 0.0045.
The roundings to bfloat16 on the way count: a program that leaves them out, or rounds other values in their place, can miss the bound.
Values may be sent and summed in bfloat16 or wider, within the bound.
No kernel may reach another device: no remote copies, remote signals or barrier semaphores. Data moves between devices by JAX's collectives and lax.ppermute only.
A program may use at most 192 MiB of HBM per device.

v0:
```python
import math

import jax
import jax.numpy as jnp
from jax import lax
from jax.sharding import PartitionSpec as P

HD = 64
BLK = 64
RAND = 3
G_DEV = 8


def with_halo(block, sides, width):
    for axis, dim in sides:
        count = lax.axis_size(axis)
        forward = [(i, i + 1) for i in range(count - 1)]
        backward = [(target, source) for source, target in forward]
        low = lax.ppermute(
            lax.slice_in_dim(block, block.shape[dim] - width, None, axis=dim), axis, forward
        )
        high = lax.ppermute(lax.slice_in_dim(block, 0, width, axis=dim), axis, backward)
        block = jnp.concatenate([low, block, high], axis=dim)
    return block


def for_sending(x):

    def short(part):
        return part.astype(jnp.bfloat16) if part.dtype == jnp.float32 else part

    return jax.tree.map(short, x)


def attend(queries, nearby, distant, global_k, global_v, block_ids, far_ids, counts):
    span, block_len, head_count, head_dim = queries.shape
    width = head_count * head_dim
    block_total = counts.shape[0]
    scaling = 1.0 / math.sqrt(head_dim)
    key_parts = []
    value_parts = []
    part_counts = []
    for offset in range(3):
        piece = nearby[offset : offset + span]
        near_ids = block_ids + (offset - 1)
        existing = (near_ids >= 0) & (near_ids < block_total)
        part_counts.append(
            jnp.where(existing, jnp.take(counts, jnp.clip(near_ids, 0, block_total - 1)), 0)
        )
        key_parts.append(piece[..., :width].reshape(span, block_len, head_count, head_dim))
        value_parts.append(piece[..., width:].reshape(span, block_len, head_count, head_dim))
    for index in range(distant.shape[1]):
        piece = distant[:, index]
        part_counts.append(jnp.take(counts, far_ids[:, index]))
        key_parts.append(piece[..., :width].reshape(span, block_len, head_count, head_dim))
        value_parts.append(piece[..., width:].reshape(span, block_len, head_count, head_dim))
    positions = jnp.arange(block_len, dtype=jnp.int32)[None, None, None, :]
    score_parts = []
    for keys_now, count_now in zip(key_parts, part_counts):
        scores = (
            jnp.einsum("bqhd,bkhd->bhqk", queries, keys_now, preferred_element_type=jnp.float32)
            * scaling
        )
        score_parts.append(jnp.where(positions < count_now[:, None, None, None], scores, -jnp.inf))
    wide_scores = (
        jnp.einsum("bqhd,khd->bhqk", queries, global_k, preferred_element_type=jnp.float32)
        * scaling
    )
    peak_score = jnp.max(wide_scores, axis=-1)
    for scores in score_parts:
        peak_score = jnp.maximum(peak_score, jnp.max(scores, axis=-1))
    peak_score = peak_score[..., None]
    wide_exp = jnp.exp(wide_scores - peak_score)
    denominator = jnp.sum(wide_exp, axis=-1, keepdims=True)
    exp_parts = []
    for scores in score_parts:
        exps = jnp.exp(scores - peak_score)
        denominator = denominator + jnp.sum(exps, axis=-1, keepdims=True)
        exp_parts.append(exps)
    wide_prob = (wide_exp / denominator).astype(jnp.bfloat16)
    result = jnp.einsum("bhqk,khd->bqhd", wide_prob, global_v, preferred_element_type=jnp.float32)
    for exps, values_now in zip(exp_parts, value_parts):
        probs = (exps / denominator).astype(jnp.bfloat16)
        result = result + jnp.einsum(
            "bhqk,bkhd->bqhd", probs, values_now, preferred_element_type=jnp.float32
        )
    return result.astype(jnp.bfloat16)


def positions_among(owners, owner_count):
    marks = (owners[..., None] == jnp.arange(owner_count, dtype=jnp.int32)).astype(jnp.int32)
    ranks = jnp.cumsum(marks, axis=-2) - 1
    return jnp.sum(ranks * marks, axis=-1)


def serve_slots(owners, offsets, target, capacity):
    matched = owners == target
    ranks = jnp.cumsum(matched.astype(jnp.int32), axis=-1) - 1
    slot_hit = matched[..., None, :] & (
        ranks[..., None, :] == jnp.arange(capacity, dtype=jnp.int32)[:, None]
    )
    return jnp.sum(jnp.where(slot_hit, offsets[..., None, :], 0), axis=-1)


def run_groups(
    queries, near_blocks, distant, far_global, global_k, global_v, first_id, span, counts
):
    block_count = queries.shape[0]

    def one_group(start):
        group_queries = lax.dynamic_slice_in_dim(queries, start, span, 0)
        nearby = lax.dynamic_slice_in_dim(near_blocks, start, span + 2, 0)
        distant_part = lax.dynamic_slice_in_dim(distant, start, span, 0)
        far_ids = lax.dynamic_slice_in_dim(far_global, start, span, 0)
        block_ids = first_id + start + jnp.arange(span, dtype=jnp.int32)
        return attend(
            group_queries, nearby, distant_part, global_k, global_v, block_ids, far_ids, counts
        )

    starts = jnp.arange(block_count // span, dtype=jnp.int32) * span
    outputs = lax.map(one_group, starts)
    return outputs.reshape(block_count * queries.shape[1], -1)


def regroup(w_qkv, groups, head_total):
    model_dim = w_qkv.shape[0]
    shaped = w_qkv.reshape(model_dim, groups, head_total // groups, 3, HD)
    return jnp.transpose(shaped, (0, 1, 3, 2, 4)).reshape(model_dim, 3 * model_dim)


def local(tokens, w_qkv, w_out, counts, rand_seg, rand_off):
    seq_count = lax.axis_size("seq")
    ctx_count = lax.axis_size("ctx")
    seq_index = lax.axis_index("seq")
    ctx_index = lax.axis_index("ctx")
    tok_rows, model_dim = tokens.shape
    head_total = model_dim // HD
    head_local = head_total // seq_count
    seg_rows = tok_rows * seq_count
    seg_blocks = seg_rows // BLK
    dev_blocks = tok_rows // BLK
    local_width = head_local * HD
    capacity = (RAND * dev_blocks + ctx_count - 1) // ctx_count + 1
    first_block = (ctx_index * seq_count + seq_index) * dev_blocks
    own_counts = lax.dynamic_slice_in_dim(counts, first_block, dev_blocks)
    usable = (jnp.arange(BLK, dtype=jnp.int32)[None, :] < own_counts[:, None]).reshape(tok_rows)
    group_rows = tok_rows // G_DEV
    member = (
        jnp.arange(tok_rows, dtype=jnp.int32)[None, :] // group_rows
        == jnp.arange(G_DEV, dtype=jnp.int32)[:, None]
    )
    pooling = (member & usable[None, :]).astype(jnp.bfloat16)
    sums = jnp.dot(pooling, tokens, preferred_element_type=jnp.float32)
    pooled = sums / jnp.sum(pooling.astype(jnp.float32), axis=1, keepdims=True)
    summary = (pooled / jnp.sqrt(jnp.mean(pooled * pooled, axis=1, keepdims=True) + 1e-05)).astype(
        jnp.bfloat16
    )
    w_summary = w_qkv.reshape(model_dim, head_total, 3, HD)[:, :, 1:, :].reshape(
        model_dim, 2 * model_dim
    )
    summary_kv = jnp.dot(summary, w_summary, preferred_element_type=jnp.float32).astype(
        jnp.bfloat16
    )
    every_head = lax.all_gather(summary_kv, ("ctx", "seq"), axis=0, tiled=True)
    summary_heads = every_head.reshape(-1, head_total, 2, HD)
    all_owner = rand_seg.reshape(ctx_count, seq_count, dev_blocks * RAND)
    all_offset = rand_off.reshape(ctx_count, seq_count, dev_blocks * RAND)
    w_ordered = regroup(w_qkv, seq_count, head_total)
    qkv = jnp.dot(tokens, w_ordered, preferred_element_type=jnp.float32).astype(jnp.bfloat16)
    seg_qkv = lax.all_to_all(qkv, "seq", split_axis=1, concat_axis=0, tiled=True)
    my_heads = lax.dynamic_slice_in_dim(summary_heads, seq_index * head_local, head_local, 1)
    global_k = my_heads[:, :, 0, :]
    global_v = my_heads[:, :, 1, :]
    queries = seg_qkv[:, :local_width].reshape(seg_blocks, BLK, head_local, HD)
    own_kv = seg_qkv[:, local_width:]
    kv_cols = 2 * local_width
    rimmed = with_halo(own_kv, (("ctx", 0),), BLK)
    near_blocks = rimmed.reshape(seg_blocks + 2, BLK, kv_cols)
    seg_first = ctx_index * seg_blocks
    my_owner = lax.dynamic_slice_in_dim(rand_seg, seg_first, seg_blocks)
    my_offset = lax.dynamic_slice_in_dim(rand_off, seg_first, seg_blocks)
    block_rows = own_kv.reshape(seg_blocks, BLK * kv_cols)
    send_off = serve_slots(all_owner, all_offset, ctx_index, capacity)
    send_ids = send_off + (jnp.arange(seq_count, dtype=jnp.int32) * dev_blocks)[None, :, None]
    outgoing = jnp.take(block_rows, send_ids.reshape(-1), axis=0).reshape(
        ctx_count, seq_count * capacity, BLK * kv_cols
    )
    incoming = lax.all_to_all(outgoing, "ctx", split_axis=0, concat_axis=0, tiled=True)
    mine = my_owner.reshape(seq_count, dev_blocks * RAND)
    slot_ids = (
        mine * (seq_count * capacity)
        + jnp.arange(seq_count, dtype=jnp.int32)[:, None] * capacity
        + positions_among(mine, ctx_count)
    )
    fetched = jnp.take(
        incoming.reshape(ctx_count * seq_count * capacity, BLK * kv_cols),
        slot_ids.reshape(-1),
        axis=0,
    )
    distant = fetched.reshape(seg_blocks, RAND, BLK, kv_cols)
    slot_of_row = jnp.arange(seg_blocks, dtype=jnp.int32) // dev_blocks
    far_global = my_owner * seg_blocks + (slot_of_row * dev_blocks)[:, None] + my_offset
    attended = run_groups(
        queries, near_blocks, distant, far_global, global_k, global_v, seg_first, 8, counts
    )
    returned = lax.all_to_all(
        for_sending(attended), "seq", split_axis=0, concat_axis=1, tiled=True
    ).astype(attended.dtype)
    mixed = tokens.astype(jnp.float32) + jnp.dot(
        returned, w_out, preferred_element_type=jnp.float32
    )
    return mixed.astype(jnp.bfloat16)


def solution(mesh):
    in_specs = (P(("ctx", "seq"), None), P(), P(), P(), P(), P())
    out_specs = P(("ctx", "seq"), None)
    return jax.shard_map(local, mesh=mesh, in_specs=in_specs, out_specs=out_specs, check_vma=False)
```

profile of v0, /device:TPU:16, one launch (start us, length us, event | category | flops | bytes accessed | tf_op | source)
XLA Modules:
  0.0 728.4 jit_solution(17863630455531703478)
XLA Ops:
  6.5 8.8 %copy.355 = bf16[1024,3072]{0,1:T(8,128)(2,1)} copy(bf16[1024,3072]{1,0:T(8,128)(2,1)} %param.11) | data formatting | bytes 12582912 | tf_op args[1]
  15.4 3.6 copy.356
  19.0 3.7 convolution_convert_fusion
  24.6 4.8 all-to-all-start
  31.7 34.7 %all-to-all-done = bf16[512,4,768]{2,0,1:T(8,128)(2,1)} async-done(((bf16[512,4,768]{2,0,1:T(8,128)(2,1)}), bf16[512,4,768]{2,0,1:T(8,128)(2,1)}, u32[]{:S(2)}, u32[]{:S(2)}) %all-to-all-start) | async-done | bytes 3145760 | tf_op jit(solution)/shard_map/all_to_all | solution.py:170
  69.4 4.5 reshape.469
  73.9 31.8 %gather_fusion.6 = bf16[128,32768]{1,0:T(8,128)(2,1)} fusion(bf16[32,32768]{1,0:T(8,128)(2,1)} %reshape.469, s32[1024]{0:T(1024)S(1)} %pad_clamp_fusion.7), kind=kCustom, calls=%fused_computation.6 | custom fusion | bytes 16777728 | tf_op jit(solution)/shard_map/jit(_take)/gather | solution.py:185
  105.7 7.5 %broadcast_select_fusion = bf16[8,16,32768]{2,1,0:T(8,128)(2,1)} fusion(bf16[8,16,32768]{2,1,0:T(8,128)(2,1)} %bitcast.152, pred[8,16]{1,0:T(8,128)(4,1)S(1)} %compare_and_fusion), kind=kLoop, calls=%fused_computation.141 | loop fusion | flops 4194304 | bytes 16777344 | tf_op jit(solution)/shard_map/jit(_take)/select_n | solution.py:185
  113.1 6.2 all-to-all-start.1
  119.3 5.0 slice.116
  125.0 4.0 convolution_convert_fusion.1
  130.6 189.5 %all-gather.2.cloned.1.call-done = bf16[256,2048]{1,0:T(8,128)(2,1)} async-done(((bf16[8,2048]{1,0:T(8,128)(2,1)}), bf16[256,2048]{1,0:T(8,128)(2,1)}) %all-gather.2.cloned.1.call-update) | async-done | bytes 1048592 | tf_op jit(solution)/shard_map/all_gather | solution.py:164
  322.4 3.8 collective-permute-start.1
  336.4 17.1 %gather_fusion.7 = bf16[96,32768]{1,0:T(8,128)(2,1)} fusion(bf16[128,32768]{1,0:T(8,128)(2,1)} %bitcast.34, s32[1024]{0:T(1024)S(1)} %pad_clamp_fusion.6), kind=kCustom, calls=%fused_computation.7 | custom fusion | bytes 12583296 | tf_op jit(solution)/shard_map/jit(_take)/gather | solution.py:195
  353.4 5.3 copy.401
  358.7 3.3 copy_select_fusion
  362.0 335.4 %while.10 = (s32[]{:T(128)}, bf16[4,8,64,4,64]{2,1,4,3,0:T(8,128)(2,1)}, s32[4]{0:T(128)S(1)}, bf16[32,64,4,64]{3,2,1,0:T(4,128)(2,1)}, bf16[256,4,64]{0,2,1:T(8...) while((s32[]{:T(128)}, ...), condition=%wide.region_21.23_spmd, body=%wide.region_6.22_spmd.sunk | while | flops 347477696 | bytes 71337048 | solution.py:121
  394.5 3.3 fusion.129
  406.7 3.2 fusion.132
  415.3 3.3 fusion.134
  478.3 3.3 fusion.129
  490.5 3.2 fusion.132
  499.1 3.3 fusion.134
  562.1 3.3 fusion.129
  574.3 3.2 fusion.132
  582.9 3.3 fusion.134
  645.8 3.3 fusion.129
  652.0 3.2 fusion.131
  658.0 3.2 fusion.132
  666.6 3.3 fusion.134
  700.7 17.0 %all_to_all.43 = bf16[4,512,256]{1,2,0:T(8,128)(2,1)S(1)} all-to-all(bf16[4,512,256]{1,2,0:T(8,128)(2,1)S(1)} %all_to_all.36), channel_id=1, replica_groups=mesh['ctx'=8,'seq'=4] {'seq'}, dimensions={0} | all-to-all | bytes 2097152 | tf_op jit(solution)/shard_map/all_to_all | solution.py:206
  717.7 3.5 add_convert_fusion
  (483 shorter events, 301.9 us)
Async XLA Ops:
  6.5 711.1 %copy-start = (bf16[1024,1024]{1,0:T(8,128)(2,1)S(1)}, bf16[1024,1024]{1,0:T(8,128)(2,1)}, u32[]{:S(2)}) copy-start(bf16[1024,1024]{1,0:T(8,128)(2,1)} %param.12) | copy-start | bytes 6291460
  15.4 3.6 copy-start.12
  24.6 4.8 copy-start.22
  24.6 5.1 copy-start.21
  24.6 41.8 %all-to-all-start = ((bf16[512,4,768]{2,0,1:T(8,128)(2,1)}), bf16[512,4,768]{2,0,1:T(8,128)(2,1)}, u32[]{:S(2)}, u32[]{:S(2)}) async-start(bf16[512,4,768]{2,0,1:T(8,128)(2,1)} %bitcast.156), calls=%async_computation | async-start | bytes 6291456 | tf_op jit(solution)/shard_map/all_to_all | solution.py:170
  30.8 43.1 %copy-start.23 = (s32[4]{0:T(128)}, s32[4]{0:T(128)S(1)}, u32[]{:S(2)}) copy-start(s32[4]{0:T(128)S(1)} %iota_multiply_fusion.1) | copy-start | bytes 52
  113.1 223.3 %all-to-all-start.1 = ((bf16[8,16,32768]{2,1,0:T(8,128)(2,1)}), bf16[8,16,32768]{2,1,0:T(8,128)(2,1)}, u32[]{:S(2)}, u32[]{:S(2)}) async-start(bf16[8,16,32768]{2,1,0:T(8,128)(2,1)} %broadcast_select_fusion), calls=%async_computation.1 | async-start | bytes 16777216 | tf_op jit(solution)/shard_map/all_to_all | solution.py:188
  119.3 200.7 %all-gather.2.cloned.1.call-start = ((), (), s32[]{:S(2)}) async-start(), calls=%async_computation.3 | async-start | bytes 1081344 | tf_op jit(solution)/shard_map/all_gather | solution.py:164
  119.3 5.0 copy-start.1
  322.4 9.7 %collective-permute-start.1 = (bf16[64,512]{1,0:T(8,128)(2,1)S(1)}, bf16[64,512]{1,0:T(8,128)(2,1)S(1)}, u32[]{:S(2)}, u32[]{:S(2)}) collective-permute-start(bf16[64,512]{1,0:T(8,128)(2,1)S(1)} %get-tuple-element.218), channel_id=1, source_target_pairs={{4,0},{8,4},{12,8},{16,12},{20,16},{24,20},{28,24},{5,1},{9,5},{13... | collective-permute-start | bytes 196616 | tf_op jit(solution)/shard_map/ppermute | solution.py:22
  326.2 7.1 collective-permute-start
  394.4 3.4 copy-start.7
  394.4 6.2 copy-start.20
  398.6 7.4 %copy-start.19 = (s32[8]{0:T(128)S(1)}, s32[8]{0:T(128)}, u32[]{:S(2)}) copy-start(s32[8]{0:T(128)} %get-tuple-element.360) | copy-start | bytes 100 | tf_op jit(solution)/shard_map/while
  423.8 4.0 copy-start.9
  438.4 4.6 copy-start.10
  478.2 3.4 copy-start.7
  478.2 6.2 copy-start.20
  482.4 7.4 %copy-start.19 = (s32[8]{0:T(128)S(1)}, s32[8]{0:T(128)}, u32[]{:S(2)}) copy-start(s32[8]{0:T(128)} %get-tuple-element.360) | copy-start | bytes 100 | tf_op jit(solution)/shard_map/while
  499.1 3.3 copy-start.2
  507.6 4.0 copy-start.9
  522.2 4.6 copy-start.10
  562.0 3.4 copy-start.7
  562.0 6.2 copy-start.20
  566.1 7.4 %copy-start.19 = (s32[8]{0:T(128)S(1)}, s32[8]{0:T(128)}, u32[]{:S(2)}) copy-start(s32[8]{0:T(128)} %get-tuple-element.360) | copy-start | bytes 100 | tf_op jit(solution)/shard_map/while
  591.3 4.0 copy-start.9
  605.9 4.6 copy-start.10
  645.7 3.4 copy-start.7
  645.7 6.2 copy-start.20
  649.9 7.4 %copy-start.19 = (s32[8]{0:T(128)S(1)}, s32[8]{0:T(128)}, u32[]{:S(2)}) copy-start(s32[8]{0:T(128)} %get-tuple-element.360) | copy-start | bytes 100 | tf_op jit(solution)/shard_map/while
  675.1 4.0 copy-start.9
  689.7 4.6 copy-start.10
  (56 other events, 108.5 us)
Sparse Core Ops, SparseCore 0:
  129.1 190.8 all-gather.1
where the time goes:
time: 737 us; the launch traced here: 728 us
  local copies, waits for them, and re-layouts  229 us (31%)
  waiting for transfers between devices  225 us (31%)
  matrix products  149 us (20%)
  other arithmetic  61.5 us (8%)
  blocking collectives  17 us (2%)
  starting transfers between devices  16.8 us (2%)
  loops' own time  16 us (2%)
  between operations  14 us (2%)
    all_gather x1, waiting for transfers between devices, local(): every_head = lax.all_gather(summary_kv, ('ctx', 'seq'), axis=0, tiled=True)  189 us
    dot_general x24, matrix products, attend(): jnp.einsum('bqhd,bkhd->bhqk', queries, keys_now, preferred_element_type=j...  67.6 us
    dot_general x24, matrix products, attend(): jnp.einsum('bhqk,bkhd->bqhd', probs, values_now, preferred_element_type=j...  53.1 us
    reshape x24, local copies, waits for them, and re-layouts, attend(): piece[..., :width].reshape(span, block_len, head_count, head_dim)  41.3 us
    all_to_all x1, waiting for transfers between devices, local(): lax.all_to_all(qkv, 'seq', split_axis=1, concat_axis=0, tiled=True)  34.7 us
    gather x1, local copies, waits for them, and re-layouts, local(): jnp.take(block_rows, send_ids.reshape(-1), axis=0)  31.8 us
    reshape x24, local copies, waits for them, and re-layouts, attend(): piece[..., width:].reshape(span, block_len, head_count, head_dim)  31.4 us
    gather x1, local copies, waits for them, and re-layouts, local(): jnp.take(incoming.reshape(ctx_count * seq_count * capacity, BLK * kv_cols...  17.1 us
  transfers between devices with their start and end apart: 5, of which 3 were waited for; matrix products, arithmetic and copies ran while one was open for 3% of the time, Pallas kernels for 0%

commit v1 on v0

v1 whole, which is shorter than its diff:
```python
import math

import jax
import jax.numpy as jnp
from jax import lax
from jax.experimental import pallas as pl
from jax.experimental.pallas import tpu as pltpu
from jax.sharding import PartitionSpec as P

HD = 64
BLK = 64
RAND = 3
LANES = 128


def positions_among(owners, owner_count):
    marks = (owners[..., None] == jnp.arange(owner_count, dtype=jnp.int32)).astype(jnp.int32)
    ranks = jnp.cumsum(marks, axis=-2) - 1
    return jnp.sum(ranks * marks, axis=-1)


def serve_slots(owners, offsets, target, capacity):
    matched = owners == target
    ranks = jnp.cumsum(matched.astype(jnp.int32), axis=-1) - 1
    slot_hit = matched[..., None, :] & (
        ranks[..., None, :] == jnp.arange(capacity, dtype=jnp.int32)[:, None]
    )
    return jnp.sum(jnp.where(slot_hit, offsets[..., None, :], 0), axis=-1)


def split_weights(w_qkv, head_total):
    model_dim = w_qkv.shape[0]
    shaped = w_qkv.reshape(model_dim, head_total, 3, HD)
    return [shaped[:, :, j, :].reshape(model_dim, head_total * HD) for j in range(3)]


def attention_kernel(
    mask_ref, q_ref, kp_ref, kc_ref, kn_ref, vp_ref, vc_ref, vn_ref, kf_ref, vf_ref, ks_ref, vs_ref,
    o_ref,
):
    width = q_ref.shape[-1]
    rows = q_ref.shape[1]
    scaling = 1.0 / math.sqrt(HD)
    valid = mask_ref[0] != 0
    lane = lax.broadcasted_iota(jnp.int32, (rows, LANES), 1)
    low = lane < HD
    far_count = kf_ref.shape[1]
    contract = (((1,), (1,)), ((), ()))
    for tile in range(width // LANES):
        cols = pl.ds(tile * LANES, LANES)
        q = q_ref[0, :, cols]
        k_local = jnp.concatenate(
            [kp_ref[0, :, cols], kc_ref[0, :, cols], kn_ref[0, :, cols]]
            + [kf_ref[0, j, :, cols] for j in range(far_count)],
            axis=0,
        )
        v_local = jnp.concatenate(
            [vp_ref[0, :, cols], vc_ref[0, :, cols], vn_ref[0, :, cols]]
            + [vf_ref[0, j, :, cols] for j in range(far_count)],
            axis=0,
        )
        k_sum = ks_ref[:, cols]
        v_sum = vs_ref[:, cols]
        halves = []
        for part in (low, jnp.logical_not(low)):
            q_head = jnp.where(part, q, jnp.zeros_like(q))
            near = lax.dot_general(q_head, k_local, contract, preferred_element_type=jnp.float32)
            near = jnp.where(valid, near * scaling, -jnp.inf)
            wide = lax.dot_general(q_head, k_sum, contract, preferred_element_type=jnp.float32)
            wide = wide * scaling
            peak = jnp.maximum(
                jnp.max(near, axis=-1, keepdims=True), jnp.max(wide, axis=-1, keepdims=True)
            )
            near_exp = jnp.exp(near - peak)
            wide_exp = jnp.exp(wide - peak)
            denominator = jnp.sum(near_exp, axis=-1, keepdims=True) + jnp.sum(
                wide_exp, axis=-1, keepdims=True
            )
            inverse = 1.0 / denominator
            near_prob = (near_exp * inverse).astype(jnp.bfloat16)
            wide_prob = (wide_exp * inverse).astype(jnp.bfloat16)
            result = jnp.dot(near_prob, v_local, preferred_element_type=jnp.float32)
            result = result + jnp.dot(wide_prob, v_sum, preferred_element_type=jnp.float32)
            halves.append(result)
        o_ref[0, :, cols] = jnp.where(low, halves[0], halves[1]).astype(o_ref.dtype)


def attend(mask, q, k_ext, v_ext, k_far, v_far, k_sum, v_sum):
    blocks, rows, width = q.shape
    far_count = k_far.shape[1]
    keys = k_sum.shape[0]
    block = lambda offset: pl.BlockSpec((1, rows, width), lambda i: (i + offset, 0, 0))
    far_spec = pl.BlockSpec((1, far_count, rows, width), lambda i: (i, 0, 0, 0))
    whole = pl.BlockSpec((keys, width), lambda i: (0, 0))
    local_keys = (3 + far_count) * rows
    heads = width // HD
    flops = blocks * heads * 2 * 2 * rows * 2 * HD * (local_keys + keys)
    bytes_accessed = 2 * (
        blocks * rows * width * (2 + 2 * 3 + 2 * far_count) + 2 * keys * width
    ) + 4 * blocks * local_keys
    return pl.pallas_call(
        attention_kernel,
        grid=(blocks,),
        in_specs=[
            pl.BlockSpec((1, 1, local_keys), lambda i: (i, 0, 0)),
            block(0),
            block(0),
            block(1),
            block(2),
            block(0),
            block(1),
            block(2),
            far_spec,
            far_spec,
            whole,
            whole,
        ],
        out_specs=block(0),
        out_shape=jax.ShapeDtypeStruct((blocks, rows, width), jnp.bfloat16),
        cost_estimate=pl.CostEstimate(
            flops=flops,
            transcendentals=blocks * heads * rows * (local_keys + keys),
            bytes_accessed=bytes_accessed,
        ),
    )(mask, q, k_ext, k_ext, k_ext, v_ext, v_ext, v_ext, k_far, v_far, k_sum, v_sum)


def local(tokens, w_qkv, w_out, counts, rand_seg, rand_off):
    seq_count = lax.axis_size("seq")
    ctx_count = lax.axis_size("ctx")
    seq_index = lax.axis_index("seq")
    ctx_index = lax.axis_index("ctx")
    dev_count = seq_count * ctx_count
    dev_index = ctx_index * seq_count + seq_index
    tok_rows, model_dim = tokens.shape
    head_total = model_dim // HD
    dev_blocks = tok_rows // BLK
    seg_blocks = dev_blocks * seq_count
    block_total = counts.shape[0]
    capacity = (RAND * dev_blocks + ctx_count - 1) // ctx_count + 1
    first_block = dev_index * dev_blocks
    token_blocks = tokens.reshape(dev_blocks, BLK, model_dim)

    all_owner = rand_seg.reshape(ctx_count, seq_count, dev_blocks * RAND)
    all_offset = rand_off.reshape(ctx_count, seq_count, dev_blocks * RAND)
    col_owner = lax.dynamic_index_in_dim(all_owner, seq_index, axis=1, keepdims=False)
    col_offset = lax.dynamic_index_in_dim(all_offset, seq_index, axis=1, keepdims=False)
    send_off = serve_slots(col_owner, col_offset, ctx_index, capacity)
    outgoing = jnp.take(token_blocks, send_off.reshape(-1), axis=0).reshape(
        ctx_count, capacity, BLK, model_dim
    )
    incoming = lax.all_to_all(outgoing, "ctx", split_axis=0, concat_axis=0, tiled=True)
    forward = [(i, i + 1) for i in range(dev_count - 1)]
    backward = [(i + 1, i) for i in range(dev_count - 1)]
    prev_tokens = lax.ppermute(token_blocks[dev_blocks - 1], ("ctx", "seq"), forward)
    next_tokens = lax.ppermute(token_blocks[0], ("ctx", "seq"), backward)

    usable = jnp.arange(BLK, dtype=jnp.int32)[None, :] < lax.dynamic_slice_in_dim(
        counts, first_block, dev_blocks
    )[:, None]
    weighted = jnp.where(usable[:, :, None], token_blocks.astype(jnp.float32), 0.0)
    sums = jnp.sum(weighted, axis=1)
    members = jnp.sum(usable.astype(jnp.float32), axis=1)
    pooled = sums / members[:, None]
    summary = (pooled / jnp.sqrt(jnp.mean(pooled * pooled, axis=1, keepdims=True) + 1e-05)).astype(
        jnp.bfloat16
    )
    summary_all = lax.all_gather(summary, ("ctx", "seq"), axis=0, tiled=True)

    w_q, w_k, w_v = split_weights(w_qkv, head_total)
    project = lambda x, w: jnp.dot(x, w, preferred_element_type=jnp.float32).astype(jnp.bfloat16)
    q_own = project(tokens, w_q).reshape(dev_blocks, BLK, model_dim)
    k_own = project(tokens, w_k).reshape(dev_blocks, BLK, model_dim)
    v_own = project(tokens, w_v).reshape(dev_blocks, BLK, model_dim)
    k_sum = project(summary_all, w_k)
    v_sum = project(summary_all, w_v)

    my_owner = lax.dynamic_slice_in_dim(rand_seg, first_block, dev_blocks)
    my_offset = lax.dynamic_slice_in_dim(rand_off, first_block, dev_blocks)
    mine = my_owner.reshape(dev_blocks * RAND)
    slot_ids = mine * capacity + positions_among(mine, ctx_count)
    fetched = jnp.take(
        incoming.reshape(ctx_count * capacity, BLK, model_dim), slot_ids, axis=0
    )
    extra = jnp.concatenate([fetched, prev_tokens[None], next_tokens[None]], axis=0).reshape(
        -1, model_dim
    )
    k_extra = project(extra, w_k).reshape(-1, BLK, model_dim)
    v_extra = project(extra, w_v).reshape(-1, BLK, model_dim)
    far_blocks = dev_blocks * RAND
    k_far = k_extra[:far_blocks].reshape(dev_blocks, RAND, BLK, model_dim)
    v_far = v_extra[:far_blocks].reshape(dev_blocks, RAND, BLK, model_dim)
    k_ext = jnp.concatenate([k_extra[far_blocks : far_blocks + 1], k_own, k_extra[far_blocks + 1 :]])
    v_ext = jnp.concatenate([v_extra[far_blocks : far_blocks + 1], v_own, v_extra[far_blocks + 1 :]])

    block_ids = first_block + jnp.arange(dev_blocks, dtype=jnp.int32)
    near_ids = block_ids[:, None] + jnp.arange(-1, 2, dtype=jnp.int32)[None, :]
    existing = (near_ids >= 0) & (near_ids < block_total)
    near_counts = jnp.where(existing, jnp.take(counts, jnp.clip(near_ids, 0, block_total - 1)), 0)
    far_global = my_owner * seg_blocks + seq_index * dev_blocks + my_offset
    far_counts = jnp.take(counts, far_global)
    key_counts = jnp.concatenate([near_counts, far_counts], axis=1)
    mask = (jnp.arange(BLK, dtype=jnp.int32)[None, None, :] < key_counts[:, :, None]).astype(
        jnp.int32
    )
    mask = mask.reshape(dev_blocks, 1, -1)

    attended = attend(mask, q_own, k_ext, v_ext, k_far, v_far, k_sum, v_sum).reshape(
        tok_rows, model_dim
    )
    mixed = tokens.astype(jnp.float32) + jnp.dot(attended, w_out, preferred_element_type=jnp.float32)
    return mixed.astype(jnp.bfloat16)


def solution(mesh):
    in_specs = (P(("ctx", "seq"), None), P(), P(), P(), P(), P())
    out_specs = P(("ctx", "seq"), None)
    return jax.shard_map(local, mesh=mesh, in_specs=in_specs, out_specs=out_specs, check_vma=False)
```

time: 737 us -> 237 us (0.32)
  waiting for transfers between devices: 225 us -> 0.01 us
  local copies, waits for them, and re-layouts: 229 us -> 33.2 us
  matrix products: 149 us -> 22.1 us
  blocking collectives: 17 us -> 98.6 us
  Pallas kernels: 0 us -> 54.7 us
  other arithmetic: 61.5 us -> 12.8 us
  loops' own time: 16 us -> 0 us
  between operations: 14 us -> 0.34 us
    all_gather x1 -> x0, waiting for transfers between devices: 189 us -> none  [local(): every_head = lax.all_gather(summary_kv, ('ctx', 'seq'), axis=0, tiled=True)]
    dot_general x60 -> x8, matrix products: 149 us -> 22.1 us  [the longest x7 18.7 us: local(): jnp.dot(x, w, preferred_element_type=jnp.float32).astype(jnp.bfloat16)]
    all_gather x0 -> x1, blocking collectives: none -> 98.6 us  [local(): summary_all = lax.all_gather(summary, ('ctx', 'seq'), axis=0, tiled=True)]
    reshape x50 -> x4, local copies, waits for them, and re-layouts: 79 us -> 0.37 us  [the longest x1 0.11 us: local(): all_owner = rand_seg.reshape(ctx_count, seq_count, dev_blocks * RAND)]
    gather x26 -> x6, local copies, waits for them, and re-layouts: 70.8 us -> 10.3 us  [the longest x1 4.7 us: local(): jnp.take(incoming.reshape(ctx_count * capacity, BLK, model_dim), slot_ids...]
    pallas_call x0 -> x1, Pallas kernels: none -> 54.7 us  [attend(): pl.pallas_call(attention_kernel, grid=(blocks,), in_specs=[pl.BlockSpec((...]
    all_to_all x1 -> x0, waiting for transfers between devices: 34.7 us -> none  [local(): lax.all_to_all(qkv, 'seq', split_axis=1, concat_axis=0, tiled=True)]
    slice x16 -> x6, local copies, waits for them, and re-layouts: 26.8 us -> 8.75 us  [the longest x1 4.1 us: split_weights(): shaped[:, :, j, :].reshape(model_dim, head_total * HD)]
  transfers between devices with their start and end apart: 5 -> 3, of which waited for: 3 -> 0; matrix products, arithmetic and copies ran while one was open for 3% -> 15% of each run, Pallas kernels for 0% -> 0%
where the time goes in v1:
time: 237 us; the launch traced here: 235 us
  blocking collectives  98.6 us (42%)
  Pallas kernels  54.7 us (23%)
  local copies, waits for them, and re-layouts  33.2 us (14%)
  matrix products  22.1 us (9%)
  starting transfers between devices  13.6 us (6%)
  other arithmetic  12.8 us (5%)
    all_gather x1, blocking collectives, local(): summary_all = lax.all_gather(summary, ('ctx', 'seq'), axis=0, tiled=True)  98.6 us
    pallas_call x1, Pallas kernels, attend(): pl.pallas_call(attention_kernel, grid=(blocks,), in_specs=[pl.BlockSpec((...  54.7 us
    dot_general x7, matrix products, local(): jnp.dot(x, w, preferred_element_type=jnp.float32).astype(jnp.bfloat16)  18.7 us
    unnamed x33, local copies, waits for them, and re-layouts  11.9 us
    all_to_all x1, starting transfers between devices, local(): lax.all_to_all(outgoing, 'ctx', split_axis=0, concat_axis=0, tiled=True)  6.3 us
    ppermute x1, starting transfers between devices, local(): next_tokens = lax.ppermute(token_blocks[0], ('ctx', 'seq'), backward)  5.44 us
  transfers between devices with their start and end apart: 3, of which 0 were waited for; matrix products, arithmetic and copies ran while one was open for 15% of the time, Pallas kernels for 0%

profile of v1, /device:TPU:16, one launch (start us, length us, event | category | flops | bytes accessed | tf_op | source)
XLA Modules:
  0.0 235.5 jit_solution(15207348529671655376)
XLA Ops:
  0.0 1.0 copy.29
  1.3 0.8 copy.30
  2.7 4.0 %gather_fusion = bf16[32,64,1024]{2,1,0:T(8,128)(2,1)} fusion(bf16[8,64,1024]{2,1,0:T(8,128)(2,1)} %bitcast.53, s32[1024]{0:T(1024)S(1)} %pad_clamp_fusion.1), kind=kCustom, calls=%fused_computation.2 | custom fusion | bytes 8388736 | tf_op jit(solution)/shard_map/jit(_take)/gather | solution.py:149
  6.7 4.7 %broadcast_select_fusion = bf16[8,4,64,1024]{3,2,1,0:T(8,128)(2,1)} fusion(bf16[8,4,64,1024]{3,2,1,0:T(8,128)(2,1)} %bitcast.55, pred[8,4]{1,0:T(8,128)(4,1)S(1)} %copy.36), kind=kLoop, calls=%fused_computation.4 | loop fusion | flops 2097152 | bytes 8388640 | tf_op jit(solution)/shard_map/jit(_take)/select_n | solution.py:149
  11.4 6.3 %all-to-all-start = ((bf16[8,4,64,1024]{3,2,1,0:T(8,128)(2,1)}), bf16[8,4,64,1024]{3,2,1,0:T(8,128)(2,1)}, u32[]{:S(2)}, u32[]{:S(2)}) async-start(bf16[8,4,64,1024]{3,2,1,0:T(8,128)(2,1)} %broadcast_select_fusion), calls=%async_computation | async-start | bytes 8388608 | tf_op jit(solution)/shard_map/all_to_all | solution.py:152
  17.7 0.7 fusion.7
  18.3 1.9 collective-permute-start
  20.2 5.4 %collective-permute-start.1 = (bf16[64,1024]{1,0:T(8,128)(2,1)S(1)}, bf16[64,1024]{1,0:T(8,128)(2,1)}, u32[]{:S(2)}, u32[]{:S(2)}) collective-permute-start(bf16[64,1024]{1,0:T(8,128)(2,1)S(1)} %get-tuple-element.18), channel_id=1, source_target_pairs={{1,0},{2,1},{3,2},{4,3},{5,4},{6,5},{7,6},{8,7},{9,8},{10,9},{11,1... | collective-permute-start | bytes 393224 | tf_op jit(solution)/shard_map/ppermute | solution.py:156
  25.7 0.5 copy-done.10
  27.0 0.7 dynamic_slice.20
  27.6 0.7 gather_fusion.2
  28.4 0.7 lt.97
  29.5 0.7 gather_fusion.3
  30.7 8.6 %copy.33 = bf16[1024,3072]{0,1:T(8,128)(2,1)} copy(bf16[1024,3072]{1,0:T(8,128)(2,1)} %param.9) | data formatting | bytes 12582912 | tf_op args[1]
  40.3 0.6 compare_convert_fusion.mask_ref
  41.0 98.6 %all_gather.3 = bf16[256,1024]{1,0:T(8,128)(2,1)S(1)} all-gather(bf16[8,1024]{1,0:T(8,128)(2,1)S(1)} %divide_convert_fusion), channel_id=1, replica_groups=mesh['ctx'=8,'seq'=4] {'ctx','seq'}, dimensions={0}, use_global_device_ids=true | all-gather | bytes 540672 | tf_op jit(solution)/shard_map/all_gather | solution.py:168
  139.7 4.1 %fusion.6 = (bf16[1024,16,1,64]{0,3,2,1:T(8,128)(2,1)S(1)}, bf16[1024,16,1,64]{0,3,2,1:T(8,128)(2,1)S(1)}, bf16[1024,16,1,64]{0,3,2,1:T(8,128)(2,1)S(1)}) fusion(bf16[1024,16,3,64]{0,3,2,1:T(8,128)(2,1)} %bitcast.54), kind=kLoop, calls=%fused_computation.65 | loop fusion | bytes 12582912 | tf_op jit(solution)/shard_map/slice | solution.py:34
  143.8 2.0 convolution_convert_fusion.6.ks_ref
  145.8 1.5 convolution_convert_fusion.5.vs_ref
  147.4 2.3 convolution_convert_fusion.3
  149.7 2.3 convolution_convert_fusion.2
  151.9 2.3 convolution_convert_fusion.4
  154.2 4.7 %gather_fusion.1 = bf16[24,64,1024]{2,1,0:T(8,128)(2,1)} fusion(bf16[32,64,1024]{2,1,0:T(8,128)(2,1)} %bitcast.7, s32[1024]{0:T(1024)S(1)} %pad_clamp_fusion), kind=kCustom, calls=%fused_computation.3 | custom fusion | bytes 6291552 | tf_op jit(solution)/shard_map/jit(_take)/gather | solution.py:182
  158.9 2.2 broadcast_select_fusion.1
  161.2 1.5 pad_maximum_fusion
  162.9 4.1 %convolution_convert_fusion = bf16[1664,1024]{1,0:T(8,128)(2,1)S(1)} fusion(bf16[1664,1024]{1,0:T(8,128)(2,1)S(1)} %bitcast.58, bf16[1024,1024]{0,1:T(8,128)(2,1)S(1)} %bitcast.65), kind=kOutput, calls=%fused_computation.5 | convolution fusion | flops 3491364864 | bytes 8912896 | tf_op jit(solution)/shard_map/dot_general | solution.py:171
  167.1 4.1 %convolution_convert_fusion.1 = bf16[1664,1024]{1,0:T(8,128)(2,1)S(1)} fusion(bf16[1664,1024]{1,0:T(8,128)(2,1)S(1)} %bitcast.59, bf16[1024,1024]{0,1:T(8,128)(2,1)S(1)} %bitcast.62), kind=kOutput, calls=%fused_computation.6 | convolution fusion | flops 3491364864 | bytes 8912896 | tf_op jit(solution)/shard_map/dot_general | solution.py:171
  171.2 2.0 slice.79
  173.2 2.0 slice.80
  175.4 1.8 pad_maximum_fusion.1
  177.3 54.7 %shard_map.64 = bf16[8,64,1024]{2,1,0:T(8,128)(2,1)} custom-call(s32[8,1,384]{2,1,0:T(1,128)} %compare_convert_fusion.mask_ref, bf16[8,64,1024]{2,1,0:T(8,128)(2,1)} %bitcast.67, bf16[10,64,1024]{2,1,0:T(8,128)(2,1)} %get-tuple-element.21.kp_ref.kc_ref.kn_ref, bf16[10,64,1024]{2,1,0:T(8,128)(2,1)} %get-tuple-element.21.kp_ref.kc_ref.kn_ref, ...), custom_call_target="tpu_custom_call" | custom-call | flops 2684354560 | bytes 15740928 | tf_op jit(solution)/shard_map/pallas_call | solution.py:101
  232.0 3.4 %add_convert_fusion = bf16[512,1024]{1,0:T(8,128)(2,1)} fusion(bf16[512,1024]{1,0:T(8,128)(2,1)S(1)} %copy-done.2, bf16[512,1024]{1,0:T(8,128)(2,1)} %bitcast.70, bf16[1024,1024]{1,0:T(8,128)(2,1)S(1)} %copy-done), kind=kOutput, calls=%fused_computation.9 | convolution fusion | flops 1075314688 | bytes 5242880 | tf_op jit(solution)/shard_map/dot_general | solution.py:211
  (78 shorter events, 4.1 us)
Async XLA Ops:
  0.0 232.0 %copy-start = (bf16[1024,1024]{1,0:T(8,128)(2,1)S(1)}, bf16[1024,1024]{1,0:T(8,128)(2,1)}, u32[]{:S(2)}) copy-start(bf16[1024,1024]{1,0:T(8,128)(2,1)} %param.10) | copy-start | bytes 6291460
  11.4 6.3 %copy-start.2 = (bf16[512,1024]{1,0:T(8,128)(2,1)S(1)}, bf16[512,1024]{1,0:T(8,128)(2,1)}, u32[]{:S(2)}) copy-start(bf16[512,1024]{1,0:T(8,128)(2,1)} %param.8) | copy-start | bytes 3145732
  11.4 15.6 %copy-start.1 = (s32[256]{0:T(256)S(1)}, s32[256]{0:T(256)}, u32[]{:S(2)}) copy-start(s32[256]{0:T(256)} %param.11) | copy-start | bytes 3076
  11.4 142.8 %all-to-all-start = ((bf16[8,4,64,1024]{3,2,1,0:T(8,128)(2,1)}), bf16[8,4,64,1024]{3,2,1,0:T(8,128)(2,1)}, u32[]{:S(2)}, u32[]{:S(2)}) async-start(bf16[8,4,64,1024]{3,2,1,0:T(8,128)(2,1)} %broadcast_select_fusion), calls=%async_computation | async-start | bytes 8388608 | tf_op jit(solution)/shard_map/all_to_all | solution.py:152
  18.3 142.8 %collective-permute-start = (bf16[64,1024]{1,0:T(8,128)(2,1)}, bf16[64,1024]{1,0:T(8,128)(2,1)}, u32[]{:S(2)}, u32[]{:S(2)}) collective-permute-start(bf16[64,1024]{1,0:T(8,128)(2,1)} %get-tuple-element.17), channel_id=1, source_target_pairs={{0,1},{1,2},{2,3},{3,4},{4,5},{5,6},{6,7},{7,8},{8,9},{9,10},{10,1... | collective-permute-start | bytes 393224 | tf_op jit(solution)/shard_map/ppermute | solution.py:155
  20.2 140.9 %collective-permute-start.1 = (bf16[64,1024]{1,0:T(8,128)(2,1)S(1)}, bf16[64,1024]{1,0:T(8,128)(2,1)}, u32[]{:S(2)}, u32[]{:S(2)}) collective-permute-start(bf16[64,1024]{1,0:T(8,128)(2,1)S(1)} %get-tuple-element.18), channel_id=1, source_target_pairs={{1,0},{2,1},{3,2},{4,3},{5,4},{6,5},{7,6},{8,7},{9,8},{10,9},{11,1... | collective-permute-start | bytes 393224 | tf_op jit(solution)/shard_map/ppermute | solution.py:156
  25.7 0.6 copy-start.10
  26.3 0.5 copy-start.12
  29.5 0.8 copy-start.11
  29.5 0.8 copy-start.13
  30.6 8.8 %copy-start.14 = (s32[8]{0:T(128)S(1)}, s32[8]{0:T(128)}, u32[]{:S(2)}) copy-start(s32[8]{0:T(128)} %dynamic_slice.20) | copy-start | bytes 100
  30.6 9.7 %copy-start.9 = (s32[384]{0:T(512)S(1)}, s32[384]{0:T(512)}, u32[]{:S(2)}) copy-start(s32[384]{0:T(512)} %lt.97) | copy-start | bytes 4612
  143.8 3.6 %copy-start.3 = (bf16[1024,16,1,64]{0,3,2,1:T(8,128)(2,1)}, bf16[1024,16,1,64]{0,3,2,1:T(8,128)(2,1)S(1)}, u32[]{:S(2)}) copy-start(bf16[1024,16,1,64]{0,3,2,1:T(8,128)(2,1)S(1)} %get-tuple-element.11) | copy-start | bytes 6291460
  143.8 5.9 %copy-start.5 = (bf16[1024,16,1,64]{0,3,2,1:T(8,128)(2,1)}, bf16[1024,16,1,64]{0,3,2,1:T(8,128)(2,1)S(1)}, u32[]{:S(2)}) copy-start(bf16[1024,16,1,64]{0,3,2,1:T(8,128)(2,1)S(1)} %get-tuple-element.10) | copy-start | bytes 6291460
  161.2 1.7 copy-start.6
  162.9 4.2 %copy-start.4 = (bf16[1024,16,1,64]{0,3,2,1:T(8,128)(2,1)S(1)}, bf16[1024,16,1,64]{0,3,2,1:T(8,128)(2,1)}, u32[]{:S(2)}) copy-start(bf16[1024,16,1,64]{0,3,2,1:T(8,128)(2,1)} %copy-done.3) | copy-start | bytes 6291460
  173.2 2.0 copy-start.7
  173.2 2.2 copy-start.8

commit v2 on v1

--- a/solution.py
+++ b/solution.py
@@ -61,28 +61,26 @@
         )
         k_sum = ks_ref[:, cols]
         v_sum = vs_ref[:, cols]
-        halves = []
-        for part in (low, jnp.logical_not(low)):
-            q_head = jnp.where(part, q, jnp.zeros_like(q))
-            near = lax.dot_general(q_head, k_local, contract, preferred_element_type=jnp.float32)
-            near = jnp.where(valid, near * scaling, -jnp.inf)
-            wide = lax.dot_general(q_head, k_sum, contract, preferred_element_type=jnp.float32)
-            wide = wide * scaling
-            peak = jnp.maximum(
-                jnp.max(near, axis=-1, keepdims=True), jnp.max(wide, axis=-1, keepdims=True)
-            )
-            near_exp = jnp.exp(near - peak)
-            wide_exp = jnp.exp(wide - peak)
-            denominator = jnp.sum(near_exp, axis=-1, keepdims=True) + jnp.sum(
-                wide_exp, axis=-1, keepdims=True
-            )
-            inverse = 1.0 / denominator
-            near_prob = (near_exp * inverse).astype(jnp.bfloat16)
-            wide_prob = (wide_exp * inverse).astype(jnp.bfloat16)
-            result = jnp.dot(near_prob, v_local, preferred_element_type=jnp.float32)
-            result = result + jnp.dot(wide_prob, v_sum, preferred_element_type=jnp.float32)
-            halves.append(result)
-        o_ref[0, :, cols] = jnp.where(low, halves[0], halves[1]).astype(o_ref.dtype)
+        blank = jnp.zeros_like(q)
+        q_pair = jnp.concatenate([jnp.where(low, q, blank), jnp.where(low, blank, q)], axis=0)
+        near = lax.dot_general(q_pair, k_local, contract, preferred_element_type=jnp.float32)
+        near = jnp.where(valid, near * scaling, -jnp.inf)
+        wide = lax.dot_general(q_pair, k_sum, contract, preferred_element_type=jnp.float32)
+        wide = wide * scaling
+        peak = jnp.maximum(
+            jnp.max(near, axis=-1, keepdims=True), jnp.max(wide, axis=-1, keepdims=True)
+        )
+        near_exp = jnp.exp(near - peak)
+        wide_exp = jnp.exp(wide - peak)
+        denominator = jnp.sum(near_exp, axis=-1, keepdims=True) + jnp.sum(
+            wide_exp, axis=-1, keepdims=True
+        )
+        inverse = 1.0 / denominator
+        near_prob = (near_exp * inverse).astype(jnp.bfloat16)
+        wide_prob = (wide_exp * inverse).astype(jnp.bfloat16)
+        result = jnp.dot(near_prob, v_local, preferred_element_type=jnp.float32)
+        result = result + jnp.dot(wide_prob, v_sum, preferred_element_type=jnp.float32)
+        o_ref[0, :, cols] = jnp.where(low, result[:rows], result[rows:]).astype(o_ref.dtype)
 
 
 def attend(mask, q, k_ext, v_ext, k_far, v_far, k_sum, v_sum):
@@ -94,7 +92,7 @@
     whole = pl.BlockSpec((keys, width), lambda i: (0, 0))
     local_keys = (3 + far_count) * rows
     heads = width // HD
-    flops = blocks * heads * 2 * 2 * rows * 2 * HD * (local_keys + keys)
+    flops = blocks * heads * 2 * rows * 2 * LANES * (local_keys + keys)
     bytes_accessed = 2 * (
         blocks * rows * width * (2 + 2 * 3 + 2 * far_count) + 2 * keys * width
     ) + 4 * blocks * local_keys
@@ -146,7 +144,7 @@
     col_owner = lax.dynamic_index_in_dim(all_owner, seq_index, axis=1, keepdims=False)
     col_offset = lax.dynamic_index_in_dim(all_offset, seq_index, axis=1, keepdims=False)
     send_off = serve_slots(col_owner, col_offset, ctx_index, capacity)
-    outgoing = jnp.take(token_blocks, send_off.reshape(-1), axis=0).reshape(
+    outgoing = jnp.take(token_blocks, send_off.reshape(-1), axis=0, mode="clip").reshape(
         ctx_count, capacity, BLK, model_dim
     )
     incoming = lax.all_to_all(outgoing, "ctx", split_axis=0, concat_axis=0, tiled=True)
@@ -165,13 +163,13 @@
     summary = (pooled / jnp.sqrt(jnp.mean(pooled * pooled, axis=1, keepdims=True) + 1e-05)).astype(
         jnp.bfloat16
     )
-    summary_all = lax.all_gather(summary, ("ctx", "seq"), axis=0, tiled=True)
-
     w_q, w_k, w_v = split_weights(w_qkv, head_total)
     project = lambda x, w: jnp.dot(x, w, preferred_element_type=jnp.float32).astype(jnp.bfloat16)
     q_own = project(tokens, w_q).reshape(dev_blocks, BLK, model_dim)
     k_own = project(tokens, w_k).reshape(dev_blocks, BLK, model_dim)
     v_own = project(tokens, w_v).reshape(dev_blocks, BLK, model_dim)
+    summary, q_own, k_own, v_own = lax.optimization_barrier((summary, q_own, k_own, v_own))
+    summary_all = lax.all_gather(summary, ("ctx", "seq"), axis=0, tiled=True)
     k_sum = project(summary_all, w_k)
     v_sum = project(summary_all, w_v)
 
@@ -180,7 +178,7 @@
     mine = my_owner.reshape(dev_blocks * RAND)
     slot_ids = mine * capacity + positions_among(mine, ctx_count)
     fetched = jnp.take(
-        incoming.reshape(ctx_count * capacity, BLK, model_dim), slot_ids, axis=0
+        incoming.reshape(ctx_count * capacity, BLK, model_dim), slot_ids, axis=0, mode="clip"
     )
     extra = jnp.concatenate([fetched, prev_tokens[None], next_tokens[None]], axis=0).reshape(
         -1, model_dim

time: 237 us -> 196 us (0.83)
  Pallas kernels: 54.7 us -> 31.5 us
  blocking collectives: 98.6 us -> 87.7 us
  other arithmetic: 12.8 us -> 6.91 us
    pallas_call x1, Pallas kernels: 54.7 us -> 31.5 us  [attend(): pl.pallas_call(attention_kernel, grid=(blocks,), in_specs=[pl.BlockSpec((...]
    all_gather x1, blocking collectives: 98.6 us -> 87.7 us  [local(): summary_all = lax.all_gather(summary, ('ctx', 'seq'), axis=0, tiled=True)]
    select_n x4 -> x0, other arithmetic: 6.93 us -> none  [the longest x2 4.68 us: local(): jnp.take(token_blocks, send_off.reshape(-1), axis=0)]
  transfers between devices with their start and end apart: 3 -> 3, of which waited for: 0 -> 0; matrix products, arithmetic and copies ran while one was open for 15% -> 17% of each run, Pallas kernels for 0% -> 0%
where the time goes in v2:
time: 196 us; the launch traced here: 195 us
  blocking collectives  87.7 us (45%)
  local copies, waits for them, and re-layouts  33.1 us (17%)
  Pallas kernels  31.5 us (16%)
  matrix products  21.6 us (11%)
  starting transfers between devices  13.6 us (7%)
  other arithmetic  6.91 us (4%)
    all_gather x1, blocking collectives, local(): summary_all = lax.all_gather(summary, ('ctx', 'seq'), axis=0, tiled=True)  87.7 us
    pallas_call x1, Pallas kernels, attend(): pl.pallas_call(attention_kernel, grid=(blocks,), in_specs=[pl.BlockSpec((...  31.5 us
    dot_general x7, matrix products, local(): jnp.dot(x, w, preferred_element_type=jnp.float32).astype(jnp.bfloat16)  18.2 us
    unnamed x33, local copies, waits for them, and re-layouts  11.8 us
    all_to_all x1, starting transfers between devices, local(): lax.all_to_all(outgoing, 'ctx', split_axis=0, concat_axis=0, tiled=True)  6.3 us
    ppermute x1, starting transfers between devices, local(): next_tokens = lax.ppermute(token_blocks[0], ('ctx', 'seq'), backward)  5.44 us
    gather x1, local copies, waits for them, and re-layouts, local(): jnp.take(incoming.reshape(ctx_count * capacity, BLK, model_dim), slot_ids...  4.71 us
    slice x1, local copies, waits for them, and re-layouts, split_weights(): shaped[:, :, j, :].reshape(model_dim, head_total * HD)  4.12 us
  transfers between devices with their start and end apart: 3, of which 0 were waited for; matrix products, arithmetic and copies ran while one was open for 17% of the time, Pallas kernels for 0%

profile of v2, /device:TPU:16, one launch (start us, length us, event | category | flops | bytes accessed | tf_op | source)
XLA Modules:
  0.0 194.8 jit_solution(6689039616055366719)
XLA Ops:
  0.0 1.0 copy.28
  1.3 0.8 copy.29
  2.6 4.1 %gather_fusion = bf16[32,64,1024]{2,1,0:T(8,128)(2,1)} fusion(bf16[8,64,1024]{2,1,0:T(8,128)(2,1)} %bitcast.51, s32[1024]{0:T(1024)S(1)} %pad_clamp_fusion.1), kind=kCustom, calls=%fused_computation.2 | custom fusion | bytes 8388736 | tf_op jit(solution)/shard_map/jit(_take)/gather | solution.py:147
  6.7 6.3 %all-to-all-start = ((bf16[8,4,64,1024]{3,2,1,0:T(8,128)(2,1)}), bf16[8,4,64,1024]{3,2,1,0:T(8,128)(2,1)}, u32[]{:S(2)}, u32[]{:S(2)}) async-start(bf16[8,4,64,1024]{3,2,1,0:T(8,128)(2,1)} %bitcast.53), calls=%async_computation | async-start | bytes 8388608 | tf_op jit(solution)/shard_map/all_to_all | solution.py:150
  13.0 0.7 fusion.6
  13.6 1.9 collective-permute-start
  15.5 5.4 %collective-permute-start.1 = (bf16[64,1024]{1,0:T(8,128)(2,1)S(1)}, bf16[64,1024]{1,0:T(8,128)(2,1)}, u32[]{:S(2)}, u32[]{:S(2)}) collective-permute-start(bf16[64,1024]{1,0:T(8,128)(2,1)S(1)} %get-tuple-element.26), channel_id=1, source_target_pairs={{1,0},{2,1},{3,2},{4,3},{5,4},{6,5},{7,6},{8,7},{9,8},{10,9},{11,1... | collective-permute-start | bytes 393224 | tf_op jit(solution)/shard_map/ppermute | solution.py:154
  21.0 0.5 copy-done.10
  21.6 0.5 copy-done.12
  22.2 0.6 dynamic_slice.18
  22.9 0.7 gather_fusion.2
  23.7 0.7 lt.60
  24.7 0.7 gather_fusion.3
  25.9 8.6 %copy.32 = bf16[1024,3072]{0,1:T(8,128)(2,1)} copy(bf16[1024,3072]{1,0:T(8,128)(2,1)} %param.9) | data formatting | bytes 12582912 | tf_op args[1]
  34.7 0.4 select_reduce_fusion
  35.4 4.1 %fusion.5 = (bf16[1024,16,1,64]{0,3,2,1:T(8,128)(2,1)S(1)}, bf16[1024,16,1,64]{0,3,2,1:T(8,128)(2,1)S(1)}, bf16[1024,16,1,64]{0,3,2,1:T(8,128)(2,1)S(1)}) fusion(bf16[1024,16,3,64]{0,3,2,1:T(8,128)(2,1)} %bitcast.52), kind=kLoop, calls=%fused_computation.56 | loop fusion | bytes 12582912 | tf_op jit(solution)/shard_map/slice | solution.py:34
  39.6 2.3 %convolution_convert_fusion.3 = bf16[512,1024]{1,0:T(8,128)(2,1)} fusion(bf16[512,1024]{1,0:T(8,128)(2,1)S(1)} %copy-done.2, bf16[1024,1024]{0,1:T(8,128)(2,1)S(1)} %bitcast.61), kind=kOutput, calls=%fused_computation.10 | convolution fusion | flops 1074266112 | bytes 4194304 | tf_op jit(solution)/shard_map/dot_general | solution.py:167
  41.9 2.3 %convolution_convert_fusion.2 = bf16[512,1024]{1,0:T(8,128)(2,1)} fusion(bf16[512,1024]{1,0:T(8,128)(2,1)S(1)} %copy-done.2, bf16[1024,1024]{0,1:T(8,128)(2,1)S(1)} %bitcast.58), kind=kOutput, calls=%fused_computation.9 | convolution fusion | flops 1074266112 | bytes 4194304 | tf_op jit(solution)/shard_map/dot_general | solution.py:167
  44.1 2.3 %convolution_convert_fusion.4 = bf16[512,1024]{1,0:T(8,128)(2,1)} fusion(bf16[512,1024]{1,0:T(8,128)(2,1)S(1)} %copy-done.2, bf16[1024,1024]{0,1:T(8,128)(2,1)S(1)} %bitcast.64), kind=kOutput, calls=%fused_computation.11 | convolution fusion | flops 1074266112 | bytes 4194304 | tf_op jit(solution)/shard_map/dot_general | solution.py:167
  46.6 0.6 compare_convert_fusion.mask_ref
  47.2 87.7 %all_gather.3 = bf16[256,1024]{1,0:T(8,128)(2,1)S(1)} all-gather(bf16[8,1024]{1,0:T(8,128)(2,1)S(1)} %divide_convert_fusion), channel_id=1, replica_groups=mesh['ctx'=8,'seq'=4] {'ctx','seq'}, dimensions={0}, use_global_device_ids=true | all-gather | bytes 540672 | tf_op jit(solution)/shard_map/all_gather | solution.py:172
  134.9 1.5 convolution_convert_fusion.5.vs_ref
  136.5 1.6 convolution_convert_fusion.6.ks_ref
  138.1 4.7 %gather_fusion.1 = bf16[24,64,1024]{2,1,0:T(8,128)(2,1)} fusion(bf16[32,64,1024]{2,1,0:T(8,128)(2,1)} %bitcast.10, s32[1024]{0:T(1024)S(1)} %pad_clamp_fusion), kind=kCustom, calls=%fused_computation.3 | custom fusion | bytes 6291552 | tf_op jit(solution)/shard_map/jit(_take)/gather | solution.py:180
  142.8 2.6 %pad_maximum_fusion = bf16[26,64,1024]{2,1,0:T(8,128)(2,1)S(1)} fusion(bf16[1,64,1024]{2,1,0:T(8,128)(2,1)} %bitcast.14, bf16[1,64,1024]{2,1,0:T(8,128)(2,1)} %bitcast.13, bf16[24,64,1024]{2,1,0:T(8,128)(2,1)} %gather_fusion.1), kind=kLoop, calls=%fused_computation.6 | loop fusion | flops 3407872 | bytes 6815744 | tf_op jit(solution)/shard_map/concatenate | solution.py:183
  145.5 4.1 %convolution_convert_fusion.1 = bf16[1664,1024]{1,0:T(8,128)(2,1)S(1)} fusion(bf16[1664,1024]{1,0:T(8,128)(2,1)S(1)} %bitcast.56, bf16[1024,1024]{0,1:T(8,128)(2,1)S(1)} %bitcast.63), kind=kOutput, calls=%fused_computation.5 | convolution fusion | flops 3491364864 | bytes 8912896 | tf_op jit(solution)/shard_map/dot_general | solution.py:167
  149.6 4.1 %convolution_convert_fusion = bf16[1664,1024]{1,0:T(8,128)(2,1)S(1)} fusion(bf16[1664,1024]{1,0:T(8,128)(2,1)S(1)} %bitcast.57, bf16[1024,1024]{0,1:T(8,128)(2,1)S(1)} %bitcast.60), kind=kOutput, calls=%fused_computation.4 | convolution fusion | flops 3491364864 | bytes 8912896 | tf_op jit(solution)/shard_map/dot_general | solution.py:167
  153.7 2.0 %slice.80 = bf16[1536,1024]{1,0:T(8,128)(2,1)} slice(bf16[1664,1024]{1,0:T(8,128)(2,1)S(1)} %convolution_convert_fusion), slice={[0:1536], [0:1024]} | slice | bytes 6291456 | tf_op jit(solution)/shard_map/slice | solution.py:190
  155.8 2.0 %slice.79 = bf16[1536,1024]{1,0:T(8,128)(2,1)} slice(bf16[1664,1024]{1,0:T(8,128)(2,1)S(1)} %convolution_convert_fusion.1), slice={[0:1536], [0:1024]} | slice | bytes 6291456 | tf_op jit(solution)/shard_map/slice | solution.py:189
  158.0 1.8 pad_maximum_fusion.1
  159.8 31.5 %shard_map.64 = bf16[8,64,1024]{2,1,0:T(8,128)(2,1)} custom-call(s32[8,1,384]{2,1,0:T(1,128)} %compare_convert_fusion.mask_ref, bf16[8,64,1024]{2,1,0:T(8,128)(2,1)} %bitcast.65, bf16[10,64,1024]{2,1,0:T(8,128)(2,1)} %get-tuple-element.29.kp_ref.kc_ref.kn_ref, bf16[10,64,1024]{2,1,0:T(8,128)(2,1)} %get-tuple-element.29.kp_ref.kc_ref.kn_ref, ...), custom_call_target="tpu_custom_call" | custom-call | flops 2684354560 | bytes 15740928 | tf_op jit(solution)/shard_map/pallas_call | solution.py:99
  191.3 3.5 %add_convert_fusion = bf16[512,1024]{1,0:T(8,128)(2,1)} fusion(bf16[512,1024]{1,0:T(8,128)(2,1)S(1)} %copy-done.2, bf16[512,1024]{1,0:T(8,128)(2,1)} %bitcast.68, bf16[1024,1024]{1,0:T(8,128)(2,1)S(1)} %copy-done), kind=kOutput, calls=%fused_computation.7 | convolution fusion | flops 1075314688 | bytes 5242880 | tf_op jit(solution)/shard_map/dot_general | solution.py:209
  (72 shorter events, 2.9 us)
Async XLA Ops:
  0.0 191.3 %copy-start = (bf16[1024,1024]{1,0:T(8,128)(2,1)S(1)}, bf16[1024,1024]{1,0:T(8,128)(2,1)}, u32[]{:S(2)}) copy-start(bf16[1024,1024]{1,0:T(8,128)(2,1)} %param.10) | copy-start | bytes 6291460
  6.7 6.3 %copy-start.2 = (bf16[512,1024]{1,0:T(8,128)(2,1)S(1)}, bf16[512,1024]{1,0:T(8,128)(2,1)}, u32[]{:S(2)}) copy-start(bf16[512,1024]{1,0:T(8,128)(2,1)} %param.8) | copy-start | bytes 3145732
  6.7 15.6 %copy-start.1 = (s32[256]{0:T(256)S(1)}, s32[256]{0:T(256)}, u32[]{:S(2)}) copy-start(s32[256]{0:T(256)} %param.11) | copy-start | bytes 3076
  6.7 131.4 %all-to-all-start = ((bf16[8,4,64,1024]{3,2,1,0:T(8,128)(2,1)}), bf16[8,4,64,1024]{3,2,1,0:T(8,128)(2,1)}, u32[]{:S(2)}, u32[]{:S(2)}) async-start(bf16[8,4,64,1024]{3,2,1,0:T(8,128)(2,1)} %bitcast.53), calls=%async_computation | async-start | bytes 8388608 | tf_op jit(solution)/shard_map/all_to_all | solution.py:150
  13.6 129.2 %collective-permute-start = (bf16[64,1024]{1,0:T(8,128)(2,1)}, bf16[64,1024]{1,0:T(8,128)(2,1)}, u32[]{:S(2)}, u32[]{:S(2)}) collective-permute-start(bf16[64,1024]{1,0:T(8,128)(2,1)} %get-tuple-element.25), channel_id=1, source_target_pairs={{0,1},{1,2},{2,3},{3,4},{4,5},{5,6},{6,7},{7,8},{8,9},{9,10},{10,1... | collective-permute-start | bytes 393224 | tf_op jit(solution)/shard_map/ppermute | solution.py:153
  15.5 127.3 %collective-permute-start.1 = (bf16[64,1024]{1,0:T(8,128)(2,1)S(1)}, bf16[64,1024]{1,0:T(8,128)(2,1)}, u32[]{:S(2)}, u32[]{:S(2)}) collective-permute-start(bf16[64,1024]{1,0:T(8,128)(2,1)S(1)} %get-tuple-element.26), channel_id=1, source_target_pairs={{1,0},{2,1},{3,2},{4,3},{5,4},{6,5},{7,6},{8,7},{9,8},{10,9},{11,1... | collective-permute-start | bytes 393224 | tf_op jit(solution)/shard_map/ppermute | solution.py:154
  21.0 0.6 copy-start.10
  21.6 0.5 copy-start.12
  24.7 0.8 copy-start.11
  24.7 0.8 copy-start.13
  25.9 8.6 %copy-start.14 = (s32[8]{0:T(128)S(1)}, s32[8]{0:T(128)}, u32[]{:S(2)}) copy-start(s32[8]{0:T(128)} %dynamic_slice.18) | copy-start | bytes 100
  39.5 95.4 %copy-start.3 = (bf16[1024,16,1,64]{0,3,2,1:T(8,128)(2,1)}, bf16[1024,16,1,64]{0,3,2,1:T(8,128)(2,1)S(1)}, u32[]{:S(2)}) copy-start(bf16[1024,16,1,64]{0,3,2,1:T(8,128)(2,1)S(1)} %get-tuple-element.18) | copy-start | bytes 6291460
  39.5 96.9 %copy-start.5 = (bf16[1024,16,1,64]{0,3,2,1:T(8,128)(2,1)}, bf16[1024,16,1,64]{0,3,2,1:T(8,128)(2,1)S(1)}, u32[]{:S(2)}) copy-start(bf16[1024,16,1,64]{0,3,2,1:T(8,128)(2,1)S(1)} %get-tuple-element.19) | copy-start | bytes 6291460
  44.1 2.4 %copy-start.9 = (s32[384]{0:T(512)S(1)}, s32[384]{0:T(512)}, u32[]{:S(2)}) copy-start(s32[384]{0:T(512)} %lt.60) | copy-start | bytes 4612
  142.8 2.7 %copy-start.6 = (bf16[1024,16,1,64]{0,3,2,1:T(8,128)(2,1)S(1)}, bf16[1024,16,1,64]{0,3,2,1:T(8,128)(2,1)}, u32[]{:S(2)}) copy-start(bf16[1024,16,1,64]{0,3,2,1:T(8,128)(2,1)} %copy-done.5) | copy-start | bytes 6291460
  145.5 4.1 %copy-start.4 = (bf16[1024,16,1,64]{0,3,2,1:T(8,128)(2,1)S(1)}, bf16[1024,16,1,64]{0,3,2,1:T(8,128)(2,1)}, u32[]{:S(2)}) copy-start(bf16[1024,16,1,64]{0,3,2,1:T(8,128)(2,1)} %copy-done.3) | copy-start | bytes 6291460
  155.7 2.0 %copy-start.7 = (bf16[512,1024]{1,0:T(8,128)(2,1)S(1)}, bf16[512,1024]{1,0:T(8,128)(2,1)}, u32[]{:S(2)}) copy-start(bf16[512,1024]{1,0:T(8,128)(2,1)} %convolution_convert_fusion.3) | copy-start | bytes 3145732
  155.8 2.2 %copy-start.8 = (bf16[512,1024]{1,0:T(8,128)(2,1)S(1)}, bf16[512,1024]{1,0:T(8,128)(2,1)}, u32[]{:S(2)}) copy-start(bf16[512,1024]{1,0:T(8,128)(2,1)} %convolution_convert_fusion.2) | copy-start | bytes 3145732

commit v3 on v2

v3 whole, which is shorter than its diff:
```python
import math

import jax
import jax.numpy as jnp
from jax import lax
from jax.experimental import pallas as pl
from jax.experimental.pallas import tpu as pltpu
from jax.sharding import PartitionSpec as P

HD = 64
BLK = 64
RAND = 3
LANES = 128


def positions_among(owners, owner_count):
    marks = (owners[..., None] == jnp.arange(owner_count, dtype=jnp.int32)).astype(jnp.int32)
    ranks = jnp.cumsum(marks, axis=-2) - 1
    return jnp.sum(ranks * marks, axis=-1)


def serve_slots(owners, offsets, target, capacity):
    matched = owners == target
    ranks = jnp.cumsum(matched.astype(jnp.int32), axis=-1) - 1
    slot_hit = matched[..., None, :] & (
        ranks[..., None, :] == jnp.arange(capacity, dtype=jnp.int32)[:, None]
    )
    return jnp.sum(jnp.where(slot_hit, offsets[..., None, :], 0), axis=-1)


def split_weights(w_qkv, head_total):
    model_dim = w_qkv.shape[0]
    shaped = w_qkv.reshape(model_dim, head_total, 3, HD)
    return [shaped[:, :, j, :].reshape(model_dim, head_total * HD) for j in range(3)]


def pair_rows(q, low):
    blank = jnp.zeros_like(q)
    return jnp.concatenate([jnp.where(low, q, blank), jnp.where(low, blank, q)], axis=0)


def pick_rows(x, low, rows):
    return jnp.where(low, x[:rows], x[rows:])


CONTRACT = (((1,), (1,)), ((), ()))


def near_kernel(mask_ref, q_ref, kp_ref, kc_ref, kn_ref, vp_ref, vc_ref, vn_ref, ks_ref, vs_ref,
                o_ref, m_ref, l_ref):
    width = q_ref.shape[-1]
    rows = q_ref.shape[1]
    scaling = 1.0 / math.sqrt(HD)
    valid = mask_ref[0] != 0
    low = lax.broadcasted_iota(jnp.int32, (rows, LANES), 1) < HD
    for tile in range(width // LANES):
        cols = pl.ds(tile * LANES, LANES)
        q_pair = pair_rows(q_ref[0, :, cols], low)
        k_local = jnp.concatenate([kp_ref[0, :, cols], kc_ref[0, :, cols], kn_ref[0, :, cols]], axis=0)
        v_local = jnp.concatenate([vp_ref[0, :, cols], vc_ref[0, :, cols], vn_ref[0, :, cols]], axis=0)
        near = lax.dot_general(q_pair, k_local, CONTRACT, preferred_element_type=jnp.float32)
        near = jnp.where(valid, near * scaling, -jnp.inf)
        wide = lax.dot_general(q_pair, ks_ref[:, cols], CONTRACT, preferred_element_type=jnp.float32)
        wide = wide * scaling
        peak = jnp.maximum(
            jnp.max(near, axis=-1, keepdims=True), jnp.max(wide, axis=-1, keepdims=True)
        )
        near_exp = jnp.exp(near - peak)
        wide_exp = jnp.exp(wide - peak)
        total = jnp.sum(near_exp, axis=-1, keepdims=True) + jnp.sum(wide_exp, axis=-1, keepdims=True)
        result = jnp.dot(near_exp.astype(jnp.bfloat16), v_local, preferred_element_type=jnp.float32)
        result = result + jnp.dot(
            wide_exp.astype(jnp.bfloat16), vs_ref[:, cols], preferred_element_type=jnp.float32
        )
        o_ref[0, :, cols] = pick_rows(result, low, rows)
        m_ref[0, :, cols] = pick_rows(jnp.broadcast_to(peak, result.shape), low, rows)
        l_ref[0, :, cols] = pick_rows(jnp.broadcast_to(total, result.shape), low, rows)


def far_kernel(ids_ref, mask_ref, q_ref, *refs):
    far_count = RAND
    token_refs = refs[:far_count]
    wk_ref, wv_ref, oa_ref, ma_ref, la_ref, out_ref = refs[far_count:]
    width = q_ref.shape[-1]
    rows = q_ref.shape[1]
    scaling = 1.0 / math.sqrt(HD)
    valid = mask_ref[0] != 0
    low = lax.broadcasted_iota(jnp.int32, (rows, LANES), 1) < HD
    far_tokens = jnp.concatenate([ref[0] for ref in token_refs], axis=0)
    k_far = jnp.dot(far_tokens, wk_ref[...], preferred_element_type=jnp.float32).astype(jnp.bfloat16)
    v_far = jnp.dot(far_tokens, wv_ref[...], preferred_element_type=jnp.float32).astype(jnp.bfloat16)
    for tile in range(width // LANES):
        lanes = slice(tile * LANES, (tile + 1) * LANES)
        cols = pl.ds(tile * LANES, LANES)
        q_pair = pair_rows(q_ref[0, :, cols], low)
        scores = lax.dot_general(q_pair, k_far[:, lanes], CONTRACT, preferred_element_type=jnp.float32)
        scores = jnp.where(valid, scores * scaling, -jnp.inf)
        peak = jnp.max(scores, axis=-1, keepdims=True)
        exps = jnp.exp(scores - peak)
        total = jnp.sum(exps, axis=-1, keepdims=True)
        result = jnp.dot(exps.astype(jnp.bfloat16), v_far[:, lanes], preferred_element_type=jnp.float32)
        o_b = pick_rows(result, low, rows)
        m_b = pick_rows(jnp.broadcast_to(peak, result.shape), low, rows)
        l_b = pick_rows(jnp.broadcast_to(total, result.shape), low, rows)
        m_a = ma_ref[0, :, cols]
        peak_all = jnp.maximum(m_a, m_b)
        scale_a = jnp.exp(m_a - peak_all)
        scale_b = jnp.exp(m_b - peak_all)
        numerator = oa_ref[0, :, cols] * scale_a + o_b * scale_b
        denominator = la_ref[0, :, cols] * scale_a + l_b * scale_b
        out_ref[0, :, cols] = (numerator / denominator).astype(out_ref.dtype)


def attend_near(mask, q, k_ext, v_ext, k_sum, v_sum):
    blocks, rows, width = q.shape
    keys = k_sum.shape[0]
    block = lambda offset: pl.BlockSpec((1, rows, width), lambda i: (i + offset, 0, 0))
    whole = pl.BlockSpec((keys, width), lambda i: (0, 0))
    local_keys = 3 * rows
    heads = width // HD
    flops = blocks * heads * 2 * rows * 2 * LANES * (local_keys + keys)
    bytes_accessed = 2 * (blocks * rows * width * 7 + 2 * keys * width) + 12 * blocks * rows * width
    part = jax.ShapeDtypeStruct((blocks, rows, width), jnp.float32)
    return pl.pallas_call(
        near_kernel,
        grid=(blocks,),
        in_specs=[pl.BlockSpec((1, 1, local_keys), lambda i: (i, 0, 0)), block(0)]
        + [block(0), block(1), block(2)] * 2
        + [whole, whole],
        out_specs=[block(0)] * 3,
        out_shape=[part] * 3,
        cost_estimate=pl.CostEstimate(
            flops=flops,
            transcendentals=blocks * heads * rows * (local_keys + keys),
            bytes_accessed=bytes_accessed,
        ),
    )(mask, q, k_ext, k_ext, k_ext, v_ext, v_ext, v_ext, k_sum, v_sum)


def attend_far(slot_ids, mask, q, incoming, w_k, w_v, o_a, m_a, l_a):
    blocks, rows, width = q.shape
    model_dim = incoming.shape[-1]
    block = pl.BlockSpec((1, rows, width), lambda i, ids: (i, 0, 0))
    token_specs = [
        pl.BlockSpec((1, rows, model_dim), lambda i, ids, j=j: (ids[RAND * i + j], 0, 0))
        for j in range(RAND)
    ]
    weight = pl.BlockSpec(w_k.shape, lambda i, ids: (0, 0))
    local_keys = RAND * rows
    heads = width // HD
    flops = blocks * (
        heads * 2 * rows * 2 * LANES * local_keys + 2 * 2 * local_keys * model_dim * width
    )
    bytes_accessed = 2 * blocks * rows * (width * 2 + model_dim * RAND) + 4 * w_k.size + (
        12 * blocks * rows * width
    )
    grid_spec = pltpu.PrefetchScalarGridSpec(
        num_scalar_prefetch=1,
        grid=(blocks,),
        in_specs=[pl.BlockSpec((1, 1, local_keys), lambda i, ids: (i, 0, 0)), block]
        + token_specs
        + [weight, weight, block, block, block],
        out_specs=block,
    )
    return pl.pallas_call(
        far_kernel,
        grid_spec=grid_spec,
        out_shape=jax.ShapeDtypeStruct((blocks, rows, width), jnp.bfloat16),
        cost_estimate=pl.CostEstimate(
            flops=flops,
            transcendentals=blocks * heads * rows * local_keys,
            bytes_accessed=bytes_accessed,
        ),
    )(slot_ids, mask, q, incoming, incoming, incoming, w_k, w_v, o_a, m_a, l_a)


def local(tokens, w_qkv, w_out, counts, rand_seg, rand_off):
    seq_count = lax.axis_size("seq")
    ctx_count = lax.axis_size("ctx")
    seq_index = lax.axis_index("seq")
    ctx_index = lax.axis_index("ctx")
    dev_count = seq_count * ctx_count
    dev_index = ctx_index * seq_count + seq_index
    tok_rows, model_dim = tokens.shape
    head_total = model_dim // HD
    dev_blocks = tok_rows // BLK
    seg_blocks = dev_blocks * seq_count
    block_total = counts.shape[0]
    capacity = (RAND * dev_blocks + ctx_count - 1) // ctx_count + 1
    first_block = dev_index * dev_blocks
    token_blocks = tokens.reshape(dev_blocks, BLK, model_dim)

    all_owner = rand_seg.reshape(ctx_count, seq_count, dev_blocks * RAND)
    all_offset = rand_off.reshape(ctx_count, seq_count, dev_blocks * RAND)
    col_owner = lax.dynamic_index_in_dim(all_owner, seq_index, axis=1, keepdims=False)
    col_offset = lax.dynamic_index_in_dim(all_offset, seq_index, axis=1, keepdims=False)
    send_off = serve_slots(col_owner, col_offset, ctx_index, capacity)
    outgoing = jnp.take(token_blocks, send_off.reshape(-1), axis=0, mode="clip").reshape(
        ctx_count, capacity, BLK, model_dim
    )
    forward = [(i, i + 1) for i in range(dev_count - 1)]
    backward = [(i + 1, i) for i in range(dev_count - 1)]
    prev_tokens = lax.ppermute(token_blocks[dev_blocks - 1], ("ctx", "seq"), forward)
    next_tokens = lax.ppermute(token_blocks[0], ("ctx", "seq"), backward)

    usable = jnp.arange(BLK, dtype=jnp.int32)[None, :] < lax.dynamic_slice_in_dim(
        counts, first_block, dev_blocks
    )[:, None]
    weighted = jnp.where(usable[:, :, None], token_blocks.astype(jnp.float32), 0.0)
    sums = jnp.sum(weighted, axis=1)
    members = jnp.sum(usable.astype(jnp.float32), axis=1)
    pooled = sums / members[:, None]
    summary = (pooled / jnp.sqrt(jnp.mean(pooled * pooled, axis=1, keepdims=True) + 1e-05)).astype(
        jnp.bfloat16
    )
    summary_all = lax.all_gather(summary, ("ctx", "seq"), axis=0, tiled=True)
    summary_all, outgoing = lax.optimization_barrier((summary_all, outgoing))
    incoming = lax.all_to_all(outgoing, "ctx", split_axis=0, concat_axis=0, tiled=True)

    w_q, w_k, w_v = split_weights(w_qkv, head_total)
    project = lambda x, w: jnp.dot(x, w, preferred_element_type=jnp.float32).astype(jnp.bfloat16)
    q_own = project(tokens, w_q).reshape(dev_blocks, BLK, model_dim)
    rimmed = jnp.concatenate([prev_tokens, tokens, next_tokens], axis=0)
    k_ext = project(rimmed, w_k).reshape(dev_blocks + 2, BLK, model_dim)
    v_ext = project(rimmed, w_v).reshape(dev_blocks + 2, BLK, model_dim)
    k_sum = project(summary_all, w_k)
    v_sum = project(summary_all, w_v)

    my_owner = lax.dynamic_slice_in_dim(rand_seg, first_block, dev_blocks)
    my_offset = lax.dynamic_slice_in_dim(rand_off, first_block, dev_blocks)
    mine = my_owner.reshape(dev_blocks * RAND)
    slot_ids = mine * capacity + positions_among(mine, ctx_count)

    block_ids = first_block + jnp.arange(dev_blocks, dtype=jnp.int32)
    near_ids = block_ids[:, None] + jnp.arange(-1, 2, dtype=jnp.int32)[None, :]
    existing = (near_ids >= 0) & (near_ids < block_total)
    near_counts = jnp.where(existing, jnp.take(counts, jnp.clip(near_ids, 0, block_total - 1)), 0)
    far_global = my_owner * seg_blocks + seq_index * dev_blocks + my_offset
    far_counts = jnp.take(counts, far_global)
    positions = jnp.arange(BLK, dtype=jnp.int32)[None, None, :]
    near_mask = (positions < near_counts[:, :, None]).astype(jnp.int32).reshape(dev_blocks, 1, -1)
    far_mask = (positions < far_counts[:, :, None]).astype(jnp.int32).reshape(dev_blocks, 1, -1)

    o_a, m_a, l_a = attend_near(near_mask, q_own, k_ext, v_ext, k_sum, v_sum)
    attended = attend_far(
        slot_ids,
        far_mask,
        q_own,
        incoming.reshape(ctx_count * capacity, BLK, model_dim),
        w_k,
        w_v,
        o_a,
        m_a,
        l_a,
    ).reshape(tok_rows, model_dim)
    mixed = tokens.astype(jnp.float32) + jnp.dot(attended, w_out, preferred_element_type=jnp.float32)
    return mixed.astype(jnp.bfloat16)


def solution(mesh):
    in_specs = (P(("ctx", "seq"), None), P(), P(), P(), P(), P())
    out_specs = P(("ctx", "seq"), None)
    return jax.shard_map(local, mesh=mesh, in_specs=in_specs, out_specs=out_specs, check_vma=False)
```

time: 196 us -> 214 us (1.092)
  waiting for transfers between devices: 0.01 us -> 53.9 us
  blocking collectives: 87.7 us -> 35.5 us
  Pallas kernels: 31.5 us -> 49.8 us
  starting transfers between devices: 13.6 us -> 19.4 us
  matrix products: 21.6 us -> 15.9 us
  other arithmetic: 6.91 us -> 4.15 us
    all_gather x1, blocking collectives: 87.7 us -> 35.5 us  [local(): summary_all = lax.all_gather(summary, ('ctx', 'seq'), axis=0, tiled=True)]
    ppermute x1, waiting for transfers between devices: 0.01 us -> 51.5 us  [local(): lax.ppermute(token_blocks[dev_blocks - 1], ('ctx', 'seq'), forward)]
    pallas_call x1 -> x2, Pallas kernels: 31.5 us -> 49.8 us  [the longest x1 27.5 us: attend_far(): pl.pallas_call(far_kernel, grid_spec=grid_spec, out_shape=jax.ShapeDtypeS...]
    all_to_all x1, starting transfers between devices: 6.3 us -> 15.1 us  [local(): lax.all_to_all(outgoing, 'ctx', split_axis=0, concat_axis=0, tiled=True)]
    another operation x0 -> x2, local copies, waits for them, and re-layouts: none -> 7.89 us  [split_weights(): shaped[:, :, j, :].reshape(model_dim, head_total * HD)]
    dot_general x7 -> x5, matrix products: 18.2 us -> 12.5 us  [local(): jnp.dot(x, w, preferred_element_type=jnp.float32).astype(jnp.bfloat16)]
    gather x1 -> x0, local copies, waits for them, and re-layouts: 4.71 us -> none  [local(): jnp.take(incoming.reshape(ctx_count * capacity, BLK, model_dim), slot_ids...]
    concatenate x3 -> x0, other arithmetic: 4.5 us -> none  [the longest x1 2.6 us: local(): jnp.concatenate([fetched, prev_tokens[None], next_tokens[None]], axis=0)]
  transfers between devices with their start and end apart: 3 -> 3, of which waited for: 0 -> 2; matrix products, arithmetic and copies ran while one was open for 17% -> 19% of each run, Pallas kernels for 0% -> 11%
where the time goes in v3:
time: 214 us; the launch traced here: 212 us
  waiting for transfers between devices  53.9 us (25%)
  Pallas kernels  49.8 us (23%)
  blocking collectives  35.5 us (17%)
  local copies, waits for them, and re-layouts  32.7 us (15%)
  starting transfers between devices  19.4 us (9%)
  matrix products  15.9 us (7%)
  other arithmetic  4.15 us (2%)
    ppermute x1, waiting for transfers between devices, local(): lax.ppermute(token_blocks[dev_blocks - 1], ('ctx', 'seq'), forward)  51.5 us
    all_gather x1, blocking collectives, local(): summary_all = lax.all_gather(summary, ('ctx', 'seq'), axis=0, tiled=True)  35.5 us
    pallas_call x1, Pallas kernels, attend_far(): pl.pallas_call(far_kernel, grid_spec=grid_spec, out_shape=jax.ShapeDtypeS...  27.5 us
    pallas_call x1, Pallas kernels, attend_near(): pl.pallas_call(near_kernel, grid=(blocks,), in_specs=[pl.BlockSpec((1, 1,...  22.2 us
    all_to_all x1, starting transfers between devices, local(): lax.all_to_all(outgoing, 'ctx', split_axis=0, concat_axis=0, tiled=True)  15.1 us
    dot_general x5, matrix products, local(): jnp.dot(x, w, preferred_element_type=jnp.float32).astype(jnp.bfloat16)  12.5 us
    unnamed x29, local copies, waits for them, and re-layouts  11.3 us
    another operation x2, local copies, waits for them, and re-layouts, split_weights(): shaped[:, :, j, :].reshape(model_dim, head_total * HD)  7.89 us
  transfers between devices with their start and end apart: 3, of which 2 were waited for; matrix products, arithmetic and copies ran while one was open for 19% of the time, Pallas kernels for 11%

profile of v3, /device:TPU:16, one launch (start us, length us, event | category | flops | bytes accessed | tf_op | source)
XLA Modules:
  0.0 211.6 jit_solution(14534844276768272535)
XLA Ops:
  0.0 0.9 dynamic_slice.18
  1.0 0.2 convert_reduce_fusion
  1.4 1.6 select_reduce_fusion
  3.0 0.2 multiply_reduce_fusion
  3.3 0.8 copy.39
  4.5 0.8 copy.40
  5.8 35.5 %all_gather.3 = bf16[256,1024]{1,0:T(8,128)(2,1)} all-gather(bf16[8,1024]{1,0:T(8,128)(2,1)S(1)} %divide_convert_fusion), channel_id=1, replica_groups=mesh['ctx'=8,'seq'=4] {'ctx','seq'}, dimensions={0}, use_global_device_ids=true | all-gather | bytes 540672 | tf_op jit(solution)/shard_map/all_gather | solution.py:216
  41.3 2.9 %gather_fusion = bf16[32,64,1024]{2,1,0:T(8,128)(2,1)} fusion(bf16[8,64,1024]{2,1,0:T(8,128)(2,1)S(1)} %bitcast.28, s32[1024]{0:T(1024)S(1)} %get-tuple-element.28), kind=kCustom, calls=%fused_computation.2 | custom fusion | bytes 8388736 | tf_op jit(solution)/shard_map/jit(_take)/gather | solution.py:198
  44.2 15.1 %all-to-all-start = ((bf16[8,4,64,1024]{3,2,1,0:T(8,128)(2,1)}), bf16[8,4,64,1024]{3,2,1,0:T(8,128)(2,1)}, u32[]{:S(2)}, u32[]{:S(2)}) async-start(bf16[8,4,64,1024]{3,2,1,0:T(8,128)(2,1)} %bitcast.30), calls=%async_computation | async-start | bytes 8388608 | tf_op jit(solution)/shard_map/all_to_all | solution.py:218
  59.3 0.7 fusion.5
  60.0 1.9 collective-permute-start.1
  61.9 2.4 %collective-permute-start = (bf16[64,1024]{1,0:T(8,128)(2,1)}, bf16[64,1024]{1,0:T(8,128)(2,1)}, u32[]{:S(2)}, u32[]{:S(2)}) collective-permute-start(bf16[64,1024]{1,0:T(8,128)(2,1)} %get-tuple-element.22), channel_id=1, source_target_pairs={{0,1},{1,2},{2,3},{3,4},{4,5},{5,6},{6,7},{7,8},{8,9},{9,10},{10,1... | collective-permute-start | bytes 393224 | tf_op jit(solution)/shard_map/ppermute | solution.py:203
  64.4 0.6 lt.87
  65.2 0.7 gather_fusion.1
  66.0 0.7 gather_fusion.2
  67.3 8.7 %copy.43 = bf16[1024,3072]{0,1:T(8,128)(2,1)} copy(bf16[1024,3072]{1,0:T(8,128)(2,1)} %param.9) | data formatting | bytes 12582912 | tf_op args[1]
  76.0 5.7 %fusion.4 = (bf16[1024,16,1,64]{0,3,2,1:T(8,128)(2,1)}, bf16[1024,16,1,64]{0,3,2,1:T(8,128)(2,1)}, bf16[1024,16,1,64]{0,3,2,1:T(8,128)(2,1)}) fusion(bf16[1024,16,3,64]{0,3,2,1:T(8,128)(2,1)} %bitcast.29), kind=kLoop, calls=%fused_computation.46 | loop fusion | bytes 12582912 | tf_op jit(solution)/shard_map/slice | solution.py:34
  81.7 3.9 %copy.49.refs_3_ = bf16[1024,1024]{1,0:T(8,128)(2,1)} copy(bf16[1024,1024]{0,1:T(8,128)(2,1)} %bitcast.40) | data formatting | bytes 4194304 | tf_op jit(solution)/shard_map/reshape;squeeze | solution.py:34
  85.6 3.9 %copy.50.refs_4_ = bf16[1024,1024]{1,0:T(8,128)(2,1)} copy(bf16[1024,1024]{0,1:T(8,128)(2,1)} %bitcast.37) | data formatting | bytes 4194304 | tf_op jit(solution)/shard_map/reshape;squeeze | solution.py:34
  89.8 0.6 compare_convert_fusion
  90.4 3.3 %convolution_convert_fusion.4.ks_ref = bf16[256,1024]{1,0:T(8,128)(2,1)} fusion(bf16[256,1024]{1,0:T(8,128)(2,1)} %all_gather.3, bf16[1024,1024]{0,1:T(8,128)(2,1)} %bitcast.41), kind=kOutput, calls=%fused_computation.9 | convolution fusion | flops 537133056 | bytes 3145728 | tf_op jit(solution)/shard_map/dot_general | solution.py:221
  93.8 1.6 convolution_convert_fusion.3.vs_ref
  95.4 2.3 %convolution_convert_fusion.2 = bf16[512,1024]{1,0:T(8,128)(2,1)} fusion(bf16[512,1024]{1,0:T(8,128)(2,1)S(1)} %copy-done.2, bf16[1024,1024]{0,1:T(8,128)(2,1)S(1)} %bitcast.43), kind=kOutput, calls=%fused_computation.7 | convolution fusion | flops 1074266112 | bytes 4194304 | tf_op jit(solution)/shard_map/dot_general | solution.py:221
  97.7 0.5 multiply_add_fusion.ids_ref
  98.2 51.5 %collective-permute-done = bf16[64,1024]{1,0:T(8,128)(2,1)} collective-permute-done((bf16[64,1024]{1,0:T(8,128)(2,1)}, bf16[64,1024]{1,0:T(8,128)(2,1)}, u32[]{:S(2)}, u32[]{:S(2)}) %collective-permute-start) | collective-permute-done | bytes 131104 | tf_op jit(solution)/shard_map/ppermute | solution.py:203
  149.7 0.9 constant_dynamic-update-slice_fusion.2
  150.6 2.4 %collective-permute-done.1 = bf16[64,1024]{1,0:T(8,128)(2,1)S(1)} collective-permute-done((bf16[64,1024]{1,0:T(8,128)(2,1)}, bf16[64,1024]{1,0:T(8,128)(2,1)S(1)}, u32[]{:S(2)}, u32[]{:S(2)}) %collective-permute-start.1) | collective-permute-done | bytes 131104 | tf_op jit(solution)/shard_map/ppermute | solution.py:204
  153.1 2.6 %convolution_convert_fusion.1 = bf16[640,1024]{1,0:T(8,128)(2,1)} fusion(bf16[640,1024]{1,0:T(8,128)(2,1)S(1)} %constant_dynamic-update-slice_fusion, bf16[1024,1024]{0,1:T(8,128)(2,1)S(1)} %bitcast.42), kind=kOutput, calls=%fused_computation.6 | convolution fusion | flops 1342832640 | bytes 4718592 | tf_op jit(solution)/shard_map/dot_general | solution.py:221
  155.7 2.6 %convolution_convert_fusion = bf16[640,1024]{1,0:T(8,128)(2,1)} fusion(bf16[640,1024]{1,0:T(8,128)(2,1)S(1)} %constant_dynamic-update-slice_fusion, bf16[1024,1024]{0,1:T(8,128)(2,1)S(1)} %bitcast.39), kind=kOutput, calls=%fused_computation.5 | convolution fusion | flops 1342832640 | bytes 4718592 | tf_op jit(solution)/shard_map/dot_general | solution.py:221
  158.3 22.2 %shard_map.64 = (f32[8,64,1024]{2,1,0:T(8,128)}, f32[8,64,1024]{2,1,0:T(8,128)}, f32[8,64,1024]{2,1,0:T(8,128)}) custom-call(s32[8,1,192]{2,1,0:T(1,128)} %get-tuple-element.25.mask_ref, bf16[8,64,1024]{2,1,0:T(8,128)(2,1)} %bitcast.44, bf16[10,64,1024]{2,1,0:T(8,128)(2,1)} %bitcast.31, bf16[10,64,1024]{2,1,0:T(8,128)(2,1)} %bitcast.32, ...), custom_call_target="tpu_custom_call" | custom-call | flops 1879048192 | bytes 14680064 | tf_op jit(solution)/shard_map/pallas_call | solution.py:124
  180.6 27.5 %shard_map.65 = bf16[8,64,1024]{2,1,0:T(8,128)(2,1)} custom-call(s32[24]{0:T(128)} %multiply_add_fusion.ids_ref, s32[8,1,192]{2,1,0:T(1,128)} %get-tuple-element.26.mask_ref, bf16[8,64,1024]{2,1,0:T(8,128)(2,1)} %bitcast.45, bf16[32,64,1024]{2,1,0:T(8,128)(2,1)} %bitcast.6.refs_0_.refs_1_.refs_2_, bf16[32,64,1024]{2,1,0:T(8,128)(2,1)} %bitcast.6.refs_0_.refs_1_.refs_2_, ...), custom_call_target="tpu_custom_call" | custom-call | flops 7247757312 | bytes 15728640 | tf_op jit(solution)/shard_map/pallas_call | solution.py:165
  208.1 3.4 %add_convert_fusion = bf16[512,1024]{1,0:T(8,128)(2,1)} fusion(bf16[512,1024]{1,0:T(8,128)(2,1)S(1)} %copy-done.2, bf16[512,1024]{1,0:T(8,128)(2,1)} %bitcast.47, bf16[1024,1024]{1,0:T(8,128)(2,1)S(1)} %copy-done), kind=kOutput, calls=%fused_computation.3 | convolution fusion | flops 1075314688 | bytes 5242880 | tf_op jit(solution)/shard_map/dot_general | solution.py:256
  (61 shorter events, 2.2 us)
Async XLA Ops:
  0.0 208.1 %copy-start = (bf16[1024,1024]{1,0:T(8,128)(2,1)S(1)}, bf16[1024,1024]{1,0:T(8,128)(2,1)}, u32[]{:S(2)}) copy-start(bf16[1024,1024]{1,0:T(8,128)(2,1)} %param.10) | copy-start | bytes 6291460
  0.0 41.3 %copy-start.2 = (bf16[512,1024]{1,0:T(8,128)(2,1)S(1)}, bf16[512,1024]{1,0:T(8,128)(2,1)}, u32[]{:S(2)}) copy-start(bf16[512,1024]{1,0:T(8,128)(2,1)} %param.8) | copy-start | bytes 3145732
  0.0 3.2 %copy-start.8 = (s32[8]{0:T(128)}, s32[8]{0:T(128)S(1)}, u32[]{:S(2)}) copy-start(s32[8]{0:T(128)S(1)} %iota_add_fusion.1) | copy-start | bytes 100
  0.0 3.2 %copy-start.10 = (s32[3]{0:T(128)}, s32[3]{0:T(128)S(1)}, u32[]{:S(2)}) copy-start(s32[3]{0:T(128)S(1)} %iota_add_fusion) | copy-start | bytes 40
  44.2 136.4 %all-to-all-start = ((bf16[8,4,64,1024]{3,2,1,0:T(8,128)(2,1)}), bf16[8,4,64,1024]{3,2,1,0:T(8,128)(2,1)}, u32[]{:S(2)}, u32[]{:S(2)}) async-start(bf16[8,4,64,1024]{3,2,1,0:T(8,128)(2,1)} %bitcast.30), calls=%async_computation | async-start | bytes 8388608 | tf_op jit(solution)/shard_map/all_to_all | solution.py:218
  59.3 5.9 %copy-start.1 = (s32[256]{0:T(256)S(1)}, s32[256]{0:T(256)}, u32[]{:S(2)}) copy-start(s32[256]{0:T(256)} %param.11) | copy-start | bytes 3076
  60.0 93.1 %collective-permute-start.1 = (bf16[64,1024]{1,0:T(8,128)(2,1)}, bf16[64,1024]{1,0:T(8,128)(2,1)S(1)}, u32[]{:S(2)}, u32[]{:S(2)}) collective-permute-start(bf16[64,1024]{1,0:T(8,128)(2,1)} %get-tuple-element.21), channel_id=1, source_target_pairs={{1,0},{2,1},{3,2},{4,3},{5,4},{6,5},{7,6},{8,7},{9,8},{10,9},{11,1... | collective-permute-start | bytes 393224 | tf_op jit(solution)/shard_map/ppermute | solution.py:204
  61.9 87.7 %collective-permute-start = (bf16[64,1024]{1,0:T(8,128)(2,1)}, bf16[64,1024]{1,0:T(8,128)(2,1)}, u32[]{:S(2)}, u32[]{:S(2)}) collective-permute-start(bf16[64,1024]{1,0:T(8,128)(2,1)} %get-tuple-element.22), channel_id=1, source_target_pairs={{0,1},{1,2},{2,3},{3,4},{4,5},{5,6},{6,7},{7,8},{8,9},{9,10},{10,1... | collective-permute-start | bytes 393224 | tf_op jit(solution)/shard_map/ppermute | solution.py:203
  66.0 0.8 copy-start.9
  66.0 0.8 copy-start.11
  85.6 4.1 %copy-start.7 = (s32[192]{0:T(256)S(1)}, s32[192]{0:T(256)}, u32[]{:S(2)}) copy-start(s32[192]{0:T(256)} %lt.87) | copy-start | bytes 2308
  89.6 4.2 %copy-start.3 = (bf16[1024,16,1,64]{0,3,2,1:T(8,128)(2,1)S(1)}, bf16[1024,16,1,64]{0,3,2,1:T(8,128)(2,1)}, u32[]{:S(2)}) copy-start(bf16[1024,16,1,64]{0,3,2,1:T(8,128)(2,1)} %get-tuple-element.18) | copy-start | bytes 6291460
  89.6 4.2 %copy-start.6 = (bf16[256,1024]{1,0:T(8,128)(2,1)S(1)}, bf16[256,1024]{1,0:T(8,128)(2,1)}, u32[]{:S(2)}) copy-start(bf16[256,1024]{1,0:T(8,128)(2,1)} %all_gather.3) | copy-start | bytes 1572868
  93.8 1.6 copy-start.5
  97.7 55.4 %copy-start.4 = (bf16[1024,16,1,64]{0,3,2,1:T(8,128)(2,1)S(1)}, bf16[1024,16,1,64]{0,3,2,1:T(8,128)(2,1)}, u32[]{:S(2)}) copy-start(bf16[1024,16,1,64]{0,3,2,1:T(8,128)(2,1)} %get-tuple-element.19) | copy-start | bytes 6291460

commit v4 on v3

--- a/solution.py
+++ b/solution.py
@@ -213,7 +213,8 @@
     summary = (pooled / jnp.sqrt(jnp.mean(pooled * pooled, axis=1, keepdims=True) + 1e-05)).astype(
         jnp.bfloat16
     )
-    summary_all = lax.all_gather(summary, ("ctx", "seq"), axis=0, tiled=True)
+    summary_seg = lax.all_gather(summary, "seq", axis=0, tiled=True)
+    summary_all = lax.all_gather(summary_seg, "ctx", axis=0, tiled=True)
     summary_all, outgoing = lax.optimization_barrier((summary_all, outgoing))
     incoming = lax.all_to_all(outgoing, "ctx", split_axis=0, concat_axis=0, tiled=True)
 

time: 214 us -> 202 us (0.944)
  waiting for transfers between devices: 53.9 us -> 49.3 us
  starting transfers between devices: 19.4 us -> 15 us
    all_to_all x1, starting transfers between devices: 15.1 us -> 10.7 us  [local(): lax.all_to_all(outgoing, 'ctx', split_axis=0, concat_axis=0, tiled=True)]
    ppermute x1, waiting for transfers between devices: 2.43 us -> 0.01 us  [local(): next_tokens = lax.ppermute(token_blocks[0], ('ctx', 'seq'), backward)]
    ppermute x1, waiting for transfers between devices: 51.5 us -> 49.3 us  [local(): lax.ppermute(token_blocks[dev_blocks - 1], ('ctx', 'seq'), forward)]
    all_gather x1 -> x2, blocking collectives: 35.5 us -> 34.2 us  [the longest x1 28.9 us: local(): summary_all = lax.all_gather(summary_seg, 'ctx', axis=0, tiled=True)]
  transfers between devices with their start and end apart: 3 -> 3, of which waited for: 2 -> 1; matrix products, arithmetic and copies ran while one was open for 19% -> 20% of each run, Pallas kernels for 11% -> 11%
where the time goes in v4:
time: 202 us; the launch traced here: 201 us
  Pallas kernels  49.8 us (25%)
  waiting for transfers between devices  49.3 us (24%)
  blocking collectives  34.2 us (17%)
  local copies, waits for them, and re-layouts  32.7 us (16%)
  matrix products  15.9 us (8%)
  starting transfers between devices  15 us (7%)
  other arithmetic  4.15 us (2%)
    ppermute x1, waiting for transfers between devices, local(): lax.ppermute(token_blocks[dev_blocks - 1], ('ctx', 'seq'), forward)  49.3 us
    all_gather x1, blocking collectives, local(): summary_all = lax.all_gather(summary_seg, 'ctx', axis=0, tiled=True)  28.9 us
    pallas_call x1, Pallas kernels, attend_far(): pl.pallas_call(far_kernel, grid_spec=grid_spec, out_shape=jax.ShapeDtypeS...  27.5 us
    pallas_call x1, Pallas kernels, attend_near(): pl.pallas_call(near_kernel, grid=(blocks,), in_specs=[pl.BlockSpec((1, 1,...  22.2 us
    dot_general x5, matrix products, local(): jnp.dot(x, w, preferred_element_type=jnp.float32).astype(jnp.bfloat16)  12.5 us
    unnamed x29, local copies, waits for them, and re-layouts  11.3 us
    all_to_all x1, starting transfers between devices, local(): lax.all_to_all(outgoing, 'ctx', split_axis=0, concat_axis=0, tiled=True)  10.7 us
    another operation x2, local copies, waits for them, and re-layouts, split_weights(): shaped[:, :, j, :].reshape(model_dim, head_total * HD)  7.89 us
  transfers between devices with their start and end apart: 3, of which 1 were waited for; matrix products, arithmetic and copies ran while one was open for 20% of the time, Pallas kernels for 11%

profile of v4, /device:TPU:16, one launch (start us, length us, event | category | flops | bytes accessed | tf_op | source)
XLA Modules:
  0.0 201.2 jit_solution(17487102363415231543)
XLA Ops:
  0.0 0.9 dynamic_slice.18
  1.0 0.2 convert_reduce_fusion
  1.4 1.6 select_reduce_fusion
  3.0 0.2 multiply_reduce_fusion
  3.3 5.2 %all_gather.6 = bf16[32,1024]{1,0:T(8,128)(2,1)S(1)} all-gather(bf16[8,1024]{1,0:T(8,128)(2,1)S(1)} %divide_convert_fusion), channel_id=1, replica_groups=mesh['ctx'=8,'seq'=4] {'seq'}, dimensions={0}, use_global_device_ids=true | all-gather | bytes 81920 | tf_op jit(solution)/shard_map/all_gather | solution.py:216
  8.6 0.8 copy.39
  9.7 0.8 copy.40
  11.0 28.9 %all_gather.7 = bf16[256,1024]{1,0:T(8,128)(2,1)} all-gather(bf16[32,1024]{1,0:T(8,128)(2,1)S(1)} %all_gather.6), channel_id=1, replica_groups=mesh['ctx'=8,'seq'=4] {'ctx'}, dimensions={0}, use_global_device_ids=true | all-gather | bytes 589824 | tf_op jit(solution)/shard_map/all_gather | solution.py:217
  40.0 2.9 %gather_fusion = bf16[32,64,1024]{2,1,0:T(8,128)(2,1)} fusion(bf16[8,64,1024]{2,1,0:T(8,128)(2,1)S(1)} %bitcast.28, s32[1024]{0:T(1024)S(1)} %get-tuple-element.28), kind=kCustom, calls=%fused_computation.2 | custom fusion | bytes 8388736 | tf_op jit(solution)/shard_map/jit(_take)/gather | solution.py:198
  42.8 10.7 %all-to-all-start = ((bf16[8,4,64,1024]{3,2,1,0:T(8,128)(2,1)}), bf16[8,4,64,1024]{3,2,1,0:T(8,128)(2,1)}, u32[]{:S(2)}, u32[]{:S(2)}) async-start(bf16[8,4,64,1024]{3,2,1,0:T(8,128)(2,1)} %bitcast.30), calls=%async_computation | async-start | bytes 8388608 | tf_op jit(solution)/shard_map/all_to_all | solution.py:219
  53.6 0.7 fusion.5
  54.3 1.9 collective-permute-start.1
  56.2 2.4 %collective-permute-start = (bf16[64,1024]{1,0:T(8,128)(2,1)}, bf16[64,1024]{1,0:T(8,128)(2,1)}, u32[]{:S(2)}, u32[]{:S(2)}) collective-permute-start(bf16[64,1024]{1,0:T(8,128)(2,1)} %get-tuple-element.22), channel_id=1, source_target_pairs={{0,1},{1,2},{2,3},{3,4},{4,5},{5,6},{6,7},{7,8},{8,9},{9,10},{10,1... | collective-permute-start | bytes 393224 | tf_op jit(solution)/shard_map/ppermute | solution.py:203
  58.6 0.6 lt.87
  59.5 0.7 gather_fusion.1
  60.3 0.7 gather_fusion.2
  61.6 8.7 %copy.43 = bf16[1024,3072]{0,1:T(8,128)(2,1)} copy(bf16[1024,3072]{1,0:T(8,128)(2,1)} %param.9) | data formatting | bytes 12582912 | tf_op args[1]
  70.3 5.7 %fusion.4 = (bf16[1024,16,1,64]{0,3,2,1:T(8,128)(2,1)}, bf16[1024,16,1,64]{0,3,2,1:T(8,128)(2,1)}, bf16[1024,16,1,64]{0,3,2,1:T(8,128)(2,1)}) fusion(bf16[1024,16,3,64]{0,3,2,1:T(8,128)(2,1)} %bitcast.29), kind=kLoop, calls=%fused_computation.46 | loop fusion | bytes 12582912 | tf_op jit(solution)/shard_map/slice | solution.py:34
  76.0 3.9 %copy.49.refs_3_ = bf16[1024,1024]{1,0:T(8,128)(2,1)} copy(bf16[1024,1024]{0,1:T(8,128)(2,1)} %bitcast.40) | data formatting | bytes 4194304 | tf_op jit(solution)/shard_map/reshape;squeeze | solution.py:34
  79.9 3.9 %copy.50.refs_4_ = bf16[1024,1024]{1,0:T(8,128)(2,1)} copy(bf16[1024,1024]{0,1:T(8,128)(2,1)} %bitcast.37) | data formatting | bytes 4194304 | tf_op jit(solution)/shard_map/reshape;squeeze | solution.py:34
  84.1 0.6 compare_convert_fusion
  84.7 3.3 %convolution_convert_fusion.4.ks_ref = bf16[256,1024]{1,0:T(8,128)(2,1)} fusion(bf16[256,1024]{1,0:T(8,128)(2,1)} %all_gather.7, bf16[1024,1024]{0,1:T(8,128)(2,1)} %bitcast.41), kind=kOutput, calls=%fused_computation.9 | convolution fusion | flops 537133056 | bytes 3145728 | tf_op jit(solution)/shard_map/dot_general | solution.py:222
  88.0 1.6 convolution_convert_fusion.3.vs_ref
  89.7 2.3 %convolution_convert_fusion.2 = bf16[512,1024]{1,0:T(8,128)(2,1)} fusion(bf16[512,1024]{1,0:T(8,128)(2,1)S(1)} %copy-done.2, bf16[1024,1024]{0,1:T(8,128)(2,1)S(1)} %bitcast.43), kind=kOutput, calls=%fused_computation.7 | convolution fusion | flops 1074266112 | bytes 4194304 | tf_op jit(solution)/shard_map/dot_general | solution.py:222
  92.0 0.5 multiply_add_fusion.ids_ref
  92.5 49.3 %collective-permute-done = bf16[64,1024]{1,0:T(8,128)(2,1)} collective-permute-done((bf16[64,1024]{1,0:T(8,128)(2,1)}, bf16[64,1024]{1,0:T(8,128)(2,1)}, u32[]{:S(2)}, u32[]{:S(2)}) %collective-permute-start) | collective-permute-done | bytes 131104 | tf_op jit(solution)/shard_map/ppermute | solution.py:203
  141.7 0.9 constant_dynamic-update-slice_fusion.2
  142.8 2.6 %convolution_convert_fusion.1 = bf16[640,1024]{1,0:T(8,128)(2,1)} fusion(bf16[640,1024]{1,0:T(8,128)(2,1)S(1)} %constant_dynamic-update-slice_fusion, bf16[1024,1024]{0,1:T(8,128)(2,1)S(1)} %bitcast.42), kind=kOutput, calls=%fused_computation.6 | convolution fusion | flops 1342832640 | bytes 4718592 | tf_op jit(solution)/shard_map/dot_general | solution.py:222
  145.4 2.6 %convolution_convert_fusion = bf16[640,1024]{1,0:T(8,128)(2,1)} fusion(bf16[640,1024]{1,0:T(8,128)(2,1)S(1)} %constant_dynamic-update-slice_fusion, bf16[1024,1024]{0,1:T(8,128)(2,1)S(1)} %bitcast.39), kind=kOutput, calls=%fused_computation.5 | convolution fusion | flops 1342832640 | bytes 4718592 | tf_op jit(solution)/shard_map/dot_general | solution.py:222
  148.0 22.2 %shard_map.64 = (f32[8,64,1024]{2,1,0:T(8,128)}, f32[8,64,1024]{2,1,0:T(8,128)}, f32[8,64,1024]{2,1,0:T(8,128)}) custom-call(s32[8,1,192]{2,1,0:T(1,128)} %get-tuple-element.25.mask_ref, bf16[8,64,1024]{2,1,0:T(8,128)(2,1)} %bitcast.44, bf16[10,64,1024]{2,1,0:T(8,128)(2,1)} %bitcast.31, bf16[10,64,1024]{2,1,0:T(8,128)(2,1)} %bitcast.32, ...), custom_call_target="tpu_custom_call" | custom-call | flops 1879048192 | bytes 14680064 | tf_op jit(solution)/shard_map/pallas_call | solution.py:124
  170.2 27.5 %shard_map.65 = bf16[8,64,1024]{2,1,0:T(8,128)(2,1)} custom-call(s32[24]{0:T(128)} %multiply_add_fusion.ids_ref, s32[8,1,192]{2,1,0:T(1,128)} %get-tuple-element.26.mask_ref, bf16[8,64,1024]{2,1,0:T(8,128)(2,1)} %bitcast.45, bf16[32,64,1024]{2,1,0:T(8,128)(2,1)} %bitcast.6.refs_0_.refs_1_.refs_2_, bf16[32,64,1024]{2,1,0:T(8,128)(2,1)} %bitcast.6.refs_0_.refs_1_.refs_2_, ...), custom_call_target="tpu_custom_call" | custom-call | flops 7247757312 | bytes 15728640 | tf_op jit(solution)/shard_map/pallas_call | solution.py:165
  197.8 3.4 %add_convert_fusion = bf16[512,1024]{1,0:T(8,128)(2,1)} fusion(bf16[512,1024]{1,0:T(8,128)(2,1)S(1)} %copy-done.2, bf16[512,1024]{1,0:T(8,128)(2,1)} %bitcast.47, bf16[1024,1024]{1,0:T(8,128)(2,1)S(1)} %copy-done), kind=kOutput, calls=%fused_computation.3 | convolution fusion | flops 1075314688 | bytes 5242880 | tf_op jit(solution)/shard_map/dot_general | solution.py:257
  (62 shorter events, 2.3 us)
Async XLA Ops:
  0.0 197.8 %copy-start = (bf16[1024,1024]{1,0:T(8,128)(2,1)S(1)}, bf16[1024,1024]{1,0:T(8,128)(2,1)}, u32[]{:S(2)}) copy-start(bf16[1024,1024]{1,0:T(8,128)(2,1)} %param.10) | copy-start | bytes 6291460
  0.0 39.9 %copy-start.2 = (bf16[512,1024]{1,0:T(8,128)(2,1)S(1)}, bf16[512,1024]{1,0:T(8,128)(2,1)}, u32[]{:S(2)}) copy-start(bf16[512,1024]{1,0:T(8,128)(2,1)} %param.8) | copy-start | bytes 3145732
  0.0 3.3 %copy-start.8 = (s32[8]{0:T(128)}, s32[8]{0:T(128)S(1)}, u32[]{:S(2)}) copy-start(s32[8]{0:T(128)S(1)} %iota_add_fusion.1) | copy-start | bytes 100
  0.0 3.3 %copy-start.10 = (s32[3]{0:T(128)}, s32[3]{0:T(128)S(1)}, u32[]{:S(2)}) copy-start(s32[3]{0:T(128)S(1)} %iota_add_fusion) | copy-start | bytes 40
  42.8 127.4 %all-to-all-start = ((bf16[8,4,64,1024]{3,2,1,0:T(8,128)(2,1)}), bf16[8,4,64,1024]{3,2,1,0:T(8,128)(2,1)}, u32[]{:S(2)}, u32[]{:S(2)}) async-start(bf16[8,4,64,1024]{3,2,1,0:T(8,128)(2,1)} %bitcast.30), calls=%async_computation | async-start | bytes 8388608 | tf_op jit(solution)/shard_map/all_to_all | solution.py:219
  53.6 5.9 %copy-start.1 = (s32[256]{0:T(256)S(1)}, s32[256]{0:T(256)}, u32[]{:S(2)}) copy-start(s32[256]{0:T(256)} %param.11) | copy-start | bytes 3076
  54.3 88.4 %collective-permute-start.1 = (bf16[64,1024]{1,0:T(8,128)(2,1)}, bf16[64,1024]{1,0:T(8,128)(2,1)S(1)}, u32[]{:S(2)}, u32[]{:S(2)}) collective-permute-start(bf16[64,1024]{1,0:T(8,128)(2,1)} %get-tuple-element.21), channel_id=1, source_target_pairs={{1,0},{2,1},{3,2},{4,3},{5,4},{6,5},{7,6},{8,7},{9,8},{10,9},{11,1... | collective-permute-start | bytes 393224 | tf_op jit(solution)/shard_map/ppermute | solution.py:204
  56.2 85.5 %collective-permute-start = (bf16[64,1024]{1,0:T(8,128)(2,1)}, bf16[64,1024]{1,0:T(8,128)(2,1)}, u32[]{:S(2)}, u32[]{:S(2)}) collective-permute-start(bf16[64,1024]{1,0:T(8,128)(2,1)} %get-tuple-element.22), channel_id=1, source_target_pairs={{0,1},{1,2},{2,3},{3,4},{4,5},{5,6},{6,7},{7,8},{8,9},{9,10},{10,1... | collective-permute-start | bytes 393224 | tf_op jit(solution)/shard_map/ppermute | solution.py:203
  60.3 0.8 copy-start.9
  60.3 0.8 copy-start.11
  79.9 4.1 %copy-start.7 = (s32[192]{0:T(256)S(1)}, s32[192]{0:T(256)}, u32[]{:S(2)}) copy-start(s32[192]{0:T(256)} %lt.87) | copy-start | bytes 2308
  83.9 4.2 %copy-start.3 = (bf16[1024,16,1,64]{0,3,2,1:T(8,128)(2,1)S(1)}, bf16[1024,16,1,64]{0,3,2,1:T(8,128)(2,1)}, u32[]{:S(2)}) copy-start(bf16[1024,16,1,64]{0,3,2,1:T(8,128)(2,1)} %get-tuple-element.18) | copy-start | bytes 6291460
  83.9 4.2 %copy-start.6 = (bf16[256,1024]{1,0:T(8,128)(2,1)S(1)}, bf16[256,1024]{1,0:T(8,128)(2,1)}, u32[]{:S(2)}) copy-start(bf16[256,1024]{1,0:T(8,128)(2,1)} %all_gather.7) | copy-start | bytes 1572868
  88.0 1.6 copy-start.5
  92.0 50.8 %copy-start.4 = (bf16[1024,16,1,64]{0,3,2,1:T(8,128)(2,1)S(1)}, bf16[1024,16,1,64]{0,3,2,1:T(8,128)(2,1)}, u32[]{:S(2)}) copy-start(bf16[1024,16,1,64]{0,3,2,1:T(8,128)(2,1)} %get-tuple-element.19) | copy-start | bytes 6291460

commit v5 on v3

--- a/solution.py
+++ b/solution.py
@@ -213,7 +213,8 @@
     summary = (pooled / jnp.sqrt(jnp.mean(pooled * pooled, axis=1, keepdims=True) + 1e-05)).astype(
         jnp.bfloat16
     )
-    summary_all = lax.all_gather(summary, ("ctx", "seq"), axis=0, tiled=True)
+    copies = jnp.broadcast_to(summary[None], (dev_count,) + summary.shape)
+    summary_all = lax.all_to_all(copies, ("ctx", "seq"), 0, 0, tiled=True).reshape(-1, model_dim)
     summary_all, outgoing = lax.optimization_barrier((summary_all, outgoing))
     incoming = lax.all_to_all(outgoing, "ctx", split_axis=0, concat_axis=0, tiled=True)
 

time: 214 us -> 190 us (0.89)
  blocking collectives: 35.5 us -> 0 us
  waiting for transfers between devices: 53.9 us -> 66.5 us
    all_gather x1 -> x0, blocking collectives: 35.5 us -> none  [local(): summary_all = lax.all_gather(summary, ('ctx', 'seq'), axis=0, tiled=True)]
    all_to_all x0 -> x1, waiting for transfers between devices: none -> 8.71 us  [local(): lax.all_to_all(copies, ('ctx', 'seq'), 0, 0, tiled=True)]
    all_to_all x1, starting transfers between devices: 15.1 us -> 7.01 us  [local(): lax.all_to_all(outgoing, 'ctx', split_axis=0, concat_axis=0, tiled=True)]
    ppermute x1, waiting for transfers between devices: 51.5 us -> 57.8 us  [local(): lax.ppermute(token_blocks[dev_blocks - 1], ('ctx', 'seq'), forward)]
    all_to_all x0 -> x1, starting transfers between devices: none -> 5.99 us  [local(): lax.all_to_all(copies, ('ctx', 'seq'), 0, 0, tiled=True)]
    ppermute x1, waiting for transfers between devices: 2.43 us -> 0.01 us  [local(): next_tokens = lax.ppermute(token_blocks[0], ('ctx', 'seq'), backward)]
  transfers between devices with their start and end apart: 3 -> 4, of which waited for: 2 -> 2; matrix products, arithmetic and copies ran while one was open for 19% -> 25% of each run, Pallas kernels for 11% -> 12%
where the time goes in v5:
time: 190 us; the launch traced here: 189 us
  waiting for transfers between devices  66.5 us (35%)
  Pallas kernels  49.8 us (26%)
  local copies, waits for them, and re-layouts  32.6 us (17%)
  starting transfers between devices  18.4 us (10%)
  matrix products  17.7 us (9%)
  other arithmetic  4.2 us (2%)
    ppermute x1, waiting for transfers between devices, local(): lax.ppermute(token_blocks[dev_blocks - 1], ('ctx', 'seq'), forward)  57.8 us
    pallas_call x1, Pallas kernels, attend_far(): pl.pallas_call(far_kernel, grid_spec=grid_spec, out_shape=jax.ShapeDtypeS...  27.5 us
    pallas_call x1, Pallas kernels, attend_near(): pl.pallas_call(near_kernel, grid=(blocks,), in_specs=[pl.BlockSpec((1, 1,...  22.2 us
    dot_general x5, matrix products, local(): jnp.dot(x, w, preferred_element_type=jnp.float32).astype(jnp.bfloat16)  14.3 us
    unnamed x29, local copies, waits for them, and re-layouts  10.3 us
    all_to_all x1, waiting for transfers between devices, local(): lax.all_to_all(copies, ('ctx', 'seq'), 0, 0, tiled=True)  8.71 us
    another operation x2, local copies, waits for them, and re-layouts, split_weights(): shaped[:, :, j, :].reshape(model_dim, head_total * HD)  7.86 us
    all_to_all x1, starting transfers between devices, local(): lax.all_to_all(outgoing, 'ctx', split_axis=0, concat_axis=0, tiled=True)  7.01 us
  transfers between devices with their start and end apart: 4, of which 2 were waited for; matrix products, arithmetic and copies ran while one was open for 25% of the time, Pallas kernels for 12%

profile of v5, /device:TPU:16, one launch (start us, length us, event | category | flops | bytes accessed | tf_op | source)
XLA Modules:
  0.0 189.5 jit_solution(248981895509151656)
XLA Ops:
  0.0 0.9 dynamic_slice.18
  0.9 0.2 convert_reduce_fusion
  1.2 1.6 select_reduce_fusion
  2.8 0.2 multiply_reduce_fusion
  3.1 0.9 broadcast_in_dim.39
  4.0 6.0 %all-to-all-start = ((bf16[32,8,1024]{2,1,0:T(8,128)(2,1)}), bf16[32,8,1024]{2,1,0:T(8,128)(2,1)}, u32[]{:S(2)}, u32[]{:S(2)}) async-start(bf16[32,8,1024]{2,1,0:T(8,128)(2,1)} %broadcast_in_dim.39), calls=%async_computation | async-start | bytes 1048576 | tf_op jit(solution)/shard_map/all_to_all | solution.py:217
  10.2 0.3 copy-done.8
  11.7 2.9 %gather_fusion = bf16[32,64,1024]{2,1,0:T(8,128)(2,1)} fusion(bf16[8,64,1024]{2,1,0:T(8,128)(2,1)S(1)} %bitcast.29, s32[1024]{0:T(1024)S(1)} %get-tuple-element.28), kind=kCustom, calls=%fused_computation.2 | custom fusion | bytes 8388736 | tf_op jit(solution)/shard_map/jit(_take)/gather | solution.py:198
  14.6 8.7 %all-to-all-done = bf16[32,8,1024]{2,1,0:T(8,128)(2,1)} async-done(((bf16[32,8,1024]{2,1,0:T(8,128)(2,1)}), bf16[32,8,1024]{2,1,0:T(8,128)(2,1)}, u32[]{:S(2)}, u32[]{:S(2)}) %all-to-all-start) | async-done | bytes 524320 | tf_op jit(solution)/shard_map/all_to_all | solution.py:217
  23.3 7.0 %all-to-all-start.1 = ((bf16[8,4,64,1024]{3,2,1,0:T(8,128)(2,1)}), bf16[8,4,64,1024]{3,2,1,0:T(8,128)(2,1)}, u32[]{:S(2)}, u32[]{:S(2)}) async-start(bf16[8,4,64,1024]{3,2,1,0:T(8,128)(2,1)} %bitcast.31), calls=%async_computation.1 | async-start | bytes 8388608 | tf_op jit(solution)/shard_map/all_to_all | solution.py:219
  30.3 0.7 fusion.5
  31.0 3.5 %collective-permute-start.1 = (bf16[64,1024]{1,0:T(8,128)(2,1)}, bf16[64,1024]{1,0:T(8,128)(2,1)S(1)}, u32[]{:S(2)}, u32[]{:S(2)}) collective-permute-start(bf16[64,1024]{1,0:T(8,128)(2,1)} %get-tuple-element.21), channel_id=1, source_target_pairs={{1,0},{2,1},{3,2},{4,3},{5,4},{6,5},{7,6},{8,7},{9,8},{10,9},{11,1... | collective-permute-start | bytes 393224 | tf_op jit(solution)/shard_map/ppermute | solution.py:204
  34.5 1.9 %collective-permute-start = (bf16[64,1024]{1,0:T(8,128)(2,1)}, bf16[64,1024]{1,0:T(8,128)(2,1)}, u32[]{:S(2)}, u32[]{:S(2)}) collective-permute-start(bf16[64,1024]{1,0:T(8,128)(2,1)} %get-tuple-element.22), channel_id=1, source_target_pairs={{0,1},{1,2},{2,3},{3,4},{4,5},{5,6},{6,7},{7,8},{8,9},{9,10},{10,1... | collective-permute-start | bytes 393224 | tf_op jit(solution)/shard_map/ppermute | solution.py:203
  36.4 0.6 lt.87
  37.2 0.7 gather_fusion.1
  38.0 0.7 gather_fusion.2
  39.4 8.6 %copy.43 = bf16[1024,3072]{0,1:T(8,128)(2,1)} copy(bf16[1024,3072]{1,0:T(8,128)(2,1)} %param.9) | data formatting | bytes 12582912 | tf_op args[1]
  48.0 5.8 %fusion.4 = (bf16[1024,16,1,64]{0,3,2,1:T(8,128)(2,1)}, bf16[1024,16,1,64]{0,3,2,1:T(8,128)(2,1)}, bf16[1024,16,1,64]{0,3,2,1:T(8,128)(2,1)}) fusion(bf16[1024,16,3,64]{0,3,2,1:T(8,128)(2,1)} %bitcast.30), kind=kLoop, calls=%fused_computation.46 | loop fusion | bytes 12582912 | tf_op jit(solution)/shard_map/slice | solution.py:34
  53.8 3.9 %copy.49.refs_3_ = bf16[1024,1024]{1,0:T(8,128)(2,1)} copy(bf16[1024,1024]{0,1:T(8,128)(2,1)} %bitcast.41) | data formatting | bytes 4194304 | tf_op jit(solution)/shard_map/reshape;squeeze | solution.py:34
  57.7 3.9 %copy.50.refs_4_ = bf16[1024,1024]{1,0:T(8,128)(2,1)} copy(bf16[1024,1024]{0,1:T(8,128)(2,1)} %bitcast.38) | data formatting | bytes 4194304 | tf_op jit(solution)/shard_map/reshape;squeeze | solution.py:34
  61.8 0.6 compare_convert_fusion
  62.5 3.8 %convolution_convert_fusion.2 = bf16[512,1024]{1,0:T(8,128)(2,1)} fusion(bf16[512,1024]{1,0:T(8,128)(2,1)S(1)} %copy-done.2, bf16[1024,1024]{0,1:T(8,128)(2,1)} %bitcast.44), kind=kOutput, calls=%fused_computation.7 | convolution fusion | flops 1074266112 | bytes 4194304 | tf_op jit(solution)/shard_map/dot_general | solution.py:222
  66.3 0.6 multiply_add_fusion.ids_ref
  66.9 57.8 %collective-permute-done = bf16[64,1024]{1,0:T(8,128)(2,1)} collective-permute-done((bf16[64,1024]{1,0:T(8,128)(2,1)}, bf16[64,1024]{1,0:T(8,128)(2,1)}, u32[]{:S(2)}, u32[]{:S(2)}) %collective-permute-start) | collective-permute-done | bytes 131104 | tf_op jit(solution)/shard_map/ppermute | solution.py:203
  124.7 0.9 constant_dynamic-update-slice_fusion.2
  125.8 2.6 %convolution_convert_fusion.1 = bf16[640,1024]{1,0:T(8,128)(2,1)} fusion(bf16[640,1024]{1,0:T(8,128)(2,1)S(1)} %constant_dynamic-update-slice_fusion, bf16[1024,1024]{0,1:T(8,128)(2,1)S(1)} %bitcast.42), kind=kOutput, calls=%fused_computation.6 | convolution fusion | flops 1342832640 | bytes 4718592 | tf_op jit(solution)/shard_map/dot_general | solution.py:222
  128.4 2.6 %convolution_convert_fusion = bf16[640,1024]{1,0:T(8,128)(2,1)} fusion(bf16[640,1024]{1,0:T(8,128)(2,1)S(1)} %constant_dynamic-update-slice_fusion, bf16[1024,1024]{0,1:T(8,128)(2,1)S(1)} %bitcast.39), kind=kOutput, calls=%fused_computation.5 | convolution fusion | flops 1342832640 | bytes 4718592 | tf_op jit(solution)/shard_map/dot_general | solution.py:222
  131.0 2.6 %convolution_convert_fusion.4.ks_ref = bf16[256,1024]{1,0:T(8,128)(2,1)} fusion(bf16[256,1024]{1,0:T(8,128)(2,1)} %bitcast.4, bf16[1024,1024]{0,1:T(8,128)(2,1)S(1)} %bitcast.43), kind=kOutput, calls=%fused_computation.9 | convolution fusion | flops 537133056 | bytes 3145728 | tf_op jit(solution)/shard_map/dot_general | solution.py:222
  133.6 2.6 %convolution_convert_fusion.3.vs_ref = bf16[256,1024]{1,0:T(8,128)(2,1)} fusion(bf16[256,1024]{1,0:T(8,128)(2,1)} %bitcast.4, bf16[1024,1024]{0,1:T(8,128)(2,1)S(1)} %bitcast.40), kind=kOutput, calls=%fused_computation.8 | convolution fusion | flops 537133056 | bytes 3145728 | tf_op jit(solution)/shard_map/dot_general | solution.py:222
  136.2 22.2 %shard_map.64 = (f32[8,64,1024]{2,1,0:T(8,128)}, f32[8,64,1024]{2,1,0:T(8,128)}, f32[8,64,1024]{2,1,0:T(8,128)}) custom-call(s32[8,1,192]{2,1,0:T(1,128)} %get-tuple-element.25.mask_ref, bf16[8,64,1024]{2,1,0:T(8,128)(2,1)} %bitcast.45, bf16[10,64,1024]{2,1,0:T(8,128)(2,1)} %bitcast.32, bf16[10,64,1024]{2,1,0:T(8,128)(2,1)} %bitcast.33, ...), custom_call_target="tpu_custom_call" | custom-call | flops 1879048192 | bytes 14680064 | tf_op jit(solution)/shard_map/pallas_call | solution.py:124
  158.5 27.5 %shard_map.65 = bf16[8,64,1024]{2,1,0:T(8,128)(2,1)} custom-call(s32[24]{0:T(128)} %multiply_add_fusion.ids_ref, s32[8,1,192]{2,1,0:T(1,128)} %get-tuple-element.26.mask_ref, bf16[8,64,1024]{2,1,0:T(8,128)(2,1)} %bitcast.46, bf16[32,64,1024]{2,1,0:T(8,128)(2,1)} %bitcast.7.refs_0_.refs_1_.refs_2_, bf16[32,64,1024]{2,1,0:T(8,128)(2,1)} %bitcast.7.refs_0_.refs_1_.refs_2_, ...), custom_call_target="tpu_custom_call" | custom-call | flops 7247757312 | bytes 15728640 | tf_op jit(solution)/shard_map/pallas_call | solution.py:165
  186.0 3.4 %add_convert_fusion = bf16[512,1024]{1,0:T(8,128)(2,1)} fusion(bf16[512,1024]{1,0:T(8,128)(2,1)S(1)} %copy-done.2, bf16[512,1024]{1,0:T(8,128)(2,1)} %bitcast.48, bf16[1024,1024]{1,0:T(8,128)(2,1)S(1)} %copy-done), kind=kOutput, calls=%fused_computation.3 | convolution fusion | flops 1075314688 | bytes 5242880 | tf_op jit(solution)/shard_map/dot_general | solution.py:257
  (63 shorter events, 2.6 us)
Async XLA Ops:
  0.0 186.0 %copy-start = (bf16[1024,1024]{1,0:T(8,128)(2,1)S(1)}, bf16[1024,1024]{1,0:T(8,128)(2,1)}, u32[]{:S(2)}) copy-start(bf16[1024,1024]{1,0:T(8,128)(2,1)} %param.10) | copy-start | bytes 6291460
  0.0 11.7 %copy-start.2 = (bf16[512,1024]{1,0:T(8,128)(2,1)S(1)}, bf16[512,1024]{1,0:T(8,128)(2,1)}, u32[]{:S(2)}) copy-start(bf16[512,1024]{1,0:T(8,128)(2,1)} %param.8) | copy-start | bytes 3145732
  0.0 10.6 %copy-start.5 = (s32[256,3]{0,1:T(4,128)S(1)}, s32[256,3]{0,1:T(4,128)}, u32[]{:S(2)}) copy-start(s32[256,3]{0,1:T(4,128)} %param.12) | copy-start | bytes 9220
  0.0 11.0 %copy-start.6 = (s32[256,3]{0,1:T(4,128)S(1)}, s32[256,3]{0,1:T(4,128)}, u32[]{:S(2)}) copy-start(s32[256,3]{0,1:T(4,128)} %param.13) | copy-start | bytes 9220
  4.0 19.3 %all-to-all-start = ((bf16[32,8,1024]{2,1,0:T(8,128)(2,1)}), bf16[32,8,1024]{2,1,0:T(8,128)(2,1)}, u32[]{:S(2)}, u32[]{:S(2)}) async-start(bf16[32,8,1024]{2,1,0:T(8,128)(2,1)} %broadcast_in_dim.39), calls=%async_computation | async-start | bytes 1048576 | tf_op jit(solution)/shard_map/all_to_all | solution.py:217
  10.0 0.5 copy-start.8
  10.0 0.6 copy-start.10
  23.3 135.2 %all-to-all-start.1 = ((bf16[8,4,64,1024]{3,2,1,0:T(8,128)(2,1)}), bf16[8,4,64,1024]{3,2,1,0:T(8,128)(2,1)}, u32[]{:S(2)}, u32[]{:S(2)}) async-start(bf16[8,4,64,1024]{3,2,1,0:T(8,128)(2,1)} %bitcast.31), calls=%async_computation.1 | async-start | bytes 8388608 | tf_op jit(solution)/shard_map/all_to_all | solution.py:219
  30.3 6.9 %copy-start.1 = (s32[256]{0:T(256)S(1)}, s32[256]{0:T(256)}, u32[]{:S(2)}) copy-start(s32[256]{0:T(256)} %param.11) | copy-start | bytes 3076
  31.0 94.7 %collective-permute-start.1 = (bf16[64,1024]{1,0:T(8,128)(2,1)}, bf16[64,1024]{1,0:T(8,128)(2,1)S(1)}, u32[]{:S(2)}, u32[]{:S(2)}) collective-permute-start(bf16[64,1024]{1,0:T(8,128)(2,1)} %get-tuple-element.21), channel_id=1, source_target_pairs={{1,0},{2,1},{3,2},{4,3},{5,4},{6,5},{7,6},{8,7},{9,8},{10,9},{11,1... | collective-permute-start | bytes 393224 | tf_op jit(solution)/shard_map/ppermute | solution.py:204
  34.5 90.3 %collective-permute-start = (bf16[64,1024]{1,0:T(8,128)(2,1)}, bf16[64,1024]{1,0:T(8,128)(2,1)}, u32[]{:S(2)}, u32[]{:S(2)}) collective-permute-start(bf16[64,1024]{1,0:T(8,128)(2,1)} %get-tuple-element.22), channel_id=1, source_target_pairs={{0,1},{1,2},{2,3},{3,4},{4,5},{5,6},{6,7},{7,8},{8,9},{9,10},{10,1... | collective-permute-start | bytes 393224 | tf_op jit(solution)/shard_map/ppermute | solution.py:203
  38.0 0.8 copy-start.9
  38.0 0.8 copy-start.11
  57.7 4.1 %copy-start.7 = (s32[192]{0:T(256)S(1)}, s32[192]{0:T(256)}, u32[]{:S(2)}) copy-start(s32[192]{0:T(256)} %lt.87) | copy-start | bytes 2308
  66.3 59.4 %copy-start.4 = (bf16[1024,16,1,64]{0,3,2,1:T(8,128)(2,1)S(1)}, bf16[1024,16,1,64]{0,3,2,1:T(8,128)(2,1)}, u32[]{:S(2)}) copy-start(bf16[1024,16,1,64]{0,3,2,1:T(8,128)(2,1)} %get-tuple-element.19) | copy-start | bytes 6291460
  125.8 2.6 %copy-start.3 = (bf16[1024,16,1,64]{0,3,2,1:T(8,128)(2,1)S(1)}, bf16[1024,16,1,64]{0,3,2,1:T(8,128)(2,1)}, u32[]{:S(2)}) copy-start(bf16[1024,16,1,64]{0,3,2,1:T(8,128)(2,1)} %get-tuple-element.18) | copy-start | bytes 6291460

commit v6 on v5

--- a/solution.py
+++ b/solution.py
@@ -1,3 +1,4 @@
+import functools
 import math
 
 import jax
@@ -77,28 +78,27 @@
         l_ref[0, :, cols] = pick_rows(jnp.broadcast_to(total, result.shape), low, rows)
 
 
-def far_kernel(ids_ref, mask_ref, q_ref, *refs):
-    far_count = RAND
-    token_refs = refs[:far_count]
-    wk_ref, wv_ref, oa_ref, ma_ref, la_ref, out_ref = refs[far_count:]
+def far_kernel(final, ids_ref, mask_ref, q_ref, *refs):
+    k_refs = refs[:RAND]
+    v_refs = refs[RAND : 2 * RAND]
+    oa_ref, ma_ref, la_ref = refs[2 * RAND : 2 * RAND + 3]
+    out_refs = refs[2 * RAND + 3 :]
     width = q_ref.shape[-1]
     rows = q_ref.shape[1]
     scaling = 1.0 / math.sqrt(HD)
     valid = mask_ref[0] != 0
     low = lax.broadcasted_iota(jnp.int32, (rows, LANES), 1) < HD
-    far_tokens = jnp.concatenate([ref[0] for ref in token_refs], axis=0)
-    k_far = jnp.dot(far_tokens, wk_ref[...], preferred_element_type=jnp.float32).astype(jnp.bfloat16)
-    v_far = jnp.dot(far_tokens, wv_ref[...], preferred_element_type=jnp.float32).astype(jnp.bfloat16)
     for tile in range(width // LANES):
-        lanes = slice(tile * LANES, (tile + 1) * LANES)
         cols = pl.ds(tile * LANES, LANES)
         q_pair = pair_rows(q_ref[0, :, cols], low)
-        scores = lax.dot_general(q_pair, k_far[:, lanes], CONTRACT, preferred_element_type=jnp.float32)
+        k_far = jnp.concatenate([ref[0, :, cols] for ref in k_refs], axis=0)
+        v_far = jnp.concatenate([ref[0, :, cols] for ref in v_refs], axis=0)
+        scores = lax.dot_general(q_pair, k_far, CONTRACT, preferred_element_type=jnp.float32)
         scores = jnp.where(valid, scores * scaling, -jnp.inf)
-        peak = jnp.max(scores, axis=-1, keepdims=True)
+        peak = jnp.maximum(jnp.max(scores, axis=-1, keepdims=True), -1e30)
         exps = jnp.exp(scores - peak)
         total = jnp.sum(exps, axis=-1, keepdims=True)
-        result = jnp.dot(exps.astype(jnp.bfloat16), v_far[:, lanes], preferred_element_type=jnp.float32)
+        result = jnp.dot(exps.astype(jnp.bfloat16), v_far, preferred_element_type=jnp.float32)
         o_b = pick_rows(result, low, rows)
         m_b = pick_rows(jnp.broadcast_to(peak, result.shape), low, rows)
         l_b = pick_rows(jnp.broadcast_to(total, result.shape), low, rows)
@@ -108,7 +108,12 @@
         scale_b = jnp.exp(m_b - peak_all)
         numerator = oa_ref[0, :, cols] * scale_a + o_b * scale_b
         denominator = la_ref[0, :, cols] * scale_a + l_b * scale_b
-        out_ref[0, :, cols] = (numerator / denominator).astype(out_ref.dtype)
+        if final:
+            out_refs[0][0, :, cols] = (numerator / denominator).astype(out_refs[0].dtype)
+        else:
+            out_refs[0][0, :, cols] = numerator
+            out_refs[1][0, :, cols] = peak_all
+            out_refs[2][0, :, cols] = denominator
 
 
 def attend_near(mask, q, k_ext, v_ext, k_sum, v_sum):
@@ -137,41 +142,42 @@
     )(mask, q, k_ext, k_ext, k_ext, v_ext, v_ext, v_ext, k_sum, v_sum)
 
 
-def attend_far(slot_ids, mask, q, incoming, w_k, w_v, o_a, m_a, l_a):
+def attend_far(final, slot_ids, mask, q, k_slots, v_slots, o_a, m_a, l_a):
     blocks, rows, width = q.shape
-    model_dim = incoming.shape[-1]
     block = pl.BlockSpec((1, rows, width), lambda i, ids: (i, 0, 0))
-    token_specs = [
-        pl.BlockSpec((1, rows, model_dim), lambda i, ids, j=j: (ids[RAND * i + j], 0, 0))
+    slot_specs = [
+        pl.BlockSpec((1, rows, width), lambda i, ids, j=j: (ids[RAND * i + j], 0, 0))
         for j in range(RAND)
     ]
-    weight = pl.BlockSpec(w_k.shape, lambda i, ids: (0, 0))
     local_keys = RAND * rows
     heads = width // HD
-    flops = blocks * (
-        heads * 2 * rows * 2 * LANES * local_keys + 2 * 2 * local_keys * model_dim * width
-    )
-    bytes_accessed = 2 * blocks * rows * (width * 2 + model_dim * RAND) + 4 * w_k.size + (
-        12 * blocks * rows * width
-    )
+    flops = blocks * heads * 2 * rows * 2 * LANES * local_keys
+    bytes_accessed = 2 * blocks * rows * width * (2 + 2 * RAND) + 24 * blocks * rows * width
+    part = jax.ShapeDtypeStruct((blocks, rows, width), jnp.float32)
+    if final:
+        out_shape = jax.ShapeDtypeStruct((blocks, rows, width), jnp.bfloat16)
+        out_specs = block
+    else:
+        out_shape = [part] * 3
+        out_specs = [block] * 3
     grid_spec = pltpu.PrefetchScalarGridSpec(
         num_scalar_prefetch=1,
         grid=(blocks,),
         in_specs=[pl.BlockSpec((1, 1, local_keys), lambda i, ids: (i, 0, 0)), block]
-        + token_specs
-        + [weight, weight, block, block, block],
-        out_specs=block,
+        + slot_specs * 2
+        + [block, block, block],
+        out_specs=out_specs,
     )
     return pl.pallas_call(
-        far_kernel,
+        functools.partial(far_kernel, final),
         grid_spec=grid_spec,
-        out_shape=jax.ShapeDtypeStruct((blocks, rows, width), jnp.bfloat16),
+        out_shape=out_shape,
         cost_estimate=pl.CostEstimate(
             flops=flops,
             transcendentals=blocks * heads * rows * local_keys,
             bytes_accessed=bytes_accessed,
         ),
-    )(slot_ids, mask, q, incoming, incoming, incoming, w_k, w_v, o_a, m_a, l_a)
+    )(slot_ids, mask, q, *([k_slots] * RAND), *([v_slots] * RAND), o_a, m_a, l_a)
 
 
 def local(tokens, w_qkv, w_out, counts, rand_seg, rand_off):
@@ -198,6 +204,7 @@
     outgoing = jnp.take(token_blocks, send_off.reshape(-1), axis=0, mode="clip").reshape(
         ctx_count, capacity, BLK, model_dim
     )
+    cap_a = capacity - 1
     forward = [(i, i + 1) for i in range(dev_count - 1)]
     backward = [(i + 1, i) for i in range(dev_count - 1)]
     prev_tokens = lax.ppermute(token_blocks[dev_blocks - 1], ("ctx", "seq"), forward)
@@ -216,7 +223,7 @@
     copies = jnp.broadcast_to(summary[None], (dev_count,) + summary.shape)
     summary_all = lax.all_to_all(copies, ("ctx", "seq"), 0, 0, tiled=True).reshape(-1, model_dim)
     summary_all, outgoing = lax.optimization_barrier((summary_all, outgoing))
-    incoming = lax.all_to_all(outgoing, "ctx", split_axis=0, concat_axis=0, tiled=True)
+    incoming_a = lax.all_to_all(outgoing[:, :cap_a], "ctx", split_axis=0, concat_axis=0, tiled=True)
 
     w_q, w_k, w_v = split_weights(w_qkv, head_total)
     project = lambda x, w: jnp.dot(x, w, preferred_element_type=jnp.float32).astype(jnp.bfloat16)
@@ -230,7 +237,10 @@
     my_owner = lax.dynamic_slice_in_dim(rand_seg, first_block, dev_blocks)
     my_offset = lax.dynamic_slice_in_dim(rand_off, first_block, dev_blocks)
     mine = my_owner.reshape(dev_blocks * RAND)
-    slot_ids = mine * capacity + positions_among(mine, ctx_count)
+    ranks = positions_among(mine, ctx_count)
+    in_a = ranks < cap_a
+    ids_a = jnp.where(in_a, mine * cap_a + ranks, 0)
+    ids_b = jnp.where(in_a, 0, mine * (capacity - cap_a) + ranks - cap_a)
 
     block_ids = first_block + jnp.arange(dev_blocks, dtype=jnp.int32)
     near_ids = block_ids[:, None] + jnp.arange(-1, 2, dtype=jnp.int32)[None, :]
@@ -240,20 +250,26 @@
     far_counts = jnp.take(counts, far_global)
     positions = jnp.arange(BLK, dtype=jnp.int32)[None, None, :]
     near_mask = (positions < near_counts[:, :, None]).astype(jnp.int32).reshape(dev_blocks, 1, -1)
-    far_mask = (positions < far_counts[:, :, None]).astype(jnp.int32).reshape(dev_blocks, 1, -1)
+    far_valid = positions < far_counts[:, :, None]
+    chunk_a = in_a.reshape(dev_blocks, RAND)[:, :, None]
+    mask_a = (far_valid & chunk_a).astype(jnp.int32).reshape(dev_blocks, 1, -1)
+    mask_b = (far_valid & ~chunk_a).astype(jnp.int32).reshape(dev_blocks, 1, -1)
 
     o_a, m_a, l_a = attend_near(near_mask, q_own, k_ext, v_ext, k_sum, v_sum)
-    attended = attend_far(
-        slot_ids,
-        far_mask,
-        q_own,
-        incoming.reshape(ctx_count * capacity, BLK, model_dim),
-        w_k,
-        w_v,
-        o_a,
-        m_a,
-        l_a,
-    ).reshape(tok_rows, model_dim)
+    incoming_a, outgoing_b, o_a, m_a, l_a = lax.optimization_barrier(
+        (incoming_a, outgoing[:, cap_a:], o_a, m_a, l_a)
+    )
+    incoming_b = lax.all_to_all(outgoing_b, "ctx", split_axis=0, concat_axis=0, tiled=True)
+    slots_a = incoming_a.reshape(-1, model_dim)
+    k_a = project(slots_a, w_k).reshape(-1, BLK, model_dim)
+    v_a = project(slots_a, w_v).reshape(-1, BLK, model_dim)
+    o_a, m_a, l_a = attend_far(False, ids_a, mask_a, q_own, k_a, v_a, o_a, m_a, l_a)
+    slots_b = incoming_b.reshape(-1, model_dim)
+    k_b = project(slots_b, w_k).reshape(-1, BLK, model_dim)
+    v_b = project(slots_b, w_v).reshape(-1, BLK, model_dim)
+    attended = attend_far(True, ids_b, mask_b, q_own, k_b, v_b, o_a, m_a, l_a).reshape(
+        tok_rows, model_dim
+    )
     mixed = tokens.astype(jnp.float32) + jnp.dot(attended, w_out, preferred_element_type=jnp.float32)
     return mixed.astype(jnp.bfloat16)
 

time: 190 us -> 215 us (1.13)
  matrix products: 17.7 us -> 38.7 us
  Pallas kernels: 49.8 us -> 62.6 us
  waiting for transfers between devices: 66.5 us -> 55.3 us
  starting transfers between devices: 18.4 us -> 22.8 us
  local copies, waits for them, and re-layouts: 32.6 us -> 29.7 us
    dot_general x5 -> x9, matrix products: 14.3 us -> 35.3 us  [local(): jnp.dot(x, w, preferred_element_type=jnp.float32).astype(jnp.bfloat16)]
    pallas_call x1 -> x2, Pallas kernels: 27.5 us -> 40.3 us  [attend_far(): pl.pallas_call(functools.partial(far_kernel, final), grid_spec=grid_spec,...]
    ppermute x1, waiting for transfers between devices: 57.8 us -> 46.5 us  [local(): lax.ppermute(token_blocks[dev_blocks - 1], ('ctx', 'seq'), forward)]
    another operation x2 -> x0, local copies, waits for them, and re-layouts: 7.86 us -> none  [split_weights(): shaped[:, :, j, :].reshape(model_dim, head_total * HD)]
    slice x0 -> x2, local copies, waits for them, and re-layouts: none -> 6.27 us  [the longest x1 3.98 us: local(): outgoing[:, :cap_a]]
    all_to_all x1 -> x2, starting transfers between devices: 7.01 us -> 11.4 us  [the longest x1 7.05 us: local(): lax.all_to_all(outgoing[:, :cap_a], 'ctx', split_axis=0, concat_axis=0, t...]
    unnamed x29 -> x33, local copies, waits for them, and re-layouts: 10.3 us -> 10.3 us
  transfers between devices with their start and end apart: 4 -> 5, of which waited for: 2 -> 2; matrix products, arithmetic and copies ran while one was open for 25% -> 25% of each run, Pallas kernels for 12% -> 20%
where the time goes in v6:
time: 215 us; the launch traced here: 214 us
  Pallas kernels  62.6 us (29%)
  waiting for transfers between devices  55.3 us (26%)
  matrix products  38.7 us (18%)
  local copies, waits for them, and re-layouts  29.7 us (14%)
  starting transfers between devices  22.8 us (11%)
  other arithmetic  4.16 us (2%)
    ppermute x1, waiting for transfers between devices, local(): lax.ppermute(token_blocks[dev_blocks - 1], ('ctx', 'seq'), forward)  46.5 us
    pallas_call x2, Pallas kernels, attend_far(): pl.pallas_call(functools.partial(far_kernel, final), grid_spec=grid_spec,...  40.3 us
    dot_general x9, matrix products, local(): jnp.dot(x, w, preferred_element_type=jnp.float32).astype(jnp.bfloat16)  35.3 us
    pallas_call x1, Pallas kernels, attend_near(): pl.pallas_call(near_kernel, grid=(blocks,), in_specs=[pl.BlockSpec((1, 1,...  22.3 us
    unnamed x33, local copies, waits for them, and re-layouts  10.3 us
    all_to_all x1, waiting for transfers between devices, local(): lax.all_to_all(copies, ('ctx', 'seq'), 0, 0, tiled=True)  8.77 us
    all_to_all x1, starting transfers between devices, local(): lax.all_to_all(outgoing[:, :cap_a], 'ctx', split_axis=0, concat_axis=0, t...  7.05 us
    all_to_all x1, starting transfers between devices, local(): lax.all_to_all(copies, ('ctx', 'seq'), 0, 0, tiled=True)  5.99 us
  transfers between devices with their start and end apart: 5, of which 2 were waited for; matrix products, arithmetic and copies ran while one was open for 25% of the time, Pallas kernels for 20%

profile of v6, /device:TPU:16, one launch (start us, length us, event | category | flops | bytes accessed | tf_op | source)
XLA Modules:
  0.0 213.6 jit_solution(3694419884095783643)
XLA Ops:
  0.0 0.9 dynamic_slice.18
  1.2 1.6 select_reduce_fusion
  3.1 0.9 broadcast_in_dim.64
  4.0 6.0 %all-to-all-start = ((bf16[32,8,1024]{2,1,0:T(8,128)(2,1)}), bf16[32,8,1024]{2,1,0:T(8,128)(2,1)}, u32[]{:S(2)}, u32[]{:S(2)}) async-start(bf16[32,8,1024]{2,1,0:T(8,128)(2,1)} %broadcast_in_dim.64), calls=%async_computation | async-start | bytes 1048576 | tf_op jit(solution)/shard_map/all_to_all | solution.py:224
  11.7 2.8 %gather_fusion = bf16[32,64,1024]{2,1,0:T(8,128)(2,1)} fusion(bf16[8,64,1024]{2,1,0:T(8,128)(2,1)S(1)} %bitcast.42, s32[1024]{0:T(1024)S(1)} %get-tuple-element.47), kind=kCustom, calls=%fused_computation.2 | custom fusion | bytes 8388736 | tf_op jit(solution)/shard_map/jit(_take)/gather | solution.py:204
  14.5 8.8 %all-to-all-done = bf16[32,8,1024]{2,1,0:T(8,128)(2,1)} async-done(((bf16[32,8,1024]{2,1,0:T(8,128)(2,1)}), bf16[32,8,1024]{2,1,0:T(8,128)(2,1)}, u32[]{:S(2)}, u32[]{:S(2)}) %all-to-all-start) | async-done | bytes 524320 | tf_op jit(solution)/shard_map/all_to_all | solution.py:224
  23.3 4.0 %slice.24 = bf16[8,3,64,1024]{3,2,1,0:T(8,128)(2,1)} slice(bf16[8,4,64,1024]{3,2,1,0:T(8,128)(2,1)} %bitcast.50), slice={[0:8], [0:3], [0:64], [0:1024]} | slice | bytes 6291456 | tf_op jit(solution)/shard_map/slice | solution.py:226
  27.3 7.0 %all-to-all-start.1 = ((bf16[8,3,64,1024]{3,2,1,0:T(8,128)(2,1)}), bf16[8,3,64,1024]{3,2,1,0:T(8,128)(2,1)}, u32[]{:S(2)}, u32[]{:S(2)}) async-start(bf16[8,3,64,1024]{3,2,1,0:T(8,128)(2,1)} %slice.24), calls=%async_computation.1 | async-start | bytes 6291456 | tf_op jit(solution)/shard_map/all_to_all | solution.py:226
  34.3 0.7 fusion.5
  35.0 3.5 %collective-permute-start.1 = (bf16[64,1024]{1,0:T(8,128)(2,1)}, bf16[64,1024]{1,0:T(8,128)(2,1)S(1)}, u32[]{:S(2)}, u32[]{:S(2)}) collective-permute-start(bf16[64,1024]{1,0:T(8,128)(2,1)} %get-tuple-element.37), channel_id=1, source_target_pairs={{1,0},{2,1},{3,2},{4,3},{5,4},{6,5},{7,6},{8,7},{9,8},{10,9},{11,1... | collective-permute-start | bytes 393224 | tf_op jit(solution)/shard_map/ppermute | solution.py:211
  38.5 1.9 collective-permute-start
  41.3 0.7 gather_fusion.1
  42.1 0.7 gather_fusion.2
  44.1 8.6 %copy.42 = bf16[1024,3072]{0,1:T(8,128)(2,1)} copy(bf16[1024,3072]{1,0:T(8,128)(2,1)} %param.9) | data formatting | bytes 12582912 | tf_op args[1]
  52.7 4.1 %fusion.4 = (bf16[1024,16,1,64]{0,3,2,1:T(8,128)(2,1)S(1)}, bf16[1024,16,1,64]{0,3,2,1:T(8,128)(2,1)S(1)}, bf16[1024,16,1,64]{0,3,2,1:T(8,128)(2,1)S(1)}) fusion(bf16[1024,16,3,64]{0,3,2,1:T(8,128)(2,1)} %bitcast.49), kind=kLoop, calls=%fused_computation.53 | loop fusion | bytes 12582912 | tf_op jit(solution)/shard_map/slice | solution.py:35
  56.8 2.3 %convolution_convert_fusion.6 = bf16[512,1024]{1,0:T(8,128)(2,1)} fusion(bf16[512,1024]{1,0:T(8,128)(2,1)S(1)} %copy-done.2, bf16[1024,1024]{0,1:T(8,128)(2,1)S(1)} %bitcast.75), kind=kOutput, calls=%fused_computation.11 | convolution fusion | flops 1074266112 | bytes 4194304 | tf_op jit(solution)/shard_map/dot_general | solution.py:229
  59.8 46.5 %collective-permute-done = bf16[64,1024]{1,0:T(8,128)(2,1)} collective-permute-done((bf16[64,1024]{1,0:T(8,128)(2,1)}, bf16[64,1024]{1,0:T(8,128)(2,1)}, u32[]{:S(2)}, u32[]{:S(2)}) %collective-permute-start) | collective-permute-done | bytes 131104 | tf_op jit(solution)/shard_map/ppermute | solution.py:210
  106.3 0.9 constant_dynamic-update-slice_fusion.2
  107.3 2.7 %convolution_convert_fusion.3 = bf16[640,1024]{1,0:T(8,128)(2,1)} fusion(bf16[640,1024]{1,0:T(8,128)(2,1)S(1)} %constant_dynamic-update-slice_fusion, bf16[1024,1024]{0,1:T(8,128)(2,1)S(1)} %bitcast.67), kind=kOutput, calls=%fused_computation.8 | convolution fusion | flops 1342832640 | bytes 4718592 | tf_op jit(solution)/shard_map/dot_general | solution.py:229
  110.0 2.6 %convolution_convert_fusion.2 = bf16[640,1024]{1,0:T(8,128)(2,1)} fusion(bf16[640,1024]{1,0:T(8,128)(2,1)S(1)} %constant_dynamic-update-slice_fusion, bf16[1024,1024]{0,1:T(8,128)(2,1)S(1)} %bitcast.71), kind=kOutput, calls=%fused_computation.7 | convolution fusion | flops 1342832640 | bytes 4718592 | tf_op jit(solution)/shard_map/dot_general | solution.py:229
  112.6 2.3 %slice.25 = bf16[8,1,64,1024]{3,2,1,0:T(8,128)(2,1)} slice(bf16[8,4,64,1024]{3,2,1,0:T(8,128)(2,1)} %bitcast.51), slice={[0:8], [3:4], [0:64], [0:1024]} | slice | bytes 2097152 | tf_op jit(solution)/shard_map/slice | solution.py:260
  114.9 2.6 %convolution_convert_fusion.8.ks_ref = bf16[256,1024]{1,0:T(8,128)(2,1)} fusion(bf16[256,1024]{1,0:T(8,128)(2,1)} %bitcast.4, bf16[1024,1024]{0,1:T(8,128)(2,1)S(1)} %bitcast.68), kind=kOutput, calls=%fused_computation.13 | convolution fusion | flops 537133056 | bytes 3145728 | tf_op jit(solution)/shard_map/dot_general | solution.py:229
  117.5 2.6 %convolution_convert_fusion.7.vs_ref = bf16[256,1024]{1,0:T(8,128)(2,1)} fusion(bf16[256,1024]{1,0:T(8,128)(2,1)} %bitcast.4, bf16[1024,1024]{0,1:T(8,128)(2,1)S(1)} %bitcast.72), kind=kOutput, calls=%fused_computation.12 | convolution fusion | flops 537133056 | bytes 3145728 | tf_op jit(solution)/shard_map/dot_general | solution.py:229
  120.1 22.3 %shard_map.64 = (f32[8,64,1024]{2,1,0:T(8,128)}, f32[8,64,1024]{2,1,0:T(8,128)}, f32[8,64,1024]{2,1,0:T(8,128)}) custom-call(s32[8,1,192]{2,1,0:T(1,128)} %get-tuple-element.43.mask_ref, bf16[8,64,1024]{2,1,0:T(8,128)(2,1)} %bitcast.64, bf16[10,64,1024]{2,1,0:T(8,128)(2,1)} %bitcast.52, bf16[10,64,1024]{2,1,0:T(8,128)(2,1)} %bitcast.53, ...), custom_call_target="tpu_custom_call" | custom-call | flops 1879048192 | bytes 14680064 | tf_op jit(solution)/shard_map/pallas_call | solution.py:129
  142.3 4.4 %all-to-all-start.2 = ((bf16[8,1,64,1024]{3,2,1,0:T(8,128)(2,1)}), bf16[8,1,64,1024]{3,2,1,0:T(8,128)(2,1)}, u32[]{:S(2)}, u32[]{:S(2)}) async-start(bf16[8,1,64,1024]{3,2,1,0:T(8,128)(2,1)} %slice.25), calls=%async_computation.2 | async-start | bytes 2097152 | tf_op jit(solution)/shard_map/all_to_all | solution.py:262
  147.3 7.8 %convolution_convert_fusion.1 = bf16[1536,1024]{1,0:T(8,128)(2,1)} fusion(bf16[1536,1024]{1,0:T(8,128)(2,1)} %bitcast.14, bf16[1024,1024]{0,1:T(8,128)(2,1)} %bitcast.69), kind=kOutput, calls=%fused_computation.4 | convolution fusion | flops 3222798336 | bytes 8388608 | tf_op jit(solution)/shard_map/dot_general | solution.py:229
  155.1 6.9 %convolution_convert_fusion = bf16[1536,1024]{1,0:T(8,128)(2,1)} fusion(bf16[1536,1024]{1,0:T(8,128)(2,1)} %bitcast.14, bf16[1024,1024]{0,1:T(8,128)(2,1)S(1)} %bitcast.74), kind=kOutput, calls=%fused_computation.3 | convolution fusion | flops 3222798336 | bytes 8388608 | tf_op jit(solution)/shard_map/dot_general | solution.py:229
  161.9 20.1 %shard_map.65 = (f32[8,64,1024]{2,1,0:T(8,128)}, f32[8,64,1024]{2,1,0:T(8,128)}, f32[8,64,1024]{2,1,0:T(8,128)}) custom-call(s32[24]{0:T(128)} %get-tuple-element.44.ids_ref, s32[8,1,192]{2,1,0:T(1,128)} %get-tuple-element.41.mask_ref, bf16[8,64,1024]{2,1,0:T(8,128)(2,1)} %bitcast.65, bf16[24,64,1024]{2,1,0:T(8,128)(2,1)} %bitcast.43, ...), custom_call_target="tpu_custom_call" | custom-call | flops 805306368 | bytes 20971520 | tf_op jit(solution)/shard_map/pallas_call | solution.py:171
  182.1 4.3 %convolution_convert_fusion.4 = bf16[512,1024]{1,0:T(8,128)(2,1)} fusion(bf16[512,1024]{1,0:T(8,128)(2,1)} %bitcast.11, bf16[1024,1024]{0,1:T(8,128)(2,1)} %bitcast.73), kind=kOutput, calls=%fused_computation.9 | convolution fusion | flops 1074266112 | bytes 4194304 | tf_op jit(solution)/shard_map/dot_general | solution.py:229
  186.4 3.5 %convolution_convert_fusion.5 = bf16[512,1024]{1,0:T(8,128)(2,1)} fusion(bf16[512,1024]{1,0:T(8,128)(2,1)} %bitcast.11, bf16[1024,1024]{0,1:T(8,128)(2,1)S(1)} %bitcast.70), kind=kOutput, calls=%fused_computation.10 | convolution fusion | flops 1074266112 | bytes 4194304 | tf_op jit(solution)/shard_map/dot_general | solution.py:229
  189.9 20.2 %shard_map.66 = bf16[8,64,1024]{2,1,0:T(8,128)(2,1)} custom-call(s32[24]{0:T(128)} %get-tuple-element.45.ids_ref, s32[8,1,192]{2,1,0:T(1,128)} %get-tuple-element.42.mask_ref, bf16[8,64,1024]{2,1,0:T(8,128)(2,1)} %bitcast.66, bf16[8,64,1024]{2,1,0:T(8,128)(2,1)} %bitcast.61, bf16[8,64,1024]{2,1,0:T(8,128)(2,1)} %bitcast.62, bf16[8,64,1024]{2,1,0:T(8,128)(2,1)} %bitcast.63, ...), custom_call_target="tpu_custom_call" | custom-call | flops 805306368 | bytes 20971520 | tf_op jit(solution)/shard_map/pallas_call | solution.py:171
  210.1 3.4 %add_convert_fusion = bf16[512,1024]{1,0:T(8,128)(2,1)} fusion(bf16[512,1024]{1,0:T(8,128)(2,1)S(1)} %copy-done.2, bf16[512,1024]{1,0:T(8,128)(2,1)} %bitcast.76, bf16[1024,1024]{1,0:T(8,128)(2,1)S(1)} %copy-done), kind=kOutput, calls=%fused_computation.5 | convolution fusion | flops 1075314688 | bytes 5242880 | tf_op jit(solution)/shard_map/dot_general | solution.py:273
  (81 shorter events, 5.6 us)
Async XLA Ops:
  0.0 210.1 %copy-start = (bf16[1024,1024]{1,0:T(8,128)(2,1)S(1)}, bf16[1024,1024]{1,0:T(8,128)(2,1)}, u32[]{:S(2)}) copy-start(bf16[1024,1024]{1,0:T(8,128)(2,1)} %param.10) | copy-start | bytes 6291460
  0.0 11.7 %copy-start.2 = (bf16[512,1024]{1,0:T(8,128)(2,1)S(1)}, bf16[512,1024]{1,0:T(8,128)(2,1)}, u32[]{:S(2)}) copy-start(bf16[512,1024]{1,0:T(8,128)(2,1)} %param.8) | copy-start | bytes 3145732
  0.0 10.6 %copy-start.8 = (s32[256,3]{0,1:T(4,128)S(1)}, s32[256,3]{0,1:T(4,128)}, u32[]{:S(2)}) copy-start(s32[256,3]{0,1:T(4,128)} %param.12) | copy-start | bytes 9220
  0.0 11.0 %copy-start.9 = (s32[256,3]{0,1:T(4,128)S(1)}, s32[256,3]{0,1:T(4,128)}, u32[]{:S(2)}) copy-start(s32[256,3]{0,1:T(4,128)} %param.13) | copy-start | bytes 9220
  4.0 19.3 %all-to-all-start = ((bf16[32,8,1024]{2,1,0:T(8,128)(2,1)}), bf16[32,8,1024]{2,1,0:T(8,128)(2,1)}, u32[]{:S(2)}, u32[]{:S(2)}) async-start(bf16[32,8,1024]{2,1,0:T(8,128)(2,1)} %broadcast_in_dim.64), calls=%async_computation | async-start | bytes 1048576 | tf_op jit(solution)/shard_map/all_to_all | solution.py:224
  10.0 0.5 copy-start.10
  10.0 0.6 copy-start.12
  27.3 14.0 %copy-start.1 = (s32[256]{0:T(256)S(1)}, s32[256]{0:T(256)}, u32[]{:S(2)}) copy-start(s32[256]{0:T(256)} %param.11) | copy-start | bytes 3076
  27.3 115.1 %all-to-all-start.1 = ((bf16[8,3,64,1024]{3,2,1,0:T(8,128)(2,1)}), bf16[8,3,64,1024]{3,2,1,0:T(8,128)(2,1)}, u32[]{:S(2)}, u32[]{:S(2)}) async-start(bf16[8,3,64,1024]{3,2,1,0:T(8,128)(2,1)} %slice.24), calls=%async_computation.1 | async-start | bytes 6291456 | tf_op jit(solution)/shard_map/all_to_all | solution.py:226
  35.0 72.2 %collective-permute-start.1 = (bf16[64,1024]{1,0:T(8,128)(2,1)}, bf16[64,1024]{1,0:T(8,128)(2,1)S(1)}, u32[]{:S(2)}, u32[]{:S(2)}) collective-permute-start(bf16[64,1024]{1,0:T(8,128)(2,1)} %get-tuple-element.37), channel_id=1, source_target_pairs={{1,0},{2,1},{3,2},{4,3},{5,4},{6,5},{7,6},{8,7},{9,8},{10,9},{11,1... | collective-permute-start | bytes 393224 | tf_op jit(solution)/shard_map/ppermute | solution.py:211
  38.5 67.8 %collective-permute-start = (bf16[64,1024]{1,0:T(8,128)(2,1)}, bf16[64,1024]{1,0:T(8,128)(2,1)}, u32[]{:S(2)}, u32[]{:S(2)}) collective-permute-start(bf16[64,1024]{1,0:T(8,128)(2,1)} %get-tuple-element.38), channel_id=1, source_target_pairs={{0,1},{1,2},{2,3},{3,4},{4,5},{5,6},{6,7},{7,8},{8,9},{9,10},{10,1... | collective-permute-start | bytes 393224 | tf_op jit(solution)/shard_map/ppermute | solution.py:210
  42.1 0.8 copy-start.11
  42.1 0.8 copy-start.13
  56.8 58.1 %copy-start.3 = (bf16[1024,16,1,64]{0,3,2,1:T(8,128)(2,1)}, bf16[1024,16,1,64]{0,3,2,1:T(8,128)(2,1)S(1)}, u32[]{:S(2)}) copy-start(bf16[1024,16,1,64]{0,3,2,1:T(8,128)(2,1)S(1)} %get-tuple-element.35) | copy-start | bytes 6291460
  56.8 60.6 %copy-start.5 = (bf16[1024,16,1,64]{0,3,2,1:T(8,128)(2,1)}, bf16[1024,16,1,64]{0,3,2,1:T(8,128)(2,1)S(1)}, u32[]{:S(2)}) copy-start(bf16[1024,16,1,64]{0,3,2,1:T(8,128)(2,1)S(1)} %get-tuple-element.34) | copy-start | bytes 6291460
  56.8 2.3 %copy-start.7 = (s32[192]{0:T(256)S(1)}, s32[192]{0:T(256)}, u32[]{:S(2)}) copy-start(s32[192]{0:T(256)} %lt.106) | copy-start | bytes 2308
  142.3 39.8 %all-to-all-start.2 = ((bf16[8,1,64,1024]{3,2,1,0:T(8,128)(2,1)}), bf16[8,1,64,1024]{3,2,1,0:T(8,128)(2,1)}, u32[]{:S(2)}, u32[]{:S(2)}) async-start(bf16[8,1,64,1024]{3,2,1,0:T(8,128)(2,1)} %slice.25), calls=%async_computation.2 | async-start | bytes 2097152 | tf_op jit(solution)/shard_map/all_to_all | solution.py:262
  147.3 7.8 %copy-start.6 = (bf16[1024,16,1,64]{0,3,2,1:T(8,128)(2,1)S(1)}, bf16[1024,16,1,64]{0,3,2,1:T(8,128)(2,1)}, u32[]{:S(2)}) copy-start(bf16[1024,16,1,64]{0,3,2,1:T(8,128)(2,1)} %copy-done.5) | copy-start | bytes 6291460
  182.1 4.3 %copy-start.4 = (bf16[1024,16,1,64]{0,3,2,1:T(8,128)(2,1)S(1)}, bf16[1024,16,1,64]{0,3,2,1:T(8,128)(2,1)}, u32[]{:S(2)}) copy-start(bf16[1024,16,1,64]{0,3,2,1:T(8,128)(2,1)} %copy-done.3) | copy-start | bytes 6291460

commit v7 on v5

--- a/solution.py
+++ b/solution.py
@@ -1,3 +1,4 @@
+import functools
 import math
 
 import jax
@@ -77,38 +78,46 @@
         l_ref[0, :, cols] = pick_rows(jnp.broadcast_to(total, result.shape), low, rows)
 
 
-def far_kernel(ids_ref, mask_ref, q_ref, *refs):
-    far_count = RAND
-    token_refs = refs[:far_count]
-    wk_ref, wv_ref, oa_ref, ma_ref, la_ref, out_ref = refs[far_count:]
+def far_kernel(group, ids_ref, mask_ref, q_ref, *refs):
+    token_refs = refs[: group * RAND]
+    wkv_ref, oa_ref, ma_ref, la_ref, out_ref = refs[group * RAND :]
     width = q_ref.shape[-1]
     rows = q_ref.shape[1]
     scaling = 1.0 / math.sqrt(HD)
-    valid = mask_ref[0] != 0
     low = lax.broadcasted_iota(jnp.int32, (rows, LANES), 1) < HD
     far_tokens = jnp.concatenate([ref[0] for ref in token_refs], axis=0)
-    k_far = jnp.dot(far_tokens, wk_ref[...], preferred_element_type=jnp.float32).astype(jnp.bfloat16)
-    v_far = jnp.dot(far_tokens, wv_ref[...], preferred_element_type=jnp.float32).astype(jnp.bfloat16)
-    for tile in range(width // LANES):
-        lanes = slice(tile * LANES, (tile + 1) * LANES)
-        cols = pl.ds(tile * LANES, LANES)
-        q_pair = pair_rows(q_ref[0, :, cols], low)
-        scores = lax.dot_general(q_pair, k_far[:, lanes], CONTRACT, preferred_element_type=jnp.float32)
-        scores = jnp.where(valid, scores * scaling, -jnp.inf)
-        peak = jnp.max(scores, axis=-1, keepdims=True)
-        exps = jnp.exp(scores - peak)
-        total = jnp.sum(exps, axis=-1, keepdims=True)
-        result = jnp.dot(exps.astype(jnp.bfloat16), v_far[:, lanes], preferred_element_type=jnp.float32)
-        o_b = pick_rows(result, low, rows)
-        m_b = pick_rows(jnp.broadcast_to(peak, result.shape), low, rows)
-        l_b = pick_rows(jnp.broadcast_to(total, result.shape), low, rows)
-        m_a = ma_ref[0, :, cols]
-        peak_all = jnp.maximum(m_a, m_b)
-        scale_a = jnp.exp(m_a - peak_all)
-        scale_b = jnp.exp(m_b - peak_all)
-        numerator = oa_ref[0, :, cols] * scale_a + o_b * scale_b
-        denominator = la_ref[0, :, cols] * scale_a + l_b * scale_b
-        out_ref[0, :, cols] = (numerator / denominator).astype(out_ref.dtype)
+    kv_far = jnp.dot(far_tokens, wkv_ref[...], preferred_element_type=jnp.float32).astype(
+        jnp.bfloat16
+    )
+    keys = RAND * rows
+    for g in range(group):
+        valid = mask_ref[g] != 0
+        kv_rows = kv_far[g * keys : (g + 1) * keys]
+        for tile in range(width // LANES):
+            lanes = slice(tile * LANES, (tile + 1) * LANES)
+            value_lanes = slice(width + tile * LANES, width + (tile + 1) * LANES)
+            cols = pl.ds(tile * LANES, LANES)
+            q_pair = pair_rows(q_ref[g, :, cols], low)
+            scores = lax.dot_general(
+                q_pair, kv_rows[:, lanes], CONTRACT, preferred_element_type=jnp.float32
+            )
+            scores = jnp.where(valid, scores * scaling, -jnp.inf)
+            peak = jnp.max(scores, axis=-1, keepdims=True)
+            exps = jnp.exp(scores - peak)
+            total = jnp.sum(exps, axis=-1, keepdims=True)
+            result = jnp.dot(
+                exps.astype(jnp.bfloat16), kv_rows[:, value_lanes], preferred_element_type=jnp.float32
+            )
+            o_b = pick_rows(result, low, rows)
+            m_b = pick_rows(jnp.broadcast_to(peak, result.shape), low, rows)
+            l_b = pick_rows(jnp.broadcast_to(total, result.shape), low, rows)
+            m_a = ma_ref[g, :, cols]
+            peak_all = jnp.maximum(m_a, m_b)
+            scale_a = jnp.exp(m_a - peak_all)
+            scale_b = jnp.exp(m_b - peak_all)
+            numerator = oa_ref[g, :, cols] * scale_a + o_b * scale_b
+            denominator = la_ref[g, :, cols] * scale_a + l_b * scale_b
+            out_ref[g, :, cols] = (numerator / denominator).astype(out_ref.dtype)
 
 
 def attend_near(mask, q, k_ext, v_ext, k_sum, v_sum):
@@ -137,33 +146,36 @@
     )(mask, q, k_ext, k_ext, k_ext, v_ext, v_ext, v_ext, k_sum, v_sum)
 
 
-def attend_far(slot_ids, mask, q, incoming, w_k, w_v, o_a, m_a, l_a):
+def attend_far(slot_ids, mask, q, incoming, w_kv, o_a, m_a, l_a):
     blocks, rows, width = q.shape
     model_dim = incoming.shape[-1]
-    block = pl.BlockSpec((1, rows, width), lambda i, ids: (i, 0, 0))
+    group = 2 if blocks % 2 == 0 else 1
+    block = pl.BlockSpec((group, rows, width), lambda i, ids: (i, 0, 0))
     token_specs = [
-        pl.BlockSpec((1, rows, model_dim), lambda i, ids, j=j: (ids[RAND * i + j], 0, 0))
-        for j in range(RAND)
+        pl.BlockSpec(
+            (1, rows, model_dim), lambda i, ids, n=n: (ids[RAND * group * i + n], 0, 0)
+        )
+        for n in range(group * RAND)
     ]
-    weight = pl.BlockSpec(w_k.shape, lambda i, ids: (0, 0))
+    weight = pl.BlockSpec(w_kv.shape, lambda i, ids: (0, 0))
     local_keys = RAND * rows
     heads = width // HD
     flops = blocks * (
-        heads * 2 * rows * 2 * LANES * local_keys + 2 * 2 * local_keys * model_dim * width
-    )
-    bytes_accessed = 2 * blocks * rows * (width * 2 + model_dim * RAND) + 4 * w_k.size + (
+        heads * 2 * rows * 2 * LANES * local_keys + 2 * local_keys * model_dim * 2 * width
+    )
+    bytes_accessed = 2 * blocks * rows * (width * 2 + model_dim * RAND) + 2 * w_kv.size + (
         12 * blocks * rows * width
     )
     grid_spec = pltpu.PrefetchScalarGridSpec(
         num_scalar_prefetch=1,
-        grid=(blocks,),
-        in_specs=[pl.BlockSpec((1, 1, local_keys), lambda i, ids: (i, 0, 0)), block]
+        grid=(blocks // group,),
+        in_specs=[pl.BlockSpec((group, 1, local_keys), lambda i, ids: (i, 0, 0)), block]
         + token_specs
-        + [weight, weight, block, block, block],
+        + [weight, block, block, block],
         out_specs=block,
     )
     return pl.pallas_call(
-        far_kernel,
+        functools.partial(far_kernel, group),
         grid_spec=grid_spec,
         out_shape=jax.ShapeDtypeStruct((blocks, rows, width), jnp.bfloat16),
         cost_estimate=pl.CostEstimate(
@@ -171,7 +183,7 @@
             transcendentals=blocks * heads * rows * local_keys,
             bytes_accessed=bytes_accessed,
         ),
-    )(slot_ids, mask, q, incoming, incoming, incoming, w_k, w_v, o_a, m_a, l_a)
+    )(slot_ids, mask, q, *([incoming] * (group * RAND)), w_kv, o_a, m_a, l_a)
 
 
 def local(tokens, w_qkv, w_out, counts, rand_seg, rand_off):
@@ -248,8 +260,7 @@
         far_mask,
         q_own,
         incoming.reshape(ctx_count * capacity, BLK, model_dim),
-        w_k,
-        w_v,
+        jnp.concatenate([w_k, w_v], axis=1),
         o_a,
         m_a,
         l_a,

time: 190 us -> 191 us (level)
  other arithmetic: 4.2 us -> 8.94 us
  waiting for transfers between devices: 66.5 us -> 63.4 us
    concatenate x0 -> x1, other arithmetic: none -> 4.83 us  [local(): jnp.concatenate([w_k, w_v], axis=1)]
    ppermute x1, waiting for transfers between devices: 57.8 us -> 54.7 us  [local(): lax.ppermute(token_blocks[dev_blocks - 1], ('ctx', 'seq'), forward)]
    unnamed x29 -> x31, local copies, waits for them, and re-layouts: 10.3 us -> 10.3 us
  transfers between devices with their start and end apart: 4 -> 4, of which waited for: 2 -> 2; matrix products, arithmetic and copies ran while one was open for 25% -> 26% of each run, Pallas kernels for 12% -> 12%
where the time goes in v7:
time: 191 us; the launch traced here: 190 us
  waiting for transfers between devices  63.4 us (33%)
  Pallas kernels  50.2 us (26%)
  local copies, waits for them, and re-layouts  32.6 us (17%)
  starting transfers between devices  18.4 us (10%)
  matrix products  16.2 us (8%)
  other arithmetic  8.94 us (5%)
    ppermute x1, waiting for transfers between devices, local(): lax.ppermute(token_blocks[dev_blocks - 1], ('ctx', 'seq'), forward)  54.7 us
    pallas_call x1, Pallas kernels, attend_far(): pl.pallas_call(functools.partial(far_kernel, group), grid_spec=grid_spec,...  28 us
    pallas_call x1, Pallas kernels, attend_near(): pl.pallas_call(near_kernel, grid=(blocks,), in_specs=[pl.BlockSpec((1, 1,...  22.2 us
    dot_general x5, matrix products, local(): jnp.dot(x, w, preferred_element_type=jnp.float32).astype(jnp.bfloat16)  12.7 us
    unnamed x31, local copies, waits for them, and re-layouts  10.3 us
    all_to_all x1, waiting for transfers between devices, local(): lax.all_to_all(copies, ('ctx', 'seq'), 0, 0, tiled=True)  8.71 us
    another operation x2, local copies, waits for them, and re-layouts, split_weights(): shaped[:, :, j, :].reshape(model_dim, head_total * HD)  7.86 us
    all_to_all x1, starting transfers between devices, local(): lax.all_to_all(outgoing, 'ctx', split_axis=0, concat_axis=0, tiled=True)  7 us
  transfers between devices with their start and end apart: 4, of which 2 were waited for; matrix products, arithmetic and copies ran while one was open for 26% of the time, Pallas kernels for 12%

profile of v7, /device:TPU:16, one launch (start us, length us, event | category | flops | bytes accessed | tf_op | source)
XLA Modules:
  0.0 189.9 jit_solution(15994794851617250786)
XLA Ops:
  0.0 0.9 dynamic_slice.18
  1.2 1.6 select_reduce_fusion
  2.8 0.2 multiply_reduce_fusion
  3.1 0.9 broadcast_in_dim.39
  4.0 6.0 %all-to-all-start = ((bf16[32,8,1024]{2,1,0:T(8,128)(2,1)}), bf16[32,8,1024]{2,1,0:T(8,128)(2,1)}, u32[]{:S(2)}, u32[]{:S(2)}) async-start(bf16[32,8,1024]{2,1,0:T(8,128)(2,1)} %broadcast_in_dim.39), calls=%async_computation | async-start | bytes 1048576 | tf_op jit(solution)/shard_map/all_to_all | solution.py:229
  10.2 0.4 copy-done.9
  11.7 2.9 %gather_fusion = bf16[32,64,1024]{2,1,0:T(8,128)(2,1)} fusion(bf16[8,64,1024]{2,1,0:T(8,128)(2,1)S(1)} %bitcast.29, s32[1024]{0:T(1024)S(1)} %get-tuple-element.28), kind=kCustom, calls=%fused_computation.2 | custom fusion | bytes 8388736 | tf_op jit(solution)/shard_map/jit(_take)/gather | solution.py:210
  14.6 8.7 %all-to-all-done = bf16[32,8,1024]{2,1,0:T(8,128)(2,1)} async-done(((bf16[32,8,1024]{2,1,0:T(8,128)(2,1)}), bf16[32,8,1024]{2,1,0:T(8,128)(2,1)}, u32[]{:S(2)}, u32[]{:S(2)}) %all-to-all-start) | async-done | bytes 524320 | tf_op jit(solution)/shard_map/all_to_all | solution.py:229
  23.3 7.0 %all-to-all-start.1 = ((bf16[8,4,64,1024]{3,2,1,0:T(8,128)(2,1)}), bf16[8,4,64,1024]{3,2,1,0:T(8,128)(2,1)}, u32[]{:S(2)}, u32[]{:S(2)}) async-start(bf16[8,4,64,1024]{3,2,1,0:T(8,128)(2,1)} %bitcast.31), calls=%async_computation.1 | async-start | bytes 8388608 | tf_op jit(solution)/shard_map/all_to_all | solution.py:231
  30.3 0.7 fusion.5
  31.0 3.5 %collective-permute-start.1 = (bf16[64,1024]{1,0:T(8,128)(2,1)}, bf16[64,1024]{1,0:T(8,128)(2,1)S(1)}, u32[]{:S(2)}, u32[]{:S(2)}) collective-permute-start(bf16[64,1024]{1,0:T(8,128)(2,1)} %get-tuple-element.21), channel_id=1, source_target_pairs={{1,0},{2,1},{3,2},{4,3},{5,4},{6,5},{7,6},{8,7},{9,8},{10,9},{11,1... | collective-permute-start | bytes 393224 | tf_op jit(solution)/shard_map/ppermute | solution.py:216
  34.5 1.9 %collective-permute-start = (bf16[64,1024]{1,0:T(8,128)(2,1)}, bf16[64,1024]{1,0:T(8,128)(2,1)}, u32[]{:S(2)}, u32[]{:S(2)}) collective-permute-start(bf16[64,1024]{1,0:T(8,128)(2,1)} %get-tuple-element.22), channel_id=1, source_target_pairs={{0,1},{1,2},{2,3},{3,4},{4,5},{5,6},{6,7},{7,8},{8,9},{9,10},{10,1... | collective-permute-start | bytes 393224 | tf_op jit(solution)/shard_map/ppermute | solution.py:215
  36.4 0.6 lt.87
  37.2 0.7 gather_fusion.1
  38.0 0.7 gather_fusion.2
  39.4 8.6 %copy.43 = bf16[1024,3072]{0,1:T(8,128)(2,1)} copy(bf16[1024,3072]{1,0:T(8,128)(2,1)} %param.9) | data formatting | bytes 12582912 | tf_op args[1]
  48.0 5.8 %fusion.4 = (bf16[1024,16,1,64]{0,3,2,1:T(8,128)(2,1)}, bf16[1024,16,1,64]{0,3,2,1:T(8,128)(2,1)}, bf16[1024,16,1,64]{0,3,2,1:T(8,128)(2,1)}) fusion(bf16[1024,16,3,64]{0,3,2,1:T(8,128)(2,1)} %bitcast.30), kind=kLoop, calls=%fused_computation.47 | loop fusion | bytes 12582912 | tf_op jit(solution)/shard_map/slice | solution.py:35
  53.8 3.9 %copy.48 = bf16[1024,1024]{1,0:T(8,128)(2,1)} copy(bf16[1024,1024]{0,1:T(8,128)(2,1)} %bitcast.41) | data formatting | bytes 4194304 | tf_op jit(solution)/shard_map/reshape;squeeze | solution.py:35
  57.7 3.9 %copy.47 = bf16[1024,1024]{1,0:T(8,128)(2,1)} copy(bf16[1024,1024]{0,1:T(8,128)(2,1)} %bitcast.38) | data formatting | bytes 4194304 | tf_op jit(solution)/shard_map/reshape;squeeze | solution.py:35
  61.8 0.6 compare_convert_fusion
  62.4 4.8 %pad_maximum_fusion.refs_6_ = bf16[1024,2048]{1,0:T(8,128)(2,1)} fusion(bf16[1024,1024]{1,0:T(8,128)(2,1)} %copy.48, bf16[1024,1024]{1,0:T(8,128)(2,1)} %copy.47), kind=kLoop, calls=%fused_computation.3 | loop fusion | flops 8388608 | bytes 8388608 | tf_op jit(solution)/shard_map/concatenate | solution.py:263
  67.3 2.3 %convolution_convert_fusion.2 = bf16[512,1024]{1,0:T(8,128)(2,1)} fusion(bf16[512,1024]{1,0:T(8,128)(2,1)S(1)} %copy-done.2, bf16[1024,1024]{0,1:T(8,128)(2,1)S(1)} %bitcast.46), kind=kOutput, calls=%fused_computation.8 | convolution fusion | flops 1074266112 | bytes 4194304 | tf_op jit(solution)/shard_map/dot_general | solution.py:234
  69.5 0.5 multiply_add_fusion.ids_ref
  70.0 54.7 %collective-permute-done = bf16[64,1024]{1,0:T(8,128)(2,1)} collective-permute-done((bf16[64,1024]{1,0:T(8,128)(2,1)}, bf16[64,1024]{1,0:T(8,128)(2,1)}, u32[]{:S(2)}, u32[]{:S(2)}) %collective-permute-start) | collective-permute-done | bytes 131104 | tf_op jit(solution)/shard_map/ppermute | solution.py:215
  124.7 0.9 constant_dynamic-update-slice_fusion.2
  125.8 2.6 %convolution_convert_fusion = bf16[640,1024]{1,0:T(8,128)(2,1)} fusion(bf16[640,1024]{1,0:T(8,128)(2,1)S(1)} %constant_dynamic-update-slice_fusion, bf16[1024,1024]{0,1:T(8,128)(2,1)S(1)} %bitcast.42), kind=kOutput, calls=%fused_computation.6 | convolution fusion | flops 1342832640 | bytes 4718592 | tf_op jit(solution)/shard_map/dot_general | solution.py:234
  128.4 2.6 %convolution_convert_fusion.1 = bf16[640,1024]{1,0:T(8,128)(2,1)} fusion(bf16[640,1024]{1,0:T(8,128)(2,1)S(1)} %constant_dynamic-update-slice_fusion, bf16[1024,1024]{0,1:T(8,128)(2,1)S(1)} %bitcast.39), kind=kOutput, calls=%fused_computation.7 | convolution fusion | flops 1342832640 | bytes 4718592 | tf_op jit(solution)/shard_map/dot_general | solution.py:234
  131.0 2.6 %convolution_convert_fusion.3.vs_ref = bf16[256,1024]{1,0:T(8,128)(2,1)} fusion(bf16[256,1024]{1,0:T(8,128)(2,1)} %bitcast.4, bf16[1024,1024]{0,1:T(8,128)(2,1)S(1)} %bitcast.43), kind=kOutput, calls=%fused_computation.9 | convolution fusion | flops 537133056 | bytes 3145728 | tf_op jit(solution)/shard_map/dot_general | solution.py:234
  133.6 2.6 %convolution_convert_fusion.4.ks_ref = bf16[256,1024]{1,0:T(8,128)(2,1)} fusion(bf16[256,1024]{1,0:T(8,128)(2,1)} %bitcast.4, bf16[1024,1024]{0,1:T(8,128)(2,1)S(1)} %bitcast.40), kind=kOutput, calls=%fused_computation.10 | convolution fusion | flops 537133056 | bytes 3145728 | tf_op jit(solution)/shard_map/dot_general | solution.py:234
  136.2 22.2 %shard_map.64 = (f32[8,64,1024]{2,1,0:T(8,128)}, f32[8,64,1024]{2,1,0:T(8,128)}, f32[8,64,1024]{2,1,0:T(8,128)}) custom-call(s32[8,1,192]{2,1,0:T(1,128)} %get-tuple-element.25.mask_ref, bf16[8,64,1024]{2,1,0:T(8,128)(2,1)} %bitcast.44, bf16[10,64,1024]{2,1,0:T(8,128)(2,1)} %bitcast.35, bf16[10,64,1024]{2,1,0:T(8,128)(2,1)} %bitcast.36, ...), custom_call_target="tpu_custom_call" | custom-call | flops 1879048192 | bytes 14680064 | tf_op jit(solution)/shard_map/pallas_call | solution.py:133
  158.4 28.0 %shard_map.65 = bf16[8,64,1024]{2,1,0:T(8,128)(2,1)} custom-call(s32[24]{0:T(128)} %multiply_add_fusion.ids_ref, s32[8,1,192]{2,1,0:T(1,128)} %get-tuple-element.26.mask_ref, bf16[8,64,1024]{2,1,0:T(8,128)(2,1)} %bitcast.45, bf16[32,64,1024]{2,1,0:T(8,128)(2,1)} %bitcast.7.refs_0_.refs_1_.refs_2_.refs_3_.refs_4_.refs_5_, ...), custom_call_target="tpu_custom_call" | custom-call | flops 7247757312 | bytes 15728640 | tf_op jit(solution)/shard_map/pallas_call | solution.py:177
  186.4 3.4 %add_convert_fusion = bf16[512,1024]{1,0:T(8,128)(2,1)} fusion(bf16[512,1024]{1,0:T(8,128)(2,1)S(1)} %copy-done.2, bf16[512,1024]{1,0:T(8,128)(2,1)} %bitcast.47, bf16[1024,1024]{1,0:T(8,128)(2,1)S(1)} %copy-done), kind=kOutput, calls=%fused_computation.4 | convolution fusion | flops 1075314688 | bytes 5242880 | tf_op jit(solution)/shard_map/dot_general | solution.py:268
  (66 shorter events, 2.7 us)
Async XLA Ops:
  0.0 186.4 %copy-start = (bf16[1024,1024]{1,0:T(8,128)(2,1)S(1)}, bf16[1024,1024]{1,0:T(8,128)(2,1)}, u32[]{:S(2)}) copy-start(bf16[1024,1024]{1,0:T(8,128)(2,1)} %param.10) | copy-start | bytes 6291460
  0.0 11.7 %copy-start.2 = (bf16[512,1024]{1,0:T(8,128)(2,1)S(1)}, bf16[512,1024]{1,0:T(8,128)(2,1)}, u32[]{:S(2)}) copy-start(bf16[512,1024]{1,0:T(8,128)(2,1)} %param.8) | copy-start | bytes 3145732
  0.0 10.6 %copy-start.6 = (s32[256,3]{0,1:T(4,128)S(1)}, s32[256,3]{0,1:T(4,128)}, u32[]{:S(2)}) copy-start(s32[256,3]{0,1:T(4,128)} %param.12) | copy-start | bytes 9220
  0.0 11.0 %copy-start.7 = (s32[256,3]{0,1:T(4,128)S(1)}, s32[256,3]{0,1:T(4,128)}, u32[]{:S(2)}) copy-start(s32[256,3]{0,1:T(4,128)} %param.13) | copy-start | bytes 9220
  4.0 19.3 %all-to-all-start = ((bf16[32,8,1024]{2,1,0:T(8,128)(2,1)}), bf16[32,8,1024]{2,1,0:T(8,128)(2,1)}, u32[]{:S(2)}, u32[]{:S(2)}) async-start(bf16[32,8,1024]{2,1,0:T(8,128)(2,1)} %broadcast_in_dim.39), calls=%async_computation | async-start | bytes 1048576 | tf_op jit(solution)/shard_map/all_to_all | solution.py:229
  10.0 0.6 copy-start.9
  10.0 0.6 copy-start.11
  23.3 135.1 %all-to-all-start.1 = ((bf16[8,4,64,1024]{3,2,1,0:T(8,128)(2,1)}), bf16[8,4,64,1024]{3,2,1,0:T(8,128)(2,1)}, u32[]{:S(2)}, u32[]{:S(2)}) async-start(bf16[8,4,64,1024]{3,2,1,0:T(8,128)(2,1)} %bitcast.31), calls=%async_computation.1 | async-start | bytes 8388608 | tf_op jit(solution)/shard_map/all_to_all | solution.py:231
  30.3 6.9 %copy-start.1 = (s32[256]{0:T(256)S(1)}, s32[256]{0:T(256)}, u32[]{:S(2)}) copy-start(s32[256]{0:T(256)} %param.11) | copy-start | bytes 3076
  31.0 94.7 %collective-permute-start.1 = (bf16[64,1024]{1,0:T(8,128)(2,1)}, bf16[64,1024]{1,0:T(8,128)(2,1)S(1)}, u32[]{:S(2)}, u32[]{:S(2)}) collective-permute-start(bf16[64,1024]{1,0:T(8,128)(2,1)} %get-tuple-element.21), channel_id=1, source_target_pairs={{1,0},{2,1},{3,2},{4,3},{5,4},{6,5},{7,6},{8,7},{9,8},{10,9},{11,1... | collective-permute-start | bytes 393224 | tf_op jit(solution)/shard_map/ppermute | solution.py:216
  34.5 90.2 %collective-permute-start = (bf16[64,1024]{1,0:T(8,128)(2,1)}, bf16[64,1024]{1,0:T(8,128)(2,1)}, u32[]{:S(2)}, u32[]{:S(2)}) collective-permute-start(bf16[64,1024]{1,0:T(8,128)(2,1)} %get-tuple-element.22), channel_id=1, source_target_pairs={{0,1},{1,2},{2,3},{3,4},{4,5},{5,6},{6,7},{7,8},{8,9},{9,10},{10,1... | collective-permute-start | bytes 393224 | tf_op jit(solution)/shard_map/ppermute | solution.py:215
  38.0 0.8 copy-start.10
  38.0 0.8 copy-start.12
  57.7 4.1 %copy-start.8 = (s32[192]{0:T(256)S(1)}, s32[192]{0:T(256)}, u32[]{:S(2)}) copy-start(s32[192]{0:T(256)} %lt.87) | copy-start | bytes 2308
  62.4 4.8 %copy-start.5 = (bf16[1024,16,1,64]{0,3,2,1:T(8,128)(2,1)S(1)}, bf16[1024,16,1,64]{0,3,2,1:T(8,128)(2,1)}, u32[]{:S(2)}) copy-start(bf16[1024,16,1,64]{0,3,2,1:T(8,128)(2,1)} %get-tuple-element.20) | copy-start | bytes 6291460
  69.5 56.2 %copy-start.4 = (bf16[1024,16,1,64]{0,3,2,1:T(8,128)(2,1)S(1)}, bf16[1024,16,1,64]{0,3,2,1:T(8,128)(2,1)}, u32[]{:S(2)}) copy-start(bf16[1024,16,1,64]{0,3,2,1:T(8,128)(2,1)} %get-tuple-element.19) | copy-start | bytes 6291460
  125.8 2.6 %copy-start.3 = (bf16[1024,16,1,64]{0,3,2,1:T(8,128)(2,1)S(1)}, bf16[1024,16,1,64]{0,3,2,1:T(8,128)(2,1)}, u32[]{:S(2)}) copy-start(bf16[1024,16,1,64]{0,3,2,1:T(8,128)(2,1)} %get-tuple-element.18) | copy-start | bytes 6291460

commit v8 on v5

--- a/solution.py
+++ b/solution.py
@@ -1,3 +1,4 @@
+import functools
 import math
 
 import jax
@@ -78,37 +79,47 @@
 
 
 def far_kernel(ids_ref, mask_ref, q_ref, *refs):
-    far_count = RAND
-    token_refs = refs[:far_count]
-    wk_ref, wv_ref, oa_ref, ma_ref, la_ref, out_ref = refs[far_count:]
+    token_refs = refs[:RAND]
+    wkv_ref, oa_ref, ma_ref, la_ref, out_ref, kv_ref = refs[RAND:]
     width = q_ref.shape[-1]
     rows = q_ref.shape[1]
     scaling = 1.0 / math.sqrt(HD)
+    low = lax.broadcasted_iota(jnp.int32, (rows, LANES), 1) < HD
+
+    @pl.when(pl.program_id(0) == 0)
+    def _():
+        kv_ref[...] = jnp.zeros_like(kv_ref)
+
     valid = mask_ref[0] != 0
-    low = lax.broadcasted_iota(jnp.int32, (rows, LANES), 1) < HD
-    far_tokens = jnp.concatenate([ref[0] for ref in token_refs], axis=0)
-    k_far = jnp.dot(far_tokens, wk_ref[...], preferred_element_type=jnp.float32).astype(jnp.bfloat16)
-    v_far = jnp.dot(far_tokens, wv_ref[...], preferred_element_type=jnp.float32).astype(jnp.bfloat16)
     for tile in range(width // LANES):
-        lanes = slice(tile * LANES, (tile + 1) * LANES)
-        cols = pl.ds(tile * LANES, LANES)
-        q_pair = pair_rows(q_ref[0, :, cols], low)
-        scores = lax.dot_general(q_pair, k_far[:, lanes], CONTRACT, preferred_element_type=jnp.float32)
+        lanes = pl.ds(tile * LANES, LANES)
+        value_lanes = pl.ds(width + tile * LANES, LANES)
+        q_pair = pair_rows(q_ref[0, :, lanes], low)
+        scores = lax.dot_general(
+            q_pair, kv_ref[:, lanes], CONTRACT, preferred_element_type=jnp.float32
+        )
         scores = jnp.where(valid, scores * scaling, -jnp.inf)
         peak = jnp.max(scores, axis=-1, keepdims=True)
         exps = jnp.exp(scores - peak)
         total = jnp.sum(exps, axis=-1, keepdims=True)
-        result = jnp.dot(exps.astype(jnp.bfloat16), v_far[:, lanes], preferred_element_type=jnp.float32)
+        result = jnp.dot(
+            exps.astype(jnp.bfloat16), kv_ref[:, value_lanes], preferred_element_type=jnp.float32
+        )
         o_b = pick_rows(result, low, rows)
         m_b = pick_rows(jnp.broadcast_to(peak, result.shape), low, rows)
         l_b = pick_rows(jnp.broadcast_to(total, result.shape), low, rows)
-        m_a = ma_ref[0, :, cols]
+        m_a = ma_ref[0, :, lanes]
         peak_all = jnp.maximum(m_a, m_b)
         scale_a = jnp.exp(m_a - peak_all)
         scale_b = jnp.exp(m_b - peak_all)
-        numerator = oa_ref[0, :, cols] * scale_a + o_b * scale_b
-        denominator = la_ref[0, :, cols] * scale_a + l_b * scale_b
-        out_ref[0, :, cols] = (numerator / denominator).astype(out_ref.dtype)
+        numerator = oa_ref[0, :, lanes] * scale_a + o_b * scale_b
+        denominator = la_ref[0, :, lanes] * scale_a + l_b * scale_b
+        out_ref[0, :, lanes] = (numerator / denominator).astype(out_ref.dtype)
+
+    far_tokens = jnp.concatenate([ref[0] for ref in token_refs], axis=0)
+    kv_ref[...] = jnp.dot(far_tokens, wkv_ref[...], preferred_element_type=jnp.float32).astype(
+        kv_ref.dtype
+    )
 
 
 def attend_near(mask, q, k_ext, v_ext, k_sum, v_sum):
@@ -137,30 +148,35 @@
     )(mask, q, k_ext, k_ext, k_ext, v_ext, v_ext, v_ext, k_sum, v_sum)
 
 
-def attend_far(slot_ids, mask, q, incoming, w_k, w_v, o_a, m_a, l_a):
+def attend_far(slot_ids, mask, q, incoming, w_kv, o_a, m_a, l_a):
     blocks, rows, width = q.shape
     model_dim = incoming.shape[-1]
-    block = pl.BlockSpec((1, rows, width), lambda i, ids: (i, 0, 0))
+    behind = lambda i: jnp.maximum(i - 1, 0)
+    block = pl.BlockSpec((1, rows, width), lambda i, ids: (behind(i), 0, 0))
     token_specs = [
-        pl.BlockSpec((1, rows, model_dim), lambda i, ids, j=j: (ids[RAND * i + j], 0, 0))
+        pl.BlockSpec(
+            (1, rows, model_dim),
+            lambda i, ids, j=j: (ids[RAND * jnp.minimum(i, blocks - 1) + j], 0, 0),
+        )
         for j in range(RAND)
     ]
-    weight = pl.BlockSpec(w_k.shape, lambda i, ids: (0, 0))
+    weight = pl.BlockSpec(w_kv.shape, lambda i, ids: (0, 0))
     local_keys = RAND * rows
     heads = width // HD
     flops = blocks * (
-        heads * 2 * rows * 2 * LANES * local_keys + 2 * 2 * local_keys * model_dim * width
-    )
-    bytes_accessed = 2 * blocks * rows * (width * 2 + model_dim * RAND) + 4 * w_k.size + (
+        heads * 2 * rows * 2 * LANES * local_keys + 2 * local_keys * model_dim * 2 * width
+    )
+    bytes_accessed = 2 * blocks * rows * (width * 2 + model_dim * RAND) + 2 * w_kv.size + (
         12 * blocks * rows * width
     )
     grid_spec = pltpu.PrefetchScalarGridSpec(
         num_scalar_prefetch=1,
-        grid=(blocks,),
-        in_specs=[pl.BlockSpec((1, 1, local_keys), lambda i, ids: (i, 0, 0)), block]
+        grid=(blocks + 1,),
+        in_specs=[pl.BlockSpec((1, 1, local_keys), lambda i, ids: (behind(i), 0, 0)), block]
         + token_specs
-        + [weight, weight, block, block, block],
+        + [weight, block, block, block],
         out_specs=block,
+        scratch_shapes=[pltpu.VMEM((local_keys, 2 * width), jnp.bfloat16)],
     )
     return pl.pallas_call(
         far_kernel,
@@ -171,7 +187,7 @@
             transcendentals=blocks * heads * rows * local_keys,
             bytes_accessed=bytes_accessed,
         ),
-    )(slot_ids, mask, q, incoming, incoming, incoming, w_k, w_v, o_a, m_a, l_a)
+    )(slot_ids, mask, q, *([incoming] * RAND), w_kv, o_a, m_a, l_a)
 
 
 def local(tokens, w_qkv, w_out, counts, rand_seg, rand_off):
@@ -248,8 +264,7 @@
         far_mask,
         q_own,
         incoming.reshape(ctx_count * capacity, BLK, model_dim),
-        w_k,
-        w_v,
+        jnp.concatenate([w_k, w_v], axis=1),
         o_a,
         m_a,
         l_a,

time: 190 us -> 193 us (1.016)
  other arithmetic: 4.2 us -> 8.94 us
  waiting for transfers between devices: 66.5 us -> 63.2 us
  Pallas kernels: 49.8 us -> 52.2 us
    concatenate x0 -> x1, other arithmetic: none -> 4.83 us  [local(): jnp.concatenate([w_k, w_v], axis=1)]
    ppermute x1, waiting for transfers between devices: 57.8 us -> 54.5 us  [local(): lax.ppermute(token_blocks[dev_blocks - 1], ('ctx', 'seq'), forward)]
    pallas_call x1, Pallas kernels: 27.5 us -> 30 us  [attend_far(): pl.pallas_call(far_kernel, grid_spec=grid_spec, out_shape=jax.ShapeDtypeS...]
    unnamed x29 -> x31, local copies, waits for them, and re-layouts: 10.3 us -> 10.5 us
  transfers between devices with their start and end apart: 4 -> 4, of which waited for: 2 -> 2; matrix products, arithmetic and copies ran while one was open for 25% -> 26% of each run, Pallas kernels for 12% -> 12%
where the time goes in v8:
time: 193 us; the launch traced here: 192 us
  waiting for transfers between devices  63.2 us (33%)
  Pallas kernels  52.2 us (27%)
  local copies, waits for them, and re-layouts  32.7 us (17%)
  starting transfers between devices  18.4 us (10%)
  matrix products  16.2 us (8%)
  other arithmetic  8.94 us (5%)
    ppermute x1, waiting for transfers between devices, local(): lax.ppermute(token_blocks[dev_blocks - 1], ('ctx', 'seq'), forward)  54.5 us
    pallas_call x1, Pallas kernels, attend_far(): pl.pallas_call(far_kernel, grid_spec=grid_spec, out_shape=jax.ShapeDtypeS...  30 us
    pallas_call x1, Pallas kernels, attend_near(): pl.pallas_call(near_kernel, grid=(blocks,), in_specs=[pl.BlockSpec((1, 1,...  22.2 us
    dot_general x5, matrix products, local(): jnp.dot(x, w, preferred_element_type=jnp.float32).astype(jnp.bfloat16)  12.7 us
    unnamed x31, local copies, waits for them, and re-layouts  10.5 us
    all_to_all x1, waiting for transfers between devices, local(): lax.all_to_all(copies, ('ctx', 'seq'), 0, 0, tiled=True)  8.71 us
    another operation x2, local copies, waits for them, and re-layouts, split_weights(): shaped[:, :, j, :].reshape(model_dim, head_total * HD)  7.86 us
    all_to_all x1, starting transfers between devices, local(): lax.all_to_all(outgoing, 'ctx', split_axis=0, concat_axis=0, tiled=True)  7 us
  transfers between devices with their start and end apart: 4, of which 2 were waited for; matrix products, arithmetic and copies ran while one was open for 26% of the time, Pallas kernels for 12%

profile of v8, /device:TPU:16, one launch (start us, length us, event | category | flops | bytes accessed | tf_op | source)
XLA Modules:
  0.0 191.9 jit_solution(802954308759791496)
XLA Ops:
  0.0 0.9 dynamic_slice.18
  1.2 1.6 select_reduce_fusion
  2.8 0.2 multiply_reduce_fusion
  3.1 0.9 broadcast_in_dim.39
  4.0 6.0 %all-to-all-start = ((bf16[32,8,1024]{2,1,0:T(8,128)(2,1)}), bf16[32,8,1024]{2,1,0:T(8,128)(2,1)}, u32[]{:S(2)}, u32[]{:S(2)}) async-start(bf16[32,8,1024]{2,1,0:T(8,128)(2,1)} %broadcast_in_dim.39), calls=%async_computation | async-start | bytes 1048576 | tf_op jit(solution)/shard_map/all_to_all | solution.py:233
  10.2 0.4 copy-done.9
  11.7 2.9 %gather_fusion = bf16[32,64,1024]{2,1,0:T(8,128)(2,1)} fusion(bf16[8,64,1024]{2,1,0:T(8,128)(2,1)S(1)} %bitcast.29, s32[1024]{0:T(1024)S(1)} %get-tuple-element.28), kind=kCustom, calls=%fused_computation.2 | custom fusion | bytes 8388736 | tf_op jit(solution)/shard_map/jit(_take)/gather | solution.py:214
  14.6 8.7 %all-to-all-done = bf16[32,8,1024]{2,1,0:T(8,128)(2,1)} async-done(((bf16[32,8,1024]{2,1,0:T(8,128)(2,1)}), bf16[32,8,1024]{2,1,0:T(8,128)(2,1)}, u32[]{:S(2)}, u32[]{:S(2)}) %all-to-all-start) | async-done | bytes 524320 | tf_op jit(solution)/shard_map/all_to_all | solution.py:233
  23.3 7.0 %all-to-all-start.1 = ((bf16[8,4,64,1024]{3,2,1,0:T(8,128)(2,1)}), bf16[8,4,64,1024]{3,2,1,0:T(8,128)(2,1)}, u32[]{:S(2)}, u32[]{:S(2)}) async-start(bf16[8,4,64,1024]{3,2,1,0:T(8,128)(2,1)} %bitcast.31), calls=%async_computation.1 | async-start | bytes 8388608 | tf_op jit(solution)/shard_map/all_to_all | solution.py:235
  30.3 0.7 fusion.5
  31.0 3.5 %collective-permute-start.1 = (bf16[64,1024]{1,0:T(8,128)(2,1)}, bf16[64,1024]{1,0:T(8,128)(2,1)S(1)}, u32[]{:S(2)}, u32[]{:S(2)}) collective-permute-start(bf16[64,1024]{1,0:T(8,128)(2,1)} %get-tuple-element.21), channel_id=1, source_target_pairs={{1,0},{2,1},{3,2},{4,3},{5,4},{6,5},{7,6},{8,7},{9,8},{10,9},{11,1... | collective-permute-start | bytes 393224 | tf_op jit(solution)/shard_map/ppermute | solution.py:220
  34.5 1.9 %collective-permute-start = (bf16[64,1024]{1,0:T(8,128)(2,1)}, bf16[64,1024]{1,0:T(8,128)(2,1)}, u32[]{:S(2)}, u32[]{:S(2)}) collective-permute-start(bf16[64,1024]{1,0:T(8,128)(2,1)} %get-tuple-element.22), channel_id=1, source_target_pairs={{0,1},{1,2},{2,3},{3,4},{4,5},{5,6},{6,7},{7,8},{8,9},{9,10},{10,1... | collective-permute-start | bytes 393224 | tf_op jit(solution)/shard_map/ppermute | solution.py:219
  36.4 0.6 lt.87
  37.2 0.7 gather_fusion.1
  38.0 0.7 gather_fusion.2
  39.4 8.8 %copy.43 = bf16[1024,3072]{0,1:T(8,128)(2,1)} copy(bf16[1024,3072]{1,0:T(8,128)(2,1)} %param.9) | data formatting | bytes 12582912 | tf_op args[1]
  48.2 5.8 %fusion.4 = (bf16[1024,16,1,64]{0,3,2,1:T(8,128)(2,1)}, bf16[1024,16,1,64]{0,3,2,1:T(8,128)(2,1)}, bf16[1024,16,1,64]{0,3,2,1:T(8,128)(2,1)}) fusion(bf16[1024,16,3,64]{0,3,2,1:T(8,128)(2,1)} %bitcast.30), kind=kLoop, calls=%fused_computation.47 | loop fusion | bytes 12582912 | tf_op jit(solution)/shard_map/slice | solution.py:35
  53.9 3.9 %copy.48 = bf16[1024,1024]{1,0:T(8,128)(2,1)} copy(bf16[1024,1024]{0,1:T(8,128)(2,1)} %bitcast.41) | data formatting | bytes 4194304 | tf_op jit(solution)/shard_map/reshape;squeeze | solution.py:35
  57.9 3.9 %copy.47 = bf16[1024,1024]{1,0:T(8,128)(2,1)} copy(bf16[1024,1024]{0,1:T(8,128)(2,1)} %bitcast.38) | data formatting | bytes 4194304 | tf_op jit(solution)/shard_map/reshape;squeeze | solution.py:35
  62.0 0.6 compare_convert_fusion
  62.6 4.8 %pad_maximum_fusion.refs_3_ = bf16[1024,2048]{1,0:T(8,128)(2,1)} fusion(bf16[1024,1024]{1,0:T(8,128)(2,1)} %copy.48, bf16[1024,1024]{1,0:T(8,128)(2,1)} %copy.47), kind=kLoop, calls=%fused_computation.3 | loop fusion | flops 8388608 | bytes 8388608 | tf_op jit(solution)/shard_map/concatenate | solution.py:267
  67.4 2.3 %convolution_convert_fusion.2 = bf16[512,1024]{1,0:T(8,128)(2,1)} fusion(bf16[512,1024]{1,0:T(8,128)(2,1)S(1)} %copy-done.2, bf16[1024,1024]{0,1:T(8,128)(2,1)S(1)} %bitcast.44), kind=kOutput, calls=%fused_computation.8 | convolution fusion | flops 1074266112 | bytes 4194304 | tf_op jit(solution)/shard_map/dot_general | solution.py:238
  69.7 0.5 multiply_add_fusion.ids_ref
  70.2 54.5 %collective-permute-done = bf16[64,1024]{1,0:T(8,128)(2,1)} collective-permute-done((bf16[64,1024]{1,0:T(8,128)(2,1)}, bf16[64,1024]{1,0:T(8,128)(2,1)}, u32[]{:S(2)}, u32[]{:S(2)}) %collective-permute-start) | collective-permute-done | bytes 131104 | tf_op jit(solution)/shard_map/ppermute | solution.py:219
  124.7 0.9 constant_dynamic-update-slice_fusion.2
  125.8 2.6 %convolution_convert_fusion = bf16[640,1024]{1,0:T(8,128)(2,1)} fusion(bf16[640,1024]{1,0:T(8,128)(2,1)S(1)} %constant_dynamic-update-slice_fusion, bf16[1024,1024]{0,1:T(8,128)(2,1)S(1)} %bitcast.42), kind=kOutput, calls=%fused_computation.6 | convolution fusion | flops 1342832640 | bytes 4718592 | tf_op jit(solution)/shard_map/dot_general | solution.py:238
  128.4 2.6 %convolution_convert_fusion.1 = bf16[640,1024]{1,0:T(8,128)(2,1)} fusion(bf16[640,1024]{1,0:T(8,128)(2,1)S(1)} %constant_dynamic-update-slice_fusion, bf16[1024,1024]{0,1:T(8,128)(2,1)S(1)} %bitcast.39), kind=kOutput, calls=%fused_computation.7 | convolution fusion | flops 1342832640 | bytes 4718592 | tf_op jit(solution)/shard_map/dot_general | solution.py:238
  131.0 2.6 %convolution_convert_fusion.3.vs_ref = bf16[256,1024]{1,0:T(8,128)(2,1)} fusion(bf16[256,1024]{1,0:T(8,128)(2,1)} %bitcast.4, bf16[1024,1024]{0,1:T(8,128)(2,1)S(1)} %bitcast.43), kind=kOutput, calls=%fused_computation.9 | convolution fusion | flops 537133056 | bytes 3145728 | tf_op jit(solution)/shard_map/dot_general | solution.py:238
  133.6 2.6 %convolution_convert_fusion.4.ks_ref = bf16[256,1024]{1,0:T(8,128)(2,1)} fusion(bf16[256,1024]{1,0:T(8,128)(2,1)} %bitcast.4, bf16[1024,1024]{0,1:T(8,128)(2,1)S(1)} %bitcast.40), kind=kOutput, calls=%fused_computation.10 | convolution fusion | flops 537133056 | bytes 3145728 | tf_op jit(solution)/shard_map/dot_general | solution.py:238
  136.2 22.2 %shard_map.64 = (f32[8,64,1024]{2,1,0:T(8,128)}, f32[8,64,1024]{2,1,0:T(8,128)}, f32[8,64,1024]{2,1,0:T(8,128)}) custom-call(s32[8,1,192]{2,1,0:T(1,128)} %get-tuple-element.25.mask_ref, bf16[8,64,1024]{2,1,0:T(8,128)(2,1)} %bitcast.45, bf16[10,64,1024]{2,1,0:T(8,128)(2,1)} %bitcast.35, bf16[10,64,1024]{2,1,0:T(8,128)(2,1)} %bitcast.36, ...), custom_call_target="tpu_custom_call" | custom-call | flops 1879048192 | bytes 14680064 | tf_op jit(solution)/shard_map/pallas_call | solution.py:135
  158.4 30.0 %shard_map.65 = bf16[8,64,1024]{2,1,0:T(8,128)(2,1)} custom-call(s32[24]{0:T(128)} %multiply_add_fusion.ids_ref, s32[8,1,192]{2,1,0:T(1,128)} %get-tuple-element.26.mask_ref, bf16[8,64,1024]{2,1,0:T(8,128)(2,1)} %bitcast.46, bf16[32,64,1024]{2,1,0:T(8,128)(2,1)} %bitcast.7.refs_0_.refs_1_.refs_2_, bf16[32,64,1024]{2,1,0:T(8,128)(2,1)} %bitcast.7.refs_0_.refs_1_.refs_2_, ...), custom_call_target="tpu_custom_call" | custom-call | flops 7247757312 | bytes 15728640 | tf_op jit(solution)/shard_map/pallas_call | solution.py:181
  188.5 3.5 %add_convert_fusion = bf16[512,1024]{1,0:T(8,128)(2,1)} fusion(bf16[512,1024]{1,0:T(8,128)(2,1)S(1)} %copy-done.2, bf16[512,1024]{1,0:T(8,128)(2,1)} %bitcast.48, bf16[1024,1024]{1,0:T(8,128)(2,1)S(1)} %copy-done), kind=kOutput, calls=%fused_computation.4 | convolution fusion | flops 1075314688 | bytes 5242880 | tf_op jit(solution)/shard_map/dot_general | solution.py:272
  (66 shorter events, 2.7 us)
Async XLA Ops:
  0.0 188.5 %copy-start = (bf16[1024,1024]{1,0:T(8,128)(2,1)S(1)}, bf16[1024,1024]{1,0:T(8,128)(2,1)}, u32[]{:S(2)}) copy-start(bf16[1024,1024]{1,0:T(8,128)(2,1)} %param.10) | copy-start | bytes 6291460
  0.0 11.7 %copy-start.2 = (bf16[512,1024]{1,0:T(8,128)(2,1)S(1)}, bf16[512,1024]{1,0:T(8,128)(2,1)}, u32[]{:S(2)}) copy-start(bf16[512,1024]{1,0:T(8,128)(2,1)} %param.8) | copy-start | bytes 3145732
  0.0 10.6 %copy-start.6 = (s32[256,3]{0,1:T(4,128)S(1)}, s32[256,3]{0,1:T(4,128)}, u32[]{:S(2)}) copy-start(s32[256,3]{0,1:T(4,128)} %param.12) | copy-start | bytes 9220
  0.0 11.0 %copy-start.7 = (s32[256,3]{0,1:T(4,128)S(1)}, s32[256,3]{0,1:T(4,128)}, u32[]{:S(2)}) copy-start(s32[256,3]{0,1:T(4,128)} %param.13) | copy-start | bytes 9220
  4.0 19.3 %all-to-all-start = ((bf16[32,8,1024]{2,1,0:T(8,128)(2,1)}), bf16[32,8,1024]{2,1,0:T(8,128)(2,1)}, u32[]{:S(2)}, u32[]{:S(2)}) async-start(bf16[32,8,1024]{2,1,0:T(8,128)(2,1)} %broadcast_in_dim.39), calls=%async_computation | async-start | bytes 1048576 | tf_op jit(solution)/shard_map/all_to_all | solution.py:233
  10.0 0.6 copy-start.9
  10.0 0.6 copy-start.11
  23.3 135.1 %all-to-all-start.1 = ((bf16[8,4,64,1024]{3,2,1,0:T(8,128)(2,1)}), bf16[8,4,64,1024]{3,2,1,0:T(8,128)(2,1)}, u32[]{:S(2)}, u32[]{:S(2)}) async-start(bf16[8,4,64,1024]{3,2,1,0:T(8,128)(2,1)} %bitcast.31), calls=%async_computation.1 | async-start | bytes 8388608 | tf_op jit(solution)/shard_map/all_to_all | solution.py:235
  30.3 6.9 %copy-start.1 = (s32[256]{0:T(256)S(1)}, s32[256]{0:T(256)}, u32[]{:S(2)}) copy-start(s32[256]{0:T(256)} %param.11) | copy-start | bytes 3076
  31.0 94.7 %collective-permute-start.1 = (bf16[64,1024]{1,0:T(8,128)(2,1)}, bf16[64,1024]{1,0:T(8,128)(2,1)S(1)}, u32[]{:S(2)}, u32[]{:S(2)}) collective-permute-start(bf16[64,1024]{1,0:T(8,128)(2,1)} %get-tuple-element.21), channel_id=1, source_target_pairs={{1,0},{2,1},{3,2},{4,3},{5,4},{6,5},{7,6},{8,7},{9,8},{10,9},{11,1... | collective-permute-start | bytes 393224 | tf_op jit(solution)/shard_map/ppermute | solution.py:220
  34.5 90.2 %collective-permute-start = (bf16[64,1024]{1,0:T(8,128)(2,1)}, bf16[64,1024]{1,0:T(8,128)(2,1)}, u32[]{:S(2)}, u32[]{:S(2)}) collective-permute-start(bf16[64,1024]{1,0:T(8,128)(2,1)} %get-tuple-element.22), channel_id=1, source_target_pairs={{0,1},{1,2},{2,3},{3,4},{4,5},{5,6},{6,7},{7,8},{8,9},{9,10},{10,1... | collective-permute-start | bytes 393224 | tf_op jit(solution)/shard_map/ppermute | solution.py:219
  38.0 0.8 copy-start.10
  38.0 0.8 copy-start.12
  57.9 4.1 %copy-start.8 = (s32[192]{0:T(256)S(1)}, s32[192]{0:T(256)}, u32[]{:S(2)}) copy-start(s32[192]{0:T(256)} %lt.87) | copy-start | bytes 2308
  62.6 4.8 %copy-start.5 = (bf16[1024,16,1,64]{0,3,2,1:T(8,128)(2,1)S(1)}, bf16[1024,16,1,64]{0,3,2,1:T(8,128)(2,1)}, u32[]{:S(2)}) copy-start(bf16[1024,16,1,64]{0,3,2,1:T(8,128)(2,1)} %get-tuple-element.20) | copy-start | bytes 6291460
  69.7 56.0 %copy-start.4 = (bf16[1024,16,1,64]{0,3,2,1:T(8,128)(2,1)S(1)}, bf16[1024,16,1,64]{0,3,2,1:T(8,128)(2,1)}, u32[]{:S(2)}) copy-start(bf16[1024,16,1,64]{0,3,2,1:T(8,128)(2,1)} %get-tuple-element.19) | copy-start | bytes 6291460
  125.8 2.6 %copy-start.3 = (bf16[1024,16,1,64]{0,3,2,1:T(8,128)(2,1)S(1)}, bf16[1024,16,1,64]{0,3,2,1:T(8,128)(2,1)}, u32[]{:S(2)}) copy-start(bf16[1024,16,1,64]{0,3,2,1:T(8,128)(2,1)} %get-tuple-element.18) | copy-start | bytes 6291460

commit v9 on v7

--- a/solution.py
+++ b/solution.py
@@ -27,6 +27,16 @@
         ranks[..., None, :] == jnp.arange(capacity, dtype=jnp.int32)[:, None]
     )
     return jnp.sum(jnp.where(slot_hit, offsets[..., None, :], 0), axis=-1)
+
+
+def ring_gather(x, axis):
+    count = lax.axis_size(axis)
+    pieces = [x] + [
+        lax.ppermute(x, axis, [(i, (i + shift) % count) for i in range(count)])
+        for shift in range(1, count)
+    ]
+    order = (lax.axis_index(axis) - jnp.arange(count, dtype=jnp.int32)) % count
+    return jnp.take(jnp.stack(pieces), order, axis=0, mode="clip").reshape(-1, x.shape[-1])
 
 
 def split_weights(w_qkv, head_total):
@@ -225,9 +235,7 @@
     summary = (pooled / jnp.sqrt(jnp.mean(pooled * pooled, axis=1, keepdims=True) + 1e-05)).astype(
         jnp.bfloat16
     )
-    copies = jnp.broadcast_to(summary[None], (dev_count,) + summary.shape)
-    summary_all = lax.all_to_all(copies, ("ctx", "seq"), 0, 0, tiled=True).reshape(-1, model_dim)
-    summary_all, outgoing = lax.optimization_barrier((summary_all, outgoing))
+    summary_all = ring_gather(ring_gather(summary, "seq"), "ctx")
     incoming = lax.all_to_all(outgoing, "ctx", split_axis=0, concat_axis=0, tiled=True)
 
     w_q, w_k, w_v = split_weights(w_qkv, head_total)

time: 191 us -> 208 us (1.089); the launches traced: 190 us -> 205 us
  waiting for transfers between devices: 63.4 us -> 71.9 us
  local copies, waits for them, and re-layouts: 32.6 us -> 41 us
  starting transfers between devices: 18.4 us -> 16.3 us
    ppermute x0 -> x10, waiting for transfers between devices: none -> 71.9 us  [ring_gather(): lax.ppermute(x, axis, [(i, (i + shift) % count) for i in range(count)])]
    ppermute x1, waiting for transfers between devices: 54.7 us -> 0.01 us  [local(): lax.ppermute(token_blocks[dev_blocks - 1], ('ctx', 'seq'), forward)]
    all_to_all x1 -> x0, waiting for transfers between devices: 8.71 us -> none  [local(): lax.all_to_all(copies, ('ctx', 'seq'), 0, 0, tiled=True)]
    all_to_all x1 -> x0, starting transfers between devices: 5.99 us -> none  [local(): lax.all_to_all(copies, ('ctx', 'seq'), 0, 0, tiled=True)]
    unnamed x31 -> x26, local copies, waits for them, and re-layouts: 10.3 us -> 15.8 us
    ppermute x0 -> x10, starting transfers between devices: none -> 4.39 us  [ring_gather(): lax.ppermute(x, axis, [(i, (i + shift) % count) for i in range(count)])]
    gather x0 -> x2, local copies, waits for them, and re-layouts: none -> 2.97 us  [ring_gather(): jnp.take(jnp.stack(pieces), order, axis=0, mode='clip')]
  transfers between devices with their start and end apart: 4 -> 13, of which waited for: 2 -> 5; matrix products, arithmetic and copies ran while one was open for 26% -> 29% of each run, Pallas kernels for 12% -> 11%
where the time goes in v9:
time: 208 us; the launch traced here: 205 us
  waiting for transfers between devices  71.9 us (35%)
  Pallas kernels  50 us (24%)
  local copies, waits for them, and re-layouts  41 us (20%)
  starting transfers between devices  16.3 us (8%)
  matrix products  16 us (8%)
  other arithmetic  9.12 us (4%)
    ppermute x10, waiting for transfers between devices, ring_gather(): lax.ppermute(x, axis, [(i, (i + shift) % count) for i in range(count)])  71.9 us
    pallas_call x1, Pallas kernels, attend_far(): pl.pallas_call(functools.partial(far_kernel, group), grid_spec=grid_spec,...  27.8 us
    pallas_call x1, Pallas kernels, attend_near(): pl.pallas_call(near_kernel, grid=(blocks,), in_specs=[pl.BlockSpec((1, 1,...  22.2 us
    unnamed x26, local copies, waits for them, and re-layouts  15.8 us
    dot_general x5, matrix products, local(): jnp.dot(x, w, preferred_element_type=jnp.float32).astype(jnp.bfloat16)  12.6 us
    another operation x2, local copies, waits for them, and re-layouts, split_weights(): shaped[:, :, j, :].reshape(model_dim, head_total * HD)  7.85 us
    all_to_all x1, starting transfers between devices, local(): lax.all_to_all(outgoing, 'ctx', split_axis=0, concat_axis=0, tiled=True)  6.17 us
    slice x1, local copies, waits for them, and re-layouts, split_weights(): shaped[:, :, j, :].reshape(model_dim, head_total * HD)  5.7 us
  transfers between devices with their start and end apart: 13, of which 5 were waited for; matrix products, arithmetic and copies ran while one was open for 29% of the time, Pallas kernels for 11%

profile of v9, /device:TPU:16, one launch (start us, length us, event | category | flops | bytes accessed | tf_op | source)
XLA Modules:
  0.0 204.6 jit_solution(1591093998915970633)
XLA Ops:
  0.0 0.9 dynamic_slice.20
  1.2 1.6 select_reduce_fusion
  3.1 0.9 collective-permute-start.4
  5.0 0.8 copy.39
  6.1 0.8 copy.40
  7.4 2.9 %gather_fusion = bf16[32,64,1024]{2,1,0:T(8,128)(2,1)} fusion(bf16[8,64,1024]{2,1,0:T(8,128)(2,1)S(1)} %bitcast.57, s32[1024]{0:T(1024)S(1)} %get-tuple-element.24), kind=kCustom, calls=%fused_computation.2 | custom fusion | bytes 8388736 | tf_op jit(solution)/shard_map/jit(_take)/gather | solution.py:220
  10.3 6.2 %all-to-all-start = ((bf16[8,4,64,1024]{3,2,1,0:T(8,128)(2,1)}), bf16[8,4,64,1024]{3,2,1,0:T(8,128)(2,1)}, u32[]{:S(2)}, u32[]{:S(2)}) async-start(bf16[8,4,64,1024]{3,2,1,0:T(8,128)(2,1)} %bitcast.59), calls=%async_computation | async-start | bytes 8388608 | tf_op jit(solution)/shard_map/all_to_all | solution.py:239
  16.5 0.7 fusion.10
  17.2 3.8 %collective-permute-start.1 = (bf16[64,1024]{1,0:T(8,128)(2,1)}, bf16[64,1024]{1,0:T(8,128)(2,1)}, u32[]{:S(2)}, u32[]{:S(2)}) collective-permute-start(bf16[64,1024]{1,0:T(8,128)(2,1)} %get-tuple-element.17), channel_id=1, source_target_pairs={{1,0},{2,1},{3,2},{4,3},{5,4},{6,5},{7,6},{8,7},{9,8},{10,9},{11,1... | collective-permute-start | bytes 393224 | tf_op jit(solution)/shard_map/ppermute | solution.py:226
  21.0 1.9 collective-permute-start
  25.4 8.6 %copy.43 = bf16[1024,3072]{0,1:T(8,128)(2,1)} copy(bf16[1024,3072]{1,0:T(8,128)(2,1)} %param.9) | data formatting | bytes 12582912 | tf_op args[1]
  34.0 5.7 %fusion.9 = (bf16[1024,16,1,64]{0,3,2,1:T(8,128)(2,1)}, bf16[1024,16,1,64]{0,3,2,1:T(8,128)(2,1)}, bf16[1024,16,1,64]{0,3,2,1:T(8,128)(2,1)}) fusion(bf16[1024,16,3,64]{0,3,2,1:T(8,128)(2,1)} %bitcast.58), kind=kLoop, calls=%fused_computation.72 | loop fusion | bytes 12582912 | tf_op jit(solution)/shard_map/slice | solution.py:45
  39.7 3.9 %copy.48 = bf16[1024,1024]{1,0:T(8,128)(2,1)} copy(bf16[1024,1024]{0,1:T(8,128)(2,1)} %bitcast.69) | data formatting | bytes 4194304 | tf_op jit(solution)/shard_map/reshape;squeeze | solution.py:45
  43.6 3.9 %copy.47 = bf16[1024,1024]{1,0:T(8,128)(2,1)} copy(bf16[1024,1024]{0,1:T(8,128)(2,1)} %bitcast.66) | data formatting | bytes 4194304 | tf_op jit(solution)/shard_map/reshape;squeeze | solution.py:45
  49.0 4.8 %pad_maximum_fusion.refs_6_ = bf16[1024,2048]{1,0:T(8,128)(2,1)} fusion(bf16[1024,1024]{1,0:T(8,128)(2,1)} %copy.48, bf16[1024,1024]{1,0:T(8,128)(2,1)} %copy.47), kind=kLoop, calls=%fused_computation.5 | loop fusion | flops 8388608 | bytes 8388608 | tf_op jit(solution)/shard_map/concatenate | solution.py:271
  53.8 2.3 %convolution_convert_fusion.2 = bf16[512,1024]{1,0:T(8,128)(2,1)} fusion(bf16[512,1024]{1,0:T(8,128)(2,1)S(1)} %copy-done.2, bf16[1024,1024]{0,1:T(8,128)(2,1)S(1)} %bitcast.74), kind=kOutput, calls=%fused_computation.10 | convolution fusion | flops 1074266112 | bytes 4194304 | tf_op jit(solution)/shard_map/dot_general | solution.py:242
  57.7 1.7 collective-permute-start.5
  60.0 53.1 %collective-permute-done.5 = bf16[32,1024]{1,0:T(8,128)(2,1)S(1)} collective-permute-done((bf16[32,1024]{1,0:T(8,128)(2,1)S(1)}, bf16[32,1024]{1,0:T(8,128)(2,1)S(1)}, u32[]{:S(2)}, u32[]{:S(2)}) %collective-permute-start.5) | collective-permute-done | bytes 65568 | tf_op jit(solution)/shard_map/ppermute | solution.py:35
  113.7 4.1 %collective-permute-done.6 = bf16[32,1024]{1,0:T(8,128)(2,1)S(1)} collective-permute-done((bf16[32,1024]{1,0:T(8,128)(2,1)S(1)}, bf16[32,1024]{1,0:T(8,128)(2,1)S(1)}, u32[]{:S(2)}, u32[]{:S(2)}) %collective-permute-start.6) | collective-permute-done | bytes 65568 | tf_op jit(solution)/shard_map/ppermute | solution.py:35
  118.5 5.4 %collective-permute-done.7 = bf16[32,1024]{1,0:T(8,128)(2,1)S(1)} collective-permute-done((bf16[32,1024]{1,0:T(8,128)(2,1)S(1)}, bf16[32,1024]{1,0:T(8,128)(2,1)S(1)}, u32[]{:S(2)}, u32[]{:S(2)}) %collective-permute-start.7) | collective-permute-done | bytes 65568 | tf_op jit(solution)/shard_map/ppermute | solution.py:35
  124.6 4.6 %collective-permute-done.8 = bf16[32,1024]{1,0:T(8,128)(2,1)S(1)} collective-permute-done((bf16[32,1024]{1,0:T(8,128)(2,1)S(1)}, bf16[32,1024]{1,0:T(8,128)(2,1)S(1)}, u32[]{:S(2)}, u32[]{:S(2)}) %collective-permute-start.8) | collective-permute-done | bytes 65568 | tf_op jit(solution)/shard_map/ppermute | solution.py:35
  129.8 4.5 %collective-permute-done.9 = bf16[32,1024]{1,0:T(8,128)(2,1)S(1)} collective-permute-done((bf16[32,1024]{1,0:T(8,128)(2,1)S(1)}, bf16[32,1024]{1,0:T(8,128)(2,1)S(1)}, u32[]{:S(2)}, u32[]{:S(2)}) %collective-permute-start.9) | collective-permute-done | bytes 65568 | tf_op jit(solution)/shard_map/ppermute | solution.py:35
  136.3 2.4 %gather_fusion.2 = bf16[8,32,1024]{2,1,0:T(8,128)(2,1)} fusion(bf16[8,32,1024]{2,1,0:T(8,128)(2,1)} %bitcast_dynamic-update-slice_fusion, s32[1024]{0:T(1024)S(1)} %pad_clamp_fusion), kind=kCustom, calls=%fused_computation.4 | custom fusion | bytes 1048608 | tf_op jit(solution)/shard_map/jit(_take)/gather | solution.py:39
  138.7 3.4 %convolution_convert_fusion.3.vs_ref = bf16[256,1024]{1,0:T(8,128)(2,1)} fusion(bf16[256,1024]{1,0:T(8,128)(2,1)} %bitcast.76, bf16[1024,1024]{0,1:T(8,128)(2,1)} %bitcast.70), kind=kOutput, calls=%fused_computation.11 | convolution fusion | flops 537133056 | bytes 3145728 | tf_op jit(solution)/shard_map/dot_general | solution.py:242
  142.1 1.6 convolution_convert_fusion.4.ks_ref
  143.8 1.1 constant_dynamic-update-slice_fusion.2
  144.9 0.9 constant_dynamic-update-slice_fusion
  145.8 2.6 %convolution_convert_fusion = bf16[640,1024]{1,0:T(8,128)(2,1)} fusion(bf16[640,1024]{1,0:T(8,128)(2,1)S(1)} %constant_dynamic-update-slice_fusion, bf16[1024,1024]{0,1:T(8,128)(2,1)S(1)} %bitcast.71), kind=kOutput, calls=%fused_computation.8 | convolution fusion | flops 1342832640 | bytes 4718592 | tf_op jit(solution)/shard_map/dot_general | solution.py:242
  148.5 2.6 %convolution_convert_fusion.1 = bf16[640,1024]{1,0:T(8,128)(2,1)} fusion(bf16[640,1024]{1,0:T(8,128)(2,1)S(1)} %constant_dynamic-update-slice_fusion, bf16[1024,1024]{0,1:T(8,128)(2,1)S(1)} %bitcast.68), kind=kOutput, calls=%fused_computation.9 | convolution fusion | flops 1342832640 | bytes 4718592 | tf_op jit(solution)/shard_map/dot_general | solution.py:242
  151.1 22.2 %shard_map.64 = (f32[8,64,1024]{2,1,0:T(8,128)}, f32[8,64,1024]{2,1,0:T(8,128)}, f32[8,64,1024]{2,1,0:T(8,128)}) custom-call(s32[8,1,192]{2,1,0:T(1,128)} %get-tuple-element.21.mask_ref, bf16[8,64,1024]{2,1,0:T(8,128)(2,1)} %bitcast.72, bf16[10,64,1024]{2,1,0:T(8,128)(2,1)} %bitcast.63, bf16[10,64,1024]{2,1,0:T(8,128)(2,1)} %bitcast.64, ...), custom_call_target="tpu_custom_call" | custom-call | flops 1879048192 | bytes 14680064 | tf_op jit(solution)/shard_map/pallas_call | solution.py:143
  173.3 27.8 %shard_map.65 = bf16[8,64,1024]{2,1,0:T(8,128)(2,1)} custom-call(s32[24]{0:T(128)} %multiply_add_fusion.ids_ref, s32[8,1,192]{2,1,0:T(1,128)} %get-tuple-element.22.mask_ref, bf16[8,64,1024]{2,1,0:T(8,128)(2,1)} %bitcast.73, bf16[32,64,1024]{2,1,0:T(8,128)(2,1)} %bitcast.6.refs_0_.refs_1_.refs_2_.refs_3_.refs_4_.refs_5_, ...), custom_call_target="tpu_custom_call" | custom-call | flops 7247757312 | bytes 15728640 | tf_op jit(solution)/shard_map/pallas_call | solution.py:187
  201.1 3.5 %add_convert_fusion = bf16[512,1024]{1,0:T(8,128)(2,1)} fusion(bf16[512,1024]{1,0:T(8,128)(2,1)S(1)} %copy-done.2, bf16[512,1024]{1,0:T(8,128)(2,1)} %bitcast.75, bf16[1024,1024]{1,0:T(8,128)(2,1)S(1)} %copy-done), kind=kOutput, calls=%fused_computation.6 | convolution fusion | flops 1075314688 | bytes 5242880 | tf_op jit(solution)/shard_map/dot_general | solution.py:276
  (87 shorter events, 12.7 us)
Async XLA Ops:
  0.0 201.1 %copy-start = (bf16[1024,1024]{1,0:T(8,128)(2,1)S(1)}, bf16[1024,1024]{1,0:T(8,128)(2,1)}, u32[]{:S(2)}) copy-start(bf16[1024,1024]{1,0:T(8,128)(2,1)} %param.10) | copy-start | bytes 6291460
  0.0 7.4 %copy-start.2 = (bf16[512,1024]{1,0:T(8,128)(2,1)S(1)}, bf16[512,1024]{1,0:T(8,128)(2,1)}, u32[]{:S(2)}) copy-start(bf16[512,1024]{1,0:T(8,128)(2,1)} %param.8) | copy-start | bytes 3145732
  3.1 53.0 %collective-permute-start.4 = (bf16[8,1024]{1,0:T(8,128)(2,1)S(1)}, bf16[8,1024]{1,0:T(8,128)(2,1)S(1)}, u32[]{:S(2)}, u32[]{:S(2)}) collective-permute-start(bf16[8,1024]{1,0:T(8,128)(2,1)S(1)} %divide_convert_fusion), channel_id=1, source_target_pairs={{0,3},{1,0},{2,1},{3,2},{4,7},{5,4},{6,5},{7,6},{8,11},{9,8},{10,9... | collective-permute-start | bytes 49160 | tf_op jit(solution)/shard_map/ppermute | solution.py:35
  4.0 52.1 %collective-permute-start.3 = (bf16[8,1024]{1,0:T(8,128)(2,1)S(1)}, bf16[8,1024]{1,0:T(8,128)(2,1)S(1)}, u32[]{:S(2)}, u32[]{:S(2)}) collective-permute-start(bf16[8,1024]{1,0:T(8,128)(2,1)S(1)} %divide_convert_fusion), channel_id=1, source_target_pairs={{0,2},{1,3},{2,0},{3,1},{4,6},{5,7},{6,4},{7,5},{8,10},{9,11},{10,... | collective-permute-start | bytes 49160 | tf_op jit(solution)/shard_map/ppermute | solution.py:35
  4.7 51.5 %collective-permute-start.2 = (bf16[8,1024]{1,0:T(8,128)(2,1)S(1)}, bf16[8,1024]{1,0:T(8,128)(2,1)S(1)}, u32[]{:S(2)}, u32[]{:S(2)}) collective-permute-start(bf16[8,1024]{1,0:T(8,128)(2,1)S(1)} %divide_convert_fusion), channel_id=1, source_target_pairs={{0,1},{1,2},{2,3},{3,0},{4,5},{5,6},{6,7},{7,4},{8,9},{9,10},{10,1... | collective-permute-start | bytes 49160 | tf_op jit(solution)/shard_map/ppermute | solution.py:35
  10.3 163.0 %all-to-all-start = ((bf16[8,4,64,1024]{3,2,1,0:T(8,128)(2,1)}), bf16[8,4,64,1024]{3,2,1,0:T(8,128)(2,1)}, u32[]{:S(2)}, u32[]{:S(2)}) async-start(bf16[8,4,64,1024]{3,2,1,0:T(8,128)(2,1)} %bitcast.59), calls=%async_computation | async-start | bytes 8388608 | tf_op jit(solution)/shard_map/all_to_all | solution.py:239
  16.5 6.7 %copy-start.1 = (s32[256]{0:T(256)S(1)}, s32[256]{0:T(256)}, u32[]{:S(2)}) copy-start(s32[256]{0:T(256)} %param.11) | copy-start | bytes 3076
  17.2 127.7 %collective-permute-start.1 = (bf16[64,1024]{1,0:T(8,128)(2,1)}, bf16[64,1024]{1,0:T(8,128)(2,1)}, u32[]{:S(2)}, u32[]{:S(2)}) collective-permute-start(bf16[64,1024]{1,0:T(8,128)(2,1)} %get-tuple-element.17), channel_id=1, source_target_pairs={{1,0},{2,1},{3,2},{4,3},{5,4},{6,5},{7,6},{8,7},{9,8},{10,9},{11,1... | collective-permute-start | bytes 393224 | tf_op jit(solution)/shard_map/ppermute | solution.py:226
  21.0 122.7 %collective-permute-start = (bf16[64,1024]{1,0:T(8,128)(2,1)}, bf16[64,1024]{1,0:T(8,128)(2,1)}, u32[]{:S(2)}, u32[]{:S(2)}) collective-permute-start(bf16[64,1024]{1,0:T(8,128)(2,1)} %get-tuple-element.18), channel_id=1, source_target_pairs={{0,1},{1,2},{2,3},{3,4},{4,5},{5,6},{6,7},{7,8},{8,9},{9,10},{10,1... | collective-permute-start | bytes 393224 | tf_op jit(solution)/shard_map/ppermute | solution.py:225
  49.0 4.8 %copy-start.5 = (bf16[1024,16,1,64]{0,3,2,1:T(8,128)(2,1)S(1)}, bf16[1024,16,1,64]{0,3,2,1:T(8,128)(2,1)}, u32[]{:S(2)}) copy-start(bf16[1024,16,1,64]{0,3,2,1:T(8,128)(2,1)} %get-tuple-element.16) | copy-start | bytes 6291460
  56.7 78.9 %collective-permute-start.11 = (bf16[32,1024]{1,0:T(8,128)(2,1)S(1)}, bf16[32,1024]{1,0:T(8,128)(2,1)S(1)}, u32[]{:S(2)}, u32[]{:S(2)}) collective-permute-start(bf16[32,1024]{1,0:T(8,128)(2,1)S(1)} %bitcast.78), channel_id=1, source_target_pairs={{0,28},{4,0},{8,4},{12,8},{16,12},{20,16},{24,20},{28,24},{1,29},{... | collective-permute-start | bytes 196616 | tf_op jit(solution)/shard_map/ppermute | solution.py:35
  57.3 77.7 %collective-permute-start.10 = (bf16[32,1024]{1,0:T(8,128)(2,1)S(1)}, bf16[32,1024]{1,0:T(8,128)(2,1)S(1)}, u32[]{:S(2)}, u32[]{:S(2)}) collective-permute-start(bf16[32,1024]{1,0:T(8,128)(2,1)S(1)} %bitcast.79), channel_id=1, source_target_pairs={{0,24},{4,28},{8,0},{12,4},{16,8},{20,12},{24,16},{28,20},{1,25},{... | collective-permute-start | bytes 196616 | tf_op jit(solution)/shard_map/ppermute | solution.py:35
  57.7 55.4 %collective-permute-start.5 = (bf16[32,1024]{1,0:T(8,128)(2,1)S(1)}, bf16[32,1024]{1,0:T(8,128)(2,1)S(1)}, u32[]{:S(2)}, u32[]{:S(2)}) collective-permute-start(bf16[32,1024]{1,0:T(8,128)(2,1)S(1)} %bitcast.80), channel_id=1, source_target_pairs={{0,4},{4,8},{8,12},{12,16},{16,20},{20,24},{24,28},{28,0},{1,5},{5... | collective-permute-start | bytes 196616 | tf_op jit(solution)/shard_map/ppermute | solution.py:35
  113.1 4.8 %collective-permute-start.6 = (bf16[32,1024]{1,0:T(8,128)(2,1)S(1)}, bf16[32,1024]{1,0:T(8,128)(2,1)S(1)}, u32[]{:S(2)}, u32[]{:S(2)}) collective-permute-start(bf16[32,1024]{1,0:T(8,128)(2,1)S(1)} %bitcast.81), channel_id=1, source_target_pairs={{0,8},{4,12},{8,16},{12,20},{16,24},{20,28},{24,0},{28,4},{1,9},{5... | collective-permute-start | bytes 196616 | tf_op jit(solution)/shard_map/ppermute | solution.py:35
  117.9 6.1 %collective-permute-start.7 = (bf16[32,1024]{1,0:T(8,128)(2,1)S(1)}, bf16[32,1024]{1,0:T(8,128)(2,1)S(1)}, u32[]{:S(2)}, u32[]{:S(2)}) collective-permute-start(bf16[32,1024]{1,0:T(8,128)(2,1)S(1)} %bitcast.82), channel_id=1, source_target_pairs={{0,12},{4,16},{8,20},{12,24},{16,28},{20,0},{24,4},{28,8},{1,13},{... | collective-permute-start | bytes 196616 | tf_op jit(solution)/shard_map/ppermute | solution.py:35
  124.0 5.3 %collective-permute-start.8 = (bf16[32,1024]{1,0:T(8,128)(2,1)S(1)}, bf16[32,1024]{1,0:T(8,128)(2,1)S(1)}, u32[]{:S(2)}, u32[]{:S(2)}) collective-permute-start(bf16[32,1024]{1,0:T(8,128)(2,1)S(1)} %bitcast.83), channel_id=1, source_target_pairs={{0,16},{4,20},{8,24},{12,28},{16,0},{20,4},{24,8},{28,12},{1,17},{... | collective-permute-start | bytes 196616 | tf_op jit(solution)/shard_map/ppermute | solution.py:35
  129.2 5.2 %collective-permute-start.9 = (bf16[32,1024]{1,0:T(8,128)(2,1)S(1)}, bf16[32,1024]{1,0:T(8,128)(2,1)S(1)}, u32[]{:S(2)}, u32[]{:S(2)}) collective-permute-start(bf16[32,1024]{1,0:T(8,128)(2,1)S(1)} %bitcast.84), channel_id=1, source_target_pairs={{0,20},{4,24},{8,28},{12,0},{16,4},{20,8},{24,12},{28,16},{1,21},{... | collective-permute-start | bytes 196616 | tf_op jit(solution)/shard_map/ppermute | solution.py:35
  138.7 3.5 %copy-start.3 = (bf16[1024,16,1,64]{0,3,2,1:T(8,128)(2,1)S(1)}, bf16[1024,16,1,64]{0,3,2,1:T(8,128)(2,1)}, u32[]{:S(2)}) copy-start(bf16[1024,16,1,64]{0,3,2,1:T(8,128)(2,1)} %get-tuple-element.14) | copy-start | bytes 6291460
  138.7 3.5 %copy-start.6 = (bf16[8,32,1024]{2,1,0:T(8,128)(2,1)S(1)}, bf16[8,32,1024]{2,1,0:T(8,128)(2,1)}, u32[]{:S(2)}) copy-start(bf16[8,32,1024]{2,1,0:T(8,128)(2,1)} %gather_fusion.2) | copy-start | bytes 1572868
  143.7 2.1 %copy-start.4 = (bf16[1024,16,1,64]{0,3,2,1:T(8,128)(2,1)S(1)}, bf16[1024,16,1,64]{0,3,2,1:T(8,128)(2,1)}, u32[]{:S(2)}) copy-start(bf16[1024,16,1,64]{0,3,2,1:T(8,128)(2,1)} %get-tuple-element.15) | copy-start | bytes 6291460

commit v10 on v9

--- a/solution.py
+++ b/solution.py
@@ -46,6 +46,7 @@
 
 
 def pair_rows(q, low):
+    q = q * jnp.asarray(1.0 / math.sqrt(HD), q.dtype)
     blank = jnp.zeros_like(q)
     return jnp.concatenate([jnp.where(low, q, blank), jnp.where(low, blank, q)], axis=0)
 
@@ -61,7 +62,6 @@
                 o_ref, m_ref, l_ref):
     width = q_ref.shape[-1]
     rows = q_ref.shape[1]
-    scaling = 1.0 / math.sqrt(HD)
     valid = mask_ref[0] != 0
     low = lax.broadcasted_iota(jnp.int32, (rows, LANES), 1) < HD
     for tile in range(width // LANES):
@@ -70,9 +70,8 @@
         k_local = jnp.concatenate([kp_ref[0, :, cols], kc_ref[0, :, cols], kn_ref[0, :, cols]], axis=0)
         v_local = jnp.concatenate([vp_ref[0, :, cols], vc_ref[0, :, cols], vn_ref[0, :, cols]], axis=0)
         near = lax.dot_general(q_pair, k_local, CONTRACT, preferred_element_type=jnp.float32)
-        near = jnp.where(valid, near * scaling, -jnp.inf)
+        near = jnp.where(valid, near, -jnp.inf)
         wide = lax.dot_general(q_pair, ks_ref[:, cols], CONTRACT, preferred_element_type=jnp.float32)
-        wide = wide * scaling
         peak = jnp.maximum(
             jnp.max(near, axis=-1, keepdims=True), jnp.max(wide, axis=-1, keepdims=True)
         )
@@ -93,7 +92,6 @@
     wkv_ref, oa_ref, ma_ref, la_ref, out_ref = refs[group * RAND :]
     width = q_ref.shape[-1]
     rows = q_ref.shape[1]
-    scaling = 1.0 / math.sqrt(HD)
     low = lax.broadcasted_iota(jnp.int32, (rows, LANES), 1) < HD
     far_tokens = jnp.concatenate([ref[0] for ref in token_refs], axis=0)
     kv_far = jnp.dot(far_tokens, wkv_ref[...], preferred_element_type=jnp.float32).astype(
@@ -111,7 +109,7 @@
             scores = lax.dot_general(
                 q_pair, kv_rows[:, lanes], CONTRACT, preferred_element_type=jnp.float32
             )
-            scores = jnp.where(valid, scores * scaling, -jnp.inf)
+            scores = jnp.where(valid, scores, -jnp.inf)
             peak = jnp.max(scores, axis=-1, keepdims=True)
             exps = jnp.exp(scores - peak)
             total = jnp.sum(exps, axis=-1, keepdims=True)
@@ -236,6 +234,7 @@
         jnp.bfloat16
     )
     summary_all = ring_gather(ring_gather(summary, "seq"), "ctx")
+    summary_all, outgoing = lax.optimization_barrier((summary_all, outgoing))
     incoming = lax.all_to_all(outgoing, "ctx", split_axis=0, concat_axis=0, tiled=True)
 
     w_q, w_k, w_v = split_weights(w_qkv, head_total)

time: 208 us -> 201 us (0.966); the launches traced: 205 us -> 200 us
  waiting for transfers between devices: 71.9 us -> 63.6 us
  starting transfers between devices: 16.3 us -> 20.9 us
    ppermute x10, waiting for transfers between devices: 71.9 us -> 15.5 us  [ring_gather(): lax.ppermute(x, axis, [(i, (i + shift) % count) for i in range(count)])]
    ppermute x1, waiting for transfers between devices: 0.01 us -> 48.2 us  [local(): lax.ppermute(token_blocks[dev_blocks - 1], ('ctx', 'seq'), forward)]
    ppermute x10, starting transfers between devices: 4.39 us -> 9.05 us  [ring_gather(): lax.ppermute(x, axis, [(i, (i + shift) % count) for i in range(count)])]
    unnamed x26 -> x40, local copies, waits for them, and re-layouts: 15.8 us -> 16.4 us
  transfers between devices with their start and end apart: 13 -> 13, of which waited for: 5 -> 4; matrix products, arithmetic and copies ran while one was open for 29% -> 27% of each run, Pallas kernels for 11% -> 11%
where the time goes in v10:
time: 201 us; the launch traced here: 200 us
  waiting for transfers between devices  63.6 us (32%)
  Pallas kernels  50.1 us (25%)
  local copies, waits for them, and re-layouts  41.4 us (21%)
  starting transfers between devices  20.9 us (10%)
  matrix products  14.1 us (7%)
  other arithmetic  9.9 us (5%)
    ppermute x1, waiting for transfers between devices, local(): lax.ppermute(token_blocks[dev_blocks - 1], ('ctx', 'seq'), forward)  48.2 us
    pallas_call x1, Pallas kernels, attend_far(): pl.pallas_call(functools.partial(far_kernel, group), grid_spec=grid_spec,...  28 us
    pallas_call x1, Pallas kernels, attend_near(): pl.pallas_call(near_kernel, grid=(blocks,), in_specs=[pl.BlockSpec((1, 1,...  22.1 us
    unnamed x40, local copies, waits for them, and re-layouts  16.4 us
    ppermute x10, waiting for transfers between devices, ring_gather(): lax.ppermute(x, axis, [(i, (i + shift) % count) for i in range(count)])  15.5 us
    dot_general x5, matrix products, local(): jnp.dot(x, w, preferred_element_type=jnp.float32).astype(jnp.bfloat16)  10.7 us
    ppermute x10, starting transfers between devices, ring_gather(): lax.ppermute(x, axis, [(i, (i + shift) % count) for i in range(count)])  9.05 us
    another operation x2, local copies, waits for them, and re-layouts, split_weights(): shaped[:, :, j, :].reshape(model_dim, head_total * HD)  7.91 us
  transfers between devices with their start and end apart: 13, of which 4 were waited for; matrix products, arithmetic and copies ran while one was open for 27% of the time, Pallas kernels for 11%

profile of v10, /device:TPU:16, one launch (start us, length us, event | category | flops | bytes accessed | tf_op | source)
XLA Modules:
  0.0 200.2 jit_solution(9401066165101941449)
XLA Ops:
  0.0 0.9 dynamic_slice.18
  1.2 1.6 select_reduce_fusion
  3.1 0.9 collective-permute-start.2
  5.1 0.8 copy.39
  6.3 0.8 copy.40
  7.6 2.9 %gather_fusion.2 = bf16[32,64,1024]{2,1,0:T(8,128)(2,1)} fusion(bf16[8,64,1024]{2,1,0:T(8,128)(2,1)S(1)} %bitcast.57, s32[1024]{0:T(1024)S(1)} %get-tuple-element.28), kind=kCustom, calls=%fused_computation.4 | custom fusion | bytes 8388736 | tf_op jit(solution)/shard_map/jit(_take)/gather | solution.py:218
  11.1 0.7 pad_maximum_fusion.1
  12.4 1.5 collective-permute-start.9
  14.3 3.5 %collective-permute-start.7 = (bf16[32,1024]{1,0:T(8,128)(2,1)S(1)}, bf16[32,1024]{1,0:T(8,128)(2,1)S(1)}, u32[]{:S(2)}, u32[]{:S(2)}) collective-permute-start(bf16[32,1024]{1,0:T(8,128)(2,1)S(1)} %bitcast.80), channel_id=1, source_target_pairs={{0,20},{4,24},{8,28},{12,0},{16,4},{20,8},{24,12},{28,16},{1,21},{... | collective-permute-start | bytes 196616 | tf_op jit(solution)/shard_map/ppermute | solution.py:35
  17.8 1.9 collective-permute-start.3
  20.3 6.1 %collective-permute-done.3 = bf16[32,1024]{1,0:T(8,128)(2,1)S(1)} collective-permute-done((bf16[32,1024]{1,0:T(8,128)(2,1)S(1)}, bf16[32,1024]{1,0:T(8,128)(2,1)S(1)}, u32[]{:S(2)}, u32[]{:S(2)}) %collective-permute-start.3) | collective-permute-done | bytes 65568 | tf_op jit(solution)/shard_map/ppermute | solution.py:35
  27.0 3.9 %collective-permute-done.4 = bf16[32,1024]{1,0:T(8,128)(2,1)S(1)} collective-permute-done((bf16[32,1024]{1,0:T(8,128)(2,1)S(1)}, bf16[32,1024]{1,0:T(8,128)(2,1)S(1)}, u32[]{:S(2)}, u32[]{:S(2)}) %collective-permute-start.4) | collective-permute-done | bytes 65568 | tf_op jit(solution)/shard_map/ppermute | solution.py:35
  31.6 5.4 %collective-permute-done.5 = bf16[32,1024]{1,0:T(8,128)(2,1)S(1)} collective-permute-done((bf16[32,1024]{1,0:T(8,128)(2,1)S(1)}, bf16[32,1024]{1,0:T(8,128)(2,1)S(1)}, u32[]{:S(2)}, u32[]{:S(2)}) %collective-permute-start.5) | collective-permute-done | bytes 65568 | tf_op jit(solution)/shard_map/ppermute | solution.py:35
  40.2 2.4 %gather_fusion.1 = bf16[8,32,1024]{2,1,0:T(8,128)(2,1)} fusion(bf16[8,32,1024]{2,1,0:T(8,128)(2,1)} %bitcast_dynamic-update-slice_fusion, s32[1024]{0:T(1024)S(1)} %pad_clamp_fusion.2), kind=kCustom, calls=%fused_computation.3 | custom fusion | bytes 1048608 | tf_op jit(solution)/shard_map/jit(_take)/gather | solution.py:39
  42.6 7.3 %all-to-all-start = ((bf16[8,4,64,1024]{3,2,1,0:T(8,128)(2,1)}), bf16[8,4,64,1024]{3,2,1,0:T(8,128)(2,1)}, u32[]{:S(2)}, u32[]{:S(2)}) async-start(bf16[8,4,64,1024]{3,2,1,0:T(8,128)(2,1)} %bitcast.59), calls=%async_computation | async-start | bytes 8388608 | tf_op jit(solution)/shard_map/all_to_all | solution.py:238
  50.7 1.9 collective-permute-start.11
  52.6 2.6 %collective-permute-start.10 = (bf16[64,1024]{1,0:T(8,128)(2,1)}, bf16[64,1024]{1,0:T(8,128)(2,1)}, u32[]{:S(2)}, u32[]{:S(2)}) collective-permute-start(bf16[64,1024]{1,0:T(8,128)(2,1)} %get-tuple-element.22), channel_id=1, source_target_pairs={{0,1},{1,2},{2,3},{3,4},{4,5},{5,6},{6,7},{7,8},{8,9},{9,10},{10,1... | collective-permute-start | bytes 393224 | tf_op jit(solution)/shard_map/ppermute | solution.py:223
  58.2 8.7 %copy.43 = bf16[1024,3072]{0,1:T(8,128)(2,1)} copy(bf16[1024,3072]{1,0:T(8,128)(2,1)} %param.9) | data formatting | bytes 12582912 | tf_op args[1]
  66.8 5.8 %fusion.9 = (bf16[1024,16,1,64]{0,3,2,1:T(8,128)(2,1)}, bf16[1024,16,1,64]{0,3,2,1:T(8,128)(2,1)}, bf16[1024,16,1,64]{0,3,2,1:T(8,128)(2,1)}) fusion(bf16[1024,16,3,64]{0,3,2,1:T(8,128)(2,1)} %bitcast.58), kind=kLoop, calls=%fused_computation.72 | loop fusion | bytes 12582912 | tf_op jit(solution)/shard_map/slice | solution.py:45
  72.6 3.9 %copy.48 = bf16[1024,1024]{1,0:T(8,128)(2,1)} copy(bf16[1024,1024]{0,1:T(8,128)(2,1)} %bitcast.69) | data formatting | bytes 4194304 | tf_op jit(solution)/shard_map/reshape;squeeze | solution.py:45
  76.5 4.0 %copy.47 = bf16[1024,1024]{1,0:T(8,128)(2,1)} copy(bf16[1024,1024]{0,1:T(8,128)(2,1)} %bitcast.66) | data formatting | bytes 4194304 | tf_op jit(solution)/shard_map/reshape;squeeze | solution.py:45
  81.9 4.8 %pad_maximum_fusion.refs_6_ = bf16[1024,2048]{1,0:T(8,128)(2,1)} fusion(bf16[1024,1024]{1,0:T(8,128)(2,1)} %copy.48, bf16[1024,1024]{1,0:T(8,128)(2,1)} %copy.47), kind=kLoop, calls=%fused_computation.5 | loop fusion | flops 8388608 | bytes 8388608 | tf_op jit(solution)/shard_map/concatenate | solution.py:270
  86.8 2.3 %convolution_convert_fusion.2 = bf16[512,1024]{1,0:T(8,128)(2,1)} fusion(bf16[512,1024]{1,0:T(8,128)(2,1)S(1)} %copy-done.2, bf16[1024,1024]{0,1:T(8,128)(2,1)S(1)} %bitcast.74), kind=kOutput, calls=%fused_computation.10 | convolution fusion | flops 1074266112 | bytes 4194304 | tf_op jit(solution)/shard_map/dot_general | solution.py:241
  89.0 1.6 convolution_convert_fusion.3.vs_ref
  90.6 1.6 convolution_convert_fusion.4.ks_ref
  92.2 48.2 %collective-permute-done.10 = bf16[64,1024]{1,0:T(8,128)(2,1)} collective-permute-done((bf16[64,1024]{1,0:T(8,128)(2,1)}, bf16[64,1024]{1,0:T(8,128)(2,1)}, u32[]{:S(2)}, u32[]{:S(2)}) %collective-permute-start.10) | collective-permute-done | bytes 131104 | tf_op jit(solution)/shard_map/ppermute | solution.py:223
  140.4 0.9 constant_dynamic-update-slice_fusion.2
  141.4 2.6 %convolution_convert_fusion = bf16[640,1024]{1,0:T(8,128)(2,1)} fusion(bf16[640,1024]{1,0:T(8,128)(2,1)S(1)} %constant_dynamic-update-slice_fusion, bf16[1024,1024]{0,1:T(8,128)(2,1)S(1)} %bitcast.71), kind=kOutput, calls=%fused_computation.8 | convolution fusion | flops 1342832640 | bytes 4718592 | tf_op jit(solution)/shard_map/dot_general | solution.py:241
  144.0 2.6 %convolution_convert_fusion.1 = bf16[640,1024]{1,0:T(8,128)(2,1)} fusion(bf16[640,1024]{1,0:T(8,128)(2,1)S(1)} %constant_dynamic-update-slice_fusion, bf16[1024,1024]{0,1:T(8,128)(2,1)S(1)} %bitcast.68), kind=kOutput, calls=%fused_computation.9 | convolution fusion | flops 1342832640 | bytes 4718592 | tf_op jit(solution)/shard_map/dot_general | solution.py:241
  146.7 22.1 %shard_map.64 = (f32[8,64,1024]{2,1,0:T(8,128)}, f32[8,64,1024]{2,1,0:T(8,128)}, f32[8,64,1024]{2,1,0:T(8,128)}) custom-call(s32[8,1,192]{2,1,0:T(1,128)} %get-tuple-element.25.mask_ref, bf16[8,64,1024]{2,1,0:T(8,128)(2,1)} %bitcast.72, bf16[10,64,1024]{2,1,0:T(8,128)(2,1)} %bitcast.63, bf16[10,64,1024]{2,1,0:T(8,128)(2,1)} %bitcast.64, ...), custom_call_target="tpu_custom_call" | custom-call | flops 1879048192 | bytes 14680064 | tf_op jit(solution)/shard_map/pallas_call | solution.py:141
  168.8 28.0 %shard_map.65 = bf16[8,64,1024]{2,1,0:T(8,128)(2,1)} custom-call(s32[24]{0:T(128)} %multiply_add_fusion.ids_ref, s32[8,1,192]{2,1,0:T(1,128)} %get-tuple-element.26.mask_ref, bf16[8,64,1024]{2,1,0:T(8,128)(2,1)} %bitcast.73, bf16[32,64,1024]{2,1,0:T(8,128)(2,1)} %bitcast.22.refs_0_.refs_1_.refs_2_.refs_3_.refs_4_.refs_5_, ...), custom_call_target="tpu_custom_call" | custom-call | flops 7247757312 | bytes 15728640 | tf_op jit(solution)/shard_map/pallas_call | solution.py:185
  196.8 3.5 %add_convert_fusion = bf16[512,1024]{1,0:T(8,128)(2,1)} fusion(bf16[512,1024]{1,0:T(8,128)(2,1)S(1)} %copy-done.2, bf16[512,1024]{1,0:T(8,128)(2,1)} %bitcast.75, bf16[1024,1024]{1,0:T(8,128)(2,1)S(1)} %copy-done), kind=kOutput, calls=%fused_computation.6 | convolution fusion | flops 1075314688 | bytes 5242880 | tf_op jit(solution)/shard_map/dot_general | solution.py:275
  (101 shorter events, 14.3 us)
Async XLA Ops:
  0.0 196.8 %copy-start = (bf16[1024,1024]{1,0:T(8,128)(2,1)S(1)}, bf16[1024,1024]{1,0:T(8,128)(2,1)}, u32[]{:S(2)}) copy-start(bf16[1024,1024]{1,0:T(8,128)(2,1)} %param.10) | copy-start | bytes 6291460
  0.0 7.6 %copy-start.2 = (bf16[512,1024]{1,0:T(8,128)(2,1)S(1)}, bf16[512,1024]{1,0:T(8,128)(2,1)}, u32[]{:S(2)}) copy-start(bf16[512,1024]{1,0:T(8,128)(2,1)} %param.8) | copy-start | bytes 3145732
  3.1 7.4 %collective-permute-start.2 = (bf16[8,1024]{1,0:T(8,128)(2,1)S(1)}, bf16[8,1024]{1,0:T(8,128)(2,1)S(1)}, u32[]{:S(2)}, u32[]{:S(2)}) collective-permute-start(bf16[8,1024]{1,0:T(8,128)(2,1)S(1)} %divide_convert_fusion), channel_id=1, source_target_pairs={{0,3},{1,0},{2,1},{3,2},{4,7},{5,4},{6,5},{7,6},{8,11},{9,8},{10,9... | collective-permute-start | bytes 49160 | tf_op jit(solution)/shard_map/ppermute | solution.py:35
  4.0 6.4 %collective-permute-start.1 = (bf16[8,1024]{1,0:T(8,128)(2,1)S(1)}, bf16[8,1024]{1,0:T(8,128)(2,1)S(1)}, u32[]{:S(2)}, u32[]{:S(2)}) collective-permute-start(bf16[8,1024]{1,0:T(8,128)(2,1)S(1)} %divide_convert_fusion), channel_id=1, source_target_pairs={{0,2},{1,3},{2,0},{3,1},{4,6},{5,7},{6,4},{7,5},{8,10},{9,11},{10,... | collective-permute-start | bytes 49160 | tf_op jit(solution)/shard_map/ppermute | solution.py:35
  4.7 5.8 %collective-permute-start = (bf16[8,1024]{1,0:T(8,128)(2,1)S(1)}, bf16[8,1024]{1,0:T(8,128)(2,1)S(1)}, u32[]{:S(2)}, u32[]{:S(2)}) collective-permute-start(bf16[8,1024]{1,0:T(8,128)(2,1)S(1)} %divide_convert_fusion), channel_id=1, source_target_pairs={{0,1},{1,2},{2,3},{3,0},{4,5},{5,6},{6,7},{7,4},{8,9},{9,10},{10,1... | collective-permute-start | bytes 49160 | tf_op jit(solution)/shard_map/ppermute | solution.py:35
  4.8 1.5 copy-start.10
  4.9 1.4 copy-start.12
  10.4 0.6 copy-start.7
  10.5 0.6 copy-start.8
  12.4 27.2 %collective-permute-start.9 = (bf16[32,1024]{1,0:T(8,128)(2,1)S(1)}, bf16[32,1024]{1,0:T(8,128)(2,1)S(1)}, u32[]{:S(2)}, u32[]{:S(2)}) collective-permute-start(bf16[32,1024]{1,0:T(8,128)(2,1)S(1)} %bitcast.78), channel_id=1, source_target_pairs={{0,28},{4,0},{8,4},{12,8},{16,12},{20,16},{24,20},{28,24},{1,29},{... | collective-permute-start | bytes 196616 | tf_op jit(solution)/shard_map/ppermute | solution.py:35
  13.8 25.1 %collective-permute-start.8 = (bf16[32,1024]{1,0:T(8,128)(2,1)S(1)}, bf16[32,1024]{1,0:T(8,128)(2,1)S(1)}, u32[]{:S(2)}, u32[]{:S(2)}) collective-permute-start(bf16[32,1024]{1,0:T(8,128)(2,1)S(1)} %bitcast.79), channel_id=1, source_target_pairs={{0,24},{4,28},{8,0},{12,4},{16,8},{20,12},{24,16},{28,20},{1,25},{... | collective-permute-start | bytes 196616 | tf_op jit(solution)/shard_map/ppermute | solution.py:35
  14.3 24.0 %collective-permute-start.7 = (bf16[32,1024]{1,0:T(8,128)(2,1)S(1)}, bf16[32,1024]{1,0:T(8,128)(2,1)S(1)}, u32[]{:S(2)}, u32[]{:S(2)}) collective-permute-start(bf16[32,1024]{1,0:T(8,128)(2,1)S(1)} %bitcast.80), channel_id=1, source_target_pairs={{0,20},{4,24},{8,28},{12,0},{16,4},{20,8},{24,12},{28,16},{1,21},{... | collective-permute-start | bytes 196616 | tf_op jit(solution)/shard_map/ppermute | solution.py:35
  17.8 19.8 %collective-permute-start.6 = (bf16[32,1024]{1,0:T(8,128)(2,1)S(1)}, bf16[32,1024]{1,0:T(8,128)(2,1)S(1)}, u32[]{:S(2)}, u32[]{:S(2)}) collective-permute-start(bf16[32,1024]{1,0:T(8,128)(2,1)S(1)} %bitcast.81), channel_id=1, source_target_pairs={{0,16},{4,20},{8,24},{12,28},{16,0},{20,4},{24,8},{28,12},{1,17},{... | collective-permute-start | bytes 196616 | tf_op jit(solution)/shard_map/ppermute | solution.py:35
  17.8 8.6 %collective-permute-start.3 = (bf16[32,1024]{1,0:T(8,128)(2,1)S(1)}, bf16[32,1024]{1,0:T(8,128)(2,1)S(1)}, u32[]{:S(2)}, u32[]{:S(2)}) collective-permute-start(bf16[32,1024]{1,0:T(8,128)(2,1)S(1)} %bitcast.82), channel_id=1, source_target_pairs={{0,4},{4,8},{8,12},{12,16},{16,20},{20,24},{24,28},{28,0},{1,5},{5... | collective-permute-start | bytes 196616 | tf_op jit(solution)/shard_map/ppermute | solution.py:35
  26.4 4.6 %collective-permute-start.4 = (bf16[32,1024]{1,0:T(8,128)(2,1)S(1)}, bf16[32,1024]{1,0:T(8,128)(2,1)S(1)}, u32[]{:S(2)}, u32[]{:S(2)}) collective-permute-start(bf16[32,1024]{1,0:T(8,128)(2,1)S(1)} %bitcast.83), channel_id=1, source_target_pairs={{0,8},{4,12},{8,16},{12,20},{16,24},{20,28},{24,0},{28,4},{1,9},{5... | collective-permute-start | bytes 196616 | tf_op jit(solution)/shard_map/ppermute | solution.py:35
  31.0 6.1 %collective-permute-start.5 = (bf16[32,1024]{1,0:T(8,128)(2,1)S(1)}, bf16[32,1024]{1,0:T(8,128)(2,1)S(1)}, u32[]{:S(2)}, u32[]{:S(2)}) collective-permute-start(bf16[32,1024]{1,0:T(8,128)(2,1)S(1)} %bitcast.84), channel_id=1, source_target_pairs={{0,12},{4,16},{8,20},{12,24},{16,28},{20,0},{24,4},{28,8},{1,13},{... | collective-permute-start | bytes 196616 | tf_op jit(solution)/shard_map/ppermute | solution.py:35
  42.6 126.2 %all-to-all-start = ((bf16[8,4,64,1024]{3,2,1,0:T(8,128)(2,1)}), bf16[8,4,64,1024]{3,2,1,0:T(8,128)(2,1)}, u32[]{:S(2)}, u32[]{:S(2)}) async-start(bf16[8,4,64,1024]{3,2,1,0:T(8,128)(2,1)} %bitcast.59), calls=%async_computation | async-start | bytes 8388608 | tf_op jit(solution)/shard_map/all_to_all | solution.py:238
  50.0 6.1 %copy-start.1 = (s32[256]{0:T(256)S(1)}, s32[256]{0:T(256)}, u32[]{:S(2)}) copy-start(s32[256]{0:T(256)} %param.11) | copy-start | bytes 3076
  50.7 90.7 %collective-permute-start.11 = (bf16[64,1024]{1,0:T(8,128)(2,1)}, bf16[64,1024]{1,0:T(8,128)(2,1)S(1)}, u32[]{:S(2)}, u32[]{:S(2)}) collective-permute-start(bf16[64,1024]{1,0:T(8,128)(2,1)} %get-tuple-element.21), channel_id=1, source_target_pairs={{1,0},{2,1},{3,2},{4,3},{5,4},{6,5},{7,6},{8,7},{9,8},{10,9},{11,1... | collective-permute-start | bytes 393224 | tf_op jit(solution)/shard_map/ppermute | solution.py:224
  52.6 87.8 %collective-permute-start.10 = (bf16[64,1024]{1,0:T(8,128)(2,1)}, bf16[64,1024]{1,0:T(8,128)(2,1)}, u32[]{:S(2)}, u32[]{:S(2)}) collective-permute-start(bf16[64,1024]{1,0:T(8,128)(2,1)} %get-tuple-element.22), channel_id=1, source_target_pairs={{0,1},{1,2},{2,3},{3,4},{4,5},{5,6},{6,7},{7,8},{8,9},{9,10},{10,1... | collective-permute-start | bytes 393224 | tf_op jit(solution)/shard_map/ppermute | solution.py:223
  56.8 0.8 copy-start.11
  56.8 0.8 copy-start.13
  76.5 4.7 %copy-start.9 = (s32[192]{0:T(256)S(1)}, s32[192]{0:T(256)}, u32[]{:S(2)}) copy-start(s32[192]{0:T(256)} %lt.99) | copy-start | bytes 2308
  81.9 4.8 %copy-start.5 = (bf16[1024,16,1,64]{0,3,2,1:T(8,128)(2,1)S(1)}, bf16[1024,16,1,64]{0,3,2,1:T(8,128)(2,1)}, u32[]{:S(2)}) copy-start(bf16[1024,16,1,64]{0,3,2,1:T(8,128)(2,1)} %get-tuple-element.20) | copy-start | bytes 6291460
  86.7 2.3 %copy-start.4 = (bf16[1024,16,1,64]{0,3,2,1:T(8,128)(2,1)S(1)}, bf16[1024,16,1,64]{0,3,2,1:T(8,128)(2,1)}, u32[]{:S(2)}) copy-start(bf16[1024,16,1,64]{0,3,2,1:T(8,128)(2,1)} %get-tuple-element.19) | copy-start | bytes 6291460
  86.8 2.3 %copy-start.6 = (bf16[8,32,1024]{2,1,0:T(8,128)(2,1)S(1)}, bf16[8,32,1024]{2,1,0:T(8,128)(2,1)}, u32[]{:S(2)}) copy-start(bf16[8,32,1024]{2,1,0:T(8,128)(2,1)} %gather_fusion.1) | copy-start | bytes 1572868
  89.0 1.6 copy-start.3

commit v11 on v7

--- a/solution.py
+++ b/solution.py
@@ -149,7 +149,7 @@
 def attend_far(slot_ids, mask, q, incoming, w_kv, o_a, m_a, l_a):
     blocks, rows, width = q.shape
     model_dim = incoming.shape[-1]
-    group = 2 if blocks % 2 == 0 else 1
+    group = 4 if blocks % 4 == 0 else 1
     block = pl.BlockSpec((group, rows, width), lambda i, ids: (i, 0, 0))
     token_specs = [
         pl.BlockSpec(

time: 191 us -> 192 us (level)
  no operation moved by 1% of the time
where the time goes in v11:
time: 192 us; the launch traced here: 191 us
  waiting for transfers between devices  63.4 us (33%)
  Pallas kernels  51.1 us (27%)
  local copies, waits for them, and re-layouts  32.6 us (17%)
  starting transfers between devices  18.4 us (10%)
  matrix products  16.2 us (8%)
  other arithmetic  8.94 us (5%)
    ppermute x1, waiting for transfers between devices, local(): lax.ppermute(token_blocks[dev_blocks - 1], ('ctx', 'seq'), forward)  54.7 us
    pallas_call x1, Pallas kernels, attend_far(): pl.pallas_call(functools.partial(far_kernel, group), grid_spec=grid_spec,...  28.9 us
    pallas_call x1, Pallas kernels, attend_near(): pl.pallas_call(near_kernel, grid=(blocks,), in_specs=[pl.BlockSpec((1, 1,...  22.2 us
    dot_general x5, matrix products, local(): jnp.dot(x, w, preferred_element_type=jnp.float32).astype(jnp.bfloat16)  12.7 us
    unnamed x31, local copies, waits for them, and re-layouts  10.3 us
    all_to_all x1, waiting for transfers between devices, local(): lax.all_to_all(copies, ('ctx', 'seq'), 0, 0, tiled=True)  8.71 us
    another operation x2, local copies, waits for them, and re-layouts, split_weights(): shaped[:, :, j, :].reshape(model_dim, head_total * HD)  7.86 us
    all_to_all x1, starting transfers between devices, local(): lax.all_to_all(outgoing, 'ctx', split_axis=0, concat_axis=0, tiled=True)  7 us
  transfers between devices with their start and end apart: 4, of which 2 were waited for; matrix products, arithmetic and copies ran while one was open for 26% of the time, Pallas kernels for 12%

profile of v11, /device:TPU:16, one launch (start us, length us, event | category | flops | bytes accessed | tf_op | source)
XLA Modules:
  0.0 190.8 jit_solution(11179110203312456943)
XLA Ops:
  0.0 0.9 dynamic_slice.18
  1.2 1.6 select_reduce_fusion
  2.8 0.2 multiply_reduce_fusion
  3.1 0.9 broadcast_in_dim.39
  4.0 6.0 %all-to-all-start = ((bf16[32,8,1024]{2,1,0:T(8,128)(2,1)}), bf16[32,8,1024]{2,1,0:T(8,128)(2,1)}, u32[]{:S(2)}, u32[]{:S(2)}) async-start(bf16[32,8,1024]{2,1,0:T(8,128)(2,1)} %broadcast_in_dim.39), calls=%async_computation | async-start | bytes 1048576 | tf_op jit(solution)/shard_map/all_to_all | solution.py:229
  10.2 0.4 copy-done.9
  11.7 2.9 %gather_fusion = bf16[32,64,1024]{2,1,0:T(8,128)(2,1)} fusion(bf16[8,64,1024]{2,1,0:T(8,128)(2,1)S(1)} %bitcast.29, s32[1024]{0:T(1024)S(1)} %get-tuple-element.28), kind=kCustom, calls=%fused_computation.2 | custom fusion | bytes 8388736 | tf_op jit(solution)/shard_map/jit(_take)/gather | solution.py:210
  14.6 8.7 %all-to-all-done = bf16[32,8,1024]{2,1,0:T(8,128)(2,1)} async-done(((bf16[32,8,1024]{2,1,0:T(8,128)(2,1)}), bf16[32,8,1024]{2,1,0:T(8,128)(2,1)}, u32[]{:S(2)}, u32[]{:S(2)}) %all-to-all-start) | async-done | bytes 524320 | tf_op jit(solution)/shard_map/all_to_all | solution.py:229
  23.3 7.0 %all-to-all-start.1 = ((bf16[8,4,64,1024]{3,2,1,0:T(8,128)(2,1)}), bf16[8,4,64,1024]{3,2,1,0:T(8,128)(2,1)}, u32[]{:S(2)}, u32[]{:S(2)}) async-start(bf16[8,4,64,1024]{3,2,1,0:T(8,128)(2,1)} %bitcast.31), calls=%async_computation.1 | async-start | bytes 8388608 | tf_op jit(solution)/shard_map/all_to_all | solution.py:231
  30.3 0.7 fusion.5
  31.0 3.5 %collective-permute-start.1 = (bf16[64,1024]{1,0:T(8,128)(2,1)}, bf16[64,1024]{1,0:T(8,128)(2,1)S(1)}, u32[]{:S(2)}, u32[]{:S(2)}) collective-permute-start(bf16[64,1024]{1,0:T(8,128)(2,1)} %get-tuple-element.21), channel_id=1, source_target_pairs={{1,0},{2,1},{3,2},{4,3},{5,4},{6,5},{7,6},{8,7},{9,8},{10,9},{11,1... | collective-permute-start | bytes 393224 | tf_op jit(solution)/shard_map/ppermute | solution.py:216
  34.5 1.9 %collective-permute-start = (bf16[64,1024]{1,0:T(8,128)(2,1)}, bf16[64,1024]{1,0:T(8,128)(2,1)}, u32[]{:S(2)}, u32[]{:S(2)}) collective-permute-start(bf16[64,1024]{1,0:T(8,128)(2,1)} %get-tuple-element.22), channel_id=1, source_target_pairs={{0,1},{1,2},{2,3},{3,4},{4,5},{5,6},{6,7},{7,8},{8,9},{9,10},{10,1... | collective-permute-start | bytes 393224 | tf_op jit(solution)/shard_map/ppermute | solution.py:215
  36.4 0.6 lt.87
  37.2 0.7 gather_fusion.1
  38.0 0.7 gather_fusion.2
  39.4 8.6 %copy.43 = bf16[1024,3072]{0,1:T(8,128)(2,1)} copy(bf16[1024,3072]{1,0:T(8,128)(2,1)} %param.9) | data formatting | bytes 12582912 | tf_op args[1]
  48.0 5.8 %fusion.4 = (bf16[1024,16,1,64]{0,3,2,1:T(8,128)(2,1)}, bf16[1024,16,1,64]{0,3,2,1:T(8,128)(2,1)}, bf16[1024,16,1,64]{0,3,2,1:T(8,128)(2,1)}) fusion(bf16[1024,16,3,64]{0,3,2,1:T(8,128)(2,1)} %bitcast.30), kind=kLoop, calls=%fused_computation.47 | loop fusion | bytes 12582912 | tf_op jit(solution)/shard_map/slice | solution.py:35
  53.8 3.9 %copy.48 = bf16[1024,1024]{1,0:T(8,128)(2,1)} copy(bf16[1024,1024]{0,1:T(8,128)(2,1)} %bitcast.41) | data formatting | bytes 4194304 | tf_op jit(solution)/shard_map/reshape;squeeze | solution.py:35
  57.7 3.9 %copy.47 = bf16[1024,1024]{1,0:T(8,128)(2,1)} copy(bf16[1024,1024]{0,1:T(8,128)(2,1)} %bitcast.38) | data formatting | bytes 4194304 | tf_op jit(solution)/shard_map/reshape;squeeze | solution.py:35
  61.8 0.6 compare_convert_fusion
  62.4 4.8 %pad_maximum_fusion.refs_12_ = bf16[1024,2048]{1,0:T(8,128)(2,1)} fusion(bf16[1024,1024]{1,0:T(8,128)(2,1)} %copy.48, bf16[1024,1024]{1,0:T(8,128)(2,1)} %copy.47), kind=kLoop, calls=%fused_computation.3 | loop fusion | flops 8388608 | bytes 8388608 | tf_op jit(solution)/shard_map/concatenate | solution.py:263
  67.3 2.3 %convolution_convert_fusion.2 = bf16[512,1024]{1,0:T(8,128)(2,1)} fusion(bf16[512,1024]{1,0:T(8,128)(2,1)S(1)} %copy-done.2, bf16[1024,1024]{0,1:T(8,128)(2,1)S(1)} %bitcast.46), kind=kOutput, calls=%fused_computation.8 | convolution fusion | flops 1074266112 | bytes 4194304 | tf_op jit(solution)/shard_map/dot_general | solution.py:234
  69.5 0.5 multiply_add_fusion.ids_ref
  70.0 54.7 %collective-permute-done = bf16[64,1024]{1,0:T(8,128)(2,1)} collective-permute-done((bf16[64,1024]{1,0:T(8,128)(2,1)}, bf16[64,1024]{1,0:T(8,128)(2,1)}, u32[]{:S(2)}, u32[]{:S(2)}) %collective-permute-start) | collective-permute-done | bytes 131104 | tf_op jit(solution)/shard_map/ppermute | solution.py:215
  124.7 0.9 constant_dynamic-update-slice_fusion.2
  125.8 2.6 %convolution_convert_fusion = bf16[640,1024]{1,0:T(8,128)(2,1)} fusion(bf16[640,1024]{1,0:T(8,128)(2,1)S(1)} %constant_dynamic-update-slice_fusion, bf16[1024,1024]{0,1:T(8,128)(2,1)S(1)} %bitcast.42), kind=kOutput, calls=%fused_computation.6 | convolution fusion | flops 1342832640 | bytes 4718592 | tf_op jit(solution)/shard_map/dot_general | solution.py:234
  128.4 2.6 %convolution_convert_fusion.1 = bf16[640,1024]{1,0:T(8,128)(2,1)} fusion(bf16[640,1024]{1,0:T(8,128)(2,1)S(1)} %constant_dynamic-update-slice_fusion, bf16[1024,1024]{0,1:T(8,128)(2,1)S(1)} %bitcast.39), kind=kOutput, calls=%fused_computation.7 | convolution fusion | flops 1342832640 | bytes 4718592 | tf_op jit(solution)/shard_map/dot_general | solution.py:234
  131.0 2.6 %convolution_convert_fusion.3.vs_ref = bf16[256,1024]{1,0:T(8,128)(2,1)} fusion(bf16[256,1024]{1,0:T(8,128)(2,1)} %bitcast.4, bf16[1024,1024]{0,1:T(8,128)(2,1)S(1)} %bitcast.43), kind=kOutput, calls=%fused_computation.9 | convolution fusion | flops 537133056 | bytes 3145728 | tf_op jit(solution)/shard_map/dot_general | solution.py:234
  133.6 2.6 %convolution_convert_fusion.4.ks_ref = bf16[256,1024]{1,0:T(8,128)(2,1)} fusion(bf16[256,1024]{1,0:T(8,128)(2,1)} %bitcast.4, bf16[1024,1024]{0,1:T(8,128)(2,1)S(1)} %bitcast.40), kind=kOutput, calls=%fused_computation.10 | convolution fusion | flops 537133056 | bytes 3145728 | tf_op jit(solution)/shard_map/dot_general | solution.py:234
  136.2 22.2 %shard_map.64 = (f32[8,64,1024]{2,1,0:T(8,128)}, f32[8,64,1024]{2,1,0:T(8,128)}, f32[8,64,1024]{2,1,0:T(8,128)}) custom-call(s32[8,1,192]{2,1,0:T(1,128)} %get-tuple-element.25.mask_ref, bf16[8,64,1024]{2,1,0:T(8,128)(2,1)} %bitcast.44, bf16[10,64,1024]{2,1,0:T(8,128)(2,1)} %bitcast.35, bf16[10,64,1024]{2,1,0:T(8,128)(2,1)} %bitcast.36, ...), custom_call_target="tpu_custom_call" | custom-call | flops 1879048192 | bytes 14680064 | tf_op jit(solution)/shard_map/pallas_call | solution.py:133
  158.4 28.9 %shard_map.65 = bf16[8,64,1024]{2,1,0:T(8,128)(2,1)} custom-call(s32[24]{0:T(128)} %multiply_add_fusion.ids_ref, s32[8,1,192]{2,1,0:T(1,128)} %get-tuple-element.26.mask_ref, bf16[8,64,1024]{2,1,0:T(8,128)(2,1)} %bitcast.45, bf16[32,64,1024]{2,1,0:T(8,128)(2,1)} %bitcast.7.refs_0_.refs_1_.refs_2_.refs_3_.refs_4_.refs_5_.refs_6_.refs_7_.refs_8_.refs_9_.refs_10_.refs_11_, ...), custom_call_target="tpu_custom_call" | custom-call | flops 7247757312 | bytes 15728640 | tf_op jit(solution)/shard_map/pallas_call | solution.py:177
  187.4 3.5 %add_convert_fusion = bf16[512,1024]{1,0:T(8,128)(2,1)} fusion(bf16[512,1024]{1,0:T(8,128)(2,1)S(1)} %copy-done.2, bf16[512,1024]{1,0:T(8,128)(2,1)} %bitcast.47, bf16[1024,1024]{1,0:T(8,128)(2,1)S(1)} %copy-done), kind=kOutput, calls=%fused_computation.4 | convolution fusion | flops 1075314688 | bytes 5242880 | tf_op jit(solution)/shard_map/dot_general | solution.py:268
  (66 shorter events, 2.7 us)
Async XLA Ops:
  0.0 187.3 %copy-start = (bf16[1024,1024]{1,0:T(8,128)(2,1)S(1)}, bf16[1024,1024]{1,0:T(8,128)(2,1)}, u32[]{:S(2)}) copy-start(bf16[1024,1024]{1,0:T(8,128)(2,1)} %param.10) | copy-start | bytes 6291460
  0.0 11.7 %copy-start.2 = (bf16[512,1024]{1,0:T(8,128)(2,1)S(1)}, bf16[512,1024]{1,0:T(8,128)(2,1)}, u32[]{:S(2)}) copy-start(bf16[512,1024]{1,0:T(8,128)(2,1)} %param.8) | copy-start | bytes 3145732
  0.0 10.6 %copy-start.6 = (s32[256,3]{0,1:T(4,128)S(1)}, s32[256,3]{0,1:T(4,128)}, u32[]{:S(2)}) copy-start(s32[256,3]{0,1:T(4,128)} %param.12) | copy-start | bytes 9220
  0.0 11.0 %copy-start.7 = (s32[256,3]{0,1:T(4,128)S(1)}, s32[256,3]{0,1:T(4,128)}, u32[]{:S(2)}) copy-start(s32[256,3]{0,1:T(4,128)} %param.13) | copy-start | bytes 9220
  4.0 19.3 %all-to-all-start = ((bf16[32,8,1024]{2,1,0:T(8,128)(2,1)}), bf16[32,8,1024]{2,1,0:T(8,128)(2,1)}, u32[]{:S(2)}, u32[]{:S(2)}) async-start(bf16[32,8,1024]{2,1,0:T(8,128)(2,1)} %broadcast_in_dim.39), calls=%async_computation | async-start | bytes 1048576 | tf_op jit(solution)/shard_map/all_to_all | solution.py:229
  10.0 0.6 copy-start.9
  10.0 0.6 copy-start.11
  23.3 135.1 %all-to-all-start.1 = ((bf16[8,4,64,1024]{3,2,1,0:T(8,128)(2,1)}), bf16[8,4,64,1024]{3,2,1,0:T(8,128)(2,1)}, u32[]{:S(2)}, u32[]{:S(2)}) async-start(bf16[8,4,64,1024]{3,2,1,0:T(8,128)(2,1)} %bitcast.31), calls=%async_computation.1 | async-start | bytes 8388608 | tf_op jit(solution)/shard_map/all_to_all | solution.py:231
  30.3 6.9 %copy-start.1 = (s32[256]{0:T(256)S(1)}, s32[256]{0:T(256)}, u32[]{:S(2)}) copy-start(s32[256]{0:T(256)} %param.11) | copy-start | bytes 3076
  31.0 94.7 %collective-permute-start.1 = (bf16[64,1024]{1,0:T(8,128)(2,1)}, bf16[64,1024]{1,0:T(8,128)(2,1)S(1)}, u32[]{:S(2)}, u32[]{:S(2)}) collective-permute-start(bf16[64,1024]{1,0:T(8,128)(2,1)} %get-tuple-element.21), channel_id=1, source_target_pairs={{1,0},{2,1},{3,2},{4,3},{5,4},{6,5},{7,6},{8,7},{9,8},{10,9},{11,1... | collective-permute-start | bytes 393224 | tf_op jit(solution)/shard_map/ppermute | solution.py:216
  34.5 90.2 %collective-permute-start = (bf16[64,1024]{1,0:T(8,128)(2,1)}, bf16[64,1024]{1,0:T(8,128)(2,1)}, u32[]{:S(2)}, u32[]{:S(2)}) collective-permute-start(bf16[64,1024]{1,0:T(8,128)(2,1)} %get-tuple-element.22), channel_id=1, source_target_pairs={{0,1},{1,2},{2,3},{3,4},{4,5},{5,6},{6,7},{7,8},{8,9},{9,10},{10,1... | collective-permute-start | bytes 393224 | tf_op jit(solution)/shard_map/ppermute | solution.py:215
  38.0 0.8 copy-start.10
  38.0 0.8 copy-start.12
  57.7 4.1 %copy-start.8 = (s32[192]{0:T(256)S(1)}, s32[192]{0:T(256)}, u32[]{:S(2)}) copy-start(s32[192]{0:T(256)} %lt.87) | copy-start | bytes 2308
  62.4 4.8 %copy-start.5 = (bf16[1024,16,1,64]{0,3,2,1:T(8,128)(2,1)S(1)}, bf16[1024,16,1,64]{0,3,2,1:T(8,128)(2,1)}, u32[]{:S(2)}) copy-start(bf16[1024,16,1,64]{0,3,2,1:T(8,128)(2,1)} %get-tuple-element.20) | copy-start | bytes 6291460
  69.5 56.2 %copy-start.4 = (bf16[1024,16,1,64]{0,3,2,1:T(8,128)(2,1)S(1)}, bf16[1024,16,1,64]{0,3,2,1:T(8,128)(2,1)}, u32[]{:S(2)}) copy-start(bf16[1024,16,1,64]{0,3,2,1:T(8,128)(2,1)} %get-tuple-element.19) | copy-start | bytes 6291460
  125.8 2.6 %copy-start.3 = (bf16[1024,16,1,64]{0,3,2,1:T(8,128)(2,1)S(1)}, bf16[1024,16,1,64]{0,3,2,1:T(8,128)(2,1)}, u32[]{:S(2)}) copy-start(bf16[1024,16,1,64]{0,3,2,1:T(8,128)(2,1)} %get-tuple-element.18) | copy-start | bytes 6291460

commit v12 on v7

--- a/solution.py
+++ b/solution.py
@@ -225,8 +225,10 @@
     summary = (pooled / jnp.sqrt(jnp.mean(pooled * pooled, axis=1, keepdims=True) + 1e-05)).astype(
         jnp.bfloat16
     )
-    copies = jnp.broadcast_to(summary[None], (dev_count,) + summary.shape)
-    summary_all = lax.all_to_all(copies, ("ctx", "seq"), 0, 0, tiled=True).reshape(-1, model_dim)
+    summary_all = summary
+    for axis, count in (("seq", seq_count), ("ctx", ctx_count)):
+        copies = jnp.broadcast_to(summary_all[None], (count,) + summary_all.shape)
+        summary_all = lax.all_to_all(copies, axis, 0, 0, tiled=True).reshape(-1, model_dim)
     summary_all, outgoing = lax.optimization_barrier((summary_all, outgoing))
     incoming = lax.all_to_all(outgoing, "ctx", split_axis=0, concat_axis=0, tiled=True)
 

time: 191 us -> 195 us (1.021)
  starting transfers between devices: 18.4 us -> 20.9 us
    all_to_all x1 -> x2, starting transfers between devices: 5.99 us -> 9.45 us  [local(): lax.all_to_all(copies, axis, 0, 0, tiled=True).reshape(-1, model_dim)]
    all_to_all x1 -> x2, waiting for transfers between devices: 8.71 us -> 11.6 us  [local(): lax.all_to_all(copies, axis, 0, 0, tiled=True).reshape(-1, model_dim)]
  transfers between devices with their start and end apart: 4 -> 5, of which waited for: 2 -> 3; matrix products, arithmetic and copies ran while one was open for 26% -> 26% of each run, Pallas kernels for 12% -> 11%
where the time goes in v12:
time: 195 us; the launch traced here: 194 us
  waiting for transfers between devices  65 us (33%)
  Pallas kernels  50.2 us (26%)
  local copies, waits for them, and re-layouts  32.8 us (17%)
  starting transfers between devices  20.9 us (11%)
  matrix products  16.1 us (8%)
  other arithmetic  8.96 us (5%)
    ppermute x1, waiting for transfers between devices, local(): lax.ppermute(token_blocks[dev_blocks - 1], ('ctx', 'seq'), forward)  53.4 us
    pallas_call x1, Pallas kernels, attend_far(): pl.pallas_call(functools.partial(far_kernel, group), grid_spec=grid_spec,...  28 us
    pallas_call x1, Pallas kernels, attend_near(): pl.pallas_call(near_kernel, grid=(blocks,), in_specs=[pl.BlockSpec((1, 1,...  22.2 us
    dot_general x5, matrix products, local(): jnp.dot(x, w, preferred_element_type=jnp.float32).astype(jnp.bfloat16)  12.7 us
    all_to_all x2, waiting for transfers between devices, local(): lax.all_to_all(copies, axis, 0, 0, tiled=True).reshape(-1, model_dim)  11.6 us
    unnamed x31, local copies, waits for them, and re-layouts  9.93 us
    all_to_all x2, starting transfers between devices, local(): lax.all_to_all(copies, axis, 0, 0, tiled=True).reshape(-1, model_dim)  9.45 us
    another operation x2, local copies, waits for them, and re-layouts, split_weights(): shaped[:, :, j, :].reshape(model_dim, head_total * HD)  7.87 us
  transfers between devices with their start and end apart: 5, of which 3 were waited for; matrix products, arithmetic and copies ran while one was open for 26% of the time, Pallas kernels for 11%

profile of v12, /device:TPU:16, one launch (start us, length us, event | category | flops | bytes accessed | tf_op | source)
XLA Modules:
  0.0 194.3 jit_solution(13757762807411526133)
XLA Ops:
  0.0 0.9 dynamic_slice.18
  1.2 1.6 select_reduce_fusion
  3.1 0.7 broadcast_in_dim.64
  3.8 3.3 %all-to-all-start = ((bf16[4,8,1024]{2,1,0:T(8,128)(2,1)}), bf16[4,8,1024]{2,1,0:T(8,128)(2,1)S(1)}, u32[]{:S(2)}, u32[]{:S(2)}) async-start(bf16[4,8,1024]{2,1,0:T(8,128)(2,1)} %broadcast_in_dim.64), calls=%async_computation | async-start | bytes 131072 | tf_op jit(solution)/shard_map/all_to_all | solution.py:231
  7.1 4.0 %all-to-all-done = bf16[4,8,1024]{2,1,0:T(8,128)(2,1)S(1)} async-done(((bf16[4,8,1024]{2,1,0:T(8,128)(2,1)}), bf16[4,8,1024]{2,1,0:T(8,128)(2,1)S(1)}, u32[]{:S(2)}, u32[]{:S(2)}) %all-to-all-start) | async-done | bytes 65568 | tf_op jit(solution)/shard_map/all_to_all | solution.py:231
  11.1 0.9 broadcast_in_dim.66
  12.0 6.2 %all-to-all-start.1 = ((bf16[8,32,1024]{2,1,0:T(8,128)(2,1)}), bf16[8,32,1024]{2,1,0:T(8,128)(2,1)}, u32[]{:S(2)}, u32[]{:S(2)}) async-start(bf16[8,32,1024]{2,1,0:T(8,128)(2,1)} %broadcast_in_dim.66), calls=%async_computation.1 | async-start | bytes 1048576 | tf_op jit(solution)/shard_map/all_to_all | solution.py:231
  19.4 2.9 %gather_fusion = bf16[32,64,1024]{2,1,0:T(8,128)(2,1)} fusion(bf16[8,64,1024]{2,1,0:T(8,128)(2,1)S(1)} %bitcast.30, s32[1024]{0:T(1024)S(1)} %get-tuple-element.28), kind=kCustom, calls=%fused_computation.2 | custom fusion | bytes 8388736 | tf_op jit(solution)/shard_map/jit(_take)/gather | solution.py:210
  22.3 7.6 %all-to-all-done.1 = bf16[8,32,1024]{2,1,0:T(8,128)(2,1)} async-done(((bf16[8,32,1024]{2,1,0:T(8,128)(2,1)}), bf16[8,32,1024]{2,1,0:T(8,128)(2,1)}, u32[]{:S(2)}, u32[]{:S(2)}) %all-to-all-start.1) | async-done | bytes 524320 | tf_op jit(solution)/shard_map/all_to_all | solution.py:231
  29.9 7.2 %all-to-all-start.2 = ((bf16[8,4,64,1024]{3,2,1,0:T(8,128)(2,1)}), bf16[8,4,64,1024]{3,2,1,0:T(8,128)(2,1)}, u32[]{:S(2)}, u32[]{:S(2)}) async-start(bf16[8,4,64,1024]{3,2,1,0:T(8,128)(2,1)} %bitcast.32), calls=%async_computation.2 | async-start | bytes 8388608 | tf_op jit(solution)/shard_map/all_to_all | solution.py:233
  37.1 0.7 fusion.5
  37.8 1.9 collective-permute-start.1
  39.7 2.4 %collective-permute-start = (bf16[64,1024]{1,0:T(8,128)(2,1)}, bf16[64,1024]{1,0:T(8,128)(2,1)}, u32[]{:S(2)}, u32[]{:S(2)}) collective-permute-start(bf16[64,1024]{1,0:T(8,128)(2,1)} %get-tuple-element.22), channel_id=1, source_target_pairs={{0,1},{1,2},{2,3},{3,4},{4,5},{5,6},{6,7},{7,8},{8,9},{9,10},{10,1... | collective-permute-start | bytes 393224 | tf_op jit(solution)/shard_map/ppermute | solution.py:215
  42.1 0.6 lt.87
  42.9 0.7 gather_fusion.1
  43.7 0.7 gather_fusion.2
  45.1 8.6 %copy.43 = bf16[1024,3072]{0,1:T(8,128)(2,1)} copy(bf16[1024,3072]{1,0:T(8,128)(2,1)} %param.9) | data formatting | bytes 12582912 | tf_op args[1]
  53.7 5.8 %fusion.4 = (bf16[1024,16,1,64]{0,3,2,1:T(8,128)(2,1)}, bf16[1024,16,1,64]{0,3,2,1:T(8,128)(2,1)}, bf16[1024,16,1,64]{0,3,2,1:T(8,128)(2,1)}) fusion(bf16[1024,16,3,64]{0,3,2,1:T(8,128)(2,1)} %bitcast.31), kind=kLoop, calls=%fused_computation.47 | loop fusion | bytes 12582912 | tf_op jit(solution)/shard_map/slice | solution.py:35
  59.5 3.9 %copy.48 = bf16[1024,1024]{1,0:T(8,128)(2,1)} copy(bf16[1024,1024]{0,1:T(8,128)(2,1)} %bitcast.42) | data formatting | bytes 4194304 | tf_op jit(solution)/shard_map/reshape;squeeze | solution.py:35
  63.4 3.9 %copy.47 = bf16[1024,1024]{1,0:T(8,128)(2,1)} copy(bf16[1024,1024]{0,1:T(8,128)(2,1)} %bitcast.39) | data formatting | bytes 4194304 | tf_op jit(solution)/shard_map/reshape;squeeze | solution.py:35
  67.5 0.6 compare_convert_fusion
  68.1 4.8 %pad_maximum_fusion.refs_6_ = bf16[1024,2048]{1,0:T(8,128)(2,1)} fusion(bf16[1024,1024]{1,0:T(8,128)(2,1)} %copy.48, bf16[1024,1024]{1,0:T(8,128)(2,1)} %copy.47), kind=kLoop, calls=%fused_computation.3 | loop fusion | flops 8388608 | bytes 8388608 | tf_op jit(solution)/shard_map/concatenate | solution.py:265
  73.0 2.3 %convolution_convert_fusion.2 = bf16[512,1024]{1,0:T(8,128)(2,1)} fusion(bf16[512,1024]{1,0:T(8,128)(2,1)S(1)} %copy-done.2, bf16[1024,1024]{0,1:T(8,128)(2,1)S(1)} %bitcast.47), kind=kOutput, calls=%fused_computation.8 | convolution fusion | flops 1074266112 | bytes 4194304 | tf_op jit(solution)/shard_map/dot_general | solution.py:236
  75.8 53.4 %collective-permute-done = bf16[64,1024]{1,0:T(8,128)(2,1)} collective-permute-done((bf16[64,1024]{1,0:T(8,128)(2,1)}, bf16[64,1024]{1,0:T(8,128)(2,1)}, u32[]{:S(2)}, u32[]{:S(2)}) %collective-permute-start) | collective-permute-done | bytes 131104 | tf_op jit(solution)/shard_map/ppermute | solution.py:215
  129.1 0.9 constant_dynamic-update-slice_fusion.2
  130.2 2.6 %convolution_convert_fusion = bf16[640,1024]{1,0:T(8,128)(2,1)} fusion(bf16[640,1024]{1,0:T(8,128)(2,1)S(1)} %constant_dynamic-update-slice_fusion, bf16[1024,1024]{0,1:T(8,128)(2,1)S(1)} %bitcast.43), kind=kOutput, calls=%fused_computation.6 | convolution fusion | flops 1342832640 | bytes 4718592 | tf_op jit(solution)/shard_map/dot_general | solution.py:236
  132.8 2.6 %convolution_convert_fusion.1 = bf16[640,1024]{1,0:T(8,128)(2,1)} fusion(bf16[640,1024]{1,0:T(8,128)(2,1)S(1)} %constant_dynamic-update-slice_fusion, bf16[1024,1024]{0,1:T(8,128)(2,1)S(1)} %bitcast.40), kind=kOutput, calls=%fused_computation.7 | convolution fusion | flops 1342832640 | bytes 4718592 | tf_op jit(solution)/shard_map/dot_general | solution.py:236
  135.4 2.6 %convolution_convert_fusion.3.vs_ref = bf16[256,1024]{1,0:T(8,128)(2,1)} fusion(bf16[256,1024]{1,0:T(8,128)(2,1)} %bitcast.5, bf16[1024,1024]{0,1:T(8,128)(2,1)S(1)} %bitcast.44), kind=kOutput, calls=%fused_computation.9 | convolution fusion | flops 537133056 | bytes 3145728 | tf_op jit(solution)/shard_map/dot_general | solution.py:236
  138.0 2.6 %convolution_convert_fusion.4.ks_ref = bf16[256,1024]{1,0:T(8,128)(2,1)} fusion(bf16[256,1024]{1,0:T(8,128)(2,1)} %bitcast.5, bf16[1024,1024]{0,1:T(8,128)(2,1)S(1)} %bitcast.41), kind=kOutput, calls=%fused_computation.10 | convolution fusion | flops 537133056 | bytes 3145728 | tf_op jit(solution)/shard_map/dot_general | solution.py:236
  140.6 22.2 %shard_map.64 = (f32[8,64,1024]{2,1,0:T(8,128)}, f32[8,64,1024]{2,1,0:T(8,128)}, f32[8,64,1024]{2,1,0:T(8,128)}) custom-call(s32[8,1,192]{2,1,0:T(1,128)} %get-tuple-element.25.mask_ref, bf16[8,64,1024]{2,1,0:T(8,128)(2,1)} %bitcast.45, bf16[10,64,1024]{2,1,0:T(8,128)(2,1)} %bitcast.36, bf16[10,64,1024]{2,1,0:T(8,128)(2,1)} %bitcast.37, ...), custom_call_target="tpu_custom_call" | custom-call | flops 1879048192 | bytes 14680064 | tf_op jit(solution)/shard_map/pallas_call | solution.py:133
  162.8 28.0 %shard_map.65 = bf16[8,64,1024]{2,1,0:T(8,128)(2,1)} custom-call(s32[24]{0:T(128)} %multiply_add_fusion.ids_ref, s32[8,1,192]{2,1,0:T(1,128)} %get-tuple-element.26.mask_ref, bf16[8,64,1024]{2,1,0:T(8,128)(2,1)} %bitcast.46, bf16[32,64,1024]{2,1,0:T(8,128)(2,1)} %bitcast.8.refs_0_.refs_1_.refs_2_.refs_3_.refs_4_.refs_5_, ...), custom_call_target="tpu_custom_call" | custom-call | flops 7247757312 | bytes 15728640 | tf_op jit(solution)/shard_map/pallas_call | solution.py:177
  190.8 3.4 %add_convert_fusion = bf16[512,1024]{1,0:T(8,128)(2,1)} fusion(bf16[512,1024]{1,0:T(8,128)(2,1)S(1)} %copy-done.2, bf16[512,1024]{1,0:T(8,128)(2,1)} %bitcast.48, bf16[1024,1024]{1,0:T(8,128)(2,1)S(1)} %copy-done), kind=kOutput, calls=%fused_computation.4 | convolution fusion | flops 1075314688 | bytes 5242880 | tf_op jit(solution)/shard_map/dot_general | solution.py:270
  (69 shorter events, 3.4 us)
Async XLA Ops:
  0.0 190.8 %copy-start = (bf16[1024,1024]{1,0:T(8,128)(2,1)S(1)}, bf16[1024,1024]{1,0:T(8,128)(2,1)}, u32[]{:S(2)}) copy-start(bf16[1024,1024]{1,0:T(8,128)(2,1)} %param.10) | copy-start | bytes 6291460
  0.0 19.4 %copy-start.2 = (bf16[512,1024]{1,0:T(8,128)(2,1)S(1)}, bf16[512,1024]{1,0:T(8,128)(2,1)}, u32[]{:S(2)}) copy-start(bf16[512,1024]{1,0:T(8,128)(2,1)} %param.8) | copy-start | bytes 3145732
  0.0 18.3 %copy-start.6 = (s32[256,3]{0,1:T(4,128)S(1)}, s32[256,3]{0,1:T(4,128)}, u32[]{:S(2)}) copy-start(s32[256,3]{0,1:T(4,128)} %param.12) | copy-start | bytes 9220
  0.0 18.8 %copy-start.7 = (s32[256,3]{0,1:T(4,128)S(1)}, s32[256,3]{0,1:T(4,128)}, u32[]{:S(2)}) copy-start(s32[256,3]{0,1:T(4,128)} %param.13) | copy-start | bytes 9220
  3.8 7.4 %all-to-all-start = ((bf16[4,8,1024]{2,1,0:T(8,128)(2,1)}), bf16[4,8,1024]{2,1,0:T(8,128)(2,1)S(1)}, u32[]{:S(2)}, u32[]{:S(2)}) async-start(bf16[4,8,1024]{2,1,0:T(8,128)(2,1)} %broadcast_in_dim.64), calls=%async_computation | async-start | bytes 131072 | tf_op jit(solution)/shard_map/all_to_all | solution.py:231
  7.1 11.2 %copy-start.9 = (s32[8]{0:T(128)}, s32[8]{0:T(128)S(1)}, u32[]{:S(2)}) copy-start(s32[8]{0:T(128)S(1)} %iota_add_fusion.1) | copy-start | bytes 100
  7.1 11.2 %copy-start.11 = (s32[3]{0:T(128)}, s32[3]{0:T(128)S(1)}, u32[]{:S(2)}) copy-start(s32[3]{0:T(128)S(1)} %iota_add_fusion) | copy-start | bytes 40
  12.0 17.9 %all-to-all-start.1 = ((bf16[8,32,1024]{2,1,0:T(8,128)(2,1)}), bf16[8,32,1024]{2,1,0:T(8,128)(2,1)}, u32[]{:S(2)}, u32[]{:S(2)}) async-start(bf16[8,32,1024]{2,1,0:T(8,128)(2,1)} %broadcast_in_dim.66), calls=%async_computation.1 | async-start | bytes 1048576 | tf_op jit(solution)/shard_map/all_to_all | solution.py:231
  29.9 132.9 %all-to-all-start.2 = ((bf16[8,4,64,1024]{3,2,1,0:T(8,128)(2,1)}), bf16[8,4,64,1024]{3,2,1,0:T(8,128)(2,1)}, u32[]{:S(2)}, u32[]{:S(2)}) async-start(bf16[8,4,64,1024]{3,2,1,0:T(8,128)(2,1)} %bitcast.32), calls=%async_computation.2 | async-start | bytes 8388608 | tf_op jit(solution)/shard_map/all_to_all | solution.py:233
  37.1 5.9 %copy-start.1 = (s32[256]{0:T(256)S(1)}, s32[256]{0:T(256)}, u32[]{:S(2)}) copy-start(s32[256]{0:T(256)} %param.11) | copy-start | bytes 3076
  37.8 92.3 %collective-permute-start.1 = (bf16[64,1024]{1,0:T(8,128)(2,1)}, bf16[64,1024]{1,0:T(8,128)(2,1)S(1)}, u32[]{:S(2)}, u32[]{:S(2)}) collective-permute-start(bf16[64,1024]{1,0:T(8,128)(2,1)} %get-tuple-element.21), channel_id=1, source_target_pairs={{1,0},{2,1},{3,2},{4,3},{5,4},{6,5},{7,6},{8,7},{9,8},{10,9},{11,1... | collective-permute-start | bytes 393224 | tf_op jit(solution)/shard_map/ppermute | solution.py:216
  39.7 89.4 %collective-permute-start = (bf16[64,1024]{1,0:T(8,128)(2,1)}, bf16[64,1024]{1,0:T(8,128)(2,1)}, u32[]{:S(2)}, u32[]{:S(2)}) collective-permute-start(bf16[64,1024]{1,0:T(8,128)(2,1)} %get-tuple-element.22), channel_id=1, source_target_pairs={{0,1},{1,2},{2,3},{3,4},{4,5},{5,6},{6,7},{7,8},{8,9},{9,10},{10,1... | collective-permute-start | bytes 393224 | tf_op jit(solution)/shard_map/ppermute | solution.py:215
  43.7 0.8 copy-start.10
  43.7 0.8 copy-start.12
  63.4 4.1 %copy-start.8 = (s32[192]{0:T(256)S(1)}, s32[192]{0:T(256)}, u32[]{:S(2)}) copy-start(s32[192]{0:T(256)} %lt.87) | copy-start | bytes 2308
  68.1 4.8 %copy-start.5 = (bf16[1024,16,1,64]{0,3,2,1:T(8,128)(2,1)S(1)}, bf16[1024,16,1,64]{0,3,2,1:T(8,128)(2,1)}, u32[]{:S(2)}) copy-start(bf16[1024,16,1,64]{0,3,2,1:T(8,128)(2,1)} %get-tuple-element.20) | copy-start | bytes 6291460
  75.2 54.9 %copy-start.4 = (bf16[1024,16,1,64]{0,3,2,1:T(8,128)(2,1)S(1)}, bf16[1024,16,1,64]{0,3,2,1:T(8,128)(2,1)}, u32[]{:S(2)}) copy-start(bf16[1024,16,1,64]{0,3,2,1:T(8,128)(2,1)} %get-tuple-element.19) | copy-start | bytes 6291460
  130.1 2.6 %copy-start.3 = (bf16[1024,16,1,64]{0,3,2,1:T(8,128)(2,1)S(1)}, bf16[1024,16,1,64]{0,3,2,1:T(8,128)(2,1)}, u32[]{:S(2)}) copy-start(bf16[1024,16,1,64]{0,3,2,1:T(8,128)(2,1)} %get-tuple-element.18) | copy-start | bytes 6291460

commit v13 on v7

--- a/solution.py
+++ b/solution.py
@@ -102,21 +102,19 @@
                 q_pair, kv_rows[:, lanes], CONTRACT, preferred_element_type=jnp.float32
             )
             scores = jnp.where(valid, scores * scaling, -jnp.inf)
-            peak = jnp.max(scores, axis=-1, keepdims=True)
+            m_a = ma_ref[g, :, cols]
+            m_a_col = jnp.concatenate([m_a[:, :1], m_a[:, HD : HD + 1]], axis=0)
+            peak = jnp.maximum(jnp.max(scores, axis=-1, keepdims=True), m_a_col)
             exps = jnp.exp(scores - peak)
             total = jnp.sum(exps, axis=-1, keepdims=True)
             result = jnp.dot(
                 exps.astype(jnp.bfloat16), kv_rows[:, value_lanes], preferred_element_type=jnp.float32
             )
-            o_b = pick_rows(result, low, rows)
-            m_b = pick_rows(jnp.broadcast_to(peak, result.shape), low, rows)
-            l_b = pick_rows(jnp.broadcast_to(total, result.shape), low, rows)
-            m_a = ma_ref[g, :, cols]
-            peak_all = jnp.maximum(m_a, m_b)
-            scale_a = jnp.exp(m_a - peak_all)
-            scale_b = jnp.exp(m_b - peak_all)
-            numerator = oa_ref[g, :, cols] * scale_a + o_b * scale_b
-            denominator = la_ref[g, :, cols] * scale_a + l_b * scale_b
+            scale_a = pick_rows(jnp.broadcast_to(jnp.exp(m_a_col - peak), result.shape), low, rows)
+            numerator = oa_ref[g, :, cols] * scale_a + pick_rows(result, low, rows)
+            denominator = la_ref[g, :, cols] * scale_a + pick_rows(
+                jnp.broadcast_to(total, result.shape), low, rows
+            )
             out_ref[g, :, cols] = (numerator / denominator).astype(out_ref.dtype)
 
 

time: 191 us -> 197 us (1.031)
  Pallas kernels: 50.2 us -> 56.8 us
    pallas_call x1, Pallas kernels: 28 us -> 34.6 us  [attend_far(): pl.pallas_call(functools.partial(far_kernel, group), grid_spec=grid_spec,...]
  transfers between devices with their start and end apart: 4 -> 4, of which waited for: 2 -> 2; matrix products, arithmetic and copies ran while one was open for 26% -> 25% of each run, Pallas kernels for 12% -> 11%
where the time goes in v13:
time: 197 us; the launch traced here: 196 us
  waiting for transfers between devices  63.4 us (32%)
  Pallas kernels  56.8 us (29%)
  local copies, waits for them, and re-layouts  32.6 us (17%)
  starting transfers between devices  18.4 us (9%)
  matrix products  16.2 us (8%)
  other arithmetic  8.94 us (5%)
    ppermute x1, waiting for transfers between devices, local(): lax.ppermute(token_blocks[dev_blocks - 1], ('ctx', 'seq'), forward)  54.7 us
    pallas_call x1, Pallas kernels, attend_far(): pl.pallas_call(functools.partial(far_kernel, group), grid_spec=grid_spec,...  34.6 us
    pallas_call x1, Pallas kernels, attend_near(): pl.pallas_call(near_kernel, grid=(blocks,), in_specs=[pl.BlockSpec((1, 1,...  22.2 us
    dot_general x5, matrix products, local(): jnp.dot(x, w, preferred_element_type=jnp.float32).astype(jnp.bfloat16)  12.7 us
    unnamed x31, local copies, waits for them, and re-layouts  10.3 us
    all_to_all x1, waiting for transfers between devices, local(): lax.all_to_all(copies, ('ctx', 'seq'), 0, 0, tiled=True)  8.71 us
    another operation x2, local copies, waits for them, and re-layouts, split_weights(): shaped[:, :, j, :].reshape(model_dim, head_total * HD)  7.86 us
    all_to_all x1, starting transfers between devices, local(): lax.all_to_all(outgoing, 'ctx', split_axis=0, concat_axis=0, tiled=True)  7 us
  transfers between devices with their start and end apart: 4, of which 2 were waited for; matrix products, arithmetic and copies ran while one was open for 25% of the time, Pallas kernels for 11%

profile of v13, /device:TPU:16, one launch (start us, length us, event | category | flops | bytes accessed | tf_op | source)
XLA Modules:
  0.0 196.5 jit_solution(25271661286140510)
XLA Ops:
  0.0 0.9 dynamic_slice.18
  1.2 1.6 select_reduce_fusion
  2.8 0.2 multiply_reduce_fusion
  3.1 0.9 broadcast_in_dim.39
  4.0 6.0 %all-to-all-start = ((bf16[32,8,1024]{2,1,0:T(8,128)(2,1)}), bf16[32,8,1024]{2,1,0:T(8,128)(2,1)}, u32[]{:S(2)}, u32[]{:S(2)}) async-start(bf16[32,8,1024]{2,1,0:T(8,128)(2,1)} %broadcast_in_dim.39), calls=%async_computation | async-start | bytes 1048576 | tf_op jit(solution)/shard_map/all_to_all | solution.py:227
  10.2 0.4 copy-done.9
  11.7 2.9 %gather_fusion = bf16[32,64,1024]{2,1,0:T(8,128)(2,1)} fusion(bf16[8,64,1024]{2,1,0:T(8,128)(2,1)S(1)} %bitcast.29, s32[1024]{0:T(1024)S(1)} %get-tuple-element.28), kind=kCustom, calls=%fused_computation.2 | custom fusion | bytes 8388736 | tf_op jit(solution)/shard_map/jit(_take)/gather | solution.py:208
  14.6 8.7 %all-to-all-done = bf16[32,8,1024]{2,1,0:T(8,128)(2,1)} async-done(((bf16[32,8,1024]{2,1,0:T(8,128)(2,1)}), bf16[32,8,1024]{2,1,0:T(8,128)(2,1)}, u32[]{:S(2)}, u32[]{:S(2)}) %all-to-all-start) | async-done | bytes 524320 | tf_op jit(solution)/shard_map/all_to_all | solution.py:227
  23.3 7.0 %all-to-all-start.1 = ((bf16[8,4,64,1024]{3,2,1,0:T(8,128)(2,1)}), bf16[8,4,64,1024]{3,2,1,0:T(8,128)(2,1)}, u32[]{:S(2)}, u32[]{:S(2)}) async-start(bf16[8,4,64,1024]{3,2,1,0:T(8,128)(2,1)} %bitcast.31), calls=%async_computation.1 | async-start | bytes 8388608 | tf_op jit(solution)/shard_map/all_to_all | solution.py:229
  30.3 0.7 fusion.5
  31.0 3.5 %collective-permute-start.1 = (bf16[64,1024]{1,0:T(8,128)(2,1)}, bf16[64,1024]{1,0:T(8,128)(2,1)S(1)}, u32[]{:S(2)}, u32[]{:S(2)}) collective-permute-start(bf16[64,1024]{1,0:T(8,128)(2,1)} %get-tuple-element.21), channel_id=1, source_target_pairs={{1,0},{2,1},{3,2},{4,3},{5,4},{6,5},{7,6},{8,7},{9,8},{10,9},{11,1... | collective-permute-start | bytes 393224 | tf_op jit(solution)/shard_map/ppermute | solution.py:214
  34.5 1.9 collective-permute-start
  36.4 0.6 lt.87
  37.2 0.7 gather_fusion.1
  38.0 0.7 gather_fusion.2
  39.4 8.6 %copy.43 = bf16[1024,3072]{0,1:T(8,128)(2,1)} copy(bf16[1024,3072]{1,0:T(8,128)(2,1)} %param.9) | data formatting | bytes 12582912 | tf_op args[1]
  48.0 5.8 %fusion.4 = (bf16[1024,16,1,64]{0,3,2,1:T(8,128)(2,1)}, bf16[1024,16,1,64]{0,3,2,1:T(8,128)(2,1)}, bf16[1024,16,1,64]{0,3,2,1:T(8,128)(2,1)}) fusion(bf16[1024,16,3,64]{0,3,2,1:T(8,128)(2,1)} %bitcast.30), kind=kLoop, calls=%fused_computation.47 | loop fusion | bytes 12582912 | tf_op jit(solution)/shard_map/slice | solution.py:35
  53.8 3.9 %copy.48 = bf16[1024,1024]{1,0:T(8,128)(2,1)} copy(bf16[1024,1024]{0,1:T(8,128)(2,1)} %bitcast.41) | data formatting | bytes 4194304 | tf_op jit(solution)/shard_map/reshape;squeeze | solution.py:35
  57.7 3.9 %copy.47 = bf16[1024,1024]{1,0:T(8,128)(2,1)} copy(bf16[1024,1024]{0,1:T(8,128)(2,1)} %bitcast.38) | data formatting | bytes 4194304 | tf_op jit(solution)/shard_map/reshape;squeeze | solution.py:35
  61.8 0.6 compare_convert_fusion
  62.4 4.8 %pad_maximum_fusion.refs_6_ = bf16[1024,2048]{1,0:T(8,128)(2,1)} fusion(bf16[1024,1024]{1,0:T(8,128)(2,1)} %copy.48, bf16[1024,1024]{1,0:T(8,128)(2,1)} %copy.47), kind=kLoop, calls=%fused_computation.3 | loop fusion | flops 8388608 | bytes 8388608 | tf_op jit(solution)/shard_map/concatenate | solution.py:261
  67.3 2.3 %convolution_convert_fusion.2 = bf16[512,1024]{1,0:T(8,128)(2,1)} fusion(bf16[512,1024]{1,0:T(8,128)(2,1)S(1)} %copy-done.2, bf16[1024,1024]{0,1:T(8,128)(2,1)S(1)} %bitcast.46), kind=kOutput, calls=%fused_computation.8 | convolution fusion | flops 1074266112 | bytes 4194304 | tf_op jit(solution)/shard_map/dot_general | solution.py:232
  69.5 0.5 multiply_add_fusion.ids_ref
  70.0 54.7 %collective-permute-done = bf16[64,1024]{1,0:T(8,128)(2,1)} collective-permute-done((bf16[64,1024]{1,0:T(8,128)(2,1)}, bf16[64,1024]{1,0:T(8,128)(2,1)}, u32[]{:S(2)}, u32[]{:S(2)}) %collective-permute-start) | collective-permute-done | bytes 131104 | tf_op jit(solution)/shard_map/ppermute | solution.py:213
  124.7 0.9 constant_dynamic-update-slice_fusion.2
  125.8 2.6 %convolution_convert_fusion = bf16[640,1024]{1,0:T(8,128)(2,1)} fusion(bf16[640,1024]{1,0:T(8,128)(2,1)S(1)} %constant_dynamic-update-slice_fusion, bf16[1024,1024]{0,1:T(8,128)(2,1)S(1)} %bitcast.42), kind=kOutput, calls=%fused_computation.6 | convolution fusion | flops 1342832640 | bytes 4718592 | tf_op jit(solution)/shard_map/dot_general | solution.py:232
  128.4 2.6 %convolution_convert_fusion.1 = bf16[640,1024]{1,0:T(8,128)(2,1)} fusion(bf16[640,1024]{1,0:T(8,128)(2,1)S(1)} %constant_dynamic-update-slice_fusion, bf16[1024,1024]{0,1:T(8,128)(2,1)S(1)} %bitcast.39), kind=kOutput, calls=%fused_computation.7 | convolution fusion | flops 1342832640 | bytes 4718592 | tf_op jit(solution)/shard_map/dot_general | solution.py:232
  131.0 2.6 %convolution_convert_fusion.3.vs_ref = bf16[256,1024]{1,0:T(8,128)(2,1)} fusion(bf16[256,1024]{1,0:T(8,128)(2,1)} %bitcast.4, bf16[1024,1024]{0,1:T(8,128)(2,1)S(1)} %bitcast.43), kind=kOutput, calls=%fused_computation.9 | convolution fusion | flops 537133056 | bytes 3145728 | tf_op jit(solution)/shard_map/dot_general | solution.py:232
  133.6 2.6 %convolution_convert_fusion.4.ks_ref = bf16[256,1024]{1,0:T(8,128)(2,1)} fusion(bf16[256,1024]{1,0:T(8,128)(2,1)} %bitcast.4, bf16[1024,1024]{0,1:T(8,128)(2,1)S(1)} %bitcast.40), kind=kOutput, calls=%fused_computation.10 | convolution fusion | flops 537133056 | bytes 3145728 | tf_op jit(solution)/shard_map/dot_general | solution.py:232
  136.2 22.2 %shard_map.64 = (f32[8,64,1024]{2,1,0:T(8,128)}, f32[8,64,1024]{2,1,0:T(8,128)}, f32[8,64,1024]{2,1,0:T(8,128)}) custom-call(s32[8,1,192]{2,1,0:T(1,128)} %get-tuple-element.25.mask_ref, bf16[8,64,1024]{2,1,0:T(8,128)(2,1)} %bitcast.44, bf16[10,64,1024]{2,1,0:T(8,128)(2,1)} %bitcast.35, bf16[10,64,1024]{2,1,0:T(8,128)(2,1)} %bitcast.36, ...), custom_call_target="tpu_custom_call" | custom-call | flops 1879048192 | bytes 14680064 | tf_op jit(solution)/shard_map/pallas_call | solution.py:131
  158.4 34.6 %shard_map.65 = bf16[8,64,1024]{2,1,0:T(8,128)(2,1)} custom-call(s32[24]{0:T(128)} %multiply_add_fusion.ids_ref, s32[8,1,192]{2,1,0:T(1,128)} %get-tuple-element.26.mask_ref, bf16[8,64,1024]{2,1,0:T(8,128)(2,1)} %bitcast.45, bf16[32,64,1024]{2,1,0:T(8,128)(2,1)} %bitcast.7.refs_0_.refs_1_.refs_2_.refs_3_.refs_4_.refs_5_, ...), custom_call_target="tpu_custom_call" | custom-call | flops 7247757312 | bytes 15728640 | tf_op jit(solution)/shard_map/pallas_call | solution.py:175
  193.0 3.5 %add_convert_fusion = bf16[512,1024]{1,0:T(8,128)(2,1)} fusion(bf16[512,1024]{1,0:T(8,128)(2,1)S(1)} %copy-done.2, bf16[512,1024]{1,0:T(8,128)(2,1)} %bitcast.47, bf16[1024,1024]{1,0:T(8,128)(2,1)S(1)} %copy-done), kind=kOutput, calls=%fused_computation.4 | convolution fusion | flops 1075314688 | bytes 5242880 | tf_op jit(solution)/shard_map/dot_general | solution.py:266
  (66 shorter events, 2.7 us)
Async XLA Ops:
  0.0 193.0 %copy-start = (bf16[1024,1024]{1,0:T(8,128)(2,1)S(1)}, bf16[1024,1024]{1,0:T(8,128)(2,1)}, u32[]{:S(2)}) copy-start(bf16[1024,1024]{1,0:T(8,128)(2,1)} %param.10) | copy-start | bytes 6291460
  0.0 11.7 %copy-start.2 = (bf16[512,1024]{1,0:T(8,128)(2,1)S(1)}, bf16[512,1024]{1,0:T(8,128)(2,1)}, u32[]{:S(2)}) copy-start(bf16[512,1024]{1,0:T(8,128)(2,1)} %param.8) | copy-start | bytes 3145732
  0.0 10.6 %copy-start.6 = (s32[256,3]{0,1:T(4,128)S(1)}, s32[256,3]{0,1:T(4,128)}, u32[]{:S(2)}) copy-start(s32[256,3]{0,1:T(4,128)} %param.12) | copy-start | bytes 9220
  0.0 11.0 %copy-start.7 = (s32[256,3]{0,1:T(4,128)S(1)}, s32[256,3]{0,1:T(4,128)}, u32[]{:S(2)}) copy-start(s32[256,3]{0,1:T(4,128)} %param.13) | copy-start | bytes 9220
  4.0 19.3 %all-to-all-start = ((bf16[32,8,1024]{2,1,0:T(8,128)(2,1)}), bf16[32,8,1024]{2,1,0:T(8,128)(2,1)}, u32[]{:S(2)}, u32[]{:S(2)}) async-start(bf16[32,8,1024]{2,1,0:T(8,128)(2,1)} %broadcast_in_dim.39), calls=%async_computation | async-start | bytes 1048576 | tf_op jit(solution)/shard_map/all_to_all | solution.py:227
  10.0 0.6 copy-start.9
  10.0 0.6 copy-start.11
  23.3 135.1 %all-to-all-start.1 = ((bf16[8,4,64,1024]{3,2,1,0:T(8,128)(2,1)}), bf16[8,4,64,1024]{3,2,1,0:T(8,128)(2,1)}, u32[]{:S(2)}, u32[]{:S(2)}) async-start(bf16[8,4,64,1024]{3,2,1,0:T(8,128)(2,1)} %bitcast.31), calls=%async_computation.1 | async-start | bytes 8388608 | tf_op jit(solution)/shard_map/all_to_all | solution.py:229
  30.3 6.9 %copy-start.1 = (s32[256]{0:T(256)S(1)}, s32[256]{0:T(256)}, u32[]{:S(2)}) copy-start(s32[256]{0:T(256)} %param.11) | copy-start | bytes 3076
  31.0 94.7 %collective-permute-start.1 = (bf16[64,1024]{1,0:T(8,128)(2,1)}, bf16[64,1024]{1,0:T(8,128)(2,1)S(1)}, u32[]{:S(2)}, u32[]{:S(2)}) collective-permute-start(bf16[64,1024]{1,0:T(8,128)(2,1)} %get-tuple-element.21), channel_id=1, source_target_pairs={{1,0},{2,1},{3,2},{4,3},{5,4},{6,5},{7,6},{8,7},{9,8},{10,9},{11,1... | collective-permute-start | bytes 393224 | tf_op jit(solution)/shard_map/ppermute | solution.py:214
  34.5 90.2 %collective-permute-start = (bf16[64,1024]{1,0:T(8,128)(2,1)}, bf16[64,1024]{1,0:T(8,128)(2,1)}, u32[]{:S(2)}, u32[]{:S(2)}) collective-permute-start(bf16[64,1024]{1,0:T(8,128)(2,1)} %get-tuple-element.22), channel_id=1, source_target_pairs={{0,1},{1,2},{2,3},{3,4},{4,5},{5,6},{6,7},{7,8},{8,9},{9,10},{10,1... | collective-permute-start | bytes 393224 | tf_op jit(solution)/shard_map/ppermute | solution.py:213
  38.0 0.8 copy-start.10
  38.0 0.8 copy-start.12
  57.7 4.1 %copy-start.8 = (s32[192]{0:T(256)S(1)}, s32[192]{0:T(256)}, u32[]{:S(2)}) copy-start(s32[192]{0:T(256)} %lt.87) | copy-start | bytes 2308
  62.4 4.8 %copy-start.5 = (bf16[1024,16,1,64]{0,3,2,1:T(8,128)(2,1)S(1)}, bf16[1024,16,1,64]{0,3,2,1:T(8,128)(2,1)}, u32[]{:S(2)}) copy-start(bf16[1024,16,1,64]{0,3,2,1:T(8,128)(2,1)} %get-tuple-element.20) | copy-start | bytes 6291460
  69.5 56.2 %copy-start.4 = (bf16[1024,16,1,64]{0,3,2,1:T(8,128)(2,1)S(1)}, bf16[1024,16,1,64]{0,3,2,1:T(8,128)(2,1)}, u32[]{:S(2)}) copy-start(bf16[1024,16,1,64]{0,3,2,1:T(8,128)(2,1)} %get-tuple-element.19) | copy-start | bytes 6291460
  125.8 2.6 %copy-start.3 = (bf16[1024,16,1,64]{0,3,2,1:T(8,128)(2,1)S(1)}, bf16[1024,16,1,64]{0,3,2,1:T(8,128)(2,1)}, u32[]{:S(2)}) copy-start(bf16[1024,16,1,64]{0,3,2,1:T(8,128)(2,1)} %get-tuple-element.18) | copy-start | bytes 6291460

commit v14 on v7

--- a/solution.py
+++ b/solution.py
@@ -80,7 +80,7 @@
 
 def far_kernel(group, ids_ref, mask_ref, q_ref, *refs):
     token_refs = refs[: group * RAND]
-    wkv_ref, oa_ref, ma_ref, la_ref, out_ref = refs[group * RAND :]
+    wkv_ref, oa_ref, ma_ref, la_ref, tok_ref, wo_ref, out_ref, att_ref = refs[group * RAND :]
     width = q_ref.shape[-1]
     rows = q_ref.shape[1]
     scaling = 1.0 / math.sqrt(HD)
@@ -117,7 +117,11 @@
             scale_b = jnp.exp(m_b - peak_all)
             numerator = oa_ref[g, :, cols] * scale_a + o_b * scale_b
             denominator = la_ref[g, :, cols] * scale_a + l_b * scale_b
-            out_ref[g, :, cols] = (numerator / denominator).astype(out_ref.dtype)
+            att_ref[g * rows : (g + 1) * rows, cols] = (numerator / denominator).astype(att_ref.dtype)
+    mixed = jnp.dot(att_ref[...], wo_ref[...], preferred_element_type=jnp.float32)
+    for g in range(group):
+        part = mixed[g * rows : (g + 1) * rows] + tok_ref[g].astype(jnp.float32)
+        out_ref[g] = part.astype(out_ref.dtype)
 
 
 def attend_near(mask, q, k_ext, v_ext, k_sum, v_sum):
@@ -146,7 +150,7 @@
     )(mask, q, k_ext, k_ext, k_ext, v_ext, v_ext, v_ext, k_sum, v_sum)
 
 
-def attend_far(slot_ids, mask, q, incoming, w_kv, o_a, m_a, l_a):
+def attend_far(slot_ids, mask, q, incoming, w_kv, o_a, m_a, l_a, token_blocks, w_out):
     blocks, rows, width = q.shape
     model_dim = incoming.shape[-1]
     group = 2 if blocks % 2 == 0 else 1
@@ -171,8 +175,9 @@
         grid=(blocks // group,),
         in_specs=[pl.BlockSpec((group, 1, local_keys), lambda i, ids: (i, 0, 0)), block]
         + token_specs
-        + [weight, block, block, block],
+        + [weight, block, block, block, block, pl.BlockSpec(w_out.shape, lambda i, ids: (0, 0))],
         out_specs=block,
+        scratch_shapes=[pltpu.VMEM((group * rows, width), jnp.bfloat16)],
     )
     return pl.pallas_call(
         functools.partial(far_kernel, group),
@@ -183,7 +188,7 @@
             transcendentals=blocks * heads * rows * local_keys,
             bytes_accessed=bytes_accessed,
         ),
-    )(slot_ids, mask, q, *([incoming] * (group * RAND)), w_kv, o_a, m_a, l_a)
+    )(slot_ids, mask, q, *([incoming] * (group * RAND)), w_kv, o_a, m_a, l_a, token_blocks, w_out)
 
 
 def local(tokens, w_qkv, w_out, counts, rand_seg, rand_off):
@@ -255,7 +260,7 @@
     far_mask = (positions < far_counts[:, :, None]).astype(jnp.int32).reshape(dev_blocks, 1, -1)
 
     o_a, m_a, l_a = attend_near(near_mask, q_own, k_ext, v_ext, k_sum, v_sum)
-    attended = attend_far(
+    mixed = attend_far(
         slot_ids,
         far_mask,
         q_own,
@@ -264,9 +269,10 @@
         o_a,
         m_a,
         l_a,
-    ).reshape(tok_rows, model_dim)
-    mixed = tokens.astype(jnp.float32) + jnp.dot(attended, w_out, preferred_element_type=jnp.float32)
-    return mixed.astype(jnp.bfloat16)
+        token_blocks,
+        w_out,
+    )
+    return mixed.reshape(tok_rows, model_dim)
 
 
 def solution(mesh):

time: 191 us -> 188 us (0.984)
  matrix products: 16.2 us -> 10.7 us
  Pallas kernels: 50.2 us -> 52.2 us
    dot_general x1 -> x0, matrix products: 3.45 us -> none  [local(): jnp.dot(attended, w_out, preferred_element_type=jnp.float32)]
    dot_general x5, matrix products: 12.7 us -> 10.7 us  [local(): jnp.dot(x, w, preferred_element_type=jnp.float32).astype(jnp.bfloat16)]
    pallas_call x1, Pallas kernels: 28 us -> 29.9 us  [attend_far(): pl.pallas_call(functools.partial(far_kernel, group), grid_spec=grid_spec,...]
    unnamed x31 -> x21, local copies, waits for them, and re-layouts: 10.3 us -> 9.84 us
where the time goes in v14:
time: 188 us; the launch traced here: 186 us
  waiting for transfers between devices  62.8 us (33%)
  Pallas kernels  52.2 us (28%)
  local copies, waits for them, and re-layouts  32 us (17%)
  starting transfers between devices  18.3 us (10%)
  matrix products  10.7 us (6%)
  other arithmetic  9.74 us (5%)
    ppermute x1, waiting for transfers between devices, local(): lax.ppermute(token_blocks[dev_blocks - 1], ('ctx', 'seq'), forward)  53.7 us
    pallas_call x1, Pallas kernels, attend_far(): pl.pallas_call(functools.partial(far_kernel, group), grid_spec=grid_spec,...  29.9 us
    pallas_call x1, Pallas kernels, attend_near(): pl.pallas_call(near_kernel, grid=(blocks,), in_specs=[pl.BlockSpec((1, 1,...  22.2 us
    dot_general x5, matrix products, local(): jnp.dot(x, w, preferred_element_type=jnp.float32).astype(jnp.bfloat16)  10.7 us
    unnamed x21, local copies, waits for them, and re-layouts  9.84 us
    all_to_all x1, waiting for transfers between devices, local(): lax.all_to_all(copies, ('ctx', 'seq'), 0, 0, tiled=True)  9.08 us
    all_to_all x1, starting transfers between devices, local(): lax.all_to_all(outgoing, 'ctx', split_axis=0, concat_axis=0, tiled=True)  6.99 us
    another operation x2, local copies, waits for them, and re-layouts, split_weights(): shaped[:, :, j, :].reshape(model_dim, head_total * HD)  6.55 us
  transfers between devices with their start and end apart: 4, of which 2 were waited for; matrix products, arithmetic and copies ran while one was open for 26% of the time, Pallas kernels for 12%

profile of v14, /device:TPU:16, one launch (start us, length us, event | category | flops | bytes accessed | tf_op | source)
XLA Modules:
  0.0 186.1 jit_solution(5268643584333201644)
XLA Ops:
  0.0 0.8 dynamic_slice.18
  1.1 1.6 select_reduce_fusion
  2.8 0.2 multiply_reduce_fusion
  3.0 0.9 broadcast_in_dim.39
  3.9 5.9 %all-to-all-start = ((bf16[32,8,1024]{2,1,0:T(8,128)(2,1)}), bf16[32,8,1024]{2,1,0:T(8,128)(2,1)S(1)}, u32[]{:S(2)}, u32[]{:S(2)}) async-start(bf16[32,8,1024]{2,1,0:T(8,128)(2,1)} %broadcast_in_dim.39), calls=%async_computation | async-start | bytes 1048576 | tf_op jit(solution)/shard_map/all_to_all | solution.py:234
  11.1 2.9 %gather_fusion = bf16[32,64,1024]{2,1,0:T(8,128)(2,1)} fusion(bf16[8,64,1024]{2,1,0:T(8,128)(2,1)S(1)} %bitcast.28, s32[1024]{0:T(1024)S(1)} %get-tuple-element.28), kind=kCustom, calls=%fused_computation.2 | custom fusion | bytes 8388736 | tf_op jit(solution)/shard_map/jit(_take)/gather | solution.py:215
  14.0 9.1 %all-to-all-done = bf16[32,8,1024]{2,1,0:T(8,128)(2,1)S(1)} async-done(((bf16[32,8,1024]{2,1,0:T(8,128)(2,1)}), bf16[32,8,1024]{2,1,0:T(8,128)(2,1)S(1)}, u32[]{:S(2)}, u32[]{:S(2)}) %all-to-all-start) | async-done | bytes 524320 | tf_op jit(solution)/shard_map/all_to_all | solution.py:234
  23.1 0.8 copy-done.4
  23.9 7.0 %all-to-all-start.1 = ((bf16[8,4,64,1024]{3,2,1,0:T(8,128)(2,1)}), bf16[8,4,64,1024]{3,2,1,0:T(8,128)(2,1)}, u32[]{:S(2)}, u32[]{:S(2)}) async-start(bf16[8,4,64,1024]{3,2,1,0:T(8,128)(2,1)} %bitcast.30), calls=%async_computation.1 | async-start | bytes 8388608 | tf_op jit(solution)/shard_map/all_to_all | solution.py:236
  30.9 0.7 fusion.5
  31.6 3.5 %collective-permute-start.1 = (bf16[64,1024]{1,0:T(8,128)(2,1)S(1)}, bf16[64,1024]{1,0:T(8,128)(2,1)S(1)}, u32[]{:S(2)}, u32[]{:S(2)}) collective-permute-start(bf16[64,1024]{1,0:T(8,128)(2,1)S(1)} %get-tuple-element.21), channel_id=1, source_target_pairs={{1,0},{2,1},{3,2},{4,3},{5,4},{6,5},{7,6},{8,7},{9,8},{10,9},{11,1... | collective-permute-start | bytes 393224 | tf_op jit(solution)/shard_map/ppermute | solution.py:221
  35.0 1.9 %collective-permute-start = (bf16[64,1024]{1,0:T(8,128)(2,1)}, bf16[64,1024]{1,0:T(8,128)(2,1)S(1)}, u32[]{:S(2)}, u32[]{:S(2)}) collective-permute-start(bf16[64,1024]{1,0:T(8,128)(2,1)} %get-tuple-element.22), channel_id=1, source_target_pairs={{0,1},{1,2},{2,3},{3,4},{4,5},{5,6},{6,7},{7,8},{8,9},{9,10},{10,1... | collective-permute-start | bytes 393224 | tf_op jit(solution)/shard_map/ppermute | solution.py:220
  37.0 0.7 lt.87
  37.8 0.7 gather_fusion.1
  38.6 0.7 gather_fusion.2
  39.5 0.7 lt.104
  40.3 0.7 lt.103
  41.1 8.7 %copy.43 = bf16[1024,3072]{0,1:T(8,128)(2,1)} copy(bf16[1024,3072]{1,0:T(8,128)(2,1)} %param.9) | data formatting | bytes 12582912 | tf_op args[1]
  49.8 6.0 %fusion.4 = (bf16[1024,16,1,64]{0,3,2,1:T(8,128)(2,1)S(1)}, bf16[1024,16,1,64]{0,3,2,1:T(8,128)(2,1)}, bf16[1024,16,1,64]{0,3,2,1:T(8,128)(2,1)}) fusion(bf16[1024,16,3,64]{0,3,2,1:T(8,128)(2,1)} %bitcast.29), kind=kLoop, calls=%fused_computation.46 | loop fusion | bytes 12582912 | tf_op jit(solution)/shard_map/slice | solution.py:35
  55.8 3.9 %copy.48 = bf16[1024,1024]{1,0:T(8,128)(2,1)} copy(bf16[1024,1024]{0,1:T(8,128)(2,1)} %bitcast.40) | data formatting | bytes 4194304 | tf_op jit(solution)/shard_map/reshape;squeeze | solution.py:35
  59.7 2.6 %copy.47 = bf16[1024,1024]{1,0:T(8,128)(2,1)} copy(bf16[1024,1024]{0,1:T(8,128)(2,1)S(1)} %bitcast.37) | data formatting | bytes 4194304 | tf_op jit(solution)/shard_map/reshape;squeeze | solution.py:35
  62.5 1.3 compare_convert_fusion
  63.8 4.8 %pad_maximum_fusion.refs_6_ = bf16[1024,2048]{1,0:T(8,128)(2,1)} fusion(bf16[1024,1024]{1,0:T(8,128)(2,1)} %copy.48, bf16[1024,1024]{1,0:T(8,128)(2,1)} %copy.47), kind=kLoop, calls=%fused_computation.3 | loop fusion | flops 8388608 | bytes 8388608 | tf_op jit(solution)/shard_map/concatenate | solution.py:268
  68.7 2.3 %convolution_convert_fusion.2 = bf16[512,1024]{1,0:T(8,128)(2,1)} fusion(bf16[512,1024]{1,0:T(8,128)(2,1)S(1)} %copy-done.1, bf16[1024,1024]{0,1:T(8,128)(2,1)S(1)} %bitcast.45), kind=kOutput, calls=%fused_computation.7 | convolution fusion | flops 1074266112 | bytes 4194304 | tf_op jit(solution)/shard_map/dot_general | solution.py:239
  71.0 0.6 multiply_add_fusion.ids_ref
  71.5 53.7 %collective-permute-done = bf16[64,1024]{1,0:T(8,128)(2,1)S(1)} collective-permute-done((bf16[64,1024]{1,0:T(8,128)(2,1)}, bf16[64,1024]{1,0:T(8,128)(2,1)S(1)}, u32[]{:S(2)}, u32[]{:S(2)}) %collective-permute-start) | collective-permute-done | bytes 131104 | tf_op jit(solution)/shard_map/ppermute | solution.py:220
  125.4 2.6 %convolution_convert_fusion = bf16[640,1024]{1,0:T(8,128)(2,1)} fusion(bf16[640,1024]{1,0:T(8,128)(2,1)S(1)} %constant_dynamic-update-slice_fusion, bf16[1024,1024]{0,1:T(8,128)(2,1)S(1)} %bitcast.41), kind=kOutput, calls=%fused_computation.5 | convolution fusion | flops 1342832640 | bytes 4718592 | tf_op jit(solution)/shard_map/dot_general | solution.py:239
  128.0 2.6 %convolution_convert_fusion.1 = bf16[640,1024]{1,0:T(8,128)(2,1)} fusion(bf16[640,1024]{1,0:T(8,128)(2,1)S(1)} %constant_dynamic-update-slice_fusion, bf16[1024,1024]{0,1:T(8,128)(2,1)S(1)} %bitcast.38), kind=kOutput, calls=%fused_computation.6 | convolution fusion | flops 1342832640 | bytes 4718592 | tf_op jit(solution)/shard_map/dot_general | solution.py:239
  130.6 1.6 convolution_convert_fusion.3.vs_ref
  132.2 1.5 convolution_convert_fusion.4.ks_ref
  133.7 22.2 %shard_map.64 = (f32[8,64,1024]{2,1,0:T(8,128)}, f32[8,64,1024]{2,1,0:T(8,128)}, f32[8,64,1024]{2,1,0:T(8,128)}) custom-call(s32[8,1,192]{2,1,0:T(1,128)} %get-tuple-element.25.mask_ref, bf16[8,64,1024]{2,1,0:T(8,128)(2,1)} %bitcast.43, bf16[10,64,1024]{2,1,0:T(8,128)(2,1)} %bitcast.34, bf16[10,64,1024]{2,1,0:T(8,128)(2,1)} %bitcast.35, ...), custom_call_target="tpu_custom_call" | custom-call | flops 1879048192 | bytes 14680064 | tf_op jit(solution)/shard_map/pallas_call | solution.py:137
  156.0 29.9 %shard_map.65 = bf16[8,64,1024]{2,1,0:T(8,128)(2,1)} custom-call(s32[24]{0:T(128)} %multiply_add_fusion.ids_ref, s32[8,1,192]{2,1,0:T(1,128)} %get-tuple-element.26.mask_ref, bf16[8,64,1024]{2,1,0:T(8,128)(2,1)} %bitcast.44, bf16[32,64,1024]{2,1,0:T(8,128)(2,1)} %bitcast.7.refs_0_.refs_1_.refs_2_.refs_3_.refs_4_.refs_5_, ...), custom_call_target="tpu_custom_call" | custom-call | flops 7247757312 | bytes 15728640 | tf_op jit(solution)/shard_map/pallas_call | solution.py:182
  (55 shorter events, 2.5 us)
Async XLA Ops:
  0.0 11.1 %copy-start.1 = (bf16[512,1024]{1,0:T(8,128)(2,1)S(1)}, bf16[512,1024]{1,0:T(8,128)(2,1)}, u32[]{:S(2)}) copy-start(bf16[512,1024]{1,0:T(8,128)(2,1)} %param.8) | copy-start | bytes 3145732
  0.0 10.0 %copy-start.6 = (s32[256,3]{0,1:T(4,128)S(1)}, s32[256,3]{0,1:T(4,128)}, u32[]{:S(2)}) copy-start(s32[256,3]{0,1:T(4,128)} %param.12) | copy-start | bytes 9220
  0.0 10.5 %copy-start.7 = (s32[256,3]{0,1:T(4,128)S(1)}, s32[256,3]{0,1:T(4,128)}, u32[]{:S(2)}) copy-start(s32[256,3]{0,1:T(4,128)} %param.13) | copy-start | bytes 9220
  3.9 19.2 %all-to-all-start = ((bf16[32,8,1024]{2,1,0:T(8,128)(2,1)}), bf16[32,8,1024]{2,1,0:T(8,128)(2,1)S(1)}, u32[]{:S(2)}, u32[]{:S(2)}) async-start(bf16[32,8,1024]{2,1,0:T(8,128)(2,1)} %broadcast_in_dim.39), calls=%async_computation | async-start | bytes 1048576 | tf_op jit(solution)/shard_map/all_to_all | solution.py:234
  23.1 0.8 copy-start.4
  23.9 132.1 %all-to-all-start.1 = ((bf16[8,4,64,1024]{3,2,1,0:T(8,128)(2,1)}), bf16[8,4,64,1024]{3,2,1,0:T(8,128)(2,1)}, u32[]{:S(2)}, u32[]{:S(2)}) async-start(bf16[8,4,64,1024]{3,2,1,0:T(8,128)(2,1)} %bitcast.30), calls=%async_computation.1 | async-start | bytes 8388608 | tf_op jit(solution)/shard_map/all_to_all | solution.py:236
  30.9 6.9 %copy-start = (s32[256]{0:T(256)S(1)}, s32[256]{0:T(256)}, u32[]{:S(2)}) copy-start(s32[256]{0:T(256)} %param.11) | copy-start | bytes 3076
  31.6 93.8 %collective-permute-start.1 = (bf16[64,1024]{1,0:T(8,128)(2,1)S(1)}, bf16[64,1024]{1,0:T(8,128)(2,1)S(1)}, u32[]{:S(2)}, u32[]{:S(2)}) collective-permute-start(bf16[64,1024]{1,0:T(8,128)(2,1)S(1)} %get-tuple-element.21), channel_id=1, source_target_pairs={{1,0},{2,1},{3,2},{4,3},{5,4},{6,5},{7,6},{8,7},{9,8},{10,9},{11,1... | collective-permute-start | bytes 393224 | tf_op jit(solution)/shard_map/ppermute | solution.py:221
  35.0 90.2 %collective-permute-start = (bf16[64,1024]{1,0:T(8,128)(2,1)}, bf16[64,1024]{1,0:T(8,128)(2,1)S(1)}, u32[]{:S(2)}, u32[]{:S(2)}) collective-permute-start(bf16[64,1024]{1,0:T(8,128)(2,1)} %get-tuple-element.22), channel_id=1, source_target_pairs={{0,1},{1,2},{2,3},{3,4},{4,5},{5,6},{6,7},{7,8},{8,9},{9,10},{10,1... | collective-permute-start | bytes 393224 | tf_op jit(solution)/shard_map/ppermute | solution.py:220
  63.8 4.8 %copy-start.3 = (bf16[1024,16,1,64]{0,3,2,1:T(8,128)(2,1)S(1)}, bf16[1024,16,1,64]{0,3,2,1:T(8,128)(2,1)}, u32[]{:S(2)}) copy-start(bf16[1024,16,1,64]{0,3,2,1:T(8,128)(2,1)} %get-tuple-element.20) | copy-start | bytes 6291460
  71.0 54.4 %copy-start.2 = (bf16[1024,16,1,64]{0,3,2,1:T(8,128)(2,1)S(1)}, bf16[1024,16,1,64]{0,3,2,1:T(8,128)(2,1)}, u32[]{:S(2)}) copy-start(bf16[1024,16,1,64]{0,3,2,1:T(8,128)(2,1)} %get-tuple-element.19) | copy-start | bytes 6291460
  128.0 2.6 %copy-start.5 = (bf16[32,8,1024]{2,1,0:T(8,128)(2,1)S(1)}, bf16[32,8,1024]{2,1,0:T(8,128)(2,1)}, u32[]{:S(2)}) copy-start(bf16[32,8,1024]{2,1,0:T(8,128)(2,1)} %copy-done.4) | copy-start | bytes 1572868

commit v15 on v14

--- a/solution.py
+++ b/solution.py
@@ -80,33 +80,51 @@
 
 def far_kernel(group, ids_ref, mask_ref, q_ref, *refs):
     token_refs = refs[: group * RAND]
-    wkv_ref, oa_ref, ma_ref, la_ref, tok_ref, wo_ref, out_ref, att_ref = refs[group * RAND :]
+    (wk_hbm, wv_hbm, wo_hbm, oa_ref, ma_ref, la_ref, tok_ref, out_ref, att_ref,
+     wk_ref, wv_ref, wo_ref, sems) = refs[group * RAND :]
     width = q_ref.shape[-1]
     rows = q_ref.shape[1]
     scaling = 1.0 / math.sqrt(HD)
     low = lax.broadcasted_iota(jnp.int32, (rows, LANES), 1) < HD
+    first = pl.program_id(0) == 0
+    loads = [
+        pltpu.make_async_copy(src, dst, sems.at[n])
+        for n, (src, dst) in enumerate(((wk_hbm, wk_ref), (wv_hbm, wv_ref), (wo_hbm, wo_ref)))
+    ]
+
+    @pl.when(first)
+    def _():
+        for load in loads:
+            load.start()
+
+    def ready(load):
+        @pl.when(first)
+        def _():
+            load.wait()
+
     far_tokens = jnp.concatenate([ref[0] for ref in token_refs], axis=0)
-    kv_far = jnp.dot(far_tokens, wkv_ref[...], preferred_element_type=jnp.float32).astype(
-        jnp.bfloat16
-    )
+    ready(loads[0])
+    k_far = jnp.dot(far_tokens, wk_ref[...], preferred_element_type=jnp.float32).astype(jnp.bfloat16)
+    ready(loads[1])
+    v_far = jnp.dot(far_tokens, wv_ref[...], preferred_element_type=jnp.float32).astype(jnp.bfloat16)
     keys = RAND * rows
     for g in range(group):
         valid = mask_ref[g] != 0
-        kv_rows = kv_far[g * keys : (g + 1) * keys]
+        k_rows = k_far[g * keys : (g + 1) * keys]
+        v_rows = v_far[g * keys : (g + 1) * keys]
         for tile in range(width // LANES):
             lanes = slice(tile * LANES, (tile + 1) * LANES)
-            value_lanes = slice(width + tile * LANES, width + (tile + 1) * LANES)
             cols = pl.ds(tile * LANES, LANES)
             q_pair = pair_rows(q_ref[g, :, cols], low)
             scores = lax.dot_general(
-                q_pair, kv_rows[:, lanes], CONTRACT, preferred_element_type=jnp.float32
+                q_pair, k_rows[:, lanes], CONTRACT, preferred_element_type=jnp.float32
             )
             scores = jnp.where(valid, scores * scaling, -jnp.inf)
             peak = jnp.max(scores, axis=-1, keepdims=True)
             exps = jnp.exp(scores - peak)
             total = jnp.sum(exps, axis=-1, keepdims=True)
             result = jnp.dot(
-                exps.astype(jnp.bfloat16), kv_rows[:, value_lanes], preferred_element_type=jnp.float32
+                exps.astype(jnp.bfloat16), v_rows[:, lanes], preferred_element_type=jnp.float32
             )
             o_b = pick_rows(result, low, rows)
             m_b = pick_rows(jnp.broadcast_to(peak, result.shape), low, rows)
@@ -118,6 +136,7 @@
             numerator = oa_ref[g, :, cols] * scale_a + o_b * scale_b
             denominator = la_ref[g, :, cols] * scale_a + l_b * scale_b
             att_ref[g * rows : (g + 1) * rows, cols] = (numerator / denominator).astype(att_ref.dtype)
+    ready(loads[2])
     mixed = jnp.dot(att_ref[...], wo_ref[...], preferred_element_type=jnp.float32)
     for g in range(group):
         part = mixed[g * rows : (g + 1) * rows] + tok_ref[g].astype(jnp.float32)
@@ -150,7 +169,7 @@
     )(mask, q, k_ext, k_ext, k_ext, v_ext, v_ext, v_ext, k_sum, v_sum)
 
 
-def attend_far(slot_ids, mask, q, incoming, w_kv, o_a, m_a, l_a, token_blocks, w_out):
+def attend_far(slot_ids, mask, q, incoming, w_k, w_v, o_a, m_a, l_a, token_blocks, w_out):
     blocks, rows, width = q.shape
     model_dim = incoming.shape[-1]
     group = 2 if blocks % 2 == 0 else 1
@@ -161,13 +180,13 @@
         )
         for n in range(group * RAND)
     ]
-    weight = pl.BlockSpec(w_kv.shape, lambda i, ids: (0, 0))
+    weight = pl.BlockSpec(memory_space=pl.ANY)
     local_keys = RAND * rows
     heads = width // HD
     flops = blocks * (
         heads * 2 * rows * 2 * LANES * local_keys + 2 * local_keys * model_dim * 2 * width
     )
-    bytes_accessed = 2 * blocks * rows * (width * 2 + model_dim * RAND) + 2 * w_kv.size + (
+    bytes_accessed = 2 * blocks * rows * (width * 2 + model_dim * RAND) + 2 * (w_k.size + w_v.size + w_out.size) + (
         12 * blocks * rows * width
     )
     grid_spec = pltpu.PrefetchScalarGridSpec(
@@ -175,9 +194,15 @@
         grid=(blocks // group,),
         in_specs=[pl.BlockSpec((group, 1, local_keys), lambda i, ids: (i, 0, 0)), block]
         + token_specs
-        + [weight, block, block, block, block, pl.BlockSpec(w_out.shape, lambda i, ids: (0, 0))],
+        + [weight, weight, weight, block, block, block, block],
         out_specs=block,
-        scratch_shapes=[pltpu.VMEM((group * rows, width), jnp.bfloat16)],
+        scratch_shapes=[
+            pltpu.VMEM((group * rows, width), jnp.bfloat16),
+            pltpu.VMEM(w_k.shape, w_k.dtype),
+            pltpu.VMEM(w_v.shape, w_v.dtype),
+            pltpu.VMEM(w_out.shape, w_out.dtype),
+            pltpu.SemaphoreType.DMA((3,)),
+        ],
     )
     return pl.pallas_call(
         functools.partial(far_kernel, group),
@@ -188,7 +213,7 @@
             transcendentals=blocks * heads * rows * local_keys,
             bytes_accessed=bytes_accessed,
         ),
-    )(slot_ids, mask, q, *([incoming] * (group * RAND)), w_kv, o_a, m_a, l_a, token_blocks, w_out)
+    )(slot_ids, mask, q, *([incoming] * (group * RAND)), w_k, w_v, w_out, o_a, m_a, l_a, token_blocks)
 
 
 def local(tokens, w_qkv, w_out, counts, rand_seg, rand_off):
@@ -265,7 +290,8 @@
         far_mask,
         q_own,
         incoming.reshape(ctx_count * capacity, BLK, model_dim),
-        jnp.concatenate([w_k, w_v], axis=1),
+        w_k,
+        w_v,
         o_a,
         m_a,
         l_a,

time: 188 us -> 189 us (level)
  other arithmetic: 9.74 us -> 4.86 us
  waiting for transfers between devices: 62.8 us -> 66.1 us
    concatenate x1 -> x0, other arithmetic: 4.83 us -> none  [local(): jnp.concatenate([w_k, w_v], axis=1)]
    ppermute x1, waiting for transfers between devices: 53.7 us -> 57 us  [local(): lax.ppermute(token_blocks[dev_blocks - 1], ('ctx', 'seq'), forward)]
    unnamed x21 -> x19, local copies, waits for them, and re-layouts: 9.84 us -> 9.83 us
  transfers between devices with their start and end apart: 4 -> 4, of which waited for: 2 -> 2; matrix products, arithmetic and copies ran while one was open for 26% -> 24% of each run, Pallas kernels for 12% -> 12%
where the time goes in v15:
time: 189 us; the launch traced here: 187 us
  waiting for transfers between devices  66.1 us (35%)
  Pallas kernels  53.4 us (28%)
  local copies, waits for them, and re-layouts  32 us (17%)
  starting transfers between devices  18.3 us (10%)
  matrix products  12.2 us (6%)
  other arithmetic  4.86 us (3%)
    ppermute x1, waiting for transfers between devices, local(): lax.ppermute(token_blocks[dev_blocks - 1], ('ctx', 'seq'), forward)  57 us
    pallas_call x1, Pallas kernels, attend_far(): pl.pallas_call(functools.partial(far_kernel, group), grid_spec=grid_spec,...  31.2 us
    pallas_call x1, Pallas kernels, attend_near(): pl.pallas_call(near_kernel, grid=(blocks,), in_specs=[pl.BlockSpec((1, 1,...  22.2 us
    dot_general x5, matrix products, local(): jnp.dot(x, w, preferred_element_type=jnp.float32).astype(jnp.bfloat16)  12.2 us
    unnamed x19, local copies, waits for them, and re-layouts  9.83 us
    all_to_all x1, waiting for transfers between devices, local(): lax.all_to_all(copies, ('ctx', 'seq'), 0, 0, tiled=True)  9.08 us
    all_to_all x1, starting transfers between devices, local(): lax.all_to_all(outgoing, 'ctx', split_axis=0, concat_axis=0, tiled=True)  7 us
    another operation x2, local copies, waits for them, and re-layouts, split_weights(): shaped[:, :, j, :].reshape(model_dim, head_total * HD)  6.54 us
  transfers between devices with their start and end apart: 4, of which 2 were waited for; matrix products, arithmetic and copies ran while one was open for 24% of the time, Pallas kernels for 12%

profile of v15, /device:TPU:16, one launch (start us, length us, event | category | flops | bytes accessed | tf_op | source)
XLA Modules:
  0.0 187.3 jit_solution(14691097921128124351)
XLA Ops:
  0.0 0.8 dynamic_slice.18
  0.9 0.2 convert_reduce_fusion
  1.1 1.6 select_reduce_fusion
  2.8 0.2 multiply_reduce_fusion
  3.0 0.9 broadcast_in_dim.39
  3.9 5.9 %all-to-all-start = ((bf16[32,8,1024]{2,1,0:T(8,128)(2,1)}), bf16[32,8,1024]{2,1,0:T(8,128)(2,1)S(1)}, u32[]{:S(2)}, u32[]{:S(2)}) async-start(bf16[32,8,1024]{2,1,0:T(8,128)(2,1)} %broadcast_in_dim.39), calls=%async_computation | async-start | bytes 1048576 | tf_op jit(solution)/shard_map/all_to_all | solution.py:259
  11.1 2.9 %gather_fusion = bf16[32,64,1024]{2,1,0:T(8,128)(2,1)} fusion(bf16[8,64,1024]{2,1,0:T(8,128)(2,1)S(1)} %bitcast.28, s32[1024]{0:T(1024)S(1)} %get-tuple-element.28), kind=kCustom, calls=%fused_computation.2 | custom fusion | bytes 8388736 | tf_op jit(solution)/shard_map/jit(_take)/gather | solution.py:240
  14.0 9.1 %all-to-all-done = bf16[32,8,1024]{2,1,0:T(8,128)(2,1)S(1)} async-done(((bf16[32,8,1024]{2,1,0:T(8,128)(2,1)}), bf16[32,8,1024]{2,1,0:T(8,128)(2,1)S(1)}, u32[]{:S(2)}, u32[]{:S(2)}) %all-to-all-start) | async-done | bytes 524320 | tf_op jit(solution)/shard_map/all_to_all | solution.py:259
  23.1 0.8 copy-done.3
  23.9 7.0 %all-to-all-start.1 = ((bf16[8,4,64,1024]{3,2,1,0:T(8,128)(2,1)}), bf16[8,4,64,1024]{3,2,1,0:T(8,128)(2,1)}, u32[]{:S(2)}, u32[]{:S(2)}) async-start(bf16[8,4,64,1024]{3,2,1,0:T(8,128)(2,1)} %bitcast.30), calls=%async_computation.1 | async-start | bytes 8388608 | tf_op jit(solution)/shard_map/all_to_all | solution.py:261
  30.9 0.7 fusion.5
  31.6 3.5 %collective-permute-start.1 = (bf16[64,1024]{1,0:T(8,128)(2,1)S(1)}, bf16[64,1024]{1,0:T(8,128)(2,1)S(1)}, u32[]{:S(2)}, u32[]{:S(2)}) collective-permute-start(bf16[64,1024]{1,0:T(8,128)(2,1)S(1)} %get-tuple-element.21), channel_id=1, source_target_pairs={{1,0},{2,1},{3,2},{4,3},{5,4},{6,5},{7,6},{8,7},{9,8},{10,9},{11,1... | collective-permute-start | bytes 393224 | tf_op jit(solution)/shard_map/ppermute | solution.py:246
  35.0 1.9 %collective-permute-start = (bf16[64,1024]{1,0:T(8,128)(2,1)}, bf16[64,1024]{1,0:T(8,128)(2,1)S(1)}, u32[]{:S(2)}, u32[]{:S(2)}) collective-permute-start(bf16[64,1024]{1,0:T(8,128)(2,1)} %get-tuple-element.22), channel_id=1, source_target_pairs={{0,1},{1,2},{2,3},{3,4},{4,5},{5,6},{6,7},{7,8},{8,9},{9,10},{10,1... | collective-permute-start | bytes 393224 | tf_op jit(solution)/shard_map/ppermute | solution.py:245
  37.0 0.7 lt.87
  37.8 0.7 gather_fusion.1
  38.6 0.7 gather_fusion.2
  39.5 0.7 lt.104
  40.3 0.7 lt.103
  41.1 8.7 %copy.43 = bf16[1024,3072]{0,1:T(8,128)(2,1)} copy(bf16[1024,3072]{1,0:T(8,128)(2,1)} %param.9) | data formatting | bytes 12582912 | tf_op args[1]
  49.8 6.0 %fusion.4 = (bf16[1024,16,1,64]{0,3,2,1:T(8,128)(2,1)S(1)}, bf16[1024,16,1,64]{0,3,2,1:T(8,128)(2,1)}, bf16[1024,16,1,64]{0,3,2,1:T(8,128)(2,1)}) fusion(bf16[1024,16,3,64]{0,3,2,1:T(8,128)(2,1)} %bitcast.29), kind=kLoop, calls=%fused_computation.45 | loop fusion | bytes 12582912 | tf_op jit(solution)/shard_map/slice | solution.py:35
  55.8 4.0 %copy.49.refs_6_ = bf16[1024,1024]{1,0:T(8,128)(2,1)} copy(bf16[1024,1024]{0,1:T(8,128)(2,1)} %bitcast.40) | data formatting | bytes 4194304 | tf_op jit(solution)/shard_map/reshape;squeeze | solution.py:35
  59.7 2.6 %copy.50.refs_7_ = bf16[1024,1024]{1,0:T(8,128)(2,1)} copy(bf16[1024,1024]{0,1:T(8,128)(2,1)S(1)} %bitcast.37) | data formatting | bytes 4194304 | tf_op jit(solution)/shard_map/reshape;squeeze | solution.py:35
  62.5 1.3 compare_convert_fusion
  63.8 3.9 %convolution_convert_fusion.2 = bf16[512,1024]{1,0:T(8,128)(2,1)} fusion(bf16[512,1024]{1,0:T(8,128)(2,1)S(1)} %copy-done.1, bf16[1024,1024]{0,1:T(8,128)(2,1)} %bitcast.45), kind=kOutput, calls=%fused_computation.6 | convolution fusion | flops 1074266112 | bytes 4194304 | tf_op jit(solution)/shard_map/dot_general | solution.py:264
  67.7 0.5 multiply_add_fusion.ids_ref
  68.2 57.0 %collective-permute-done = bf16[64,1024]{1,0:T(8,128)(2,1)S(1)} collective-permute-done((bf16[64,1024]{1,0:T(8,128)(2,1)}, bf16[64,1024]{1,0:T(8,128)(2,1)S(1)}, u32[]{:S(2)}, u32[]{:S(2)}) %collective-permute-start) | collective-permute-done | bytes 131104 | tf_op jit(solution)/shard_map/ppermute | solution.py:245
  125.4 2.6 %convolution_convert_fusion.1 = bf16[640,1024]{1,0:T(8,128)(2,1)} fusion(bf16[640,1024]{1,0:T(8,128)(2,1)S(1)} %constant_dynamic-update-slice_fusion, bf16[1024,1024]{0,1:T(8,128)(2,1)S(1)} %bitcast.41), kind=kOutput, calls=%fused_computation.5 | convolution fusion | flops 1342832640 | bytes 4718592 | tf_op jit(solution)/shard_map/dot_general | solution.py:264
  128.0 2.6 %convolution_convert_fusion = bf16[640,1024]{1,0:T(8,128)(2,1)} fusion(bf16[640,1024]{1,0:T(8,128)(2,1)S(1)} %constant_dynamic-update-slice_fusion, bf16[1024,1024]{0,1:T(8,128)(2,1)S(1)} %bitcast.38), kind=kOutput, calls=%fused_computation.4 | convolution fusion | flops 1342832640 | bytes 4718592 | tf_op jit(solution)/shard_map/dot_general | solution.py:264
  130.6 1.5 convolution_convert_fusion.4.ks_ref
  132.1 1.6 convolution_convert_fusion.3.vs_ref
  133.7 22.2 %shard_map.64 = (f32[8,64,1024]{2,1,0:T(8,128)}, f32[8,64,1024]{2,1,0:T(8,128)}, f32[8,64,1024]{2,1,0:T(8,128)}) custom-call(s32[8,1,192]{2,1,0:T(1,128)} %get-tuple-element.25.mask_ref, bf16[8,64,1024]{2,1,0:T(8,128)(2,1)} %bitcast.43, bf16[10,64,1024]{2,1,0:T(8,128)(2,1)} %bitcast.31, bf16[10,64,1024]{2,1,0:T(8,128)(2,1)} %bitcast.32, ...), custom_call_target="tpu_custom_call" | custom-call | flops 1879048192 | bytes 14680064 | tf_op jit(solution)/shard_map/pallas_call | solution.py:156
  156.0 31.2 %shard_map.65 = bf16[8,64,1024]{2,1,0:T(8,128)(2,1)} custom-call(s32[24]{0:T(128)} %multiply_add_fusion.ids_ref, s32[8,1,192]{2,1,0:T(1,128)} %get-tuple-element.26.mask_ref, bf16[8,64,1024]{2,1,0:T(8,128)(2,1)} %bitcast.44, bf16[32,64,1024]{2,1,0:T(8,128)(2,1)} %bitcast.7.refs_0_.refs_1_.refs_2_.refs_3_.refs_4_.refs_5_, ...), custom_call_target="tpu_custom_call" | custom-call | flops 7247757312 | bytes 17825792 | tf_op jit(solution)/shard_map/pallas_call | solution.py:207
  (52 shorter events, 2.3 us)
Async XLA Ops:
  0.0 11.1 %copy-start.1 = (bf16[512,1024]{1,0:T(8,128)(2,1)S(1)}, bf16[512,1024]{1,0:T(8,128)(2,1)}, u32[]{:S(2)}) copy-start(bf16[512,1024]{1,0:T(8,128)(2,1)} %param.8) | copy-start | bytes 3145732
  0.0 10.0 %copy-start.5 = (s32[256,3]{0,1:T(4,128)S(1)}, s32[256,3]{0,1:T(4,128)}, u32[]{:S(2)}) copy-start(s32[256,3]{0,1:T(4,128)} %param.12) | copy-start | bytes 9220
  0.0 10.5 %copy-start.6 = (s32[256,3]{0,1:T(4,128)S(1)}, s32[256,3]{0,1:T(4,128)}, u32[]{:S(2)}) copy-start(s32[256,3]{0,1:T(4,128)} %param.13) | copy-start | bytes 9220
  3.9 19.2 %all-to-all-start = ((bf16[32,8,1024]{2,1,0:T(8,128)(2,1)}), bf16[32,8,1024]{2,1,0:T(8,128)(2,1)S(1)}, u32[]{:S(2)}, u32[]{:S(2)}) async-start(bf16[32,8,1024]{2,1,0:T(8,128)(2,1)} %broadcast_in_dim.39), calls=%async_computation | async-start | bytes 1048576 | tf_op jit(solution)/shard_map/all_to_all | solution.py:259
  23.1 0.8 copy-start.3
  23.9 132.1 %all-to-all-start.1 = ((bf16[8,4,64,1024]{3,2,1,0:T(8,128)(2,1)}), bf16[8,4,64,1024]{3,2,1,0:T(8,128)(2,1)}, u32[]{:S(2)}, u32[]{:S(2)}) async-start(bf16[8,4,64,1024]{3,2,1,0:T(8,128)(2,1)} %bitcast.30), calls=%async_computation.1 | async-start | bytes 8388608 | tf_op jit(solution)/shard_map/all_to_all | solution.py:261
  30.9 6.9 %copy-start = (s32[256]{0:T(256)S(1)}, s32[256]{0:T(256)}, u32[]{:S(2)}) copy-start(s32[256]{0:T(256)} %param.11) | copy-start | bytes 3076
  31.6 93.8 %collective-permute-start.1 = (bf16[64,1024]{1,0:T(8,128)(2,1)S(1)}, bf16[64,1024]{1,0:T(8,128)(2,1)S(1)}, u32[]{:S(2)}, u32[]{:S(2)}) collective-permute-start(bf16[64,1024]{1,0:T(8,128)(2,1)S(1)} %get-tuple-element.21), channel_id=1, source_target_pairs={{1,0},{2,1},{3,2},{4,3},{5,4},{6,5},{7,6},{8,7},{9,8},{10,9},{11,1... | collective-permute-start | bytes 393224 | tf_op jit(solution)/shard_map/ppermute | solution.py:246
  35.0 90.2 %collective-permute-start = (bf16[64,1024]{1,0:T(8,128)(2,1)}, bf16[64,1024]{1,0:T(8,128)(2,1)S(1)}, u32[]{:S(2)}, u32[]{:S(2)}) collective-permute-start(bf16[64,1024]{1,0:T(8,128)(2,1)} %get-tuple-element.22), channel_id=1, source_target_pairs={{0,1},{1,2},{2,3},{3,4},{4,5},{5,6},{6,7},{7,8},{8,9},{9,10},{10,1... | collective-permute-start | bytes 393224 | tf_op jit(solution)/shard_map/ppermute | solution.py:245
  67.7 57.7 %copy-start.2 = (bf16[1024,16,1,64]{0,3,2,1:T(8,128)(2,1)S(1)}, bf16[1024,16,1,64]{0,3,2,1:T(8,128)(2,1)}, u32[]{:S(2)}) copy-start(bf16[1024,16,1,64]{0,3,2,1:T(8,128)(2,1)} %get-tuple-element.19) | copy-start | bytes 6291460
  128.0 2.6 %copy-start.4 = (bf16[32,8,1024]{2,1,0:T(8,128)(2,1)S(1)}, bf16[32,8,1024]{2,1,0:T(8,128)(2,1)}, u32[]{:S(2)}) copy-start(bf16[32,8,1024]{2,1,0:T(8,128)(2,1)} %copy-done.3) | copy-start | bytes 1572868

commit v16 on v14

--- a/solution.py
+++ b/solution.py
@@ -153,7 +153,7 @@
 def attend_far(slot_ids, mask, q, incoming, w_kv, o_a, m_a, l_a, token_blocks, w_out):
     blocks, rows, width = q.shape
     model_dim = incoming.shape[-1]
-    group = 2 if blocks % 2 == 0 else 1
+    group = 4 if blocks % 4 == 0 else 1
     block = pl.BlockSpec((group, rows, width), lambda i, ids: (i, 0, 0))
     token_specs = [
         pl.BlockSpec(

time: 188 us -> 189 us (level)
  no operation moved by 1% of the time
where the time goes in v16:
time: 189 us; the launch traced here: 187 us
  waiting for transfers between devices  62.8 us (33%)
  Pallas kernels  53.1 us (28%)
  local copies, waits for them, and re-layouts  32 us (17%)
  starting transfers between devices  18.3 us (10%)
  matrix products  10.7 us (6%)
  other arithmetic  9.74 us (5%)
    ppermute x1, waiting for transfers between devices, local(): lax.ppermute(token_blocks[dev_blocks - 1], ('ctx', 'seq'), forward)  53.7 us
    pallas_call x1, Pallas kernels, attend_far(): pl.pallas_call(functools.partial(far_kernel, group), grid_spec=grid_spec,...  30.8 us
    pallas_call x1, Pallas kernels, attend_near(): pl.pallas_call(near_kernel, grid=(blocks,), in_specs=[pl.BlockSpec((1, 1,...  22.2 us
    dot_general x5, matrix products, local(): jnp.dot(x, w, preferred_element_type=jnp.float32).astype(jnp.bfloat16)  10.7 us
    unnamed x21, local copies, waits for them, and re-layouts  9.84 us
    all_to_all x1, waiting for transfers between devices, local(): lax.all_to_all(copies, ('ctx', 'seq'), 0, 0, tiled=True)  9.08 us
    all_to_all x1, starting transfers between devices, local(): lax.all_to_all(outgoing, 'ctx', split_axis=0, concat_axis=0, tiled=True)  6.99 us
    another operation x2, local copies, waits for them, and re-layouts, split_weights(): shaped[:, :, j, :].reshape(model_dim, head_total * HD)  6.55 us
  transfers between devices with their start and end apart: 4, of which 2 were waited for; matrix products, arithmetic and copies ran while one was open for 26% of the time, Pallas kernels for 12%

profile of v16, /device:TPU:16, one launch (start us, length us, event | category | flops | bytes accessed | tf_op | source)
XLA Modules:
  0.0 186.9 jit_solution(13380767351091251350)
XLA Ops:
  0.0 0.8 dynamic_slice.18
  1.1 1.6 select_reduce_fusion
  2.8 0.2 multiply_reduce_fusion
  3.0 0.9 broadcast_in_dim.39
  3.9 5.9 %all-to-all-start = ((bf16[32,8,1024]{2,1,0:T(8,128)(2,1)}), bf16[32,8,1024]{2,1,0:T(8,128)(2,1)S(1)}, u32[]{:S(2)}, u32[]{:S(2)}) async-start(bf16[32,8,1024]{2,1,0:T(8,128)(2,1)} %broadcast_in_dim.39), calls=%async_computation | async-start | bytes 1048576 | tf_op jit(solution)/shard_map/all_to_all | solution.py:234
  11.1 2.9 %gather_fusion = bf16[32,64,1024]{2,1,0:T(8,128)(2,1)} fusion(bf16[8,64,1024]{2,1,0:T(8,128)(2,1)S(1)} %bitcast.28, s32[1024]{0:T(1024)S(1)} %get-tuple-element.28), kind=kCustom, calls=%fused_computation.2 | custom fusion | bytes 8388736 | tf_op jit(solution)/shard_map/jit(_take)/gather | solution.py:215
  14.0 9.1 %all-to-all-done = bf16[32,8,1024]{2,1,0:T(8,128)(2,1)S(1)} async-done(((bf16[32,8,1024]{2,1,0:T(8,128)(2,1)}), bf16[32,8,1024]{2,1,0:T(8,128)(2,1)S(1)}, u32[]{:S(2)}, u32[]{:S(2)}) %all-to-all-start) | async-done | bytes 524320 | tf_op jit(solution)/shard_map/all_to_all | solution.py:234
  23.1 0.8 copy-done.4
  23.9 7.0 %all-to-all-start.1 = ((bf16[8,4,64,1024]{3,2,1,0:T(8,128)(2,1)}), bf16[8,4,64,1024]{3,2,1,0:T(8,128)(2,1)}, u32[]{:S(2)}, u32[]{:S(2)}) async-start(bf16[8,4,64,1024]{3,2,1,0:T(8,128)(2,1)} %bitcast.30), calls=%async_computation.1 | async-start | bytes 8388608 | tf_op jit(solution)/shard_map/all_to_all | solution.py:236
  30.9 0.7 fusion.5
  31.6 3.5 %collective-permute-start.1 = (bf16[64,1024]{1,0:T(8,128)(2,1)S(1)}, bf16[64,1024]{1,0:T(8,128)(2,1)S(1)}, u32[]{:S(2)}, u32[]{:S(2)}) collective-permute-start(bf16[64,1024]{1,0:T(8,128)(2,1)S(1)} %get-tuple-element.21), channel_id=1, source_target_pairs={{1,0},{2,1},{3,2},{4,3},{5,4},{6,5},{7,6},{8,7},{9,8},{10,9},{11,1... | collective-permute-start | bytes 393224 | tf_op jit(solution)/shard_map/ppermute | solution.py:221
  35.0 1.9 %collective-permute-start = (bf16[64,1024]{1,0:T(8,128)(2,1)}, bf16[64,1024]{1,0:T(8,128)(2,1)S(1)}, u32[]{:S(2)}, u32[]{:S(2)}) collective-permute-start(bf16[64,1024]{1,0:T(8,128)(2,1)} %get-tuple-element.22), channel_id=1, source_target_pairs={{0,1},{1,2},{2,3},{3,4},{4,5},{5,6},{6,7},{7,8},{8,9},{9,10},{10,1... | collective-permute-start | bytes 393224 | tf_op jit(solution)/shard_map/ppermute | solution.py:220
  37.0 0.7 lt.87
  37.8 0.7 gather_fusion.1
  38.6 0.7 gather_fusion.2
  39.5 0.7 lt.104
  40.3 0.7 lt.103
  41.1 8.7 %copy.43 = bf16[1024,3072]{0,1:T(8,128)(2,1)} copy(bf16[1024,3072]{1,0:T(8,128)(2,1)} %param.9) | data formatting | bytes 12582912 | tf_op args[1]
  49.8 6.0 %fusion.4 = (bf16[1024,16,1,64]{0,3,2,1:T(8,128)(2,1)S(1)}, bf16[1024,16,1,64]{0,3,2,1:T(8,128)(2,1)}, bf16[1024,16,1,64]{0,3,2,1:T(8,128)(2,1)}) fusion(bf16[1024,16,3,64]{0,3,2,1:T(8,128)(2,1)} %bitcast.29), kind=kLoop, calls=%fused_computation.46 | loop fusion | bytes 12582912 | tf_op jit(solution)/shard_map/slice | solution.py:35
  55.8 3.9 %copy.48 = bf16[1024,1024]{1,0:T(8,128)(2,1)} copy(bf16[1024,1024]{0,1:T(8,128)(2,1)} %bitcast.40) | data formatting | bytes 4194304 | tf_op jit(solution)/shard_map/reshape;squeeze | solution.py:35
  59.7 2.6 %copy.47 = bf16[1024,1024]{1,0:T(8,128)(2,1)} copy(bf16[1024,1024]{0,1:T(8,128)(2,1)S(1)} %bitcast.37) | data formatting | bytes 4194304 | tf_op jit(solution)/shard_map/reshape;squeeze | solution.py:35
  62.5 1.3 compare_convert_fusion
  63.8 4.8 %pad_maximum_fusion.refs_12_ = bf16[1024,2048]{1,0:T(8,128)(2,1)} fusion(bf16[1024,1024]{1,0:T(8,128)(2,1)} %copy.48, bf16[1024,1024]{1,0:T(8,128)(2,1)} %copy.47), kind=kLoop, calls=%fused_computation.3 | loop fusion | flops 8388608 | bytes 8388608 | tf_op jit(solution)/shard_map/concatenate | solution.py:268
  68.7 2.3 %convolution_convert_fusion.2 = bf16[512,1024]{1,0:T(8,128)(2,1)} fusion(bf16[512,1024]{1,0:T(8,128)(2,1)S(1)} %copy-done.1, bf16[1024,1024]{0,1:T(8,128)(2,1)S(1)} %bitcast.45), kind=kOutput, calls=%fused_computation.7 | convolution fusion | flops 1074266112 | bytes 4194304 | tf_op jit(solution)/shard_map/dot_general | solution.py:239
  71.0 0.6 multiply_add_fusion.ids_ref
  71.5 53.7 %collective-permute-done = bf16[64,1024]{1,0:T(8,128)(2,1)S(1)} collective-permute-done((bf16[64,1024]{1,0:T(8,128)(2,1)}, bf16[64,1024]{1,0:T(8,128)(2,1)S(1)}, u32[]{:S(2)}, u32[]{:S(2)}) %collective-permute-start) | collective-permute-done | bytes 131104 | tf_op jit(solution)/shard_map/ppermute | solution.py:220
  125.4 2.6 %convolution_convert_fusion = bf16[640,1024]{1,0:T(8,128)(2,1)} fusion(bf16[640,1024]{1,0:T(8,128)(2,1)S(1)} %constant_dynamic-update-slice_fusion, bf16[1024,1024]{0,1:T(8,128)(2,1)S(1)} %bitcast.41), kind=kOutput, calls=%fused_computation.5 | convolution fusion | flops 1342832640 | bytes 4718592 | tf_op jit(solution)/shard_map/dot_general | solution.py:239
  128.0 2.6 %convolution_convert_fusion.1 = bf16[640,1024]{1,0:T(8,128)(2,1)} fusion(bf16[640,1024]{1,0:T(8,128)(2,1)S(1)} %constant_dynamic-update-slice_fusion, bf16[1024,1024]{0,1:T(8,128)(2,1)S(1)} %bitcast.38), kind=kOutput, calls=%fused_computation.6 | convolution fusion | flops 1342832640 | bytes 4718592 | tf_op jit(solution)/shard_map/dot_general | solution.py:239
  130.6 1.6 convolution_convert_fusion.3.vs_ref
  132.2 1.5 convolution_convert_fusion.4.ks_ref
  133.7 22.2 %shard_map.64 = (f32[8,64,1024]{2,1,0:T(8,128)}, f32[8,64,1024]{2,1,0:T(8,128)}, f32[8,64,1024]{2,1,0:T(8,128)}) custom-call(s32[8,1,192]{2,1,0:T(1,128)} %get-tuple-element.25.mask_ref, bf16[8,64,1024]{2,1,0:T(8,128)(2,1)} %bitcast.43, bf16[10,64,1024]{2,1,0:T(8,128)(2,1)} %bitcast.34, bf16[10,64,1024]{2,1,0:T(8,128)(2,1)} %bitcast.35, ...), custom_call_target="tpu_custom_call" | custom-call | flops 1879048192 | bytes 14680064 | tf_op jit(solution)/shard_map/pallas_call | solution.py:137
  156.0 30.8 %shard_map.65 = bf16[8,64,1024]{2,1,0:T(8,128)(2,1)} custom-call(s32[24]{0:T(128)} %multiply_add_fusion.ids_ref, s32[8,1,192]{2,1,0:T(1,128)} %get-tuple-element.26.mask_ref, bf16[8,64,1024]{2,1,0:T(8,128)(2,1)} %bitcast.44, bf16[32,64,1024]{2,1,0:T(8,128)(2,1)} %bitcast.7.refs_0_.refs_1_.refs_2_.refs_3_.refs_4_.refs_5_.refs_6_.refs_7_.refs_8_.refs_9_.refs_10_.refs_11_, ...), custom_call_target="tpu_custom_call" | custom-call | flops 7247757312 | bytes 15728640 | tf_op jit(solution)/shard_map/pallas_call | solution.py:182
  (55 shorter events, 2.5 us)
Async XLA Ops:
  0.0 11.1 %copy-start.1 = (bf16[512,1024]{1,0:T(8,128)(2,1)S(1)}, bf16[512,1024]{1,0:T(8,128)(2,1)}, u32[]{:S(2)}) copy-start(bf16[512,1024]{1,0:T(8,128)(2,1)} %param.8) | copy-start | bytes 3145732
  0.0 10.0 %copy-start.6 = (s32[256,3]{0,1:T(4,128)S(1)}, s32[256,3]{0,1:T(4,128)}, u32[]{:S(2)}) copy-start(s32[256,3]{0,1:T(4,128)} %param.12) | copy-start | bytes 9220
  0.0 10.5 %copy-start.7 = (s32[256,3]{0,1:T(4,128)S(1)}, s32[256,3]{0,1:T(4,128)}, u32[]{:S(2)}) copy-start(s32[256,3]{0,1:T(4,128)} %param.13) | copy-start | bytes 9220
  3.9 19.2 %all-to-all-start = ((bf16[32,8,1024]{2,1,0:T(8,128)(2,1)}), bf16[32,8,1024]{2,1,0:T(8,128)(2,1)S(1)}, u32[]{:S(2)}, u32[]{:S(2)}) async-start(bf16[32,8,1024]{2,1,0:T(8,128)(2,1)} %broadcast_in_dim.39), calls=%async_computation | async-start | bytes 1048576 | tf_op jit(solution)/shard_map/all_to_all | solution.py:234
  23.1 0.8 copy-start.4
  23.9 132.1 %all-to-all-start.1 = ((bf16[8,4,64,1024]{3,2,1,0:T(8,128)(2,1)}), bf16[8,4,64,1024]{3,2,1,0:T(8,128)(2,1)}, u32[]{:S(2)}, u32[]{:S(2)}) async-start(bf16[8,4,64,1024]{3,2,1,0:T(8,128)(2,1)} %bitcast.30), calls=%async_computation.1 | async-start | bytes 8388608 | tf_op jit(solution)/shard_map/all_to_all | solution.py:236
  30.9 6.9 %copy-start = (s32[256]{0:T(256)S(1)}, s32[256]{0:T(256)}, u32[]{:S(2)}) copy-start(s32[256]{0:T(256)} %param.11) | copy-start | bytes 3076
  31.6 93.8 %collective-permute-start.1 = (bf16[64,1024]{1,0:T(8,128)(2,1)S(1)}, bf16[64,1024]{1,0:T(8,128)(2,1)S(1)}, u32[]{:S(2)}, u32[]{:S(2)}) collective-permute-start(bf16[64,1024]{1,0:T(8,128)(2,1)S(1)} %get-tuple-element.21), channel_id=1, source_target_pairs={{1,0},{2,1},{3,2},{4,3},{5,4},{6,5},{7,6},{8,7},{9,8},{10,9},{11,1... | collective-permute-start | bytes 393224 | tf_op jit(solution)/shard_map/ppermute | solution.py:221
  35.0 90.2 %collective-permute-start = (bf16[64,1024]{1,0:T(8,128)(2,1)}, bf16[64,1024]{1,0:T(8,128)(2,1)S(1)}, u32[]{:S(2)}, u32[]{:S(2)}) collective-permute-start(bf16[64,1024]{1,0:T(8,128)(2,1)} %get-tuple-element.22), channel_id=1, source_target_pairs={{0,1},{1,2},{2,3},{3,4},{4,5},{5,6},{6,7},{7,8},{8,9},{9,10},{10,1... | collective-permute-start | bytes 393224 | tf_op jit(solution)/shard_map/ppermute | solution.py:220
  63.8 4.8 %copy-start.3 = (bf16[1024,16,1,64]{0,3,2,1:T(8,128)(2,1)S(1)}, bf16[1024,16,1,64]{0,3,2,1:T(8,128)(2,1)}, u32[]{:S(2)}) copy-start(bf16[1024,16,1,64]{0,3,2,1:T(8,128)(2,1)} %get-tuple-element.20) | copy-start | bytes 6291460
  71.0 54.4 %copy-start.2 = (bf16[1024,16,1,64]{0,3,2,1:T(8,128)(2,1)S(1)}, bf16[1024,16,1,64]{0,3,2,1:T(8,128)(2,1)}, u32[]{:S(2)}) copy-start(bf16[1024,16,1,64]{0,3,2,1:T(8,128)(2,1)} %get-tuple-element.19) | copy-start | bytes 6291460
  128.0 2.6 %copy-start.5 = (bf16[32,8,1024]{2,1,0:T(8,128)(2,1)S(1)}, bf16[32,8,1024]{2,1,0:T(8,128)(2,1)}, u32[]{:S(2)}) copy-start(bf16[32,8,1024]{2,1,0:T(8,128)(2,1)} %copy-done.4) | copy-start | bytes 1572868

commit v17 on v14

--- a/solution.py
+++ b/solution.py
@@ -220,17 +220,18 @@
     prev_tokens = lax.ppermute(token_blocks[dev_blocks - 1], ("ctx", "seq"), forward)
     next_tokens = lax.ppermute(token_blocks[0], ("ctx", "seq"), backward)
 
-    usable = jnp.arange(BLK, dtype=jnp.int32)[None, :] < lax.dynamic_slice_in_dim(
-        counts, first_block, dev_blocks
-    )[:, None]
+    own = (first_block + jnp.arange(dev_blocks, dtype=jnp.int32))[:, None] == jnp.arange(
+        block_total, dtype=jnp.int32
+    )[None, :]
+    own_counts = jnp.sum(jnp.where(own, counts[None, :], 0), axis=1)
+    usable = jnp.arange(BLK, dtype=jnp.int32)[None, :] < own_counts[:, None]
     weighted = jnp.where(usable[:, :, None], token_blocks.astype(jnp.float32), 0.0)
     sums = jnp.sum(weighted, axis=1)
     members = jnp.sum(usable.astype(jnp.float32), axis=1)
     pooled = sums / members[:, None]
-    summary = (pooled / jnp.sqrt(jnp.mean(pooled * pooled, axis=1, keepdims=True) + 1e-05)).astype(
-        jnp.bfloat16
-    )
-    copies = jnp.broadcast_to(summary[None], (dev_count,) + summary.shape)
+    scale = jnp.sqrt(jnp.mean(pooled * pooled, axis=1, keepdims=True) + 1e-05)
+    copies = jnp.broadcast_to(pooled[None], (dev_count,) + pooled.shape)
+    copies = (copies / jnp.broadcast_to(scale[None], (dev_count,) + scale.shape)).astype(jnp.bfloat16)
     summary_all = lax.all_to_all(copies, ("ctx", "seq"), 0, 0, tiled=True).reshape(-1, model_dim)
     summary_all, outgoing = lax.optimization_barrier((summary_all, outgoing))
     incoming = lax.all_to_all(outgoing, "ctx", split_axis=0, concat_axis=0, tiled=True)

time: 188 us -> 188 us (level)
  no operation moved by 1% of the time
where the time goes in v17:
time: 188 us; the launch traced here: 186 us
  waiting for transfers between devices  62.9 us (33%)
  Pallas kernels  52.2 us (28%)
  local copies, waits for them, and re-layouts  30.3 us (16%)
  starting transfers between devices  18.3 us (10%)
  other arithmetic  11.5 us (6%)
  matrix products  10.7 us (6%)
    ppermute x1, waiting for transfers between devices, local(): lax.ppermute(token_blocks[dev_blocks - 1], ('ctx', 'seq'), forward)  53.8 us
    pallas_call x1, Pallas kernels, attend_far(): pl.pallas_call(functools.partial(far_kernel, group), grid_spec=grid_spec,...  29.9 us
    pallas_call x1, Pallas kernels, attend_near(): pl.pallas_call(near_kernel, grid=(blocks,), in_specs=[pl.BlockSpec((1, 1,...  22.2 us
    dot_general x5, matrix products, local(): jnp.dot(x, w, preferred_element_type=jnp.float32).astype(jnp.bfloat16)  10.7 us
    unnamed x21, local copies, waits for them, and re-layouts  9.84 us
    all_to_all x1, waiting for transfers between devices, local(): lax.all_to_all(copies, ('ctx', 'seq'), 0, 0, tiled=True)  9.09 us
    all_to_all x1, starting transfers between devices, local(): lax.all_to_all(outgoing, 'ctx', split_axis=0, concat_axis=0, tiled=True)  7 us
    another operation x2, local copies, waits for them, and re-layouts, split_weights(): shaped[:, :, j, :].reshape(model_dim, head_total * HD)  6.54 us
  transfers between devices with their start and end apart: 4, of which 2 were waited for; matrix products, arithmetic and copies ran while one was open for 26% of the time, Pallas kernels for 12%

profile of v17, /device:TPU:16, one launch (start us, length us, event | category | flops | bytes accessed | tf_op | source)
XLA Modules:
  0.0 186.2 jit_solution(17353224491217635417)
XLA Ops:
  0.0 0.9 select_reduce_fusion.3
  1.2 1.6 select_reduce_fusion
  2.9 0.2 multiply_reduce_fusion
  3.1 0.9 divide_convert_fusion
  4.0 5.9 %all-to-all-start = ((bf16[32,8,1024]{2,1,0:T(8,128)(2,1)}), bf16[32,8,1024]{2,1,0:T(8,128)(2,1)S(1)}, u32[]{:S(2)}, u32[]{:S(2)}) async-start(bf16[32,8,1024]{2,1,0:T(8,128)(2,1)} %divide_convert_fusion), calls=%async_computation | async-start | bytes 1048576 | tf_op jit(solution)/shard_map/all_to_all | solution.py:235
  11.2 2.9 %gather_fusion = bf16[32,64,1024]{2,1,0:T(8,128)(2,1)} fusion(bf16[8,64,1024]{2,1,0:T(8,128)(2,1)S(1)} %bitcast.28, s32[1024]{0:T(1024)S(1)} %get-tuple-element.30), kind=kCustom, calls=%fused_computation.2 | custom fusion | bytes 8388736 | tf_op jit(solution)/shard_map/jit(_take)/gather | solution.py:215
  14.1 9.1 %all-to-all-done = bf16[32,8,1024]{2,1,0:T(8,128)(2,1)S(1)} async-done(((bf16[32,8,1024]{2,1,0:T(8,128)(2,1)}), bf16[32,8,1024]{2,1,0:T(8,128)(2,1)S(1)}, u32[]{:S(2)}, u32[]{:S(2)}) %all-to-all-start) | async-done | bytes 524320 | tf_op jit(solution)/shard_map/all_to_all | solution.py:235
  23.2 0.8 copy-done.4
  24.0 7.0 %all-to-all-start.1 = ((bf16[8,4,64,1024]{3,2,1,0:T(8,128)(2,1)}), bf16[8,4,64,1024]{3,2,1,0:T(8,128)(2,1)}, u32[]{:S(2)}, u32[]{:S(2)}) async-start(bf16[8,4,64,1024]{3,2,1,0:T(8,128)(2,1)} %bitcast.30), calls=%async_computation.1 | async-start | bytes 8388608 | tf_op jit(solution)/shard_map/all_to_all | solution.py:237
  31.0 0.7 fusion.5
  31.7 3.5 %collective-permute-start.1 = (bf16[64,1024]{1,0:T(8,128)(2,1)S(1)}, bf16[64,1024]{1,0:T(8,128)(2,1)S(1)}, u32[]{:S(2)}, u32[]{:S(2)}) collective-permute-start(bf16[64,1024]{1,0:T(8,128)(2,1)S(1)} %get-tuple-element.23), channel_id=1, source_target_pairs={{1,0},{2,1},{3,2},{4,3},{5,4},{6,5},{7,6},{8,7},{9,8},{10,9},{11,1... | collective-permute-start | bytes 393224 | tf_op jit(solution)/shard_map/ppermute | solution.py:221
  35.1 1.9 %collective-permute-start = (bf16[64,1024]{1,0:T(8,128)(2,1)}, bf16[64,1024]{1,0:T(8,128)(2,1)S(1)}, u32[]{:S(2)}, u32[]{:S(2)}) collective-permute-start(bf16[64,1024]{1,0:T(8,128)(2,1)} %get-tuple-element.24), channel_id=1, source_target_pairs={{0,1},{1,2},{2,3},{3,4},{4,5},{5,6},{6,7},{7,8},{8,9},{9,10},{10,1... | collective-permute-start | bytes 393224 | tf_op jit(solution)/shard_map/ppermute | solution.py:220
  37.1 0.6 lt.86
  37.9 0.7 gather_fusion.1
  38.7 0.7 gather_fusion.2
  39.6 0.7 lt.103
  40.4 0.7 lt.102
  41.2 8.7 %copy.43 = bf16[1024,3072]{0,1:T(8,128)(2,1)} copy(bf16[1024,3072]{1,0:T(8,128)(2,1)} %param.9) | data formatting | bytes 12582912 | tf_op args[1]
  49.9 6.0 %fusion.4 = (bf16[1024,16,1,64]{0,3,2,1:T(8,128)(2,1)S(1)}, bf16[1024,16,1,64]{0,3,2,1:T(8,128)(2,1)}, bf16[1024,16,1,64]{0,3,2,1:T(8,128)(2,1)}) fusion(bf16[1024,16,3,64]{0,3,2,1:T(8,128)(2,1)} %bitcast.29), kind=kLoop, calls=%fused_computation.49 | loop fusion | bytes 12582912 | tf_op jit(solution)/shard_map/slice | solution.py:35
  55.9 3.9 %copy.48 = bf16[1024,1024]{1,0:T(8,128)(2,1)} copy(bf16[1024,1024]{0,1:T(8,128)(2,1)} %bitcast.40) | data formatting | bytes 4194304 | tf_op jit(solution)/shard_map/reshape;squeeze | solution.py:35
  59.8 2.6 %copy.47 = bf16[1024,1024]{1,0:T(8,128)(2,1)} copy(bf16[1024,1024]{0,1:T(8,128)(2,1)S(1)} %bitcast.37) | data formatting | bytes 4194304 | tf_op jit(solution)/shard_map/reshape;squeeze | solution.py:35
  62.6 1.3 compare_convert_fusion
  63.9 4.8 %pad_maximum_fusion.refs_6_ = bf16[1024,2048]{1,0:T(8,128)(2,1)} fusion(bf16[1024,1024]{1,0:T(8,128)(2,1)} %copy.48, bf16[1024,1024]{1,0:T(8,128)(2,1)} %copy.47), kind=kLoop, calls=%fused_computation.3 | loop fusion | flops 8388608 | bytes 8388608 | tf_op jit(solution)/shard_map/concatenate | solution.py:269
  68.7 2.3 %convolution_convert_fusion.2 = bf16[512,1024]{1,0:T(8,128)(2,1)} fusion(bf16[512,1024]{1,0:T(8,128)(2,1)S(1)} %copy-done.1, bf16[1024,1024]{0,1:T(8,128)(2,1)S(1)} %bitcast.45), kind=kOutput, calls=%fused_computation.7 | convolution fusion | flops 1074266112 | bytes 4194304 | tf_op jit(solution)/shard_map/dot_general | solution.py:240
  71.0 0.5 multiply_add_fusion.ids_ref
  71.6 53.8 %collective-permute-done = bf16[64,1024]{1,0:T(8,128)(2,1)S(1)} collective-permute-done((bf16[64,1024]{1,0:T(8,128)(2,1)}, bf16[64,1024]{1,0:T(8,128)(2,1)S(1)}, u32[]{:S(2)}, u32[]{:S(2)}) %collective-permute-start) | collective-permute-done | bytes 131104 | tf_op jit(solution)/shard_map/ppermute | solution.py:220
  125.5 2.6 %convolution_convert_fusion = bf16[640,1024]{1,0:T(8,128)(2,1)} fusion(bf16[640,1024]{1,0:T(8,128)(2,1)S(1)} %constant_dynamic-update-slice_fusion, bf16[1024,1024]{0,1:T(8,128)(2,1)S(1)} %bitcast.41), kind=kOutput, calls=%fused_computation.5 | convolution fusion | flops 1342832640 | bytes 4718592 | tf_op jit(solution)/shard_map/dot_general | solution.py:240
  128.1 2.6 %convolution_convert_fusion.1 = bf16[640,1024]{1,0:T(8,128)(2,1)} fusion(bf16[640,1024]{1,0:T(8,128)(2,1)S(1)} %constant_dynamic-update-slice_fusion, bf16[1024,1024]{0,1:T(8,128)(2,1)S(1)} %bitcast.38), kind=kOutput, calls=%fused_computation.6 | convolution fusion | flops 1342832640 | bytes 4718592 | tf_op jit(solution)/shard_map/dot_general | solution.py:240
  130.7 1.6 convolution_convert_fusion.3.vs_ref
  132.3 1.5 convolution_convert_fusion.4.ks_ref
  133.8 22.2 %shard_map.64 = (f32[8,64,1024]{2,1,0:T(8,128)}, f32[8,64,1024]{2,1,0:T(8,128)}, f32[8,64,1024]{2,1,0:T(8,128)}) custom-call(s32[8,1,192]{2,1,0:T(1,128)} %get-tuple-element.27.mask_ref, bf16[8,64,1024]{2,1,0:T(8,128)(2,1)} %bitcast.43, bf16[10,64,1024]{2,1,0:T(8,128)(2,1)} %bitcast.34, bf16[10,64,1024]{2,1,0:T(8,128)(2,1)} %bitcast.35, ...), custom_call_target="tpu_custom_call" | custom-call | flops 1879048192 | bytes 14680064 | tf_op jit(solution)/shard_map/pallas_call | solution.py:137
  156.1 29.9 %shard_map.65 = bf16[8,64,1024]{2,1,0:T(8,128)(2,1)} custom-call(s32[24]{0:T(128)} %multiply_add_fusion.ids_ref, s32[8,1,192]{2,1,0:T(1,128)} %get-tuple-element.28.mask_ref, bf16[8,64,1024]{2,1,0:T(8,128)(2,1)} %bitcast.44, bf16[32,64,1024]{2,1,0:T(8,128)(2,1)} %bitcast.7.refs_0_.refs_1_.refs_2_.refs_3_.refs_4_.refs_5_, ...), custom_call_target="tpu_custom_call" | custom-call | flops 7247757312 | bytes 15728640 | tf_op jit(solution)/shard_map/pallas_call | solution.py:182
  (54 shorter events, 2.4 us)
Async XLA Ops:
  0.0 11.2 %copy-start.1 = (bf16[512,1024]{1,0:T(8,128)(2,1)S(1)}, bf16[512,1024]{1,0:T(8,128)(2,1)}, u32[]{:S(2)}) copy-start(bf16[512,1024]{1,0:T(8,128)(2,1)} %param.8) | copy-start | bytes 3145732
  0.0 10.1 %copy-start.6 = (s32[256,3]{0,1:T(4,128)S(1)}, s32[256,3]{0,1:T(4,128)}, u32[]{:S(2)}) copy-start(s32[256,3]{0,1:T(4,128)} %param.12) | copy-start | bytes 9220
  0.0 10.6 %copy-start.7 = (s32[256,3]{0,1:T(4,128)S(1)}, s32[256,3]{0,1:T(4,128)}, u32[]{:S(2)}) copy-start(s32[256,3]{0,1:T(4,128)} %param.13) | copy-start | bytes 9220
  4.0 19.2 %all-to-all-start = ((bf16[32,8,1024]{2,1,0:T(8,128)(2,1)}), bf16[32,8,1024]{2,1,0:T(8,128)(2,1)S(1)}, u32[]{:S(2)}, u32[]{:S(2)}) async-start(bf16[32,8,1024]{2,1,0:T(8,128)(2,1)} %divide_convert_fusion), calls=%async_computation | async-start | bytes 1048576 | tf_op jit(solution)/shard_map/all_to_all | solution.py:235
  23.2 0.8 copy-start.4
  24.0 132.0 %all-to-all-start.1 = ((bf16[8,4,64,1024]{3,2,1,0:T(8,128)(2,1)}), bf16[8,4,64,1024]{3,2,1,0:T(8,128)(2,1)}, u32[]{:S(2)}, u32[]{:S(2)}) async-start(bf16[8,4,64,1024]{3,2,1,0:T(8,128)(2,1)} %bitcast.30), calls=%async_computation.1 | async-start | bytes 8388608 | tf_op jit(solution)/shard_map/all_to_all | solution.py:237
  31.0 6.9 %copy-start = (s32[256]{0:T(256)S(1)}, s32[256]{0:T(256)}, u32[]{:S(2)}) copy-start(s32[256]{0:T(256)} %param.11) | copy-start | bytes 3076
  31.7 93.8 %collective-permute-start.1 = (bf16[64,1024]{1,0:T(8,128)(2,1)S(1)}, bf16[64,1024]{1,0:T(8,128)(2,1)S(1)}, u32[]{:S(2)}, u32[]{:S(2)}) collective-permute-start(bf16[64,1024]{1,0:T(8,128)(2,1)S(1)} %get-tuple-element.23), channel_id=1, source_target_pairs={{1,0},{2,1},{3,2},{4,3},{5,4},{6,5},{7,6},{8,7},{9,8},{10,9},{11,1... | collective-permute-start | bytes 393224 | tf_op jit(solution)/shard_map/ppermute | solution.py:221
  35.1 90.2 %collective-permute-start = (bf16[64,1024]{1,0:T(8,128)(2,1)}, bf16[64,1024]{1,0:T(8,128)(2,1)S(1)}, u32[]{:S(2)}, u32[]{:S(2)}) collective-permute-start(bf16[64,1024]{1,0:T(8,128)(2,1)} %get-tuple-element.24), channel_id=1, source_target_pairs={{0,1},{1,2},{2,3},{3,4},{4,5},{5,6},{6,7},{7,8},{8,9},{9,10},{10,1... | collective-permute-start | bytes 393224 | tf_op jit(solution)/shard_map/ppermute | solution.py:220
  63.9 4.8 %copy-start.3 = (bf16[1024,16,1,64]{0,3,2,1:T(8,128)(2,1)S(1)}, bf16[1024,16,1,64]{0,3,2,1:T(8,128)(2,1)}, u32[]{:S(2)}) copy-start(bf16[1024,16,1,64]{0,3,2,1:T(8,128)(2,1)} %get-tuple-element.22) | copy-start | bytes 6291460
  71.0 54.4 %copy-start.2 = (bf16[1024,16,1,64]{0,3,2,1:T(8,128)(2,1)S(1)}, bf16[1024,16,1,64]{0,3,2,1:T(8,128)(2,1)}, u32[]{:S(2)}) copy-start(bf16[1024,16,1,64]{0,3,2,1:T(8,128)(2,1)} %get-tuple-element.21) | copy-start | bytes 6291460
  128.1 2.6 %copy-start.5 = (bf16[32,8,1024]{2,1,0:T(8,128)(2,1)S(1)}, bf16[32,8,1024]{2,1,0:T(8,128)(2,1)}, u32[]{:S(2)}) copy-start(bf16[32,8,1024]{2,1,0:T(8,128)(2,1)} %copy-done.4) | copy-start | bytes 1572868

commit v18 on v17

--- a/solution.py
+++ b/solution.py
@@ -85,14 +85,14 @@
     rows = q_ref.shape[1]
     scaling = 1.0 / math.sqrt(HD)
     low = lax.broadcasted_iota(jnp.int32, (rows, LANES), 1) < HD
-    far_tokens = jnp.concatenate([ref[0] for ref in token_refs], axis=0)
-    kv_far = jnp.dot(far_tokens, wkv_ref[...], preferred_element_type=jnp.float32).astype(
-        jnp.bfloat16
-    )
-    keys = RAND * rows
     for g in range(group):
         valid = mask_ref[g] != 0
-        kv_rows = kv_far[g * keys : (g + 1) * keys]
+        far_tokens = jnp.concatenate(
+            [ref[0] for ref in token_refs[g * RAND : (g + 1) * RAND]], axis=0
+        )
+        kv_rows = jnp.dot(far_tokens, wkv_ref[...], preferred_element_type=jnp.float32).astype(
+            jnp.bfloat16
+        )
         for tile in range(width // LANES):
             lanes = slice(tile * LANES, (tile + 1) * LANES)
             value_lanes = slice(width + tile * LANES, width + (tile + 1) * LANES)

time: 188 us -> 187 us (level)
  no operation moved by 1% of the time
where the time goes in v18:
time: 187 us; the launch traced here: 185 us
  waiting for transfers between devices  62.9 us (34%)
  Pallas kernels  51.3 us (27%)
  local copies, waits for them, and re-layouts  30.3 us (16%)
  starting transfers between devices  18.3 us (10%)
  other arithmetic  11.5 us (6%)
  matrix products  10.7 us (6%)
    ppermute x1, waiting for transfers between devices, local(): lax.ppermute(token_blocks[dev_blocks - 1], ('ctx', 'seq'), forward)  53.8 us
    pallas_call x1, Pallas kernels, attend_far(): pl.pallas_call(functools.partial(far_kernel, group), grid_spec=grid_spec,...  29.1 us
    pallas_call x1, Pallas kernels, attend_near(): pl.pallas_call(near_kernel, grid=(blocks,), in_specs=[pl.BlockSpec((1, 1,...  22.2 us
    dot_general x5, matrix products, local(): jnp.dot(x, w, preferred_element_type=jnp.float32).astype(jnp.bfloat16)  10.7 us
    unnamed x21, local copies, waits for them, and re-layouts  9.84 us
    all_to_all x1, waiting for transfers between devices, local(): lax.all_to_all(copies, ('ctx', 'seq'), 0, 0, tiled=True)  9.09 us
    all_to_all x1, starting transfers between devices, local(): lax.all_to_all(outgoing, 'ctx', split_axis=0, concat_axis=0, tiled=True)  7 us
    another operation x2, local copies, waits for them, and re-layouts, split_weights(): shaped[:, :, j, :].reshape(model_dim, head_total * HD)  6.54 us
  transfers between devices with their start and end apart: 4, of which 2 were waited for; matrix products, arithmetic and copies ran while one was open for 26% of the time, Pallas kernels for 12%

profile of v18, /device:TPU:16, one launch (start us, length us, event | category | flops | bytes accessed | tf_op | source)
XLA Modules:
  0.0 185.3 jit_solution(5429945990054334226)
XLA Ops:
  0.0 0.9 select_reduce_fusion.3
  1.2 1.6 select_reduce_fusion
  2.9 0.2 multiply_reduce_fusion
  3.1 0.9 divide_convert_fusion
  4.0 5.9 %all-to-all-start = ((bf16[32,8,1024]{2,1,0:T(8,128)(2,1)}), bf16[32,8,1024]{2,1,0:T(8,128)(2,1)S(1)}, u32[]{:S(2)}, u32[]{:S(2)}) async-start(bf16[32,8,1024]{2,1,0:T(8,128)(2,1)} %divide_convert_fusion), calls=%async_computation | async-start | bytes 1048576 | tf_op jit(solution)/shard_map/all_to_all | solution.py:235
  11.2 2.9 %gather_fusion = bf16[32,64,1024]{2,1,0:T(8,128)(2,1)} fusion(bf16[8,64,1024]{2,1,0:T(8,128)(2,1)S(1)} %bitcast.28, s32[1024]{0:T(1024)S(1)} %get-tuple-element.30), kind=kCustom, calls=%fused_computation.2 | custom fusion | bytes 8388736 | tf_op jit(solution)/shard_map/jit(_take)/gather | solution.py:215
  14.1 9.1 %all-to-all-done = bf16[32,8,1024]{2,1,0:T(8,128)(2,1)S(1)} async-done(((bf16[32,8,1024]{2,1,0:T(8,128)(2,1)}), bf16[32,8,1024]{2,1,0:T(8,128)(2,1)S(1)}, u32[]{:S(2)}, u32[]{:S(2)}) %all-to-all-start) | async-done | bytes 524320 | tf_op jit(solution)/shard_map/all_to_all | solution.py:235
  23.2 0.8 copy-done.4
  24.0 7.0 %all-to-all-start.1 = ((bf16[8,4,64,1024]{3,2,1,0:T(8,128)(2,1)}), bf16[8,4,64,1024]{3,2,1,0:T(8,128)(2,1)}, u32[]{:S(2)}, u32[]{:S(2)}) async-start(bf16[8,4,64,1024]{3,2,1,0:T(8,128)(2,1)} %bitcast.30), calls=%async_computation.1 | async-start | bytes 8388608 | tf_op jit(solution)/shard_map/all_to_all | solution.py:237
  31.0 0.7 fusion.5
  31.7 3.5 %collective-permute-start.1 = (bf16[64,1024]{1,0:T(8,128)(2,1)S(1)}, bf16[64,1024]{1,0:T(8,128)(2,1)S(1)}, u32[]{:S(2)}, u32[]{:S(2)}) collective-permute-start(bf16[64,1024]{1,0:T(8,128)(2,1)S(1)} %get-tuple-element.23), channel_id=1, source_target_pairs={{1,0},{2,1},{3,2},{4,3},{5,4},{6,5},{7,6},{8,7},{9,8},{10,9},{11,1... | collective-permute-start | bytes 393224 | tf_op jit(solution)/shard_map/ppermute | solution.py:221
  35.1 1.9 %collective-permute-start = (bf16[64,1024]{1,0:T(8,128)(2,1)}, bf16[64,1024]{1,0:T(8,128)(2,1)S(1)}, u32[]{:S(2)}, u32[]{:S(2)}) collective-permute-start(bf16[64,1024]{1,0:T(8,128)(2,1)} %get-tuple-element.24), channel_id=1, source_target_pairs={{0,1},{1,2},{2,3},{3,4},{4,5},{5,6},{6,7},{7,8},{8,9},{9,10},{10,1... | collective-permute-start | bytes 393224 | tf_op jit(solution)/shard_map/ppermute | solution.py:220
  37.1 0.6 lt.86
  37.9 0.7 gather_fusion.1
  38.7 0.7 gather_fusion.2
  39.6 0.7 lt.103
  40.4 0.7 lt.102
  41.2 8.7 %copy.43 = bf16[1024,3072]{0,1:T(8,128)(2,1)} copy(bf16[1024,3072]{1,0:T(8,128)(2,1)} %param.9) | data formatting | bytes 12582912 | tf_op args[1]
  49.9 6.0 %fusion.4 = (bf16[1024,16,1,64]{0,3,2,1:T(8,128)(2,1)S(1)}, bf16[1024,16,1,64]{0,3,2,1:T(8,128)(2,1)}, bf16[1024,16,1,64]{0,3,2,1:T(8,128)(2,1)}) fusion(bf16[1024,16,3,64]{0,3,2,1:T(8,128)(2,1)} %bitcast.29), kind=kLoop, calls=%fused_computation.49 | loop fusion | bytes 12582912 | tf_op jit(solution)/shard_map/slice | solution.py:35
  55.9 3.9 %copy.48 = bf16[1024,1024]{1,0:T(8,128)(2,1)} copy(bf16[1024,1024]{0,1:T(8,128)(2,1)} %bitcast.40) | data formatting | bytes 4194304 | tf_op jit(solution)/shard_map/reshape;squeeze | solution.py:35
  59.8 2.6 %copy.47 = bf16[1024,1024]{1,0:T(8,128)(2,1)} copy(bf16[1024,1024]{0,1:T(8,128)(2,1)S(1)} %bitcast.37) | data formatting | bytes 4194304 | tf_op jit(solution)/shard_map/reshape;squeeze | solution.py:35
  62.6 1.3 compare_convert_fusion
  63.9 4.8 %pad_maximum_fusion.refs_6_ = bf16[1024,2048]{1,0:T(8,128)(2,1)} fusion(bf16[1024,1024]{1,0:T(8,128)(2,1)} %copy.48, bf16[1024,1024]{1,0:T(8,128)(2,1)} %copy.47), kind=kLoop, calls=%fused_computation.3 | loop fusion | flops 8388608 | bytes 8388608 | tf_op jit(solution)/shard_map/concatenate | solution.py:269
  68.7 2.3 %convolution_convert_fusion.2 = bf16[512,1024]{1,0:T(8,128)(2,1)} fusion(bf16[512,1024]{1,0:T(8,128)(2,1)S(1)} %copy-done.1, bf16[1024,1024]{0,1:T(8,128)(2,1)S(1)} %bitcast.45), kind=kOutput, calls=%fused_computation.7 | convolution fusion | flops 1074266112 | bytes 4194304 | tf_op jit(solution)/shard_map/dot_general | solution.py:240
  71.0 0.5 multiply_add_fusion.ids_ref
  71.6 53.8 %collective-permute-done = bf16[64,1024]{1,0:T(8,128)(2,1)S(1)} collective-permute-done((bf16[64,1024]{1,0:T(8,128)(2,1)}, bf16[64,1024]{1,0:T(8,128)(2,1)S(1)}, u32[]{:S(2)}, u32[]{:S(2)}) %collective-permute-start) | collective-permute-done | bytes 131104 | tf_op jit(solution)/shard_map/ppermute | solution.py:220
  125.5 2.6 %convolution_convert_fusion = bf16[640,1024]{1,0:T(8,128)(2,1)} fusion(bf16[640,1024]{1,0:T(8,128)(2,1)S(1)} %constant_dynamic-update-slice_fusion, bf16[1024,1024]{0,1:T(8,128)(2,1)S(1)} %bitcast.41), kind=kOutput, calls=%fused_computation.5 | convolution fusion | flops 1342832640 | bytes 4718592 | tf_op jit(solution)/shard_map/dot_general | solution.py:240
  128.1 2.6 %convolution_convert_fusion.1 = bf16[640,1024]{1,0:T(8,128)(2,1)} fusion(bf16[640,1024]{1,0:T(8,128)(2,1)S(1)} %constant_dynamic-update-slice_fusion, bf16[1024,1024]{0,1:T(8,128)(2,1)S(1)} %bitcast.38), kind=kOutput, calls=%fused_computation.6 | convolution fusion | flops 1342832640 | bytes 4718592 | tf_op jit(solution)/shard_map/dot_general | solution.py:240
  130.7 1.6 convolution_convert_fusion.3.vs_ref
  132.3 1.5 convolution_convert_fusion.4.ks_ref
  133.8 22.2 %shard_map.64 = (f32[8,64,1024]{2,1,0:T(8,128)}, f32[8,64,1024]{2,1,0:T(8,128)}, f32[8,64,1024]{2,1,0:T(8,128)}) custom-call(s32[8,1,192]{2,1,0:T(1,128)} %get-tuple-element.27.mask_ref, bf16[8,64,1024]{2,1,0:T(8,128)(2,1)} %bitcast.43, bf16[10,64,1024]{2,1,0:T(8,128)(2,1)} %bitcast.34, bf16[10,64,1024]{2,1,0:T(8,128)(2,1)} %bitcast.35, ...), custom_call_target="tpu_custom_call" | custom-call | flops 1879048192 | bytes 14680064 | tf_op jit(solution)/shard_map/pallas_call | solution.py:137
  156.1 29.1 %shard_map.65 = bf16[8,64,1024]{2,1,0:T(8,128)(2,1)} custom-call(s32[24]{0:T(128)} %multiply_add_fusion.ids_ref, s32[8,1,192]{2,1,0:T(1,128)} %get-tuple-element.28.mask_ref, bf16[8,64,1024]{2,1,0:T(8,128)(2,1)} %bitcast.44, bf16[32,64,1024]{2,1,0:T(8,128)(2,1)} %bitcast.7.refs_0_.refs_1_.refs_2_.refs_3_.refs_4_.refs_5_, ...), custom_call_target="tpu_custom_call" | custom-call | flops 7247757312 | bytes 15728640 | tf_op jit(solution)/shard_map/pallas_call | solution.py:182
  (54 shorter events, 2.4 us)
Async XLA Ops:
  0.0 11.2 %copy-start.1 = (bf16[512,1024]{1,0:T(8,128)(2,1)S(1)}, bf16[512,1024]{1,0:T(8,128)(2,1)}, u32[]{:S(2)}) copy-start(bf16[512,1024]{1,0:T(8,128)(2,1)} %param.8) | copy-start | bytes 3145732
  0.0 10.1 %copy-start.6 = (s32[256,3]{0,1:T(4,128)S(1)}, s32[256,3]{0,1:T(4,128)}, u32[]{:S(2)}) copy-start(s32[256,3]{0,1:T(4,128)} %param.12) | copy-start | bytes 9220
  0.0 10.6 %copy-start.7 = (s32[256,3]{0,1:T(4,128)S(1)}, s32[256,3]{0,1:T(4,128)}, u32[]{:S(2)}) copy-start(s32[256,3]{0,1:T(4,128)} %param.13) | copy-start | bytes 9220
  4.0 19.2 %all-to-all-start = ((bf16[32,8,1024]{2,1,0:T(8,128)(2,1)}), bf16[32,8,1024]{2,1,0:T(8,128)(2,1)S(1)}, u32[]{:S(2)}, u32[]{:S(2)}) async-start(bf16[32,8,1024]{2,1,0:T(8,128)(2,1)} %divide_convert_fusion), calls=%async_computation | async-start | bytes 1048576 | tf_op jit(solution)/shard_map/all_to_all | solution.py:235
  23.2 0.8 copy-start.4
  24.0 132.0 %all-to-all-start.1 = ((bf16[8,4,64,1024]{3,2,1,0:T(8,128)(2,1)}), bf16[8,4,64,1024]{3,2,1,0:T(8,128)(2,1)}, u32[]{:S(2)}, u32[]{:S(2)}) async-start(bf16[8,4,64,1024]{3,2,1,0:T(8,128)(2,1)} %bitcast.30), calls=%async_computation.1 | async-start | bytes 8388608 | tf_op jit(solution)/shard_map/all_to_all | solution.py:237
  31.0 6.9 %copy-start = (s32[256]{0:T(256)S(1)}, s32[256]{0:T(256)}, u32[]{:S(2)}) copy-start(s32[256]{0:T(256)} %param.11) | copy-start | bytes 3076
  31.7 93.8 %collective-permute-start.1 = (bf16[64,1024]{1,0:T(8,128)(2,1)S(1)}, bf16[64,1024]{1,0:T(8,128)(2,1)S(1)}, u32[]{:S(2)}, u32[]{:S(2)}) collective-permute-start(bf16[64,1024]{1,0:T(8,128)(2,1)S(1)} %get-tuple-element.23), channel_id=1, source_target_pairs={{1,0},{2,1},{3,2},{4,3},{5,4},{6,5},{7,6},{8,7},{9,8},{10,9},{11,1... | collective-permute-start | bytes 393224 | tf_op jit(solution)/shard_map/ppermute | solution.py:221
  35.1 90.2 %collective-permute-start = (bf16[64,1024]{1,0:T(8,128)(2,1)}, bf16[64,1024]{1,0:T(8,128)(2,1)S(1)}, u32[]{:S(2)}, u32[]{:S(2)}) collective-permute-start(bf16[64,1024]{1,0:T(8,128)(2,1)} %get-tuple-element.24), channel_id=1, source_target_pairs={{0,1},{1,2},{2,3},{3,4},{4,5},{5,6},{6,7},{7,8},{8,9},{9,10},{10,1... | collective-permute-start | bytes 393224 | tf_op jit(solution)/shard_map/ppermute | solution.py:220
  63.9 4.8 %copy-start.3 = (bf16[1024,16,1,64]{0,3,2,1:T(8,128)(2,1)S(1)}, bf16[1024,16,1,64]{0,3,2,1:T(8,128)(2,1)}, u32[]{:S(2)}) copy-start(bf16[1024,16,1,64]{0,3,2,1:T(8,128)(2,1)} %get-tuple-element.22) | copy-start | bytes 6291460
  71.0 54.4 %copy-start.2 = (bf16[1024,16,1,64]{0,3,2,1:T(8,128)(2,1)S(1)}, bf16[1024,16,1,64]{0,3,2,1:T(8,128)(2,1)}, u32[]{:S(2)}) copy-start(bf16[1024,16,1,64]{0,3,2,1:T(8,128)(2,1)} %get-tuple-element.21) | copy-start | bytes 6291460
  128.1 2.6 %copy-start.5 = (bf16[32,8,1024]{2,1,0:T(8,128)(2,1)S(1)}, bf16[32,8,1024]{2,1,0:T(8,128)(2,1)}, u32[]{:S(2)}) copy-start(bf16[32,8,1024]{2,1,0:T(8,128)(2,1)} %copy-done.4) | copy-start | bytes 1572868

commit v19 on v18

--- a/solution.py
+++ b/solution.py
@@ -153,7 +153,7 @@
 def attend_far(slot_ids, mask, q, incoming, w_kv, o_a, m_a, l_a, token_blocks, w_out):
     blocks, rows, width = q.shape
     model_dim = incoming.shape[-1]
-    group = 2 if blocks % 2 == 0 else 1
+    group = 4 if blocks % 4 == 0 else 1
     block = pl.BlockSpec((group, rows, width), lambda i, ids: (i, 0, 0))
     token_specs = [
         pl.BlockSpec(

time: 187 us -> 187 us (level)
  no operation moved by 1% of the time
where the time goes in v19:
time: 187 us; the launch traced here: 186 us
  waiting for transfers between devices  62.9 us (34%)
  Pallas kernels  51.7 us (28%)
  local copies, waits for them, and re-layouts  30.3 us (16%)
  starting transfers between devices  18.3 us (10%)
  other arithmetic  11.5 us (6%)
  matrix products  10.7 us (6%)
    ppermute x1, waiting for transfers between devices, local(): lax.ppermute(token_blocks[dev_blocks - 1], ('ctx', 'seq'), forward)  53.8 us
    pallas_call x1, Pallas kernels, attend_far(): pl.pallas_call(functools.partial(far_kernel, group), grid_spec=grid_spec,...  29.5 us
    pallas_call x1, Pallas kernels, attend_near(): pl.pallas_call(near_kernel, grid=(blocks,), in_specs=[pl.BlockSpec((1, 1,...  22.2 us
    dot_general x5, matrix products, local(): jnp.dot(x, w, preferred_element_type=jnp.float32).astype(jnp.bfloat16)  10.7 us
    unnamed x21, local copies, waits for them, and re-layouts  9.84 us
    all_to_all x1, waiting for transfers between devices, local(): lax.all_to_all(copies, ('ctx', 'seq'), 0, 0, tiled=True)  9.09 us
    all_to_all x1, starting transfers between devices, local(): lax.all_to_all(outgoing, 'ctx', split_axis=0, concat_axis=0, tiled=True)  7 us
    another operation x2, local copies, waits for them, and re-layouts, split_weights(): shaped[:, :, j, :].reshape(model_dim, head_total * HD)  6.54 us
  transfers between devices with their start and end apart: 4, of which 2 were waited for; matrix products, arithmetic and copies ran while one was open for 26% of the time, Pallas kernels for 12%

profile of v19, /device:TPU:16, one launch (start us, length us, event | category | flops | bytes accessed | tf_op | source)
XLA Modules:
  0.0 185.7 jit_solution(12667549072037620561)
XLA Ops:
  0.0 0.9 select_reduce_fusion.3
  1.2 1.6 select_reduce_fusion
  2.9 0.2 multiply_reduce_fusion
  3.1 0.9 divide_convert_fusion
  4.0 5.9 %all-to-all-start = ((bf16[32,8,1024]{2,1,0:T(8,128)(2,1)}), bf16[32,8,1024]{2,1,0:T(8,128)(2,1)S(1)}, u32[]{:S(2)}, u32[]{:S(2)}) async-start(bf16[32,8,1024]{2,1,0:T(8,128)(2,1)} %divide_convert_fusion), calls=%async_computation | async-start | bytes 1048576 | tf_op jit(solution)/shard_map/all_to_all | solution.py:235
  11.2 2.9 %gather_fusion = bf16[32,64,1024]{2,1,0:T(8,128)(2,1)} fusion(bf16[8,64,1024]{2,1,0:T(8,128)(2,1)S(1)} %bitcast.28, s32[1024]{0:T(1024)S(1)} %get-tuple-element.30), kind=kCustom, calls=%fused_computation.2 | custom fusion | bytes 8388736 | tf_op jit(solution)/shard_map/jit(_take)/gather | solution.py:215
  14.1 9.1 %all-to-all-done = bf16[32,8,1024]{2,1,0:T(8,128)(2,1)S(1)} async-done(((bf16[32,8,1024]{2,1,0:T(8,128)(2,1)}), bf16[32,8,1024]{2,1,0:T(8,128)(2,1)S(1)}, u32[]{:S(2)}, u32[]{:S(2)}) %all-to-all-start) | async-done | bytes 524320 | tf_op jit(solution)/shard_map/all_to_all | solution.py:235
  23.2 0.8 copy-done.4
  24.0 7.0 %all-to-all-start.1 = ((bf16[8,4,64,1024]{3,2,1,0:T(8,128)(2,1)}), bf16[8,4,64,1024]{3,2,1,0:T(8,128)(2,1)}, u32[]{:S(2)}, u32[]{:S(2)}) async-start(bf16[8,4,64,1024]{3,2,1,0:T(8,128)(2,1)} %bitcast.30), calls=%async_computation.1 | async-start | bytes 8388608 | tf_op jit(solution)/shard_map/all_to_all | solution.py:237
  31.0 0.7 fusion.5
  31.7 3.5 %collective-permute-start.1 = (bf16[64,1024]{1,0:T(8,128)(2,1)S(1)}, bf16[64,1024]{1,0:T(8,128)(2,1)S(1)}, u32[]{:S(2)}, u32[]{:S(2)}) collective-permute-start(bf16[64,1024]{1,0:T(8,128)(2,1)S(1)} %get-tuple-element.23), channel_id=1, source_target_pairs={{1,0},{2,1},{3,2},{4,3},{5,4},{6,5},{7,6},{8,7},{9,8},{10,9},{11,1... | collective-permute-start | bytes 393224 | tf_op jit(solution)/shard_map/ppermute | solution.py:221
  35.1 1.9 %collective-permute-start = (bf16[64,1024]{1,0:T(8,128)(2,1)}, bf16[64,1024]{1,0:T(8,128)(2,1)S(1)}, u32[]{:S(2)}, u32[]{:S(2)}) collective-permute-start(bf16[64,1024]{1,0:T(8,128)(2,1)} %get-tuple-element.24), channel_id=1, source_target_pairs={{0,1},{1,2},{2,3},{3,4},{4,5},{5,6},{6,7},{7,8},{8,9},{9,10},{10,1... | collective-permute-start | bytes 393224 | tf_op jit(solution)/shard_map/ppermute | solution.py:220
  37.1 0.6 lt.86
  37.9 0.7 gather_fusion.1
  38.7 0.7 gather_fusion.2
  39.6 0.7 lt.103
  40.4 0.7 lt.102
  41.2 8.7 %copy.43 = bf16[1024,3072]{0,1:T(8,128)(2,1)} copy(bf16[1024,3072]{1,0:T(8,128)(2,1)} %param.9) | data formatting | bytes 12582912 | tf_op args[1]
  49.9 6.0 %fusion.4 = (bf16[1024,16,1,64]{0,3,2,1:T(8,128)(2,1)S(1)}, bf16[1024,16,1,64]{0,3,2,1:T(8,128)(2,1)}, bf16[1024,16,1,64]{0,3,2,1:T(8,128)(2,1)}) fusion(bf16[1024,16,3,64]{0,3,2,1:T(8,128)(2,1)} %bitcast.29), kind=kLoop, calls=%fused_computation.49 | loop fusion | bytes 12582912 | tf_op jit(solution)/shard_map/slice | solution.py:35
  55.9 3.9 %copy.48 = bf16[1024,1024]{1,0:T(8,128)(2,1)} copy(bf16[1024,1024]{0,1:T(8,128)(2,1)} %bitcast.40) | data formatting | bytes 4194304 | tf_op jit(solution)/shard_map/reshape;squeeze | solution.py:35
  59.8 2.6 %copy.47 = bf16[1024,1024]{1,0:T(8,128)(2,1)} copy(bf16[1024,1024]{0,1:T(8,128)(2,1)S(1)} %bitcast.37) | data formatting | bytes 4194304 | tf_op jit(solution)/shard_map/reshape;squeeze | solution.py:35
  62.6 1.3 compare_convert_fusion
  63.9 4.8 %pad_maximum_fusion.refs_12_ = bf16[1024,2048]{1,0:T(8,128)(2,1)} fusion(bf16[1024,1024]{1,0:T(8,128)(2,1)} %copy.48, bf16[1024,1024]{1,0:T(8,128)(2,1)} %copy.47), kind=kLoop, calls=%fused_computation.3 | loop fusion | flops 8388608 | bytes 8388608 | tf_op jit(solution)/shard_map/concatenate | solution.py:269
  68.7 2.3 %convolution_convert_fusion.2 = bf16[512,1024]{1,0:T(8,128)(2,1)} fusion(bf16[512,1024]{1,0:T(8,128)(2,1)S(1)} %copy-done.1, bf16[1024,1024]{0,1:T(8,128)(2,1)S(1)} %bitcast.45), kind=kOutput, calls=%fused_computation.7 | convolution fusion | flops 1074266112 | bytes 4194304 | tf_op jit(solution)/shard_map/dot_general | solution.py:240
  71.0 0.5 multiply_add_fusion.ids_ref
  71.6 53.8 %collective-permute-done = bf16[64,1024]{1,0:T(8,128)(2,1)S(1)} collective-permute-done((bf16[64,1024]{1,0:T(8,128)(2,1)}, bf16[64,1024]{1,0:T(8,128)(2,1)S(1)}, u32[]{:S(2)}, u32[]{:S(2)}) %collective-permute-start) | collective-permute-done | bytes 131104 | tf_op jit(solution)/shard_map/ppermute | solution.py:220
  125.5 2.6 %convolution_convert_fusion = bf16[640,1024]{1,0:T(8,128)(2,1)} fusion(bf16[640,1024]{1,0:T(8,128)(2,1)S(1)} %constant_dynamic-update-slice_fusion, bf16[1024,1024]{0,1:T(8,128)(2,1)S(1)} %bitcast.41), kind=kOutput, calls=%fused_computation.5 | convolution fusion | flops 1342832640 | bytes 4718592 | tf_op jit(solution)/shard_map/dot_general | solution.py:240
  128.1 2.6 %convolution_convert_fusion.1 = bf16[640,1024]{1,0:T(8,128)(2,1)} fusion(bf16[640,1024]{1,0:T(8,128)(2,1)S(1)} %constant_dynamic-update-slice_fusion, bf16[1024,1024]{0,1:T(8,128)(2,1)S(1)} %bitcast.38), kind=kOutput, calls=%fused_computation.6 | convolution fusion | flops 1342832640 | bytes 4718592 | tf_op jit(solution)/shard_map/dot_general | solution.py:240
  130.7 1.6 convolution_convert_fusion.3.vs_ref
  132.3 1.5 convolution_convert_fusion.4.ks_ref
  133.8 22.2 %shard_map.64 = (f32[8,64,1024]{2,1,0:T(8,128)}, f32[8,64,1024]{2,1,0:T(8,128)}, f32[8,64,1024]{2,1,0:T(8,128)}) custom-call(s32[8,1,192]{2,1,0:T(1,128)} %get-tuple-element.27.mask_ref, bf16[8,64,1024]{2,1,0:T(8,128)(2,1)} %bitcast.43, bf16[10,64,1024]{2,1,0:T(8,128)(2,1)} %bitcast.34, bf16[10,64,1024]{2,1,0:T(8,128)(2,1)} %bitcast.35, ...), custom_call_target="tpu_custom_call" | custom-call | flops 1879048192 | bytes 14680064 | tf_op jit(solution)/shard_map/pallas_call | solution.py:137
  156.1 29.5 %shard_map.65 = bf16[8,64,1024]{2,1,0:T(8,128)(2,1)} custom-call(s32[24]{0:T(128)} %multiply_add_fusion.ids_ref, s32[8,1,192]{2,1,0:T(1,128)} %get-tuple-element.28.mask_ref, bf16[8,64,1024]{2,1,0:T(8,128)(2,1)} %bitcast.44, bf16[32,64,1024]{2,1,0:T(8,128)(2,1)} %bitcast.7.refs_0_.refs_1_.refs_2_.refs_3_.refs_4_.refs_5_.refs_6_.refs_7_.refs_8_.refs_9_.refs_10_.refs_11_, ...), custom_call_target="tpu_custom_call" | custom-call | flops 7247757312 | bytes 15728640 | tf_op jit(solution)/shard_map/pallas_call | solution.py:182
  (54 shorter events, 2.4 us)
Async XLA Ops:
  0.0 11.2 %copy-start.1 = (bf16[512,1024]{1,0:T(8,128)(2,1)S(1)}, bf16[512,1024]{1,0:T(8,128)(2,1)}, u32[]{:S(2)}) copy-start(bf16[512,1024]{1,0:T(8,128)(2,1)} %param.8) | copy-start | bytes 3145732
  0.0 10.1 %copy-start.6 = (s32[256,3]{0,1:T(4,128)S(1)}, s32[256,3]{0,1:T(4,128)}, u32[]{:S(2)}) copy-start(s32[256,3]{0,1:T(4,128)} %param.12) | copy-start | bytes 9220
  0.0 10.6 %copy-start.7 = (s32[256,3]{0,1:T(4,128)S(1)}, s32[256,3]{0,1:T(4,128)}, u32[]{:S(2)}) copy-start(s32[256,3]{0,1:T(4,128)} %param.13) | copy-start | bytes 9220
  4.0 19.2 %all-to-all-start = ((bf16[32,8,1024]{2,1,0:T(8,128)(2,1)}), bf16[32,8,1024]{2,1,0:T(8,128)(2,1)S(1)}, u32[]{:S(2)}, u32[]{:S(2)}) async-start(bf16[32,8,1024]{2,1,0:T(8,128)(2,1)} %divide_convert_fusion), calls=%async_computation | async-start | bytes 1048576 | tf_op jit(solution)/shard_map/all_to_all | solution.py:235
  23.2 0.8 copy-start.4
  24.0 132.0 %all-to-all-start.1 = ((bf16[8,4,64,1024]{3,2,1,0:T(8,128)(2,1)}), bf16[8,4,64,1024]{3,2,1,0:T(8,128)(2,1)}, u32[]{:S(2)}, u32[]{:S(2)}) async-start(bf16[8,4,64,1024]{3,2,1,0:T(8,128)(2,1)} %bitcast.30), calls=%async_computation.1 | async-start | bytes 8388608 | tf_op jit(solution)/shard_map/all_to_all | solution.py:237
  31.0 6.9 %copy-start = (s32[256]{0:T(256)S(1)}, s32[256]{0:T(256)}, u32[]{:S(2)}) copy-start(s32[256]{0:T(256)} %param.11) | copy-start | bytes 3076
  31.7 93.8 %collective-permute-start.1 = (bf16[64,1024]{1,0:T(8,128)(2,1)S(1)}, bf16[64,1024]{1,0:T(8,128)(2,1)S(1)}, u32[]{:S(2)}, u32[]{:S(2)}) collective-permute-start(bf16[64,1024]{1,0:T(8,128)(2,1)S(1)} %get-tuple-element.23), channel_id=1, source_target_pairs={{1,0},{2,1},{3,2},{4,3},{5,4},{6,5},{7,6},{8,7},{9,8},{10,9},{11,1... | collective-permute-start | bytes 393224 | tf_op jit(solution)/shard_map/ppermute | solution.py:221
  35.1 90.2 %collective-permute-start = (bf16[64,1024]{1,0:T(8,128)(2,1)}, bf16[64,1024]{1,0:T(8,128)(2,1)S(1)}, u32[]{:S(2)}, u32[]{:S(2)}) collective-permute-start(bf16[64,1024]{1,0:T(8,128)(2,1)} %get-tuple-element.24), channel_id=1, source_target_pairs={{0,1},{1,2},{2,3},{3,4},{4,5},{5,6},{6,7},{7,8},{8,9},{9,10},{10,1... | collective-permute-start | bytes 393224 | tf_op jit(solution)/shard_map/ppermute | solution.py:220
  63.9 4.8 %copy-start.3 = (bf16[1024,16,1,64]{0,3,2,1:T(8,128)(2,1)S(1)}, bf16[1024,16,1,64]{0,3,2,1:T(8,128)(2,1)}, u32[]{:S(2)}) copy-start(bf16[1024,16,1,64]{0,3,2,1:T(8,128)(2,1)} %get-tuple-element.22) | copy-start | bytes 6291460
  71.0 54.4 %copy-start.2 = (bf16[1024,16,1,64]{0,3,2,1:T(8,128)(2,1)S(1)}, bf16[1024,16,1,64]{0,3,2,1:T(8,128)(2,1)}, u32[]{:S(2)}) copy-start(bf16[1024,16,1,64]{0,3,2,1:T(8,128)(2,1)} %get-tuple-element.21) | copy-start | bytes 6291460
  128.1 2.6 %copy-start.5 = (bf16[32,8,1024]{2,1,0:T(8,128)(2,1)S(1)}, bf16[32,8,1024]{2,1,0:T(8,128)(2,1)}, u32[]{:S(2)}) copy-start(bf16[32,8,1024]{2,1,0:T(8,128)(2,1)} %copy-done.4) | copy-start | bytes 1572868

commit v20 on v18

--- a/solution.py
+++ b/solution.py
@@ -118,10 +118,10 @@
             numerator = oa_ref[g, :, cols] * scale_a + o_b * scale_b
             denominator = la_ref[g, :, cols] * scale_a + l_b * scale_b
             att_ref[g * rows : (g + 1) * rows, cols] = (numerator / denominator).astype(att_ref.dtype)
-    mixed = jnp.dot(att_ref[...], wo_ref[...], preferred_element_type=jnp.float32)
-    for g in range(group):
-        part = mixed[g * rows : (g + 1) * rows] + tok_ref[g].astype(jnp.float32)
-        out_ref[g] = part.astype(out_ref.dtype)
+        mixed = jnp.dot(
+            att_ref[g * rows : (g + 1) * rows, :], wo_ref[...], preferred_element_type=jnp.float32
+        )
+        out_ref[g] = (mixed + tok_ref[g].astype(jnp.float32)).astype(out_ref.dtype)
 
 
 def attend_near(mask, q, k_ext, v_ext, k_sum, v_sum):

time: 187 us -> 189 us (1.011)
  transfers between devices with their start and end apart: 4 -> 4, of which waited for: 2 -> 2; matrix products, arithmetic and copies ran while one was open for 26% -> 25% of each run, Pallas kernels for 12% -> 12%
where the time goes in v20:
time: 189 us; the launch traced here: 187 us
  waiting for transfers between devices  62.9 us (33%)
  Pallas kernels  52.9 us (28%)
  local copies, waits for them, and re-layouts  30.3 us (16%)
  starting transfers between devices  18.3 us (10%)
  other arithmetic  11.5 us (6%)
  matrix products  10.7 us (6%)
    ppermute x1, waiting for transfers between devices, local(): lax.ppermute(token_blocks[dev_blocks - 1], ('ctx', 'seq'), forward)  53.8 us
    pallas_call x1, Pallas kernels, attend_far(): pl.pallas_call(functools.partial(far_kernel, group), grid_spec=grid_spec,...  30.7 us
    pallas_call x1, Pallas kernels, attend_near(): pl.pallas_call(near_kernel, grid=(blocks,), in_specs=[pl.BlockSpec((1, 1,...  22.2 us
    dot_general x5, matrix products, local(): jnp.dot(x, w, preferred_element_type=jnp.float32).astype(jnp.bfloat16)  10.7 us
    unnamed x21, local copies, waits for them, and re-layouts  9.84 us
    all_to_all x1, waiting for transfers between devices, local(): lax.all_to_all(copies, ('ctx', 'seq'), 0, 0, tiled=True)  9.09 us
    all_to_all x1, starting transfers between devices, local(): lax.all_to_all(outgoing, 'ctx', split_axis=0, concat_axis=0, tiled=True)  7 us
    another operation x2, local copies, waits for them, and re-layouts, split_weights(): shaped[:, :, j, :].reshape(model_dim, head_total * HD)  6.54 us
  transfers between devices with their start and end apart: 4, of which 2 were waited for; matrix products, arithmetic and copies ran while one was open for 25% of the time, Pallas kernels for 12%

profile of v20, /device:TPU:16, one launch (start us, length us, event | category | flops | bytes accessed | tf_op | source)
XLA Modules:
  0.0 186.9 jit_solution(8632014624675005762)
XLA Ops:
  0.0 0.9 select_reduce_fusion.3
  1.2 1.6 select_reduce_fusion
  2.9 0.2 multiply_reduce_fusion
  3.1 0.9 divide_convert_fusion
  4.0 5.9 %all-to-all-start = ((bf16[32,8,1024]{2,1,0:T(8,128)(2,1)}), bf16[32,8,1024]{2,1,0:T(8,128)(2,1)S(1)}, u32[]{:S(2)}, u32[]{:S(2)}) async-start(bf16[32,8,1024]{2,1,0:T(8,128)(2,1)} %divide_convert_fusion), calls=%async_computation | async-start | bytes 1048576 | tf_op jit(solution)/shard_map/all_to_all | solution.py:235
  11.2 2.9 %gather_fusion = bf16[32,64,1024]{2,1,0:T(8,128)(2,1)} fusion(bf16[8,64,1024]{2,1,0:T(8,128)(2,1)S(1)} %bitcast.28, s32[1024]{0:T(1024)S(1)} %get-tuple-element.30), kind=kCustom, calls=%fused_computation.2 | custom fusion | bytes 8388736 | tf_op jit(solution)/shard_map/jit(_take)/gather | solution.py:215
  14.1 9.1 %all-to-all-done = bf16[32,8,1024]{2,1,0:T(8,128)(2,1)S(1)} async-done(((bf16[32,8,1024]{2,1,0:T(8,128)(2,1)}), bf16[32,8,1024]{2,1,0:T(8,128)(2,1)S(1)}, u32[]{:S(2)}, u32[]{:S(2)}) %all-to-all-start) | async-done | bytes 524320 | tf_op jit(solution)/shard_map/all_to_all | solution.py:235
  23.2 0.8 copy-done.4
  24.0 7.0 %all-to-all-start.1 = ((bf16[8,4,64,1024]{3,2,1,0:T(8,128)(2,1)}), bf16[8,4,64,1024]{3,2,1,0:T(8,128)(2,1)}, u32[]{:S(2)}, u32[]{:S(2)}) async-start(bf16[8,4,64,1024]{3,2,1,0:T(8,128)(2,1)} %bitcast.30), calls=%async_computation.1 | async-start | bytes 8388608 | tf_op jit(solution)/shard_map/all_to_all | solution.py:237
  31.0 0.7 fusion.5
  31.7 3.5 %collective-permute-start.1 = (bf16[64,1024]{1,0:T(8,128)(2,1)S(1)}, bf16[64,1024]{1,0:T(8,128)(2,1)S(1)}, u32[]{:S(2)}, u32[]{:S(2)}) collective-permute-start(bf16[64,1024]{1,0:T(8,128)(2,1)S(1)} %get-tuple-element.23), channel_id=1, source_target_pairs={{1,0},{2,1},{3,2},{4,3},{5,4},{6,5},{7,6},{8,7},{9,8},{10,9},{11,1... | collective-permute-start | bytes 393224 | tf_op jit(solution)/shard_map/ppermute | solution.py:221
  35.1 1.9 %collective-permute-start = (bf16[64,1024]{1,0:T(8,128)(2,1)}, bf16[64,1024]{1,0:T(8,128)(2,1)S(1)}, u32[]{:S(2)}, u32[]{:S(2)}) collective-permute-start(bf16[64,1024]{1,0:T(8,128)(2,1)} %get-tuple-element.24), channel_id=1, source_target_pairs={{0,1},{1,2},{2,3},{3,4},{4,5},{5,6},{6,7},{7,8},{8,9},{9,10},{10,1... | collective-permute-start | bytes 393224 | tf_op jit(solution)/shard_map/ppermute | solution.py:220
  37.1 0.6 lt.86
  37.9 0.7 gather_fusion.1
  38.7 0.7 gather_fusion.2
  39.6 0.7 lt.103
  40.4 0.7 lt.102
  41.2 8.7 %copy.43 = bf16[1024,3072]{0,1:T(8,128)(2,1)} copy(bf16[1024,3072]{1,0:T(8,128)(2,1)} %param.9) | data formatting | bytes 12582912 | tf_op args[1]
  49.9 6.0 %fusion.4 = (bf16[1024,16,1,64]{0,3,2,1:T(8,128)(2,1)S(1)}, bf16[1024,16,1,64]{0,3,2,1:T(8,128)(2,1)}, bf16[1024,16,1,64]{0,3,2,1:T(8,128)(2,1)}) fusion(bf16[1024,16,3,64]{0,3,2,1:T(8,128)(2,1)} %bitcast.29), kind=kLoop, calls=%fused_computation.49 | loop fusion | bytes 12582912 | tf_op jit(solution)/shard_map/slice | solution.py:35
  55.9 3.9 %copy.48 = bf16[1024,1024]{1,0:T(8,128)(2,1)} copy(bf16[1024,1024]{0,1:T(8,128)(2,1)} %bitcast.40) | data formatting | bytes 4194304 | tf_op jit(solution)/shard_map/reshape;squeeze | solution.py:35
  59.8 2.6 %copy.47 = bf16[1024,1024]{1,0:T(8,128)(2,1)} copy(bf16[1024,1024]{0,1:T(8,128)(2,1)S(1)} %bitcast.37) | data formatting | bytes 4194304 | tf_op jit(solution)/shard_map/reshape;squeeze | solution.py:35
  62.6 1.3 compare_convert_fusion
  63.9 4.8 %pad_maximum_fusion.refs_6_ = bf16[1024,2048]{1,0:T(8,128)(2,1)} fusion(bf16[1024,1024]{1,0:T(8,128)(2,1)} %copy.48, bf16[1024,1024]{1,0:T(8,128)(2,1)} %copy.47), kind=kLoop, calls=%fused_computation.3 | loop fusion | flops 8388608 | bytes 8388608 | tf_op jit(solution)/shard_map/concatenate | solution.py:269
  68.7 2.3 %convolution_convert_fusion.2 = bf16[512,1024]{1,0:T(8,128)(2,1)} fusion(bf16[512,1024]{1,0:T(8,128)(2,1)S(1)} %copy-done.1, bf16[1024,1024]{0,1:T(8,128)(2,1)S(1)} %bitcast.45), kind=kOutput, calls=%fused_computation.7 | convolution fusion | flops 1074266112 | bytes 4194304 | tf_op jit(solution)/shard_map/dot_general | solution.py:240
  71.0 0.5 multiply_add_fusion.ids_ref
  71.6 53.8 %collective-permute-done = bf16[64,1024]{1,0:T(8,128)(2,1)S(1)} collective-permute-done((bf16[64,1024]{1,0:T(8,128)(2,1)}, bf16[64,1024]{1,0:T(8,128)(2,1)S(1)}, u32[]{:S(2)}, u32[]{:S(2)}) %collective-permute-start) | collective-permute-done | bytes 131104 | tf_op jit(solution)/shard_map/ppermute | solution.py:220
  125.5 2.6 %convolution_convert_fusion = bf16[640,1024]{1,0:T(8,128)(2,1)} fusion(bf16[640,1024]{1,0:T(8,128)(2,1)S(1)} %constant_dynamic-update-slice_fusion, bf16[1024,1024]{0,1:T(8,128)(2,1)S(1)} %bitcast.41), kind=kOutput, calls=%fused_computation.5 | convolution fusion | flops 1342832640 | bytes 4718592 | tf_op jit(solution)/shard_map/dot_general | solution.py:240
  128.1 2.6 %convolution_convert_fusion.1 = bf16[640,1024]{1,0:T(8,128)(2,1)} fusion(bf16[640,1024]{1,0:T(8,128)(2,1)S(1)} %constant_dynamic-update-slice_fusion, bf16[1024,1024]{0,1:T(8,128)(2,1)S(1)} %bitcast.38), kind=kOutput, calls=%fused_computation.6 | convolution fusion | flops 1342832640 | bytes 4718592 | tf_op jit(solution)/shard_map/dot_general | solution.py:240
  130.7 1.6 convolution_convert_fusion.3.vs_ref
  132.3 1.5 convolution_convert_fusion.4.ks_ref
  133.8 22.2 %shard_map.64 = (f32[8,64,1024]{2,1,0:T(8,128)}, f32[8,64,1024]{2,1,0:T(8,128)}, f32[8,64,1024]{2,1,0:T(8,128)}) custom-call(s32[8,1,192]{2,1,0:T(1,128)} %get-tuple-element.27.mask_ref, bf16[8,64,1024]{2,1,0:T(8,128)(2,1)} %bitcast.43, bf16[10,64,1024]{2,1,0:T(8,128)(2,1)} %bitcast.34, bf16[10,64,1024]{2,1,0:T(8,128)(2,1)} %bitcast.35, ...), custom_call_target="tpu_custom_call" | custom-call | flops 1879048192 | bytes 14680064 | tf_op jit(solution)/shard_map/pallas_call | solution.py:137
  156.1 30.7 %shard_map.65 = bf16[8,64,1024]{2,1,0:T(8,128)(2,1)} custom-call(s32[24]{0:T(128)} %multiply_add_fusion.ids_ref, s32[8,1,192]{2,1,0:T(1,128)} %get-tuple-element.28.mask_ref, bf16[8,64,1024]{2,1,0:T(8,128)(2,1)} %bitcast.44, bf16[32,64,1024]{2,1,0:T(8,128)(2,1)} %bitcast.7.refs_0_.refs_1_.refs_2_.refs_3_.refs_4_.refs_5_, ...), custom_call_target="tpu_custom_call" | custom-call | flops 7247757312 | bytes 15728640 | tf_op jit(solution)/shard_map/pallas_call | solution.py:182
  (54 shorter events, 2.4 us)
Async XLA Ops:
  0.0 11.2 %copy-start.1 = (bf16[512,1024]{1,0:T(8,128)(2,1)S(1)}, bf16[512,1024]{1,0:T(8,128)(2,1)}, u32[]{:S(2)}) copy-start(bf16[512,1024]{1,0:T(8,128)(2,1)} %param.8) | copy-start | bytes 3145732
  0.0 10.1 %copy-start.6 = (s32[256,3]{0,1:T(4,128)S(1)}, s32[256,3]{0,1:T(4,128)}, u32[]{:S(2)}) copy-start(s32[256,3]{0,1:T(4,128)} %param.12) | copy-start | bytes 9220
  0.0 10.6 %copy-start.7 = (s32[256,3]{0,1:T(4,128)S(1)}, s32[256,3]{0,1:T(4,128)}, u32[]{:S(2)}) copy-start(s32[256,3]{0,1:T(4,128)} %param.13) | copy-start | bytes 9220
  4.0 19.2 %all-to-all-start = ((bf16[32,8,1024]{2,1,0:T(8,128)(2,1)}), bf16[32,8,1024]{2,1,0:T(8,128)(2,1)S(1)}, u32[]{:S(2)}, u32[]{:S(2)}) async-start(bf16[32,8,1024]{2,1,0:T(8,128)(2,1)} %divide_convert_fusion), calls=%async_computation | async-start | bytes 1048576 | tf_op jit(solution)/shard_map/all_to_all | solution.py:235
  23.2 0.8 copy-start.4
  24.0 132.0 %all-to-all-start.1 = ((bf16[8,4,64,1024]{3,2,1,0:T(8,128)(2,1)}), bf16[8,4,64,1024]{3,2,1,0:T(8,128)(2,1)}, u32[]{:S(2)}, u32[]{:S(2)}) async-start(bf16[8,4,64,1024]{3,2,1,0:T(8,128)(2,1)} %bitcast.30), calls=%async_computation.1 | async-start | bytes 8388608 | tf_op jit(solution)/shard_map/all_to_all | solution.py:237
  31.0 6.9 %copy-start = (s32[256]{0:T(256)S(1)}, s32[256]{0:T(256)}, u32[]{:S(2)}) copy-start(s32[256]{0:T(256)} %param.11) | copy-start | bytes 3076
  31.7 93.8 %collective-permute-start.1 = (bf16[64,1024]{1,0:T(8,128)(2,1)S(1)}, bf16[64,1024]{1,0:T(8,128)(2,1)S(1)}, u32[]{:S(2)}, u32[]{:S(2)}) collective-permute-start(bf16[64,1024]{1,0:T(8,128)(2,1)S(1)} %get-tuple-element.23), channel_id=1, source_target_pairs={{1,0},{2,1},{3,2},{4,3},{5,4},{6,5},{7,6},{8,7},{9,8},{10,9},{11,1... | collective-permute-start | bytes 393224 | tf_op jit(solution)/shard_map/ppermute | solution.py:221
  35.1 90.2 %collective-permute-start = (bf16[64,1024]{1,0:T(8,128)(2,1)}, bf16[64,1024]{1,0:T(8,128)(2,1)S(1)}, u32[]{:S(2)}, u32[]{:S(2)}) collective-permute-start(bf16[64,1024]{1,0:T(8,128)(2,1)} %get-tuple-element.24), channel_id=1, source_target_pairs={{0,1},{1,2},{2,3},{3,4},{4,5},{5,6},{6,7},{7,8},{8,9},{9,10},{10,1... | collective-permute-start | bytes 393224 | tf_op jit(solution)/shard_map/ppermute | solution.py:220
  63.9 4.8 %copy-start.3 = (bf16[1024,16,1,64]{0,3,2,1:T(8,128)(2,1)S(1)}, bf16[1024,16,1,64]{0,3,2,1:T(8,128)(2,1)}, u32[]{:S(2)}) copy-start(bf16[1024,16,1,64]{0,3,2,1:T(8,128)(2,1)} %get-tuple-element.22) | copy-start | bytes 6291460
  71.0 54.4 %copy-start.2 = (bf16[1024,16,1,64]{0,3,2,1:T(8,128)(2,1)S(1)}, bf16[1024,16,1,64]{0,3,2,1:T(8,128)(2,1)}, u32[]{:S(2)}) copy-start(bf16[1024,16,1,64]{0,3,2,1:T(8,128)(2,1)} %get-tuple-element.21) | copy-start | bytes 6291460
  128.1 2.6 %copy-start.5 = (bf16[32,8,1024]{2,1,0:T(8,128)(2,1)S(1)}, bf16[32,8,1024]{2,1,0:T(8,128)(2,1)}, u32[]{:S(2)}) copy-start(bf16[32,8,1024]{2,1,0:T(8,128)(2,1)} %copy-done.4) | copy-start | bytes 1572868

commit v21 on v18

--- a/solution.py
+++ b/solution.py
@@ -80,7 +80,7 @@
 
 def far_kernel(group, ids_ref, mask_ref, q_ref, *refs):
     token_refs = refs[: group * RAND]
-    wkv_ref, oa_ref, ma_ref, la_ref, tok_ref, wo_ref, out_ref, att_ref = refs[group * RAND :]
+    wk_ref, wv_ref, oa_ref, ma_ref, la_ref, tok_ref, wo_ref, out_ref, att_ref = refs[group * RAND :]
     width = q_ref.shape[-1]
     rows = q_ref.shape[1]
     scaling = 1.0 / math.sqrt(HD)
@@ -90,23 +90,25 @@
         far_tokens = jnp.concatenate(
             [ref[0] for ref in token_refs[g * RAND : (g + 1) * RAND]], axis=0
         )
-        kv_rows = jnp.dot(far_tokens, wkv_ref[...], preferred_element_type=jnp.float32).astype(
+        k_rows = jnp.dot(far_tokens, wk_ref[...], preferred_element_type=jnp.float32).astype(
+            jnp.bfloat16
+        )
+        v_rows = jnp.dot(far_tokens, wv_ref[...], preferred_element_type=jnp.float32).astype(
             jnp.bfloat16
         )
         for tile in range(width // LANES):
             lanes = slice(tile * LANES, (tile + 1) * LANES)
-            value_lanes = slice(width + tile * LANES, width + (tile + 1) * LANES)
             cols = pl.ds(tile * LANES, LANES)
             q_pair = pair_rows(q_ref[g, :, cols], low)
             scores = lax.dot_general(
-                q_pair, kv_rows[:, lanes], CONTRACT, preferred_element_type=jnp.float32
+                q_pair, k_rows[:, lanes], CONTRACT, preferred_element_type=jnp.float32
             )
             scores = jnp.where(valid, scores * scaling, -jnp.inf)
             peak = jnp.max(scores, axis=-1, keepdims=True)
             exps = jnp.exp(scores - peak)
             total = jnp.sum(exps, axis=-1, keepdims=True)
             result = jnp.dot(
-                exps.astype(jnp.bfloat16), kv_rows[:, value_lanes], preferred_element_type=jnp.float32
+                exps.astype(jnp.bfloat16), v_rows[:, lanes], preferred_element_type=jnp.float32
             )
             o_b = pick_rows(result, low, rows)
             m_b = pick_rows(jnp.broadcast_to(peak, result.shape), low, rows)
@@ -150,7 +152,7 @@
     )(mask, q, k_ext, k_ext, k_ext, v_ext, v_ext, v_ext, k_sum, v_sum)
 
 
-def attend_far(slot_ids, mask, q, incoming, w_kv, o_a, m_a, l_a, token_blocks, w_out):
+def attend_far(slot_ids, mask, q, incoming, w_k, w_v, o_a, m_a, l_a, token_blocks, w_out):
     blocks, rows, width = q.shape
     model_dim = incoming.shape[-1]
     group = 2 if blocks % 2 == 0 else 1
@@ -161,13 +163,13 @@
         )
         for n in range(group * RAND)
     ]
-    weight = pl.BlockSpec(w_kv.shape, lambda i, ids: (0, 0))
+    weight = pl.BlockSpec(w_k.shape, lambda i, ids: (0, 0))
     local_keys = RAND * rows
     heads = width // HD
     flops = blocks * (
         heads * 2 * rows * 2 * LANES * local_keys + 2 * local_keys * model_dim * 2 * width
     )
-    bytes_accessed = 2 * blocks * rows * (width * 2 + model_dim * RAND) + 2 * w_kv.size + (
+    bytes_accessed = 2 * blocks * rows * (width * 2 + model_dim * RAND) + 2 * (w_k.size + w_v.size) + (
         12 * blocks * rows * width
     )
     grid_spec = pltpu.PrefetchScalarGridSpec(
@@ -175,7 +177,7 @@
         grid=(blocks // group,),
         in_specs=[pl.BlockSpec((group, 1, local_keys), lambda i, ids: (i, 0, 0)), block]
         + token_specs
-        + [weight, block, block, block, block, pl.BlockSpec(w_out.shape, lambda i, ids: (0, 0))],
+        + [weight, weight, block, block, block, block, pl.BlockSpec(w_out.shape, lambda i, ids: (0, 0))],
         out_specs=block,
         scratch_shapes=[pltpu.VMEM((group * rows, width), jnp.bfloat16)],
     )
@@ -188,7 +190,7 @@
             transcendentals=blocks * heads * rows * local_keys,
             bytes_accessed=bytes_accessed,
         ),
-    )(slot_ids, mask, q, *([incoming] * (group * RAND)), w_kv, o_a, m_a, l_a, token_blocks, w_out)
+    )(slot_ids, mask, q, *([incoming] * (group * RAND)), w_k, w_v, o_a, m_a, l_a, token_blocks, w_out)
 
 
 def local(tokens, w_qkv, w_out, counts, rand_seg, rand_off):
@@ -266,7 +268,8 @@
         far_mask,
         q_own,
         incoming.reshape(ctx_count * capacity, BLK, model_dim),
-        jnp.concatenate([w_k, w_v], axis=1),
+        w_k,
+        w_v,
         o_a,
         m_a,
         l_a,

time: 187 us -> 187 us (level)
  other arithmetic: 11.5 us -> 6.67 us
  waiting for transfers between devices: 62.9 us -> 66.1 us
    concatenate x1 -> x0, other arithmetic: 4.82 us -> none  [local(): jnp.concatenate([w_k, w_v], axis=1)]
    ppermute x1, waiting for transfers between devices: 53.8 us -> 57 us  [local(): lax.ppermute(token_blocks[dev_blocks - 1], ('ctx', 'seq'), forward)]
    unnamed x21 -> x19, local copies, waits for them, and re-layouts: 9.84 us -> 9.83 us
  transfers between devices with their start and end apart: 4 -> 4, of which waited for: 2 -> 2; matrix products, arithmetic and copies ran while one was open for 26% -> 24% of each run, Pallas kernels for 12% -> 12%
where the time goes in v21:
time: 187 us; the launch traced here: 185 us
  waiting for transfers between devices  66.1 us (35%)
  Pallas kernels  51.3 us (27%)
  local copies, waits for them, and re-layouts  30.3 us (16%)
  starting transfers between devices  18.3 us (10%)
  matrix products  12.2 us (7%)
  other arithmetic  6.67 us (4%)
    ppermute x1, waiting for transfers between devices, local(): lax.ppermute(token_blocks[dev_blocks - 1], ('ctx', 'seq'), forward)  57 us
    pallas_call x1, Pallas kernels, attend_far(): pl.pallas_call(functools.partial(far_kernel, group), grid_spec=grid_spec,...  29.1 us
    pallas_call x1, Pallas kernels, attend_near(): pl.pallas_call(near_kernel, grid=(blocks,), in_specs=[pl.BlockSpec((1, 1,...  22.2 us
    dot_general x5, matrix products, local(): jnp.dot(x, w, preferred_element_type=jnp.float32).astype(jnp.bfloat16)  12.2 us
    unnamed x19, local copies, waits for them, and re-layouts  9.83 us
    all_to_all x1, waiting for transfers between devices, local(): lax.all_to_all(copies, ('ctx', 'seq'), 0, 0, tiled=True)  9.09 us
    all_to_all x1, starting transfers between devices, local(): lax.all_to_all(outgoing, 'ctx', split_axis=0, concat_axis=0, tiled=True)  7 us
    another operation x2, local copies, waits for them, and re-layouts, split_weights(): shaped[:, :, j, :].reshape(model_dim, head_total * HD)  6.54 us
  transfers between devices with their start and end apart: 4, of which 2 were waited for; matrix products, arithmetic and copies ran while one was open for 24% of the time, Pallas kernels for 12%

profile of v21, /device:TPU:16, one launch (start us, length us, event | category | flops | bytes accessed | tf_op | source)
XLA Modules:
  0.0 185.3 jit_solution(9789066939662833558)
XLA Ops:
  0.0 0.9 select_reduce_fusion.3
  1.0 0.2 convert_reduce_fusion
  1.2 1.6 select_reduce_fusion
  2.9 0.2 multiply_reduce_fusion
  3.1 0.9 divide_convert_fusion
  4.0 5.9 %all-to-all-start = ((bf16[32,8,1024]{2,1,0:T(8,128)(2,1)}), bf16[32,8,1024]{2,1,0:T(8,128)(2,1)S(1)}, u32[]{:S(2)}, u32[]{:S(2)}) async-start(bf16[32,8,1024]{2,1,0:T(8,128)(2,1)} %divide_convert_fusion), calls=%async_computation | async-start | bytes 1048576 | tf_op jit(solution)/shard_map/all_to_all | solution.py:237
  11.2 2.9 %gather_fusion = bf16[32,64,1024]{2,1,0:T(8,128)(2,1)} fusion(bf16[8,64,1024]{2,1,0:T(8,128)(2,1)S(1)} %bitcast.28, s32[1024]{0:T(1024)S(1)} %get-tuple-element.30), kind=kCustom, calls=%fused_computation.2 | custom fusion | bytes 8388736 | tf_op jit(solution)/shard_map/jit(_take)/gather | solution.py:217
  14.1 9.1 %all-to-all-done = bf16[32,8,1024]{2,1,0:T(8,128)(2,1)S(1)} async-done(((bf16[32,8,1024]{2,1,0:T(8,128)(2,1)}), bf16[32,8,1024]{2,1,0:T(8,128)(2,1)S(1)}, u32[]{:S(2)}, u32[]{:S(2)}) %all-to-all-start) | async-done | bytes 524320 | tf_op jit(solution)/shard_map/all_to_all | solution.py:237
  23.2 0.8 copy-done.3
  24.0 7.0 %all-to-all-start.1 = ((bf16[8,4,64,1024]{3,2,1,0:T(8,128)(2,1)}), bf16[8,4,64,1024]{3,2,1,0:T(8,128)(2,1)}, u32[]{:S(2)}, u32[]{:S(2)}) async-start(bf16[8,4,64,1024]{3,2,1,0:T(8,128)(2,1)} %bitcast.30), calls=%async_computation.1 | async-start | bytes 8388608 | tf_op jit(solution)/shard_map/all_to_all | solution.py:239
  31.0 0.7 fusion.5
  31.7 3.5 %collective-permute-start.1 = (bf16[64,1024]{1,0:T(8,128)(2,1)S(1)}, bf16[64,1024]{1,0:T(8,128)(2,1)S(1)}, u32[]{:S(2)}, u32[]{:S(2)}) collective-permute-start(bf16[64,1024]{1,0:T(8,128)(2,1)S(1)} %get-tuple-element.23), channel_id=1, source_target_pairs={{1,0},{2,1},{3,2},{4,3},{5,4},{6,5},{7,6},{8,7},{9,8},{10,9},{11,1... | collective-permute-start | bytes 393224 | tf_op jit(solution)/shard_map/ppermute | solution.py:223
  35.1 1.9 %collective-permute-start = (bf16[64,1024]{1,0:T(8,128)(2,1)}, bf16[64,1024]{1,0:T(8,128)(2,1)S(1)}, u32[]{:S(2)}, u32[]{:S(2)}) collective-permute-start(bf16[64,1024]{1,0:T(8,128)(2,1)} %get-tuple-element.24), channel_id=1, source_target_pairs={{0,1},{1,2},{2,3},{3,4},{4,5},{5,6},{6,7},{7,8},{8,9},{9,10},{10,1... | collective-permute-start | bytes 393224 | tf_op jit(solution)/shard_map/ppermute | solution.py:222
  37.1 0.7 lt.86
  37.9 0.7 gather_fusion.1
  38.7 0.7 gather_fusion.2
  39.7 0.7 lt.103
  40.4 0.7 lt.102
  41.2 8.7 %copy.43 = bf16[1024,3072]{0,1:T(8,128)(2,1)} copy(bf16[1024,3072]{1,0:T(8,128)(2,1)} %param.9) | data formatting | bytes 12582912 | tf_op args[1]
  49.9 6.0 %fusion.4 = (bf16[1024,16,1,64]{0,3,2,1:T(8,128)(2,1)S(1)}, bf16[1024,16,1,64]{0,3,2,1:T(8,128)(2,1)}, bf16[1024,16,1,64]{0,3,2,1:T(8,128)(2,1)}) fusion(bf16[1024,16,3,64]{0,3,2,1:T(8,128)(2,1)} %bitcast.29), kind=kLoop, calls=%fused_computation.48 | loop fusion | bytes 12582912 | tf_op jit(solution)/shard_map/slice | solution.py:35
  55.9 4.0 %copy.49.refs_6_ = bf16[1024,1024]{1,0:T(8,128)(2,1)} copy(bf16[1024,1024]{0,1:T(8,128)(2,1)} %bitcast.40) | data formatting | bytes 4194304 | tf_op jit(solution)/shard_map/reshape;squeeze | solution.py:35
  59.8 2.6 %copy.50.refs_7_ = bf16[1024,1024]{1,0:T(8,128)(2,1)} copy(bf16[1024,1024]{0,1:T(8,128)(2,1)S(1)} %bitcast.37) | data formatting | bytes 4194304 | tf_op jit(solution)/shard_map/reshape;squeeze | solution.py:35
  62.6 1.3 compare_convert_fusion
  63.9 3.9 %convolution_convert_fusion.2 = bf16[512,1024]{1,0:T(8,128)(2,1)} fusion(bf16[512,1024]{1,0:T(8,128)(2,1)S(1)} %copy-done.1, bf16[1024,1024]{0,1:T(8,128)(2,1)} %bitcast.45), kind=kOutput, calls=%fused_computation.6 | convolution fusion | flops 1074266112 | bytes 4194304 | tf_op jit(solution)/shard_map/dot_general | solution.py:242
  67.8 0.5 multiply_add_fusion.ids_ref
  68.4 57.0 %collective-permute-done = bf16[64,1024]{1,0:T(8,128)(2,1)S(1)} collective-permute-done((bf16[64,1024]{1,0:T(8,128)(2,1)}, bf16[64,1024]{1,0:T(8,128)(2,1)S(1)}, u32[]{:S(2)}, u32[]{:S(2)}) %collective-permute-start) | collective-permute-done | bytes 131104 | tf_op jit(solution)/shard_map/ppermute | solution.py:222
  125.5 2.6 %convolution_convert_fusion.1 = bf16[640,1024]{1,0:T(8,128)(2,1)} fusion(bf16[640,1024]{1,0:T(8,128)(2,1)S(1)} %constant_dynamic-update-slice_fusion, bf16[1024,1024]{0,1:T(8,128)(2,1)S(1)} %bitcast.41), kind=kOutput, calls=%fused_computation.5 | convolution fusion | flops 1342832640 | bytes 4718592 | tf_op jit(solution)/shard_map/dot_general | solution.py:242
  128.1 2.6 %convolution_convert_fusion = bf16[640,1024]{1,0:T(8,128)(2,1)} fusion(bf16[640,1024]{1,0:T(8,128)(2,1)S(1)} %constant_dynamic-update-slice_fusion, bf16[1024,1024]{0,1:T(8,128)(2,1)S(1)} %bitcast.38), kind=kOutput, calls=%fused_computation.4 | convolution fusion | flops 1342832640 | bytes 4718592 | tf_op jit(solution)/shard_map/dot_general | solution.py:242
  130.7 1.5 convolution_convert_fusion.4.ks_ref
  132.3 1.6 convolution_convert_fusion.3.vs_ref
  133.8 22.2 %shard_map.64 = (f32[8,64,1024]{2,1,0:T(8,128)}, f32[8,64,1024]{2,1,0:T(8,128)}, f32[8,64,1024]{2,1,0:T(8,128)}) custom-call(s32[8,1,192]{2,1,0:T(1,128)} %get-tuple-element.27.mask_ref, bf16[8,64,1024]{2,1,0:T(8,128)(2,1)} %bitcast.43, bf16[10,64,1024]{2,1,0:T(8,128)(2,1)} %bitcast.31, bf16[10,64,1024]{2,1,0:T(8,128)(2,1)} %bitcast.32, ...), custom_call_target="tpu_custom_call" | custom-call | flops 1879048192 | bytes 14680064 | tf_op jit(solution)/shard_map/pallas_call | solution.py:139
  156.1 29.1 %shard_map.65 = bf16[8,64,1024]{2,1,0:T(8,128)(2,1)} custom-call(s32[24]{0:T(128)} %multiply_add_fusion.ids_ref, s32[8,1,192]{2,1,0:T(1,128)} %get-tuple-element.28.mask_ref, bf16[8,64,1024]{2,1,0:T(8,128)(2,1)} %bitcast.44, bf16[32,64,1024]{2,1,0:T(8,128)(2,1)} %bitcast.7.refs_0_.refs_1_.refs_2_.refs_3_.refs_4_.refs_5_, ...), custom_call_target="tpu_custom_call" | custom-call | flops 7247757312 | bytes 15728640 | tf_op jit(solution)/shard_map/pallas_call | solution.py:184
  (51 shorter events, 2.2 us)
Async XLA Ops:
  0.0 11.2 %copy-start.1 = (bf16[512,1024]{1,0:T(8,128)(2,1)S(1)}, bf16[512,1024]{1,0:T(8,128)(2,1)}, u32[]{:S(2)}) copy-start(bf16[512,1024]{1,0:T(8,128)(2,1)} %param.8) | copy-start | bytes 3145732
  0.0 10.1 %copy-start.5 = (s32[256,3]{0,1:T(4,128)S(1)}, s32[256,3]{0,1:T(4,128)}, u32[]{:S(2)}) copy-start(s32[256,3]{0,1:T(4,128)} %param.12) | copy-start | bytes 9220
  0.0 10.6 %copy-start.6 = (s32[256,3]{0,1:T(4,128)S(1)}, s32[256,3]{0,1:T(4,128)}, u32[]{:S(2)}) copy-start(s32[256,3]{0,1:T(4,128)} %param.13) | copy-start | bytes 9220
  4.0 19.2 %all-to-all-start = ((bf16[32,8,1024]{2,1,0:T(8,128)(2,1)}), bf16[32,8,1024]{2,1,0:T(8,128)(2,1)S(1)}, u32[]{:S(2)}, u32[]{:S(2)}) async-start(bf16[32,8,1024]{2,1,0:T(8,128)(2,1)} %divide_convert_fusion), calls=%async_computation | async-start | bytes 1048576 | tf_op jit(solution)/shard_map/all_to_all | solution.py:237
  23.2 0.8 copy-start.3
  24.0 132.0 %all-to-all-start.1 = ((bf16[8,4,64,1024]{3,2,1,0:T(8,128)(2,1)}), bf16[8,4,64,1024]{3,2,1,0:T(8,128)(2,1)}, u32[]{:S(2)}, u32[]{:S(2)}) async-start(bf16[8,4,64,1024]{3,2,1,0:T(8,128)(2,1)} %bitcast.30), calls=%async_computation.1 | async-start | bytes 8388608 | tf_op jit(solution)/shard_map/all_to_all | solution.py:239
  31.0 6.9 %copy-start = (s32[256]{0:T(256)S(1)}, s32[256]{0:T(256)}, u32[]{:S(2)}) copy-start(s32[256]{0:T(256)} %param.11) | copy-start | bytes 3076
  31.7 93.8 %collective-permute-start.1 = (bf16[64,1024]{1,0:T(8,128)(2,1)S(1)}, bf16[64,1024]{1,0:T(8,128)(2,1)S(1)}, u32[]{:S(2)}, u32[]{:S(2)}) collective-permute-start(bf16[64,1024]{1,0:T(8,128)(2,1)S(1)} %get-tuple-element.23), channel_id=1, source_target_pairs={{1,0},{2,1},{3,2},{4,3},{5,4},{6,5},{7,6},{8,7},{9,8},{10,9},{11,1... | collective-permute-start | bytes 393224 | tf_op jit(solution)/shard_map/ppermute | solution.py:223
  35.1 90.2 %collective-permute-start = (bf16[64,1024]{1,0:T(8,128)(2,1)}, bf16[64,1024]{1,0:T(8,128)(2,1)S(1)}, u32[]{:S(2)}, u32[]{:S(2)}) collective-permute-start(bf16[64,1024]{1,0:T(8,128)(2,1)} %get-tuple-element.24), channel_id=1, source_target_pairs={{0,1},{1,2},{2,3},{3,4},{4,5},{5,6},{6,7},{7,8},{8,9},{9,10},{10,1... | collective-permute-start | bytes 393224 | tf_op jit(solution)/shard_map/ppermute | solution.py:222
  67.8 57.7 %copy-start.2 = (bf16[1024,16,1,64]{0,3,2,1:T(8,128)(2,1)S(1)}, bf16[1024,16,1,64]{0,3,2,1:T(8,128)(2,1)}, u32[]{:S(2)}) copy-start(bf16[1024,16,1,64]{0,3,2,1:T(8,128)(2,1)} %get-tuple-element.21) | copy-start | bytes 6291460
  128.1 2.6 %copy-start.4 = (bf16[32,8,1024]{2,1,0:T(8,128)(2,1)S(1)}, bf16[32,8,1024]{2,1,0:T(8,128)(2,1)}, u32[]{:S(2)}) copy-start(bf16[32,8,1024]{2,1,0:T(8,128)(2,1)} %copy-done.3) | copy-start | bytes 1572868

commit v22 on v21

--- a/solution.py
+++ b/solution.py
@@ -155,7 +155,7 @@
 def attend_far(slot_ids, mask, q, incoming, w_k, w_v, o_a, m_a, l_a, token_blocks, w_out):
     blocks, rows, width = q.shape
     model_dim = incoming.shape[-1]
-    group = 2 if blocks % 2 == 0 else 1
+    group = 1
     block = pl.BlockSpec((group, rows, width), lambda i, ids: (i, 0, 0))
     token_specs = [
         pl.BlockSpec(

time: 187 us -> 189 us (1.011)
  Pallas kernels: 51.3 us -> 53.3 us
    pallas_call x1, Pallas kernels: 29.1 us -> 31 us  [attend_far(): pl.pallas_call(functools.partial(far_kernel, group), grid_spec=grid_spec,...]
where the time goes in v22:
time: 189 us; the launch traced here: 187 us
  waiting for transfers between devices  66.1 us (35%)
  Pallas kernels  53.3 us (28%)
  local copies, waits for them, and re-layouts  30.3 us (16%)
  starting transfers between devices  18.3 us (10%)
  matrix products  12.2 us (6%)
  other arithmetic  6.67 us (4%)
    ppermute x1, waiting for transfers between devices, local(): lax.ppermute(token_blocks[dev_blocks - 1], ('ctx', 'seq'), forward)  57 us
    pallas_call x1, Pallas kernels, attend_far(): pl.pallas_call(functools.partial(far_kernel, group), grid_spec=grid_spec,...  31 us
    pallas_call x1, Pallas kernels, attend_near(): pl.pallas_call(near_kernel, grid=(blocks,), in_specs=[pl.BlockSpec((1, 1,...  22.2 us
    dot_general x5, matrix products, local(): jnp.dot(x, w, preferred_element_type=jnp.float32).astype(jnp.bfloat16)  12.2 us
    unnamed x19, local copies, waits for them, and re-layouts  9.83 us
    all_to_all x1, waiting for transfers between devices, local(): lax.all_to_all(copies, ('ctx', 'seq'), 0, 0, tiled=True)  9.09 us
    all_to_all x1, starting transfers between devices, local(): lax.all_to_all(outgoing, 'ctx', split_axis=0, concat_axis=0, tiled=True)  7 us
    another operation x2, local copies, waits for them, and re-layouts, split_weights(): shaped[:, :, j, :].reshape(model_dim, head_total * HD)  6.54 us
  transfers between devices with their start and end apart: 4, of which 2 were waited for; matrix products, arithmetic and copies ran while one was open for 24% of the time, Pallas kernels for 12%

profile of v22, /device:TPU:16, one launch (start us, length us, event | category | flops | bytes accessed | tf_op | source)
XLA Modules:
  0.0 187.1 jit_solution(12744229157869923808)
XLA Ops:
  0.0 0.9 select_reduce_fusion.3
  1.0 0.2 convert_reduce_fusion
  1.2 1.6 select_reduce_fusion
  2.9 0.2 multiply_reduce_fusion
  3.1 0.9 divide_convert_fusion
  4.0 5.9 %all-to-all-start = ((bf16[32,8,1024]{2,1,0:T(8,128)(2,1)}), bf16[32,8,1024]{2,1,0:T(8,128)(2,1)S(1)}, u32[]{:S(2)}, u32[]{:S(2)}) async-start(bf16[32,8,1024]{2,1,0:T(8,128)(2,1)} %divide_convert_fusion), calls=%async_computation | async-start | bytes 1048576 | tf_op jit(solution)/shard_map/all_to_all | solution.py:237
  11.2 2.9 %gather_fusion = bf16[32,64,1024]{2,1,0:T(8,128)(2,1)} fusion(bf16[8,64,1024]{2,1,0:T(8,128)(2,1)S(1)} %bitcast.28, s32[1024]{0:T(1024)S(1)} %get-tuple-element.30), kind=kCustom, calls=%fused_computation.2 | custom fusion | bytes 8388736 | tf_op jit(solution)/shard_map/jit(_take)/gather | solution.py:217
  14.1 9.1 %all-to-all-done = bf16[32,8,1024]{2,1,0:T(8,128)(2,1)S(1)} async-done(((bf16[32,8,1024]{2,1,0:T(8,128)(2,1)}), bf16[32,8,1024]{2,1,0:T(8,128)(2,1)S(1)}, u32[]{:S(2)}, u32[]{:S(2)}) %all-to-all-start) | async-done | bytes 524320 | tf_op jit(solution)/shard_map/all_to_all | solution.py:237
  23.2 0.8 copy-done.3
  24.0 7.0 %all-to-all-start.1 = ((bf16[8,4,64,1024]{3,2,1,0:T(8,128)(2,1)}), bf16[8,4,64,1024]{3,2,1,0:T(8,128)(2,1)}, u32[]{:S(2)}, u32[]{:S(2)}) async-start(bf16[8,4,64,1024]{3,2,1,0:T(8,128)(2,1)} %bitcast.30), calls=%async_computation.1 | async-start | bytes 8388608 | tf_op jit(solution)/shard_map/all_to_all | solution.py:239
  31.0 0.7 fusion.5
  31.7 3.5 %collective-permute-start.1 = (bf16[64,1024]{1,0:T(8,128)(2,1)S(1)}, bf16[64,1024]{1,0:T(8,128)(2,1)S(1)}, u32[]{:S(2)}, u32[]{:S(2)}) collective-permute-start(bf16[64,1024]{1,0:T(8,128)(2,1)S(1)} %get-tuple-element.23), channel_id=1, source_target_pairs={{1,0},{2,1},{3,2},{4,3},{5,4},{6,5},{7,6},{8,7},{9,8},{10,9},{11,1... | collective-permute-start | bytes 393224 | tf_op jit(solution)/shard_map/ppermute | solution.py:223
  35.1 1.9 %collective-permute-start = (bf16[64,1024]{1,0:T(8,128)(2,1)}, bf16[64,1024]{1,0:T(8,128)(2,1)S(1)}, u32[]{:S(2)}, u32[]{:S(2)}) collective-permute-start(bf16[64,1024]{1,0:T(8,128)(2,1)} %get-tuple-element.24), channel_id=1, source_target_pairs={{0,1},{1,2},{2,3},{3,4},{4,5},{5,6},{6,7},{7,8},{8,9},{9,10},{10,1... | collective-permute-start | bytes 393224 | tf_op jit(solution)/shard_map/ppermute | solution.py:222
  37.1 0.7 lt.86
  37.9 0.7 gather_fusion.1
  38.7 0.7 gather_fusion.2
  39.7 0.7 lt.103
  40.4 0.7 lt.102
  41.2 8.7 %copy.43 = bf16[1024,3072]{0,1:T(8,128)(2,1)} copy(bf16[1024,3072]{1,0:T(8,128)(2,1)} %param.9) | data formatting | bytes 12582912 | tf_op args[1]
  49.9 6.0 %fusion.4 = (bf16[1024,16,1,64]{0,3,2,1:T(8,128)(2,1)S(1)}, bf16[1024,16,1,64]{0,3,2,1:T(8,128)(2,1)}, bf16[1024,16,1,64]{0,3,2,1:T(8,128)(2,1)}) fusion(bf16[1024,16,3,64]{0,3,2,1:T(8,128)(2,1)} %bitcast.29), kind=kLoop, calls=%fused_computation.48 | loop fusion | bytes 12582912 | tf_op jit(solution)/shard_map/slice | solution.py:35
  55.9 4.0 %copy.49.refs_3_ = bf16[1024,1024]{1,0:T(8,128)(2,1)} copy(bf16[1024,1024]{0,1:T(8,128)(2,1)} %bitcast.40) | data formatting | bytes 4194304 | tf_op jit(solution)/shard_map/reshape;squeeze | solution.py:35
  59.8 2.6 %copy.50.refs_4_ = bf16[1024,1024]{1,0:T(8,128)(2,1)} copy(bf16[1024,1024]{0,1:T(8,128)(2,1)S(1)} %bitcast.37) | data formatting | bytes 4194304 | tf_op jit(solution)/shard_map/reshape;squeeze | solution.py:35
  62.6 1.3 compare_convert_fusion
  63.9 3.9 %convolution_convert_fusion.2 = bf16[512,1024]{1,0:T(8,128)(2,1)} fusion(bf16[512,1024]{1,0:T(8,128)(2,1)S(1)} %copy-done.1, bf16[1024,1024]{0,1:T(8,128)(2,1)} %bitcast.45), kind=kOutput, calls=%fused_computation.6 | convolution fusion | flops 1074266112 | bytes 4194304 | tf_op jit(solution)/shard_map/dot_general | solution.py:242
  67.8 0.5 multiply_add_fusion.ids_ref
  68.4 57.0 %collective-permute-done = bf16[64,1024]{1,0:T(8,128)(2,1)S(1)} collective-permute-done((bf16[64,1024]{1,0:T(8,128)(2,1)}, bf16[64,1024]{1,0:T(8,128)(2,1)S(1)}, u32[]{:S(2)}, u32[]{:S(2)}) %collective-permute-start) | collective-permute-done | bytes 131104 | tf_op jit(solution)/shard_map/ppermute | solution.py:222
  125.5 2.6 %convolution_convert_fusion.1 = bf16[640,1024]{1,0:T(8,128)(2,1)} fusion(bf16[640,1024]{1,0:T(8,128)(2,1)S(1)} %constant_dynamic-update-slice_fusion, bf16[1024,1024]{0,1:T(8,128)(2,1)S(1)} %bitcast.41), kind=kOutput, calls=%fused_computation.5 | convolution fusion | flops 1342832640 | bytes 4718592 | tf_op jit(solution)/shard_map/dot_general | solution.py:242
  128.1 2.6 %convolution_convert_fusion = bf16[640,1024]{1,0:T(8,128)(2,1)} fusion(bf16[640,1024]{1,0:T(8,128)(2,1)S(1)} %constant_dynamic-update-slice_fusion, bf16[1024,1024]{0,1:T(8,128)(2,1)S(1)} %bitcast.38), kind=kOutput, calls=%fused_computation.4 | convolution fusion | flops 1342832640 | bytes 4718592 | tf_op jit(solution)/shard_map/dot_general | solution.py:242
  130.7 1.5 convolution_convert_fusion.4.ks_ref
  132.3 1.6 convolution_convert_fusion.3.vs_ref
  133.8 22.2 %shard_map.64 = (f32[8,64,1024]{2,1,0:T(8,128)}, f32[8,64,1024]{2,1,0:T(8,128)}, f32[8,64,1024]{2,1,0:T(8,128)}) custom-call(s32[8,1,192]{2,1,0:T(1,128)} %get-tuple-element.27.mask_ref, bf16[8,64,1024]{2,1,0:T(8,128)(2,1)} %bitcast.43, bf16[10,64,1024]{2,1,0:T(8,128)(2,1)} %bitcast.31, bf16[10,64,1024]{2,1,0:T(8,128)(2,1)} %bitcast.32, ...), custom_call_target="tpu_custom_call" | custom-call | flops 1879048192 | bytes 14680064 | tf_op jit(solution)/shard_map/pallas_call | solution.py:139
  156.1 31.0 %shard_map.65 = bf16[8,64,1024]{2,1,0:T(8,128)(2,1)} custom-call(s32[24]{0:T(128)} %multiply_add_fusion.ids_ref, s32[8,1,192]{2,1,0:T(1,128)} %get-tuple-element.28.mask_ref, bf16[8,64,1024]{2,1,0:T(8,128)(2,1)} %bitcast.44, bf16[32,64,1024]{2,1,0:T(8,128)(2,1)} %bitcast.7.refs_0_.refs_1_.refs_2_, bf16[32,64,1024]{2,1,0:T(8,128)(2,1)} %bitcast.7.refs_0_.refs_1_.refs_2_, ...), custom_call_target="tpu_custom_call" | custom-call | flops 7247757312 | bytes 15728640 | tf_op jit(solution)/shard_map/pallas_call | solution.py:184
  (51 shorter events, 2.2 us)
Async XLA Ops:
  0.0 11.2 %copy-start.1 = (bf16[512,1024]{1,0:T(8,128)(2,1)S(1)}, bf16[512,1024]{1,0:T(8,128)(2,1)}, u32[]{:S(2)}) copy-start(bf16[512,1024]{1,0:T(8,128)(2,1)} %param.8) | copy-start | bytes 3145732
  0.0 10.1 %copy-start.5 = (s32[256,3]{0,1:T(4,128)S(1)}, s32[256,3]{0,1:T(4,128)}, u32[]{:S(2)}) copy-start(s32[256,3]{0,1:T(4,128)} %param.12) | copy-start | bytes 9220
  0.0 10.6 %copy-start.6 = (s32[256,3]{0,1:T(4,128)S(1)}, s32[256,3]{0,1:T(4,128)}, u32[]{:S(2)}) copy-start(s32[256,3]{0,1:T(4,128)} %param.13) | copy-start | bytes 9220
  4.0 19.2 %all-to-all-start = ((bf16[32,8,1024]{2,1,0:T(8,128)(2,1)}), bf16[32,8,1024]{2,1,0:T(8,128)(2,1)S(1)}, u32[]{:S(2)}, u32[]{:S(2)}) async-start(bf16[32,8,1024]{2,1,0:T(8,128)(2,1)} %divide_convert_fusion), calls=%async_computation | async-start | bytes 1048576 | tf_op jit(solution)/shard_map/all_to_all | solution.py:237
  23.2 0.8 copy-start.3
  24.0 132.1 %all-to-all-start.1 = ((bf16[8,4,64,1024]{3,2,1,0:T(8,128)(2,1)}), bf16[8,4,64,1024]{3,2,1,0:T(8,128)(2,1)}, u32[]{:S(2)}, u32[]{:S(2)}) async-start(bf16[8,4,64,1024]{3,2,1,0:T(8,128)(2,1)} %bitcast.30), calls=%async_computation.1 | async-start | bytes 8388608 | tf_op jit(solution)/shard_map/all_to_all | solution.py:239
  31.0 6.9 %copy-start = (s32[256]{0:T(256)S(1)}, s32[256]{0:T(256)}, u32[]{:S(2)}) copy-start(s32[256]{0:T(256)} %param.11) | copy-start | bytes 3076
  31.7 93.8 %collective-permute-start.1 = (bf16[64,1024]{1,0:T(8,128)(2,1)S(1)}, bf16[64,1024]{1,0:T(8,128)(2,1)S(1)}, u32[]{:S(2)}, u32[]{:S(2)}) collective-permute-start(bf16[64,1024]{1,0:T(8,128)(2,1)S(1)} %get-tuple-element.23), channel_id=1, source_target_pairs={{1,0},{2,1},{3,2},{4,3},{5,4},{6,5},{7,6},{8,7},{9,8},{10,9},{11,1... | collective-permute-start | bytes 393224 | tf_op jit(solution)/shard_map/ppermute | solution.py:223
  35.1 90.2 %collective-permute-start = (bf16[64,1024]{1,0:T(8,128)(2,1)}, bf16[64,1024]{1,0:T(8,128)(2,1)S(1)}, u32[]{:S(2)}, u32[]{:S(2)}) collective-permute-start(bf16[64,1024]{1,0:T(8,128)(2,1)} %get-tuple-element.24), channel_id=1, source_target_pairs={{0,1},{1,2},{2,3},{3,4},{4,5},{5,6},{6,7},{7,8},{8,9},{9,10},{10,1... | collective-permute-start | bytes 393224 | tf_op jit(solution)/shard_map/ppermute | solution.py:222
  67.8 57.7 %copy-start.2 = (bf16[1024,16,1,64]{0,3,2,1:T(8,128)(2,1)S(1)}, bf16[1024,16,1,64]{0,3,2,1:T(8,128)(2,1)}, u32[]{:S(2)}) copy-start(bf16[1024,16,1,64]{0,3,2,1:T(8,128)(2,1)} %get-tuple-element.21) | copy-start | bytes 6291460
  128.1 2.6 %copy-start.4 = (bf16[32,8,1024]{2,1,0:T(8,128)(2,1)S(1)}, bf16[32,8,1024]{2,1,0:T(8,128)(2,1)}, u32[]{:S(2)}) copy-start(bf16[32,8,1024]{2,1,0:T(8,128)(2,1)} %copy-done.3) | copy-start | bytes 1572868

commit v23 on v22

--- a/solution.py
+++ b/solution.py
@@ -155,7 +155,7 @@
 def attend_far(slot_ids, mask, q, incoming, w_k, w_v, o_a, m_a, l_a, token_blocks, w_out):
     blocks, rows, width = q.shape
     model_dim = incoming.shape[-1]
-    group = 1
+    group = 4 if blocks % 4 == 0 else 1
     block = pl.BlockSpec((group, rows, width), lambda i, ids: (i, 0, 0))
     token_specs = [
         pl.BlockSpec(

time: 189 us -> 187 us (0.989)
  no operation moved by 1% of the time
where the time goes in v23:
time: 187 us; the launch traced here: 186 us
  waiting for transfers between devices  66.1 us (35%)
  Pallas kernels  51.7 us (28%)
  local copies, waits for them, and re-layouts  30.3 us (16%)
  starting transfers between devices  18.3 us (10%)
  matrix products  12.2 us (7%)
  other arithmetic  6.67 us (4%)
    ppermute x1, waiting for transfers between devices, local(): lax.ppermute(token_blocks[dev_blocks - 1], ('ctx', 'seq'), forward)  57 us
    pallas_call x1, Pallas kernels, attend_far(): pl.pallas_call(functools.partial(far_kernel, group), grid_spec=grid_spec,...  29.5 us
    pallas_call x1, Pallas kernels, attend_near(): pl.pallas_call(near_kernel, grid=(blocks,), in_specs=[pl.BlockSpec((1, 1,...  22.2 us
    dot_general x5, matrix products, local(): jnp.dot(x, w, preferred_element_type=jnp.float32).astype(jnp.bfloat16)  12.2 us
    unnamed x19, local copies, waits for them, and re-layouts  9.83 us
    all_to_all x1, waiting for transfers between devices, local(): lax.all_to_all(copies, ('ctx', 'seq'), 0, 0, tiled=True)  9.09 us
    all_to_all x1, starting transfers between devices, local(): lax.all_to_all(outgoing, 'ctx', split_axis=0, concat_axis=0, tiled=True)  7 us
    another operation x2, local copies, waits for them, and re-layouts, split_weights(): shaped[:, :, j, :].reshape(model_dim, head_total * HD)  6.54 us
  transfers between devices with their start and end apart: 4, of which 2 were waited for; matrix products, arithmetic and copies ran while one was open for 24% of the time, Pallas kernels for 12%

profile of v23, /device:TPU:16, one launch (start us, length us, event | category | flops | bytes accessed | tf_op | source)
XLA Modules:
  0.0 185.7 jit_solution(4960594385108139360)
XLA Ops:
  0.0 0.9 select_reduce_fusion.3
  1.0 0.2 convert_reduce_fusion
  1.2 1.6 select_reduce_fusion
  2.9 0.2 multiply_reduce_fusion
  3.1 0.9 divide_convert_fusion
  4.0 5.9 %all-to-all-start = ((bf16[32,8,1024]{2,1,0:T(8,128)(2,1)}), bf16[32,8,1024]{2,1,0:T(8,128)(2,1)S(1)}, u32[]{:S(2)}, u32[]{:S(2)}) async-start(bf16[32,8,1024]{2,1,0:T(8,128)(2,1)} %divide_convert_fusion), calls=%async_computation | async-start | bytes 1048576 | tf_op jit(solution)/shard_map/all_to_all | solution.py:237
  11.2 2.9 %gather_fusion = bf16[32,64,1024]{2,1,0:T(8,128)(2,1)} fusion(bf16[8,64,1024]{2,1,0:T(8,128)(2,1)S(1)} %bitcast.28, s32[1024]{0:T(1024)S(1)} %get-tuple-element.30), kind=kCustom, calls=%fused_computation.2 | custom fusion | bytes 8388736 | tf_op jit(solution)/shard_map/jit(_take)/gather | solution.py:217
  14.1 9.1 %all-to-all-done = bf16[32,8,1024]{2,1,0:T(8,128)(2,1)S(1)} async-done(((bf16[32,8,1024]{2,1,0:T(8,128)(2,1)}), bf16[32,8,1024]{2,1,0:T(8,128)(2,1)S(1)}, u32[]{:S(2)}, u32[]{:S(2)}) %all-to-all-start) | async-done | bytes 524320 | tf_op jit(solution)/shard_map/all_to_all | solution.py:237
  23.2 0.8 copy-done.3
  24.0 7.0 %all-to-all-start.1 = ((bf16[8,4,64,1024]{3,2,1,0:T(8,128)(2,1)}), bf16[8,4,64,1024]{3,2,1,0:T(8,128)(2,1)}, u32[]{:S(2)}, u32[]{:S(2)}) async-start(bf16[8,4,64,1024]{3,2,1,0:T(8,128)(2,1)} %bitcast.30), calls=%async_computation.1 | async-start | bytes 8388608 | tf_op jit(solution)/shard_map/all_to_all | solution.py:239
  31.0 0.7 fusion.5
  31.7 3.5 %collective-permute-start.1 = (bf16[64,1024]{1,0:T(8,128)(2,1)S(1)}, bf16[64,1024]{1,0:T(8,128)(2,1)S(1)}, u32[]{:S(2)}, u32[]{:S(2)}) collective-permute-start(bf16[64,1024]{1,0:T(8,128)(2,1)S(1)} %get-tuple-element.23), channel_id=1, source_target_pairs={{1,0},{2,1},{3,2},{4,3},{5,4},{6,5},{7,6},{8,7},{9,8},{10,9},{11,1... | collective-permute-start | bytes 393224 | tf_op jit(solution)/shard_map/ppermute | solution.py:223
  35.1 1.9 %collective-permute-start = (bf16[64,1024]{1,0:T(8,128)(2,1)}, bf16[64,1024]{1,0:T(8,128)(2,1)S(1)}, u32[]{:S(2)}, u32[]{:S(2)}) collective-permute-start(bf16[64,1024]{1,0:T(8,128)(2,1)} %get-tuple-element.24), channel_id=1, source_target_pairs={{0,1},{1,2},{2,3},{3,4},{4,5},{5,6},{6,7},{7,8},{8,9},{9,10},{10,1... | collective-permute-start | bytes 393224 | tf_op jit(solution)/shard_map/ppermute | solution.py:222
  37.1 0.7 lt.86
  37.9 0.7 gather_fusion.1
  38.7 0.7 gather_fusion.2
  39.7 0.7 lt.103
  40.4 0.7 lt.102
  41.2 8.7 %copy.43 = bf16[1024,3072]{0,1:T(8,128)(2,1)} copy(bf16[1024,3072]{1,0:T(8,128)(2,1)} %param.9) | data formatting | bytes 12582912 | tf_op args[1]
  49.9 6.0 %fusion.4 = (bf16[1024,16,1,64]{0,3,2,1:T(8,128)(2,1)S(1)}, bf16[1024,16,1,64]{0,3,2,1:T(8,128)(2,1)}, bf16[1024,16,1,64]{0,3,2,1:T(8,128)(2,1)}) fusion(bf16[1024,16,3,64]{0,3,2,1:T(8,128)(2,1)} %bitcast.29), kind=kLoop, calls=%fused_computation.48 | loop fusion | bytes 12582912 | tf_op jit(solution)/shard_map/slice | solution.py:35
  55.9 4.0 %copy.49.refs_12_ = bf16[1024,1024]{1,0:T(8,128)(2,1)} copy(bf16[1024,1024]{0,1:T(8,128)(2,1)} %bitcast.40) | data formatting | bytes 4194304 | tf_op jit(solution)/shard_map/reshape;squeeze | solution.py:35
  59.8 2.6 %copy.50.refs_13_ = bf16[1024,1024]{1,0:T(8,128)(2,1)} copy(bf16[1024,1024]{0,1:T(8,128)(2,1)S(1)} %bitcast.37) | data formatting | bytes 4194304 | tf_op jit(solution)/shard_map/reshape;squeeze | solution.py:35
  62.6 1.3 compare_convert_fusion
  63.9 3.9 %convolution_convert_fusion.2 = bf16[512,1024]{1,0:T(8,128)(2,1)} fusion(bf16[512,1024]{1,0:T(8,128)(2,1)S(1)} %copy-done.1, bf16[1024,1024]{0,1:T(8,128)(2,1)} %bitcast.45), kind=kOutput, calls=%fused_computation.6 | convolution fusion | flops 1074266112 | bytes 4194304 | tf_op jit(solution)/shard_map/dot_general | solution.py:242
  67.8 0.5 multiply_add_fusion.ids_ref
  68.4 57.0 %collective-permute-done = bf16[64,1024]{1,0:T(8,128)(2,1)S(1)} collective-permute-done((bf16[64,1024]{1,0:T(8,128)(2,1)}, bf16[64,1024]{1,0:T(8,128)(2,1)S(1)}, u32[]{:S(2)}, u32[]{:S(2)}) %collective-permute-start) | collective-permute-done | bytes 131104 | tf_op jit(solution)/shard_map/ppermute | solution.py:222
  125.5 2.6 %convolution_convert_fusion.1 = bf16[640,1024]{1,0:T(8,128)(2,1)} fusion(bf16[640,1024]{1,0:T(8,128)(2,1)S(1)} %constant_dynamic-update-slice_fusion, bf16[1024,1024]{0,1:T(8,128)(2,1)S(1)} %bitcast.41), kind=kOutput, calls=%fused_computation.5 | convolution fusion | flops 1342832640 | bytes 4718592 | tf_op jit(solution)/shard_map/dot_general | solution.py:242
  128.1 2.6 %convolution_convert_fusion = bf16[640,1024]{1,0:T(8,128)(2,1)} fusion(bf16[640,1024]{1,0:T(8,128)(2,1)S(1)} %constant_dynamic-update-slice_fusion, bf16[1024,1024]{0,1:T(8,128)(2,1)S(1)} %bitcast.38), kind=kOutput, calls=%fused_computation.4 | convolution fusion | flops 1342832640 | bytes 4718592 | tf_op jit(solution)/shard_map/dot_general | solution.py:242
  130.7 1.5 convolution_convert_fusion.4.ks_ref
  132.3 1.6 convolution_convert_fusion.3.vs_ref
  133.8 22.2 %shard_map.64 = (f32[8,64,1024]{2,1,0:T(8,128)}, f32[8,64,1024]{2,1,0:T(8,128)}, f32[8,64,1024]{2,1,0:T(8,128)}) custom-call(s32[8,1,192]{2,1,0:T(1,128)} %get-tuple-element.27.mask_ref, bf16[8,64,1024]{2,1,0:T(8,128)(2,1)} %bitcast.43, bf16[10,64,1024]{2,1,0:T(8,128)(2,1)} %bitcast.31, bf16[10,64,1024]{2,1,0:T(8,128)(2,1)} %bitcast.32, ...), custom_call_target="tpu_custom_call" | custom-call | flops 1879048192 | bytes 14680064 | tf_op jit(solution)/shard_map/pallas_call | solution.py:139
  156.1 29.5 %shard_map.65 = bf16[8,64,1024]{2,1,0:T(8,128)(2,1)} custom-call(s32[24]{0:T(128)} %multiply_add_fusion.ids_ref, s32[8,1,192]{2,1,0:T(1,128)} %get-tuple-element.28.mask_ref, bf16[8,64,1024]{2,1,0:T(8,128)(2,1)} %bitcast.44, bf16[32,64,1024]{2,1,0:T(8,128)(2,1)} %bitcast.7.refs_0_.refs_1_.refs_2_.refs_3_.refs_4_.refs_5_.refs_6_.refs_7_.refs_8_.refs_9_.refs_10_.refs_11_, ...), custom_call_target="tpu_custom_call" | custom-call | flops 7247757312 | bytes 15728640 | tf_op jit(solution)/shard_map/pallas_call | solution.py:184
  (51 shorter events, 2.2 us)
Async XLA Ops:
  0.0 11.2 %copy-start.1 = (bf16[512,1024]{1,0:T(8,128)(2,1)S(1)}, bf16[512,1024]{1,0:T(8,128)(2,1)}, u32[]{:S(2)}) copy-start(bf16[512,1024]{1,0:T(8,128)(2,1)} %param.8) | copy-start | bytes 3145732
  0.0 10.1 %copy-start.5 = (s32[256,3]{0,1:T(4,128)S(1)}, s32[256,3]{0,1:T(4,128)}, u32[]{:S(2)}) copy-start(s32[256,3]{0,1:T(4,128)} %param.12) | copy-start | bytes 9220
  0.0 10.6 %copy-start.6 = (s32[256,3]{0,1:T(4,128)S(1)}, s32[256,3]{0,1:T(4,128)}, u32[]{:S(2)}) copy-start(s32[256,3]{0,1:T(4,128)} %param.13) | copy-start | bytes 9220
  4.0 19.2 %all-to-all-start = ((bf16[32,8,1024]{2,1,0:T(8,128)(2,1)}), bf16[32,8,1024]{2,1,0:T(8,128)(2,1)S(1)}, u32[]{:S(2)}, u32[]{:S(2)}) async-start(bf16[32,8,1024]{2,1,0:T(8,128)(2,1)} %divide_convert_fusion), calls=%async_computation | async-start | bytes 1048576 | tf_op jit(solution)/shard_map/all_to_all | solution.py:237
  23.2 0.8 copy-start.3
  24.0 132.0 %all-to-all-start.1 = ((bf16[8,4,64,1024]{3,2,1,0:T(8,128)(2,1)}), bf16[8,4,64,1024]{3,2,1,0:T(8,128)(2,1)}, u32[]{:S(2)}, u32[]{:S(2)}) async-start(bf16[8,4,64,1024]{3,2,1,0:T(8,128)(2,1)} %bitcast.30), calls=%async_computation.1 | async-start | bytes 8388608 | tf_op jit(solution)/shard_map/all_to_all | solution.py:239
  31.0 6.9 %copy-start = (s32[256]{0:T(256)S(1)}, s32[256]{0:T(256)}, u32[]{:S(2)}) copy-start(s32[256]{0:T(256)} %param.11) | copy-start | bytes 3076
  31.7 93.8 %collective-permute-start.1 = (bf16[64,1024]{1,0:T(8,128)(2,1)S(1)}, bf16[64,1024]{1,0:T(8,128)(2,1)S(1)}, u32[]{:S(2)}, u32[]{:S(2)}) collective-permute-start(bf16[64,1024]{1,0:T(8,128)(2,1)S(1)} %get-tuple-element.23), channel_id=1, source_target_pairs={{1,0},{2,1},{3,2},{4,3},{5,4},{6,5},{7,6},{8,7},{9,8},{10,9},{11,1... | collective-permute-start | bytes 393224 | tf_op jit(solution)/shard_map/ppermute | solution.py:223
  35.1 90.2 %collective-permute-start = (bf16[64,1024]{1,0:T(8,128)(2,1)}, bf16[64,1024]{1,0:T(8,128)(2,1)S(1)}, u32[]{:S(2)}, u32[]{:S(2)}) collective-permute-start(bf16[64,1024]{1,0:T(8,128)(2,1)} %get-tuple-element.24), channel_id=1, source_target_pairs={{0,1},{1,2},{2,3},{3,4},{4,5},{5,6},{6,7},{7,8},{8,9},{9,10},{10,1... | collective-permute-start | bytes 393224 | tf_op jit(solution)/shard_map/ppermute | solution.py:222
  67.8 57.7 %copy-start.2 = (bf16[1024,16,1,64]{0,3,2,1:T(8,128)(2,1)S(1)}, bf16[1024,16,1,64]{0,3,2,1:T(8,128)(2,1)}, u32[]{:S(2)}) copy-start(bf16[1024,16,1,64]{0,3,2,1:T(8,128)(2,1)} %get-tuple-element.21) | copy-start | bytes 6291460
  128.1 2.6 %copy-start.4 = (bf16[32,8,1024]{2,1,0:T(8,128)(2,1)S(1)}, bf16[32,8,1024]{2,1,0:T(8,128)(2,1)}, u32[]{:S(2)}) copy-start(bf16[32,8,1024]{2,1,0:T(8,128)(2,1)} %copy-done.3) | copy-start | bytes 1572868
